TPU v7x, 128 devices: a whole 4x4x4 slice. The times are simulated.
128 devices in a mesh: oy: 8 (over x, core), ox: 16 (over y, z).
Axes of the slice: x: 4, y: 4, z: 4, core: 2. Of those that a mesh axis runs over, the one named last changes fastest.
Arguments:
- atm_flux: float32 [8, 256, 1024], P(None, ('oy', 'ox')), may hold values from -6 to 6
- remap_index: int32 [4, 512, 4096], P(None, 'oy', 'ox'), may hold values from 0 to 2447, as said below
- remap_weight: float32 [4, 512, 4096], P(None, 'oy', 'ox'), may hold values from 0.1 to 1
- coupling: float32 [2, 8], replicated, may hold values from -0.3 to 0.3
- land_mask: int32 [512, 4096], P('oy', 'ox'), may hold values 0 or 1
- tracers: float32 [2, 16, 512, 4096], P(None, None, 'oy', 'ox'), may hold values from -6 to 6
- u_vel: bfloat16 [16, 512, 4096], P(None, 'oy', 'ox'), may hold values from -0.23925781 to 0.23925781
- v_vel: bfloat16 [16, 512, 4096], P(None, 'oy', 'ox'), may hold values from -0.23925781 to 0.23925781
Outputs:
- ocean_flux: float32 [8, 512, 4096], P(None, 'oy', 'ox')
- new_tracers: float32 [2, 16, 512, 4096], P(None, None, 'oy', 'ox')
Inputs may be any that keep to these rules, and one draw needn't show every extreme that they name: `remap_index`: each index lies within 2 rows and 2 columns of the atmosphere cell below its ocean cell in the tile's block padded by 2 on each side, flattened row by row with 68 per row.
All inputs are finite; a program needn't handle non-finite values. No bound on the sum of `land_mask` on one device may be relied on, other than what follows from the above.
Results may differ from a plain program's by a relative error of at most 0.0003.
Values sent between devices are 32-bit elements; how exact they have to be, the bound alone decides.
No kernel may reach another device: no remote copies, remote signals or barrier semaphores. Data moves between devices by JAX's collectives and lax.ppermute only.
A program may use at most 128 MiB of HBM per device.

v0:
```python
import jax
import jax.numpy as jnp
from jax import lax
from jax.sharding import PartitionSpec as P
from jax.experimental import pallas as pl
from jax.experimental.pallas import tpu as pltpu

H = 2
STEPS = 8
WIDE = 8
LANES = 384
HIGH = lax.Precision.HIGHEST


def with_halo(cells, sides, width, closed):
    for axis, dim in sides:
        count = lax.axis_size(axis)
        ends = count if closed else count - 1
        head = lax.slice_in_dim(cells, 0, width, axis=dim)
        tail = lax.slice_in_dim(cells, cells.shape[dim] - width, cells.shape[dim], axis=dim)
        cells = jnp.concatenate(
            [
                lax.ppermute(tail, axis, [(i, (i + 1) % count) for i in range(ends)]),
                cells,
                lax.ppermute(head, axis, [((i + 1) % count, i) for i in range(ends)]),
            ],
            axis=dim,
        )
    return cells


def extend(blocks, flips):
    rows_n = lax.axis_size("oy")
    cols_n = lax.axis_size("ox")
    on_top = lax.axis_index("oy") == rows_n - 1
    sizes = [b.shape[0] for b in blocks]
    sign = jnp.concatenate(
        [jnp.full((n,), -1.0 if neg else 1.0, jnp.float32) for n, neg in zip(sizes, flips)]
    )[:, None, None]
    own = jnp.concatenate(blocks, axis=0) if len(blocks) > 1 else blocks[0]
    tops = own[:, -WIDE:, :]
    bots = own[:, :WIDE, :]
    south = lax.ppermute(tops, "oy", [(i, i + 1) for i in range(rows_n - 1)])
    north = lax.ppermute(bots, "oy", [(i + 1, i) for i in range(rows_n - 1)])
    top_row = (rows_n - 1) * cols_n
    fold = lax.ppermute(
        tops,
        ("oy", "ox"),
        [(top_row + (cols_n // 2 - j) % cols_n, top_row + j) for j in range(cols_n)],
    )
    north = jnp.where(on_top, fold[:, ::-1, ::-1] * sign, north)
    easts = jnp.concatenate([own[..., -WIDE:], north[..., -WIDE:], south[..., -WIDE:]], axis=1)
    wests = jnp.concatenate([own[..., :WIDE], north[..., :WIDE], south[..., :WIDE]], axis=1)
    from_w = lax.ppermute(easts, "ox", [(i, (i + 1) % cols_n) for i in range(cols_n)])
    from_e = lax.ppermute(wests, "ox", [((i + 1) % cols_n, i) for i in range(cols_n)])
    out = []
    at = 0
    for b, n in zip(blocks, sizes):
        rows = jnp.concatenate([b, north[at:at + n], south[at:at + n]], axis=1)
        gap = jnp.zeros(rows.shape[:-1] + (LANES - b.shape[-1] - 2 * WIDE,), b.dtype)
        out.append(jnp.concatenate([rows, from_e[at:at + n], gap, from_w[at:at + n]], axis=-1))
        at += n
    return out


def stencil_kernel(s_ref, u_ref, v_ref, m_ref, f_ref, o_ref, buf, cw, ce, cs, cn, cc, m8, mf):
    nt, nk, rows, lanes = s_ref.shape
    mask = m_ref[...]
    m8[...] = mask * 0.08
    for t in range(nt):
        mf[t] = mask * f_ref[t]

    def coef(k, carry):
        u = u_ref[k]
        v = v_ref[k]
        up = jnp.maximum(u, 0.0)
        um = jnp.minimum(u, 0.0)
        vp = jnp.maximum(v, 0.0)
        vm = jnp.minimum(v, 0.0)
        cw[k] = mask * (up + 0.08)
        ce[k] = mask * (0.08 - um)
        cs[k] = mask * (vp + 0.08)
        cn[k] = mask * (0.08 - vm)
        cc[k] = mask * ((um - up) + (vm - vp) - 0.48)
        return carry

    lax.fori_loop(0, nk, coef, 0)
    buf[0] = s_ref[...]

    def plane(src, dst, t, k, above, below, forced):
        s = buf[src, t, k]
        west = pltpu.roll(s, 1, 1)
        east = pltpu.roll(s, lanes - 1, 1)
        south = pltpu.roll(s, 1, 0)
        north = pltpu.roll(s, rows - 1, 0)
        if above is None:
            above = s
        if below is None:
            below = s
        tend = cw[k] * west + ce[k] * east + cs[k] * south + cn[k] * north + cc[k] * s
        tend = tend + m8[...] * (above + below)
        if forced:
            tend = tend + mf[t]
        buf[dst, t, k] = s + tend

    def step(i, carry):
        src = i % 2
        dst = 1 - src
        for t in range(nt):
            plane(src, dst, t, 0, None, buf[src, t, 1], True)

            def mid(k, c):
                plane(src, dst, t, k, buf[src, t, k - 1], buf[src, t, k + 1], False)
                return c

            lax.fori_loop(1, nk - 1, mid, 0)
            plane(src, dst, t, nk - 1, buf[src, t, nk - 2], None, False)
        return carry

    lax.fori_loop(0, STEPS, step, 0)
    o_ref[...] = buf[STEPS % 2, :, :, : o_ref.shape[2], : o_ref.shape[3]]


def evolve(state, u_x, v_x, m_x, f_x, out_rows, out_cols):
    nt, nk, rows, lanes = state.shape
    plane = (rows, lanes)
    return pl.pallas_call(
        stencil_kernel,
        out_shape=jax.ShapeDtypeStruct((nt, nk, out_rows, out_cols), jnp.float32),
        scratch_shapes=[
            pltpu.VMEM((2, nt, nk) + plane, jnp.float32),
            pltpu.VMEM((nk,) + plane, jnp.float32),
            pltpu.VMEM((nk,) + plane, jnp.float32),
            pltpu.VMEM((nk,) + plane, jnp.float32),
            pltpu.VMEM((nk,) + plane, jnp.float32),
            pltpu.VMEM((nk,) + plane, jnp.float32),
            pltpu.VMEM(plane, jnp.float32),
            pltpu.VMEM((nt,) + plane, jnp.float32),
        ],
        compiler_params=pltpu.CompilerParams(vmem_limit_bytes=60 * 1024 * 1024),
    )(state, u_x, v_x, m_x, f_x)


def remap(padded, remap_index, remap_weight):
    nf, arows, acols = padded.shape
    kk, orows, ocols = remap_index.shape
    base_r = jnp.arange(orows, dtype=jnp.int32) * (arows - 2 * H - 1) // (orows - 1) + H
    base_c = jnp.arange(ocols, dtype=jnp.int32) * (acols - 2 * H - 1) // (ocols - 1) + H
    offs = jnp.arange(2 * H + 1, dtype=jnp.int32) - H
    pick_r = (
        (base_r[None, :, None] + offs[:, None, None])
        == jnp.arange(arows, dtype=jnp.int32)[None, None, :]
    ).astype(jnp.float32).reshape(-1, arows)
    pick_c = (
        jnp.arange(acols, dtype=jnp.int32)[:, None, None]
        == (base_c[None, None, :] + offs[None, :, None])
    ).astype(jnp.float32).reshape(acols, -1)
    lifted = jnp.einsum("pa,fab->fpb", pick_r, padded, precision=HIGH)
    window = jnp.einsum("fpb,bq->fpq", lifted, pick_c, precision=HIGH)
    window = window.reshape(nf, 2 * H + 1, orows, 2 * H + 1, ocols)
    row_of = remap_index // acols - base_r[None, :, None] + H
    col_of = remap_index % acols - base_c[None, None, :] + H
    inside = (row_of >= 0) & (row_of <= 2 * H) & (col_of >= 0) & (col_of <= 2 * H)
    slot = jnp.where(inside, row_of * (2 * H + 1) + col_of, -1)
    slots = jnp.arange((2 * H + 1) ** 2, dtype=jnp.int32)
    wsum = jnp.sum(
        jnp.where(slot[:, None] == slots[None, :, None, None], remap_weight[:, None], 0.0),
        axis=0,
    ).reshape(2 * H + 1, 2 * H + 1, orows, ocols)
    fast = jnp.sum(window * wsum.transpose(0, 2, 1, 3)[None], axis=(1, 3))
    missed = jnp.logical_not(jnp.all(inside))

    def general():
        flat = padded.reshape(nf, -1)
        total = jnp.zeros((nf,) + remap_index.shape[1:], jnp.float32)
        for source in range(kk):
            picked = jnp.take(flat, remap_index[source], axis=1)
            total = total + remap_weight[source][None] * picked
        return total

    return lax.cond(missed, general, lambda: fast)


def on_device(atm_flux, remap_index, remap_weight, coupling, land_mask, tracers, u_vel, v_vel):
    lev = tracers.shape[1]
    fields = [
        tracers.reshape((-1,) + tracers.shape[2:]),
        u_vel.astype(jnp.float32),
        v_vel.astype(jnp.float32),
        land_mask.astype(jnp.float32)[None],
    ]
    state, u_x, v_x, m_x = extend(fields, [False, True, True, False])
    state = state.reshape((-1, lev) + state.shape[1:])

    atm_tile = lax.all_to_all(atm_flux, "ox", split_axis=2, concat_axis=1, tiled=True)
    lon_wide = with_halo(atm_tile, (("ox", 2),), H, True)
    padded = with_halo(lon_wide, (("oy", 1),), H, False)
    ocean_flux = remap(padded, remap_index, remap_weight)
    forcing = jnp.einsum("tf,frc->trc", coupling, ocean_flux, precision=HIGH)
    (f_x,) = extend([forcing], [False])
    rows, cols = tracers.shape[-2:]
    final = evolve(state, u_x, v_x, m_x[0], f_x, rows, cols)
    return (ocean_flux, final)


def solution(mesh):
    placed = (
        P(None, ("oy", "ox"), None),
        P(None, "oy", "ox"),
        P(None, "oy", "ox"),
        P(),
        P("oy", "ox"),
        P(None, None, "oy", "ox"),
        P(None, "oy", "ox"),
        P(None, "oy", "ox"),
    )
    return jax.shard_map(
        on_device,
        mesh=mesh,
        in_specs=placed,
        out_specs=(P(None, "oy", "ox"), P(None, None, "oy", "ox")),
        check_vma=False,
    )
```

profile of v0, /device:TPU:1, one launch (start us, length us, event | category | flops | bytes accessed | tf_op | source)
XLA Modules:
  0.0 225.3 jit_solution(13329397842085235100)
XLA Ops:
  7.1 4.5 %collective-permute-start.6 = (f32[65,8,256]{2,1,0:T(8,128)}, f32[65,8,256]{2,1,0:T(8,128)}, u32[]{:S(2)}, u32[]{:S(2)}) collective-permute-start(f32[65,8,256]{2,1,0:T(8,128)} %get-tuple-element.64), channel_id=1, source_target_pairs={{0,16},{16,32},{32,48},{48,64},{64,80},{80,96},{96,112},{1,17},{17... | collective-permute-start | bytes 1597448 | tf_op jit(solution)/shard_map/ppermute | solution.py:43
  11.6 2.0 copy.104
  13.6 3.5 %reshape.182 = f32[16,1,1024]{2,1,0:T(1,128)} reshape(f32[1024,2,8]{2,1,0:T(2,128)} %bitcast.116) | data formatting | bytes 131072
  17.0 7.8 %all-to-all-start = ((f32[16,1,1024]{2,1,0:T(1,128)}), f32[16,1,1024]{2,1,0:T(1,128)}, u32[]{:S(2)}, u32[]{:S(2)}) async-start(f32[16,1,1024]{2,1,0:T(1,128)} %reshape.182), calls=%async_computation | async-start | bytes 131072 | tf_op jit(solution)/shard_map/all_to_all | solution.py:195
  24.8 1.9 collective-permute-start.5
  28.6 3.0 %select_reduce_fusion = f32[25,64,256]{2,1,0:T(8,128)} fusion(f32[4,64,256]{2,1,0:T(8,128)} %param.14, s32[4,64,256]{2,1,0:T(8,128)S(1)} %get-tuple-element.47), kind=kLoop, calls=%fused_computation.32 | loop fusion | flops 4505600 | bytes 2162688 | tf_op jit(solution)/shard_map/reduce_sum | solution.py:166
  33.8 2.6 %reshape.183 = f32[1024,2,8]{2,1,0:T(2,128)} reshape(f32[16,1024]{1,0:T(8,128)S(1)} %reduce.4) | data formatting | bytes 131072
  39.4 3.4 %collective-permute-start.1 = (f32[8,32,2]{2,1,0:T(8,128)S(1)}, f32[8,32,2]{2,1,0:T(8,128)S(1)}, u32[]{:S(2)}, u32[]{:S(2)}) collective-permute-start(f32[8,32,2]{2,1,0:T(8,128)S(1)} %get-tuple-element.84), channel_id=1, source_target_pairs={{1,0},{2,1},{3,2},{4,3},{5,4},{6,5},{7,6},{8,7},{9,8},{10,9},{11,1... | collective-permute-start | bytes 6152 | tf_op jit(solution)/shard_map/ppermute | solution.py:25
  42.8 3.9 %pad_maximum_fusion = f32[65,64,256]{2,1,0:T(8,128)} fusion(f32[1,64,256]{2,1,0:T(8,128)S(1)} %convert_bitcast_fusion, f32[16,64,256]{2,1,0:T(8,128)} %copy-done.4, f32[16,64,256]{2,1,0:T(8,128)S(1)} %convert_element_type.15, f32[32,64,256]{2,1,0:T(8,128)S(1)} %bitcast.106), kind=kLoop, calls=%fused_computation.34 | loop fusion | flops 3194880 | bytes 8519680 | tf_op jit(solution)/shard_map/concatenate | solution.py:40
  47.5 4.2 %collective-permute-start.2 = (f32[8,2,68]{2,1,0:T(2,128)S(1)}, f32[8,2,68]{2,1,0:T(2,128)S(1)}, u32[]{:S(2)}, u32[]{:S(2)}) collective-permute-start(f32[8,2,68]{2,1,0:T(2,128)S(1)} %get-tuple-element.73), channel_id=1, source_target_pairs={{0,16},{16,32},{32,48},{48,64},{64,80},{80,96},{96,112},{1,17},{17... | collective-permute-start | bytes 13064 | tf_op jit(solution)/shard_map/ppermute | solution.py:23
  51.7 1.9 collective-permute-start.3
  62.8 9.2 %fusion.7 = f32[8,5,64,5,256]{4,2,3,1,0:T(8,128)} fusion(f32[8,5,64,68,1]{3,2,4,1,0:T(8,128)S(1)} %bitcast.109, pred[5,256,68,1,1]{1,0,2,4,3:T(8,128)(4,1)} %bitcast.123), kind=kOutput, calls=%fused_computation.45 | convolution fusion | flops 2673868800 | bytes 13890560 | tf_op jit(solution)/shard_map/fpb,bq->fpq/dot_general | solution.py:159
  71.9 11.1 %conditional.1 = (f32[8,64,256]{0,2,1:T(8,128)}) conditional(s32[]{:T(128)} %convert_element_type.14, (f32[5,64,5,256]{3,1,2,0:T(8,128)S(1)}, f32[8,5,64,5,256]{4,2,3,1,0:T(8,128)}) %tuple.57, (f32[4,64,256]{2,1,0:T(8,128)}, f32[8,36,68]{2,1,0:T(8,128)}, s32[4,64,256]{2,1,0:T(8,128)}) %tuple.58), branch_computations={%region_2.4_spmd, %region_4.6_spmd} | conditional | flops 6422528 | bytes 16318472 | solution.py:181
  71.9 6.4 %multiply_reduce_fusion = f32[8,64,256]{2,1,0:T(8,128)S(1)} fusion(f32[8,5,64,5,256]{4,2,3,1,0:T(8,128)} %get-tuple-element.19, f32[5,64,5,256]{3,1,2,0:T(8,128)S(1)} %get-tuple-element.20), kind=kLoop, calls=%fused_computation.4 | loop fusion | flops 6422528 | bytes 15269888 | tf_op jit(solution)/shard_map/reduce_sum | solution.py:170
  78.3 4.7 %copy.99 = f32[8,64,256]{0,2,1:T(8,128)} copy(f32[8,64,256]{2,1,0:T(8,128)S(1)} %multiply_reduce_fusion) | data formatting | bytes 1048576 | tf_op jit(solution)/shard_map/reduce_sum | solution.py:170
  83.0 10.7 %fusion.17 = f32[64,256,2]{1,2,0:T(2,128)S(1)} fusion(f32[8,64,256]{0,2,1:T(8,128)} %get-tuple-element.91, f32[2,8]{1,0:T(2,128)S(1)} %copy-done), kind=kOutput, calls=%fused_computation.76 | convolution fusion | flops 3145728 | bytes 655424 | tf_op jit(solution)/shard_map/tf,frc->trc/dot_general | solution.py:199
  94.4 1.9 collective-permute-start.10
  96.4 3.7 %collective-permute-start.11 = (f32[2,8,256]{2,1,0:T(8,128)S(1)}, f32[2,8,256]{2,1,0:T(8,128)S(1)}, u32[]{:S(2)}, u32[]{:S(2)}) collective-permute-start(f32[2,8,256]{2,1,0:T(8,128)S(1)} %get-tuple-element.82), channel_id=1, source_target_pairs={{0,16},{16,32},{32,48},{48,64},{64,80},{80,96},{96,112},{1,17},{17... | collective-permute-start | bytes 49160 | tf_op jit(solution)/shard_map/ppermute | solution.py:43
  101.0 4.2 %collective-permute-start.12 = (f32[2,80,8]{2,1,0:T(8,128)S(1)}, f32[2,80,8]{2,1,0:T(8,128)S(1)}, u32[]{:S(2)}, u32[]{:S(2)}) collective-permute-start(f32[2,80,8]{2,1,0:T(8,128)S(1)} %pad_maximum_fusion.10), channel_id=1, source_target_pairs={{1,0},{2,1},{3,2},{4,3},{5,4},{6,5},{7,6},{8,7},{9,8},{10,9},{11,1... | collective-permute-start | bytes 15368 | tf_op jit(solution)/shard_map/ppermute | solution.py:55
  105.5 5.1 %fusion.21 = (f32[65,64,8]{2,1,0:T(8,128)}, f32[65,64,8]{2,1,0:T(8,128)}) fusion(f32[65,64,256]{2,1,0:T(8,128)} %pad_maximum_fusion), kind=kLoop, calls=%fused_computation.81 | loop fusion | bytes 532480 | tf_op jit(solution)/shard_map/slice | solution.py:53
  110.6 2.9 %copy.108 = f32[65,64,8]{1,2,0:T(8,128)} copy(f32[65,64,8]{2,1,0:T(8,128)} %get-tuple-element.61) | data formatting | bytes 266240 | tf_op jit(solution)/shard_map/slice | solution.py:53
  113.5 2.2 copy.111
  115.7 5.9 %copy.124 = f32[8,64,256]{2,1,0:T(8,128)} copy(f32[8,64,256]{0,2,1:T(8,128)} %get-tuple-element.91) | data formatting | bytes 1048576
  128.3 1.9 fusion.25
  130.2 1.8 copy.110
  132.0 1.9 pad_maximum_fusion.6
  133.9 4.8 %collective-permute-start.7 = (f32[65,80,8]{1,2,0:T(8,128)}, f32[65,80,8]{1,2,0:T(8,128)}, u32[]{:S(2)}, u32[]{:S(2)}) collective-permute-start(f32[65,80,8]{1,2,0:T(8,128)} %pad_maximum_fusion.6), channel_id=1, source_target_pairs={{1,0},{2,1},{3,2},{4,3},{5,4},{6,5},{7,6},{8,7},{9,8},{10,9},{11,1... | collective-permute-start | bytes 499208 | tf_op jit(solution)/shard_map/ppermute | solution.py:55
  147.0 5.8 %collective-permute-done.8 = f32[65,80,8]{1,2,0:T(8,128)S(1)} collective-permute-done((f32[65,80,8]{1,2,0:T(8,128)}, f32[65,80,8]{1,2,0:T(8,128)S(1)}, u32[]{:S(2)}, u32[]{:S(2)}) %collective-permute-start.8) | collective-permute-done | bytes 166432 | tf_op jit(solution)/shard_map/ppermute | solution.py:54
  162.0 2.4 %copy.115 = f32[32,80,8]{2,1,0:T(8,128)} copy(f32[32,80,8]{1,2,0:T(8,128)} %slice.187) | data formatting | bytes 163840 | tf_op jit(solution)/shard_map/slice | solution.py:61
  165.9 4.0 %pad_maximum_fusion.1 = f32[32,80,384]{2,1,0:T(8,128)} fusion(f32[32,80,8]{2,1,0:T(8,128)} %copy.115, f32[32,80,8]{2,1,0:T(8,128)S(1)} %copy.114, f32[32,8,256]{2,1,0:T(8,128)} %slice.179, f32[32,8,256]{2,1,0:T(8,128)} %slice.178, f32[32,64,256]{2,1,0:T(8,128)S(1)} %bitcast.107, f32[384]{0:T(512)S(1)} %pad.34.clone), kind=kLoop, calls=%fused_computation.35 | loop fusion | flops 4915200 | bytes 6718976 | tf_op jit(solution)/shard_map/concatenate | solution.py:61
  170.0 2.5 %pad_maximum_fusion.3 = (f32[16,80,384]{2,1,0:T(8,128)}, f32[16,80,384]{2,1,0:T(8,128)}) fusion(f32[16,80,8]{2,1,0:T(8,128)S(1)} %copy-done.11, f32[16,80,8]{2,1,0:T(8,128)S(1)} %copy-done.10, f32[16,8,256]{2,1,0:T(8,128)S(1)} %copy-done.16, f32[16,8,256]{2,1,0:T(8,128)S(1)} %copy-done.14, f32[16,64,256]{2,1,0:T(8,128)S(1)} %copy-done.5, ...), kind=kLoop, calls=%fused_computation.37 | loop fusion | flops 4915200 | bytes 6718976 | tf_op jit(solution)/shard_map/concatenate | solution.py:61
  172.5 52.8 %shard_map.95 = f32[2,16,64,256]{3,2,1,0:T(8,128)} custom-call(f32[2,16,80,384]{3,2,1,0:T(8,128)} %bitcast.108, f32[16,80,384]{2,1,0:T(8,128)} %get-tuple-element.90.u_ref, f32[16,80,384]{2,1,0:T(8,128)} %get-tuple-element.89.v_ref, f32[80,384]{1,0:T(8,128)} %maximum_bitcast_fusion.m_ref, f32[2,80,384]{2,1,0:T(8,128)} %pad_maximum_fusion.8.f_ref), custom_call_target="tpu_custom_call" | custom-call | tf_op jit(solution)/shard_map/pallas_call | solution.py:127
  (130 shorter events, 50.3 us)
Async XLA Ops:
  0.6 82.4 %copy-start = (f32[2,8]{1,0:T(2,128)S(1)}, f32[2,8]{1,0:T(2,128)}, u32[]{:S(2)}) copy-start(f32[2,8]{1,0:T(2,128)} %param.15) | copy-start | bytes 196
  2.0 40.9 %copy-start.2 = (f32[16,64,256]{2,1,0:T(8,128)}, f32[16,64,256]{2,1,0:T(8,128)S(1)}, u32[]{:S(2)}) copy-start(f32[16,64,256]{2,1,0:T(8,128)S(1)} %convert_element_type.15) | copy-start | bytes 3145732
  4.5 23.1 %copy-start.12 = (s32[4,64,256]{2,1,0:T(8,128)S(1)}, s32[4,64,256]{2,1,0:T(8,128)}, u32[]{:S(2)}) copy-start(s32[4,64,256]{2,1,0:T(8,128)} %param.13) | copy-start | bytes 786436
  5.6 116.8 %collective-permute-start.4 = (f32[65,8,256]{2,1,0:T(8,128)}, f32[65,8,256]{2,1,0:T(8,128)}, u32[]{:S(2)}, u32[]{:S(2)}) collective-permute-start(f32[65,8,256]{2,1,0:T(8,128)} %get-tuple-element.64), channel_id=1, source_target_pairs={{120,112},{119,113},{118,114},{117,115},{116,116},{115,117},{114,1... | collective-permute-start | bytes 1597448 | tf_op jit(solution)/shard_map/ppermute | solution.py:46
  7.1 121.2 %collective-permute-start.6 = (f32[65,8,256]{2,1,0:T(8,128)}, f32[65,8,256]{2,1,0:T(8,128)}, u32[]{:S(2)}, u32[]{:S(2)}) collective-permute-start(f32[65,8,256]{2,1,0:T(8,128)} %get-tuple-element.64), channel_id=1, source_target_pairs={{0,16},{16,32},{32,48},{48,64},{64,80},{80,96},{96,112},{1,17},{17... | collective-permute-start | bytes 1597448 | tf_op jit(solution)/shard_map/ppermute | solution.py:43
  17.0 14.6 %all-to-all-start = ((f32[16,1,1024]{2,1,0:T(1,128)}), f32[16,1,1024]{2,1,0:T(1,128)}, u32[]{:S(2)}, u32[]{:S(2)}) async-start(f32[16,1,1024]{2,1,0:T(1,128)} %reshape.182), calls=%async_computation | async-start | bytes 131072 | tf_op jit(solution)/shard_map/all_to_all | solution.py:195
  24.8 98.8 %collective-permute-start.5 = (f32[65,8,256]{2,1,0:T(8,128)}, f32[65,8,256]{2,1,0:T(8,128)}, u32[]{:S(2)}, u32[]{:S(2)}) collective-permute-start(f32[65,8,256]{2,1,0:T(8,128)} %get-tuple-element.63), channel_id=1, source_target_pairs={{16,0},{32,16},{48,32},{64,48},{80,64},{96,80},{112,96},{17,1},{33... | collective-permute-start | bytes 1597448 | tf_op jit(solution)/shard_map/ppermute | solution.py:44
  38.0 8.8 %collective-permute-start = (f32[8,32,2]{2,1,0:T(8,128)S(1)}, f32[8,32,2]{2,1,0:T(8,128)S(1)}, u32[]{:S(2)}, u32[]{:S(2)}) collective-permute-start(f32[8,32,2]{2,1,0:T(8,128)S(1)} %get-tuple-element.83), channel_id=1, source_target_pairs={{0,1},{1,2},{2,3},{3,4},{4,5},{5,6},{6,7},{7,8},{8,9},{9,10},{10,1... | collective-permute-start | bytes 6152 | tf_op jit(solution)/shard_map/ppermute | solution.py:23
  39.4 7.3 %collective-permute-start.1 = (f32[8,32,2]{2,1,0:T(8,128)S(1)}, f32[8,32,2]{2,1,0:T(8,128)S(1)}, u32[]{:S(2)}, u32[]{:S(2)}) collective-permute-start(f32[8,32,2]{2,1,0:T(8,128)S(1)} %get-tuple-element.84), channel_id=1, source_target_pairs={{1,0},{2,1},{3,2},{4,3},{5,4},{6,5},{7,6},{8,7},{9,8},{10,9},{11,1... | collective-permute-start | bytes 6152 | tf_op jit(solution)/shard_map/ppermute | solution.py:25
  47.5 10.4 %collective-permute-start.2 = (f32[8,2,68]{2,1,0:T(2,128)S(1)}, f32[8,2,68]{2,1,0:T(2,128)S(1)}, u32[]{:S(2)}, u32[]{:S(2)}) collective-permute-start(f32[8,2,68]{2,1,0:T(2,128)S(1)} %get-tuple-element.73), channel_id=1, source_target_pairs={{0,16},{16,32},{32,48},{48,64},{64,80},{80,96},{96,112},{1,17},{17... | collective-permute-start | bytes 13064 | tf_op jit(solution)/shard_map/ppermute | solution.py:23
  51.7 6.2 %collective-permute-start.3 = (f32[8,2,68]{2,1,0:T(2,128)S(1)}, f32[8,2,68]{2,1,0:T(2,128)S(1)}, u32[]{:S(2)}, u32[]{:S(2)}) collective-permute-start(f32[8,2,68]{2,1,0:T(2,128)S(1)} %get-tuple-element.74), channel_id=1, source_target_pairs={{16,0},{32,16},{48,32},{64,48},{80,64},{96,80},{112,96},{17,1},{33... | collective-permute-start | bytes 13064 | tf_op jit(solution)/shard_map/ppermute | solution.py:25
  62.7 9.2 %copy-start.6 = (f32[25,64,256]{2,1,0:T(8,128)S(1)}, f32[25,64,256]{2,1,0:T(8,128)}, u32[]{:S(2)}) copy-start(f32[25,64,256]{2,1,0:T(8,128)} %select_reduce_fusion) | copy-start | bytes 4915204
  93.7 2.7 %collective-permute-start.9 = (f32[2,8,256]{2,1,0:T(8,128)S(1)}, f32[2,8,256]{2,1,0:T(8,128)S(1)}, u32[]{:S(2)}, u32[]{:S(2)}) collective-permute-start(f32[2,8,256]{2,1,0:T(8,128)S(1)} %get-tuple-element.82), channel_id=1, source_target_pairs={{120,112},{119,113},{118,114},{117,115},{116,116},{115,117},{114,1... | collective-permute-start | bytes 49160 | tf_op jit(solution)/shard_map/ppermute | solution.py:46
  94.4 5.8 %collective-permute-start.10 = (f32[2,8,256]{2,1,0:T(8,128)S(1)}, f32[2,8,256]{2,1,0:T(8,128)S(1)}, u32[]{:S(2)}, u32[]{:S(2)}) collective-permute-start(f32[2,8,256]{2,1,0:T(8,128)S(1)} %get-tuple-element.81), channel_id=1, source_target_pairs={{16,0},{32,16},{48,32},{64,48},{80,64},{96,80},{112,96},{17,1},{33... | collective-permute-start | bytes 49160 | tf_op jit(solution)/shard_map/ppermute | solution.py:44
  96.4 4.5 %collective-permute-start.11 = (f32[2,8,256]{2,1,0:T(8,128)S(1)}, f32[2,8,256]{2,1,0:T(8,128)S(1)}, u32[]{:S(2)}, u32[]{:S(2)}) collective-permute-start(f32[2,8,256]{2,1,0:T(8,128)S(1)} %get-tuple-element.82), channel_id=1, source_target_pairs={{0,16},{16,32},{32,48},{48,64},{64,80},{80,96},{96,112},{1,17},{17... | collective-permute-start | bytes 49160 | tf_op jit(solution)/shard_map/ppermute | solution.py:43
  101.0 20.6 %collective-permute-start.12 = (f32[2,80,8]{2,1,0:T(8,128)S(1)}, f32[2,80,8]{2,1,0:T(8,128)S(1)}, u32[]{:S(2)}, u32[]{:S(2)}) collective-permute-start(f32[2,80,8]{2,1,0:T(8,128)S(1)} %pad_maximum_fusion.10), channel_id=1, source_target_pairs={{1,0},{2,1},{3,2},{4,3},{5,4},{6,5},{7,6},{8,7},{9,8},{10,9},{11,1... | collective-permute-start | bytes 15368 | tf_op jit(solution)/shard_map/ppermute | solution.py:55
  105.2 16.4 %collective-permute-start.13 = (f32[2,80,8]{2,1,0:T(8,128)S(1)}, f32[2,80,8]{2,1,0:T(8,128)S(1)}, u32[]{:S(2)}, u32[]{:S(2)}) collective-permute-start(f32[2,80,8]{2,1,0:T(8,128)S(1)} %pad_maximum_fusion.11), channel_id=1, source_target_pairs={{0,1},{1,2},{2,3},{3,4},{4,5},{5,6},{6,7},{7,8},{8,9},{9,10},{10,1... | collective-permute-start | bytes 15368 | tf_op jit(solution)/shard_map/ppermute | solution.py:54
  115.7 8.0 %copy-start.20 = (f32[65]{0:T(128)S(1)}, f32[65]{0:T(128)}, u32[]{:S(2)}) copy-start(f32[65]{0:T(128)} %constant.81.clone.1) | copy-start | bytes 784
  124.9 18.3 %copy-start.7 = (f32[65,8,256]{2,1,0:T(8,128)}, f32[65,8,256]{2,1,0:T(8,128)S(1)}, u32[]{:S(2)}) copy-start(f32[65,8,256]{2,1,0:T(8,128)S(1)} %multiply_select_fusion) | copy-start | bytes 1597444
  133.9 11.1 %collective-permute-start.7 = (f32[65,80,8]{1,2,0:T(8,128)}, f32[65,80,8]{1,2,0:T(8,128)}, u32[]{:S(2)}, u32[]{:S(2)}) collective-permute-start(f32[65,80,8]{1,2,0:T(8,128)} %pad_maximum_fusion.6), channel_id=1, source_target_pairs={{1,0},{2,1},{3,2},{4,3},{5,4},{6,5},{7,6},{8,7},{9,8},{10,9},{11,1... | collective-permute-start | bytes 499208 | tf_op jit(solution)/shard_map/ppermute | solution.py:55
  140.8 11.9 %collective-permute-start.8 = (f32[65,80,8]{1,2,0:T(8,128)}, f32[65,80,8]{1,2,0:T(8,128)S(1)}, u32[]{:S(2)}, u32[]{:S(2)}) collective-permute-start(f32[65,80,8]{1,2,0:T(8,128)} %pad_maximum_fusion.7), channel_id=1, source_target_pairs={{0,1},{1,2},{2,3},{3,4},{4,5},{5,6},{6,7},{7,8},{8,9},{9,10},{10,1... | collective-permute-start | bytes 499208 | tf_op jit(solution)/shard_map/ppermute | solution.py:54
  144.9 19.5 %slice-start = ((f32[65,8,256]{2,1,0:T(8,128)}), f32[1,8,256]{2,1,0:T(8,128)S(1)}, s32[]{:S(2)}) async-start(f32[65,8,256]{2,1,0:T(8,128)} %copy-done.7), calls=%async_computation.1 | async-start | bytes 16384 | tf_op jit(solution)/shard_map/slice | solution.py:59
  152.7 4.8 %copy-start.19 = (f32[65,80,8]{1,2,0:T(8,128)}, f32[65,80,8]{1,2,0:T(8,128)S(1)}, u32[]{:S(2)}) copy-start(f32[65,80,8]{1,2,0:T(8,128)S(1)} %collective-permute-done.8) | copy-start | bytes 499204
  165.9 4.1 %copy-start.5 = (f32[16,64,256]{2,1,0:T(8,128)S(1)}, f32[16,64,256]{2,1,0:T(8,128)}, u32[]{:S(2)}) copy-start(f32[16,64,256]{2,1,0:T(8,128)} %copy-done.4) | copy-start | bytes 3145732
  165.9 4.1 %copy-start.8 = (f32[16,80,8]{2,1,0:T(8,128)S(1)}, f32[16,80,8]{2,1,0:T(8,128)}, u32[]{:S(2)}) copy-start(f32[16,80,8]{2,1,0:T(8,128)} %copy.116) | copy-start | bytes 122884
  165.9 4.1 %copy-start.9 = (f32[16,80,8]{2,1,0:T(8,128)S(1)}, f32[16,80,8]{2,1,0:T(8,128)}, u32[]{:S(2)}) copy-start(f32[16,80,8]{2,1,0:T(8,128)} %copy.117) | copy-start | bytes 122884
  165.9 4.1 %copy-start.10 = (f32[16,80,8]{2,1,0:T(8,128)S(1)}, f32[16,80,8]{2,1,0:T(8,128)}, u32[]{:S(2)}) copy-start(f32[16,80,8]{2,1,0:T(8,128)} %copy.118) | copy-start | bytes 122884
  165.9 4.1 %copy-start.11 = (f32[16,80,8]{2,1,0:T(8,128)S(1)}, f32[16,80,8]{2,1,0:T(8,128)}, u32[]{:S(2)}) copy-start(f32[16,80,8]{2,1,0:T(8,128)} %copy.119) | copy-start | bytes 122884
  165.9 4.1 %copy-start.14 = (f32[16,8,256]{2,1,0:T(8,128)S(1)}, f32[16,8,256]{2,1,0:T(8,128)}, u32[]{:S(2)}) copy-start(f32[16,8,256]{2,1,0:T(8,128)} %get-tuple-element.65) | copy-start | bytes 393220
  165.9 4.1 %copy-start.15 = (f32[16,8,256]{2,1,0:T(8,128)S(1)}, f32[16,8,256]{2,1,0:T(8,128)}, u32[]{:S(2)}) copy-start(f32[16,8,256]{2,1,0:T(8,128)} %get-tuple-element.66) | copy-start | bytes 393220
  165.9 4.1 %copy-start.16 = (f32[16,8,256]{2,1,0:T(8,128)S(1)}, f32[16,8,256]{2,1,0:T(8,128)}, u32[]{:S(2)}) copy-start(f32[16,8,256]{2,1,0:T(8,128)} %get-tuple-element.67) | copy-start | bytes 393220
  165.9 4.1 %copy-start.17 = (f32[16,8,256]{2,1,0:T(8,128)S(1)}, f32[16,8,256]{2,1,0:T(8,128)}, u32[]{:S(2)}) copy-start(f32[16,8,256]{2,1,0:T(8,128)} %get-tuple-element.68) | copy-start | bytes 393220
  (5 other events, 10.4 us)
where the time goes:
time: 228 us; the launch traced here: 225 us
  local copies, waits for them, and re-layouts  63.6 us (28%)
  Pallas kernels  52.8 us (23%)
  starting transfers between devices  42.2 us (19%)
  other arithmetic  37.1 us (16%)
  matrix products  21.3 us (9%)
  waiting for transfers between devices  6.49 us (3%)
    pallas_call x1, Pallas kernels, evolve(): pl.pallas_call(stencil_kernel, out_shape=jax.ShapeDtypeStruct((nt, nk, ou...  52.8 us
    unnamed x46, local copies, waits for them, and re-layouts  15.4 us
    dot_general x1, matrix products, on_device(): forcing = jnp.einsum('tf,frc->trc', coupling, ocean_flux, precision=HIGH)  10.7 us
    dot_general x1, matrix products, remap(): window = jnp.einsum('fpb,bq->fpq', lifted, pick_c, precision=HIGH)  9.16 us
    ppermute x2, starting transfers between devices, extend(): lax.ppermute(wests, 'ox', [((i + 1) % cols_n, i) for i in range(cols_n)])  8.96 us
    ppermute x2, starting transfers between devices, extend(): south = lax.ppermute(tops, 'oy', [(i, i + 1) for i in range(rows_n - 1)])  8.15 us
    slice x3, local copies, waits for them, and re-layouts, extend(): own[..., :WIDE]  8.04 us
    all_to_all x1, starting transfers between devices, on_device(): lax.all_to_all(atm_flux, 'ox', split_axis=2, concat_axis=1, tiled=True)  7.82 us
  transfers between devices with their start and end apart: 15, of which 3 were waited for; matrix products, arithmetic and copies ran while one was open for 40% of the time, Pallas kernels for 0%

commit v1 on v0

--- a/solution.py
+++ b/solution.py
@@ -87,34 +87,47 @@
     lax.fori_loop(0, nk, coef, 0)
     buf[0] = s_ref[...]
 
-    def plane(src, dst, t, k, above, below, forced):
-        s = buf[src, t, k]
-        west = pltpu.roll(s, 1, 1)
-        east = pltpu.roll(s, lanes - 1, 1)
-        south = pltpu.roll(s, 1, 0)
-        north = pltpu.roll(s, rows - 1, 0)
-        if above is None:
-            above = s
-        if below is None:
-            below = s
-        tend = cw[k] * west + ce[k] * east + cs[k] * south + cn[k] * north + cc[k] * s
-        tend = tend + m8[...] * (above + below)
-        if forced:
-            tend = tend + mf[t]
-        buf[dst, t, k] = s + tend
+    strips = rows // 8
+
+    def plane(src, dst, k, above, below, forced):
+        for i in range(strips):
+            r0 = i * 8
+            rp = (i - 1) % strips * 8
+            rn = (i + 1) % strips * 8
+            at = pl.ds(r0, 8)
+            c_w = cw[k, at, :]
+            c_e = ce[k, at, :]
+            c_s = cs[k, at, :]
+            c_n = cn[k, at, :]
+            c_c = cc[k, at, :]
+            c_8 = m8[at, :]
+            for t in range(nt):
+                cur = buf[src, t, k, at, :]
+                prev = buf[src, t, k, pl.ds(rp, 8), :]
+                nxt = buf[src, t, k, pl.ds(rn, 8), :]
+                south = pltpu.roll(jnp.concatenate([prev, cur], axis=0), 1, 0)[8:]
+                north = pltpu.roll(jnp.concatenate([cur, nxt], axis=0), 15, 0)[:8]
+                west = pltpu.roll(cur, 1, 1)
+                east = pltpu.roll(cur, lanes - 1, 1)
+                up = cur if above is None else buf[src, t, above, at, :]
+                down = cur if below is None else buf[src, t, below, at, :]
+                tend = c_w * west + c_e * east + c_s * south + c_n * north + c_c * cur
+                tend = tend + c_8 * (up + down)
+                if forced:
+                    tend = tend + mf[t, at, :]
+                buf[dst, t, k, at, :] = cur + tend
 
     def step(i, carry):
         src = i % 2
         dst = 1 - src
-        for t in range(nt):
-            plane(src, dst, t, 0, None, buf[src, t, 1], True)
-
-            def mid(k, c):
-                plane(src, dst, t, k, buf[src, t, k - 1], buf[src, t, k + 1], False)
-                return c
-
-            lax.fori_loop(1, nk - 1, mid, 0)
-            plane(src, dst, t, nk - 1, buf[src, t, nk - 2], None, False)
+        plane(src, dst, 0, None, 1, True)
+
+        def mid(k, c):
+            plane(src, dst, k, k - 1, k + 1, False)
+            return c
+
+        lax.fori_loop(1, nk - 1, mid, 0)
+        plane(src, dst, nk - 1, nk - 2, None, False)
         return carry
 
     lax.fori_loop(0, STEPS, step, 0)
@@ -196,7 +209,7 @@
     lon_wide = with_halo(atm_tile, (("ox", 2),), H, True)
     padded = with_halo(lon_wide, (("oy", 1),), H, False)
     ocean_flux = remap(padded, remap_index, remap_weight)
-    forcing = jnp.einsum("tf,frc->trc", coupling, ocean_flux, precision=HIGH)
+    forcing = jnp.sum(coupling[:, :, None, None] * ocean_flux[None], axis=1)
     (f_x,) = extend([forcing], [False])
     rows, cols = tracers.shape[-2:]
     final = evolve(state, u_x, v_x, m_x[0], f_x, rows, cols)

time: 228 us -> 350 us (1.54)
  Pallas kernels: 52.8 us -> 193 us
  matrix products: 21.3 us -> 10.7 us
  local copies, waits for them, and re-layouts: 63.6 us -> 53.2 us
    pallas_call x1, Pallas kernels: 52.8 us -> 193 us  [evolve(): pl.pallas_call(stencil_kernel, out_shape=jax.ShapeDtypeStruct((nt, nk, ou...]
    dot_general x1 -> x0, matrix products: 10.7 us -> none  [on_device(): forcing = jnp.einsum('tf,frc->trc', coupling, ocean_flux, precision=HIGH)]
    unnamed x46 -> x47, local copies, waits for them, and re-layouts: 15.4 us -> 9.54 us
    reduce_sum x1 -> x0, local copies, waits for them, and re-layouts: 4.66 us -> none  [remap(): fast = jnp.sum(window * wsum.transpose(0, 2, 1, 3)[None], axis=(1, 3))]
  transfers between devices with their start and end apart: 15 -> 15, of which waited for: 3 -> 3; matrix products, arithmetic and copies ran while one was open for 40% -> 21% of each run, Pallas kernels for 0% -> 0%
where the time goes in v1:
time: 350 us; the launch traced here: 347 us
  Pallas kernels  193 us (55%)
  local copies, waits for them, and re-layouts  53.2 us (15%)
  starting transfers between devices  42.2 us (12%)
  other arithmetic  39.1 us (11%)
  matrix products  10.7 us (3%)
  waiting for transfers between devices  6.48 us (2%)
    pallas_call x1, Pallas kernels, evolve(): pl.pallas_call(stencil_kernel, out_shape=jax.ShapeDtypeStruct((nt, nk, ou...  193 us
    unnamed x47, local copies, waits for them, and re-layouts  9.54 us
    dot_general x1, matrix products, remap(): window = jnp.einsum('fpb,bq->fpq', lifted, pick_c, precision=HIGH)  9.22 us
    ppermute x2, starting transfers between devices, extend(): lax.ppermute(wests, 'ox', [((i + 1) % cols_n, i) for i in range(cols_n)])  9.2 us
    ppermute x2, starting transfers between devices, extend(): south = lax.ppermute(tops, 'oy', [(i, i + 1) for i in range(rows_n - 1)])  8.14 us
    slice x3, local copies, waits for them, and re-layouts, extend(): own[..., :WIDE]  8.11 us
    all_to_all x1, starting transfers between devices, on_device(): lax.all_to_all(atm_flux, 'ox', split_axis=2, concat_axis=1, tiled=True)  7.82 us
    reduce_sum x1, other arithmetic, remap(): fast = jnp.sum(window * wsum.transpose(0, 2, 1, 3)[None], axis=(1, 3))  7.38 us
  transfers between devices with their start and end apart: 15, of which 3 were waited for; matrix products, arithmetic and copies ran while one was open for 21% of the time, Pallas kernels for 0%

profile of v1, /device:TPU:1, one launch (start us, length us, event | category | flops | bytes accessed | tf_op | source)
XLA Modules:
  0.0 346.7 jit_solution(8699303853251424001)
XLA Ops:
  7.1 4.5 %collective-permute-start.6 = (f32[65,8,256]{2,1,0:T(8,128)}, f32[65,8,256]{2,1,0:T(8,128)}, u32[]{:S(2)}, u32[]{:S(2)}) collective-permute-start(f32[65,8,256]{2,1,0:T(8,128)} %get-tuple-element.65), channel_id=1, source_target_pairs={{0,16},{16,32},{32,48},{48,64},{64,80},{80,96},{96,112},{1,17},{17... | collective-permute-start | bytes 1597448 | tf_op jit(solution)/shard_map/ppermute | solution.py:43
  11.6 2.0 copy.100
  13.6 3.5 reshape.183
  17.0 7.8 %all-to-all-start = ((f32[16,1,1024]{2,1,0:T(1,128)}), f32[16,1,1024]{2,1,0:T(1,128)}, u32[]{:S(2)}, u32[]{:S(2)}) async-start(f32[16,1,1024]{2,1,0:T(1,128)} %reshape.183), calls=%async_computation | async-start | bytes 131072 | tf_op jit(solution)/shard_map/all_to_all | solution.py:208
  24.8 1.9 collective-permute-start.5
  28.7 3.0 select_reduce_fusion
  33.8 2.6 reshape.184
  39.5 3.4 collective-permute-start.1
  42.9 3.7 %pad_maximum_fusion = f32[65,64,256]{2,1,0:T(8,128)} fusion(f32[1,64,256]{2,1,0:T(8,128)S(1)} %convert_bitcast_fusion, f32[16,64,256]{2,1,0:T(8,128)} %copy-done.3, f32[16,64,256]{2,1,0:T(8,128)S(1)} %convert_element_type.15, f32[32,64,256]{2,1,0:T(8,128)S(1)} %bitcast.99), kind=kLoop, calls=%fused_computation.34 | loop fusion | flops 3194880 | bytes 8519680 | tf_op jit(solution)/shard_map/concatenate | solution.py:40
  47.3 4.2 %collective-permute-start.2 = (f32[8,2,68]{2,1,0:T(2,128)S(1)}, f32[8,2,68]{2,1,0:T(2,128)S(1)}, u32[]{:S(2)}, u32[]{:S(2)}) collective-permute-start(f32[8,2,68]{2,1,0:T(2,128)S(1)} %get-tuple-element.74), channel_id=1, source_target_pairs={{0,16},{16,32},{32,48},{48,64},{64,80},{80,96},{96,112},{1,17},{17... | collective-permute-start | bytes 13064 | tf_op jit(solution)/shard_map/ppermute | solution.py:23
  51.5 1.9 collective-permute-start.3
  53.6 1.8 eq.65
  62.6 9.2 %fusion.7 = f32[8,5,64,5,256]{4,2,3,1,0:T(8,128)} fusion(f32[8,5,64,68,1]{3,2,4,1,0:T(8,128)S(1)} %bitcast.102, pred[5,256,68,1,1]{1,0,2,4,3:T(8,128)(4,1)} %bitcast.113), kind=kOutput, calls=%fused_computation.46 | convolution fusion | flops 2673868800 | bytes 13890560 | tf_op jit(solution)/shard_map/fpb,bq->fpq/dot_general | solution.py:172
  71.8 7.6 %conditional.1 = (f32[8,64,256]{2,1,0:T(8,128)}) conditional(s32[]{:T(128)} %convert_element_type.14, (f32[5,64,5,256]{3,1,2,0:T(8,128)S(1)}, f32[8,5,64,5,256]{4,2,3,1,0:T(8,128)}) %tuple.59, (f32[4,64,256]{2,1,0:T(8,128)}, f32[8,36,68]{2,1,0:T(8,128)}, s32[4,64,256]{2,1,0:T(8,128)S(1)}) %tuple.61), branch_computations={%region_2.4_spmd, %region_4.6_spmd} | conditional | flops 6422528 | bytes 15269896 | solution.py:194
  72.0 7.4 %multiply_reduce_fusion = f32[8,64,256]{2,1,0:T(8,128)} fusion(f32[8,5,64,5,256]{4,2,3,1,0:T(8,128)} %get-tuple-element.19, f32[5,64,5,256]{3,1,2,0:T(8,128)S(1)} %get-tuple-element.20), kind=kLoop, calls=%fused_computation.4 | loop fusion | flops 6422528 | bytes 15269888 | tf_op jit(solution)/shard_map/reduce_sum | solution.py:183
  81.3 1.9 collective-permute-start.10
  83.3 3.6 %collective-permute-start.11 = (f32[2,8,256]{2,1,0:T(8,128)S(1)}, f32[2,8,256]{2,1,0:T(8,128)S(1)}, u32[]{:S(2)}, u32[]{:S(2)}) collective-permute-start(f32[2,8,256]{2,1,0:T(8,128)S(1)} %get-tuple-element.83), channel_id=1, source_target_pairs={{0,16},{16,32},{32,48},{48,64},{64,80},{80,96},{96,112},{1,17},{17... | collective-permute-start | bytes 49160 | tf_op jit(solution)/shard_map/ppermute | solution.py:43
  87.9 4.4 %collective-permute-start.12 = (f32[2,80,8]{2,1,0:T(8,128)S(1)}, f32[2,80,8]{2,1,0:T(8,128)S(1)}, u32[]{:S(2)}, u32[]{:S(2)}) collective-permute-start(f32[2,80,8]{2,1,0:T(8,128)S(1)} %pad_maximum_fusion.10), channel_id=1, source_target_pairs={{1,0},{2,1},{3,2},{4,3},{5,4},{6,5},{7,6},{8,7},{9,8},{10,9},{11,1... | collective-permute-start | bytes 15368 | tf_op jit(solution)/shard_map/ppermute | solution.py:55
  92.4 5.1 %fusion.19 = (f32[65,64,8]{2,1,0:T(8,128)}, f32[65,64,8]{2,1,0:T(8,128)}) fusion(f32[65,64,256]{2,1,0:T(8,128)} %pad_maximum_fusion), kind=kLoop, calls=%fused_computation.79 | loop fusion | bytes 532480 | tf_op jit(solution)/shard_map/slice | solution.py:53
  97.5 2.9 copy.104
  100.4 2.2 copy.107
  109.4 1.9 fusion.23
  111.3 1.8 copy.106
  113.1 1.9 pad_maximum_fusion.6
  115.0 4.8 %collective-permute-start.7 = (f32[65,80,8]{1,2,0:T(8,128)}, f32[65,80,8]{1,2,0:T(8,128)}, u32[]{:S(2)}, u32[]{:S(2)}) collective-permute-start(f32[65,80,8]{1,2,0:T(8,128)} %pad_maximum_fusion.6), channel_id=1, source_target_pairs={{1,0},{2,1},{3,2},{4,3},{5,4},{6,5},{7,6},{8,7},{9,8},{10,9},{11,1... | collective-permute-start | bytes 499208 | tf_op jit(solution)/shard_map/ppermute | solution.py:55
  122.7 1.7 slice.179
  124.3 1.7 fusion.21
  128.1 5.8 %collective-permute-done.8 = f32[65,80,8]{1,2,0:T(8,128)S(1)} collective-permute-done((f32[65,80,8]{1,2,0:T(8,128)}, f32[65,80,8]{1,2,0:T(8,128)S(1)}, u32[]{:S(2)}, u32[]{:S(2)}) %collective-permute-start.8) | collective-permute-done | bytes 166432 | tf_op jit(solution)/shard_map/ppermute | solution.py:54
  143.2 2.4 copy.111
  147.2 4.0 %pad_maximum_fusion.1 = f32[32,80,384]{2,1,0:T(8,128)} fusion(f32[32,80,8]{2,1,0:T(8,128)} %copy.111, f32[32,80,8]{2,1,0:T(8,128)S(1)} %copy.110, f32[32,8,256]{2,1,0:T(8,128)} %slice.179, f32[32,8,256]{2,1,0:T(8,128)} %slice.178, f32[32,64,256]{2,1,0:T(8,128)S(1)} %bitcast.100, f32[384]{0:T(512)S(1)} %pad.34.clone), kind=kLoop, calls=%fused_computation.35 | loop fusion | flops 4915200 | bytes 6718976 | tf_op jit(solution)/shard_map/concatenate | solution.py:61
  151.2 2.5 pad_maximum_fusion.3
  153.7 193.0 %shard_map.95 = f32[2,16,64,256]{3,2,1,0:T(8,128)} custom-call(f32[2,16,80,384]{3,2,1,0:T(8,128)} %bitcast.101, f32[16,80,384]{2,1,0:T(8,128)} %get-tuple-element.91.u_ref, f32[16,80,384]{2,1,0:T(8,128)} %get-tuple-element.90.v_ref, f32[80,384]{1,0:T(8,128)} %maximum_bitcast_fusion.m_ref, f32[2,80,384]{2,1,0:T(8,128)} %pad_maximum_fusion.8.f_ref), custom_call_target="tpu_custom_call" | custom-call | tf_op jit(solution)/shard_map/pallas_call | solution.py:140
  (129 shorter events, 46.3 us)
Async XLA Ops:
  1.9 40.9 %copy-start.1 = (f32[16,64,256]{2,1,0:T(8,128)}, f32[16,64,256]{2,1,0:T(8,128)S(1)}, u32[]{:S(2)}) copy-start(f32[16,64,256]{2,1,0:T(8,128)S(1)} %convert_element_type.15) | copy-start | bytes 3145732
  4.5 23.1 %copy-start.11 = (s32[4,64,256]{2,1,0:T(8,128)S(1)}, s32[4,64,256]{2,1,0:T(8,128)}, u32[]{:S(2)}) copy-start(s32[4,64,256]{2,1,0:T(8,128)} %param.13) | copy-start | bytes 786436
  5.6 97.9 %collective-permute-start.4 = (f32[65,8,256]{2,1,0:T(8,128)}, f32[65,8,256]{2,1,0:T(8,128)}, u32[]{:S(2)}, u32[]{:S(2)}) collective-permute-start(f32[65,8,256]{2,1,0:T(8,128)} %get-tuple-element.65), channel_id=1, source_target_pairs={{120,112},{119,113},{118,114},{117,115},{116,116},{115,117},{114,1... | collective-permute-start | bytes 1597448 | tf_op jit(solution)/shard_map/ppermute | solution.py:46
  7.1 102.3 %collective-permute-start.6 = (f32[65,8,256]{2,1,0:T(8,128)}, f32[65,8,256]{2,1,0:T(8,128)}, u32[]{:S(2)}, u32[]{:S(2)}) collective-permute-start(f32[65,8,256]{2,1,0:T(8,128)} %get-tuple-element.65), channel_id=1, source_target_pairs={{0,16},{16,32},{32,48},{48,64},{64,80},{80,96},{96,112},{1,17},{17... | collective-permute-start | bytes 1597448 | tf_op jit(solution)/shard_map/ppermute | solution.py:43
  17.0 14.7 %all-to-all-start = ((f32[16,1,1024]{2,1,0:T(1,128)}), f32[16,1,1024]{2,1,0:T(1,128)}, u32[]{:S(2)}, u32[]{:S(2)}) async-start(f32[16,1,1024]{2,1,0:T(1,128)} %reshape.183), calls=%async_computation | async-start | bytes 131072 | tf_op jit(solution)/shard_map/all_to_all | solution.py:208
  24.8 79.9 %collective-permute-start.5 = (f32[65,8,256]{2,1,0:T(8,128)}, f32[65,8,256]{2,1,0:T(8,128)}, u32[]{:S(2)}, u32[]{:S(2)}) collective-permute-start(f32[65,8,256]{2,1,0:T(8,128)} %get-tuple-element.64), channel_id=1, source_target_pairs={{16,0},{32,16},{48,32},{64,48},{80,64},{96,80},{112,96},{17,1},{33... | collective-permute-start | bytes 1597448 | tf_op jit(solution)/shard_map/ppermute | solution.py:44
  38.0 8.5 %collective-permute-start = (f32[8,32,2]{2,1,0:T(8,128)S(1)}, f32[8,32,2]{2,1,0:T(8,128)S(1)}, u32[]{:S(2)}, u32[]{:S(2)}) collective-permute-start(f32[8,32,2]{2,1,0:T(8,128)S(1)} %get-tuple-element.84), channel_id=1, source_target_pairs={{0,1},{1,2},{2,3},{3,4},{4,5},{5,6},{6,7},{7,8},{8,9},{9,10},{10,1... | collective-permute-start | bytes 6152 | tf_op jit(solution)/shard_map/ppermute | solution.py:23
  39.5 7.1 %collective-permute-start.1 = (f32[8,32,2]{2,1,0:T(8,128)S(1)}, f32[8,32,2]{2,1,0:T(8,128)S(1)}, u32[]{:S(2)}, u32[]{:S(2)}) collective-permute-start(f32[8,32,2]{2,1,0:T(8,128)S(1)} %get-tuple-element.85), channel_id=1, source_target_pairs={{1,0},{2,1},{3,2},{4,3},{5,4},{6,5},{7,6},{8,7},{9,8},{10,9},{11,1... | collective-permute-start | bytes 6152 | tf_op jit(solution)/shard_map/ppermute | solution.py:25
  47.3 10.4 %collective-permute-start.2 = (f32[8,2,68]{2,1,0:T(2,128)S(1)}, f32[8,2,68]{2,1,0:T(2,128)S(1)}, u32[]{:S(2)}, u32[]{:S(2)}) collective-permute-start(f32[8,2,68]{2,1,0:T(2,128)S(1)} %get-tuple-element.74), channel_id=1, source_target_pairs={{0,16},{16,32},{32,48},{48,64},{64,80},{80,96},{96,112},{1,17},{17... | collective-permute-start | bytes 13064 | tf_op jit(solution)/shard_map/ppermute | solution.py:23
  51.5 6.2 %collective-permute-start.3 = (f32[8,2,68]{2,1,0:T(2,128)S(1)}, f32[8,2,68]{2,1,0:T(2,128)S(1)}, u32[]{:S(2)}, u32[]{:S(2)}) collective-permute-start(f32[8,2,68]{2,1,0:T(2,128)S(1)} %get-tuple-element.75), channel_id=1, source_target_pairs={{16,0},{32,16},{48,32},{64,48},{80,64},{96,80},{112,96},{17,1},{33... | collective-permute-start | bytes 13064 | tf_op jit(solution)/shard_map/ppermute | solution.py:25
  62.5 9.2 %copy-start.5 = (f32[25,64,256]{2,1,0:T(8,128)S(1)}, f32[25,64,256]{2,1,0:T(8,128)}, u32[]{:S(2)}) copy-start(f32[25,64,256]{2,1,0:T(8,128)} %select_reduce_fusion) | copy-start | bytes 4915204
  62.6 9.2 %copy-start.12 = (s32[4,64,256]{2,1,0:T(8,128)S(1)}, s32[4,64,256]{2,1,0:T(8,128)}, u32[]{:S(2)}) copy-start(s32[4,64,256]{2,1,0:T(8,128)} %param.13) | copy-start | bytes 786436
  71.8 7.6 %copy-start.21 = (f32[2,8]{1,0:T(2,128)S(1)}, f32[2,8]{1,0:T(2,128)}, u32[]{:S(2)}) copy-start(f32[2,8]{1,0:T(2,128)} %param.15) | copy-start | bytes 196
  80.6 2.7 collective-permute-start.9
  81.3 5.8 %collective-permute-start.10 = (f32[2,8,256]{2,1,0:T(8,128)S(1)}, f32[2,8,256]{2,1,0:T(8,128)S(1)}, u32[]{:S(2)}, u32[]{:S(2)}) collective-permute-start(f32[2,8,256]{2,1,0:T(8,128)S(1)} %get-tuple-element.82), channel_id=1, source_target_pairs={{16,0},{32,16},{48,32},{64,48},{80,64},{96,80},{112,96},{17,1},{33... | collective-permute-start | bytes 49160 | tf_op jit(solution)/shard_map/ppermute | solution.py:44
  83.3 4.5 %collective-permute-start.11 = (f32[2,8,256]{2,1,0:T(8,128)S(1)}, f32[2,8,256]{2,1,0:T(8,128)S(1)}, u32[]{:S(2)}, u32[]{:S(2)}) collective-permute-start(f32[2,8,256]{2,1,0:T(8,128)S(1)} %get-tuple-element.83), channel_id=1, source_target_pairs={{0,16},{16,32},{32,48},{48,64},{64,80},{80,96},{96,112},{1,17},{17... | collective-permute-start | bytes 49160 | tf_op jit(solution)/shard_map/ppermute | solution.py:43
  87.9 14.8 %collective-permute-start.12 = (f32[2,80,8]{2,1,0:T(8,128)S(1)}, f32[2,80,8]{2,1,0:T(8,128)S(1)}, u32[]{:S(2)}, u32[]{:S(2)}) collective-permute-start(f32[2,80,8]{2,1,0:T(8,128)S(1)} %pad_maximum_fusion.10), channel_id=1, source_target_pairs={{1,0},{2,1},{3,2},{4,3},{5,4},{6,5},{7,6},{8,7},{9,8},{10,9},{11,1... | collective-permute-start | bytes 15368 | tf_op jit(solution)/shard_map/ppermute | solution.py:55
  92.3 10.4 %collective-permute-start.13 = (f32[2,80,8]{2,1,0:T(8,128)S(1)}, f32[2,80,8]{2,1,0:T(8,128)S(1)}, u32[]{:S(2)}, u32[]{:S(2)}) collective-permute-start(f32[2,80,8]{2,1,0:T(8,128)S(1)} %pad_maximum_fusion.11), channel_id=1, source_target_pairs={{0,1},{1,2},{2,3},{3,4},{4,5},{5,6},{6,7},{7,8},{8,9},{9,10},{10,1... | collective-permute-start | bytes 15368 | tf_op jit(solution)/shard_map/ppermute | solution.py:54
  97.5 7.3 %copy-start.22 = (f32[65]{0:T(128)S(1)}, f32[65]{0:T(128)}, u32[]{:S(2)}) copy-start(f32[65]{0:T(128)} %constant.81.clone.1) | copy-start | bytes 784
  106.0 18.3 %copy-start.6 = (f32[65,8,256]{2,1,0:T(8,128)}, f32[65,8,256]{2,1,0:T(8,128)S(1)}, u32[]{:S(2)}) copy-start(f32[65,8,256]{2,1,0:T(8,128)S(1)} %multiply_select_fusion) | copy-start | bytes 1597444
  115.0 11.1 %collective-permute-start.7 = (f32[65,80,8]{1,2,0:T(8,128)}, f32[65,80,8]{1,2,0:T(8,128)}, u32[]{:S(2)}, u32[]{:S(2)}) collective-permute-start(f32[65,80,8]{1,2,0:T(8,128)} %pad_maximum_fusion.6), channel_id=1, source_target_pairs={{1,0},{2,1},{3,2},{4,3},{5,4},{6,5},{7,6},{8,7},{9,8},{10,9},{11,1... | collective-permute-start | bytes 499208 | tf_op jit(solution)/shard_map/ppermute | solution.py:55
  122.0 11.9 %collective-permute-start.8 = (f32[65,80,8]{1,2,0:T(8,128)}, f32[65,80,8]{1,2,0:T(8,128)S(1)}, u32[]{:S(2)}, u32[]{:S(2)}) collective-permute-start(f32[65,80,8]{1,2,0:T(8,128)} %pad_maximum_fusion.7), channel_id=1, source_target_pairs={{0,1},{1,2},{2,3},{3,4},{4,5},{5,6},{6,7},{7,8},{8,9},{9,10},{10,1... | collective-permute-start | bytes 499208 | tf_op jit(solution)/shard_map/ppermute | solution.py:54
  126.0 19.6 %slice-start = ((f32[65,8,256]{2,1,0:T(8,128)}), f32[1,8,256]{2,1,0:T(8,128)S(1)}, s32[]{:S(2)}) async-start(f32[65,8,256]{2,1,0:T(8,128)} %copy-done.6), calls=%async_computation.1 | async-start | bytes 16384 | tf_op jit(solution)/shard_map/slice | solution.py:59
  133.9 4.9 %copy-start.20 = (f32[65,80,8]{1,2,0:T(8,128)}, f32[65,80,8]{1,2,0:T(8,128)S(1)}, u32[]{:S(2)}) copy-start(f32[65,80,8]{1,2,0:T(8,128)S(1)} %collective-permute-done.8) | copy-start | bytes 499204
  147.1 4.1 %copy-start.7 = (f32[16,80,8]{2,1,0:T(8,128)S(1)}, f32[16,80,8]{2,1,0:T(8,128)}, u32[]{:S(2)}) copy-start(f32[16,80,8]{2,1,0:T(8,128)} %copy.112) | copy-start | bytes 122884
  147.1 4.1 %copy-start.8 = (f32[16,80,8]{2,1,0:T(8,128)S(1)}, f32[16,80,8]{2,1,0:T(8,128)}, u32[]{:S(2)}) copy-start(f32[16,80,8]{2,1,0:T(8,128)} %copy.113) | copy-start | bytes 122884
  147.1 4.1 %copy-start.9 = (f32[16,80,8]{2,1,0:T(8,128)S(1)}, f32[16,80,8]{2,1,0:T(8,128)}, u32[]{:S(2)}) copy-start(f32[16,80,8]{2,1,0:T(8,128)} %copy.114) | copy-start | bytes 122884
  147.1 4.1 %copy-start.10 = (f32[16,80,8]{2,1,0:T(8,128)S(1)}, f32[16,80,8]{2,1,0:T(8,128)}, u32[]{:S(2)}) copy-start(f32[16,80,8]{2,1,0:T(8,128)} %copy.115) | copy-start | bytes 122884
  147.1 4.1 %copy-start.15 = (f32[16,8,256]{2,1,0:T(8,128)S(1)}, f32[16,8,256]{2,1,0:T(8,128)}, u32[]{:S(2)}) copy-start(f32[16,8,256]{2,1,0:T(8,128)} %get-tuple-element.66) | copy-start | bytes 393220
  147.1 4.1 %copy-start.16 = (f32[16,8,256]{2,1,0:T(8,128)S(1)}, f32[16,8,256]{2,1,0:T(8,128)}, u32[]{:S(2)}) copy-start(f32[16,8,256]{2,1,0:T(8,128)} %get-tuple-element.67) | copy-start | bytes 393220
  147.1 4.1 %copy-start.17 = (f32[16,8,256]{2,1,0:T(8,128)S(1)}, f32[16,8,256]{2,1,0:T(8,128)}, u32[]{:S(2)}) copy-start(f32[16,8,256]{2,1,0:T(8,128)} %get-tuple-element.68) | copy-start | bytes 393220
  147.1 4.1 %copy-start.18 = (f32[16,8,256]{2,1,0:T(8,128)S(1)}, f32[16,8,256]{2,1,0:T(8,128)}, u32[]{:S(2)}) copy-start(f32[16,8,256]{2,1,0:T(8,128)} %get-tuple-element.69) | copy-start | bytes 393220
  (6 other events, 14.4 us)

commit v2 on v0

--- a/solution.py
+++ b/solution.py
@@ -29,7 +29,7 @@
     return cells
 
 
-def extend(blocks, flips):
+def exchange(blocks, flips):
     rows_n = lax.axis_size("oy")
     cols_n = lax.axis_size("ox")
     on_top = lax.axis_index("oy") == rows_n - 1
@@ -37,9 +37,8 @@
     sign = jnp.concatenate(
         [jnp.full((n,), -1.0 if neg else 1.0, jnp.float32) for n, neg in zip(sizes, flips)]
     )[:, None, None]
-    own = jnp.concatenate(blocks, axis=0) if len(blocks) > 1 else blocks[0]
-    tops = own[:, -WIDE:, :]
-    bots = own[:, :WIDE, :]
+    tops = jnp.concatenate([b[:, -WIDE:, :] for b in blocks], axis=0)
+    bots = jnp.concatenate([b[:, :WIDE, :] for b in blocks], axis=0)
     south = lax.ppermute(tops, "oy", [(i, i + 1) for i in range(rows_n - 1)])
     north = lax.ppermute(bots, "oy", [(i + 1, i) for i in range(rows_n - 1)])
     top_row = (rows_n - 1) * cols_n
@@ -49,30 +48,58 @@
         [(top_row + (cols_n // 2 - j) % cols_n, top_row + j) for j in range(cols_n)],
     )
     north = jnp.where(on_top, fold[:, ::-1, ::-1] * sign, north)
-    easts = jnp.concatenate([own[..., -WIDE:], north[..., -WIDE:], south[..., -WIDE:]], axis=1)
-    wests = jnp.concatenate([own[..., :WIDE], north[..., :WIDE], south[..., :WIDE]], axis=1)
+    easts = jnp.concatenate(
+        [jnp.concatenate([b[..., -WIDE:] for b in blocks], axis=0), north[..., -WIDE:], south[..., -WIDE:]],
+        axis=1,
+    )
+    wests = jnp.concatenate(
+        [jnp.concatenate([b[..., :WIDE] for b in blocks], axis=0), north[..., :WIDE], south[..., :WIDE]],
+        axis=1,
+    )
     from_w = lax.ppermute(easts, "ox", [(i, (i + 1) % cols_n) for i in range(cols_n)])
     from_e = lax.ppermute(wests, "ox", [((i + 1) % cols_n, i) for i in range(cols_n)])
-    out = []
-    at = 0
-    for b, n in zip(blocks, sizes):
-        rows = jnp.concatenate([b, north[at:at + n], south[at:at + n]], axis=1)
-        gap = jnp.zeros(rows.shape[:-1] + (LANES - b.shape[-1] - 2 * WIDE,), b.dtype)
-        out.append(jnp.concatenate([rows, from_e[at:at + n], gap, from_w[at:at + n]], axis=-1))
-        at += n
-    return out
-
-
-def stencil_kernel(s_ref, u_ref, v_ref, m_ref, f_ref, o_ref, buf, cw, ce, cs, cn, cc, m8, mf):
-    nt, nk, rows, lanes = s_ref.shape
-    mask = m_ref[...]
+    gap = jnp.zeros(from_e.shape[:-1] + (LANES - blocks[0].shape[-1] - 2 * WIDE,), jnp.float32)
+    return north, south, jnp.concatenate([from_e, gap, from_w], axis=-1)
+
+
+def stencil_kernel(tr_ref, u_ref, v_ref, m_ref, f_ref, hn_ref, hs_ref, hc_ref, fn_ref, fs_ref, fc_ref,
+                   o_ref, buf, uu, vv, mm, ff, cw, ce, cs, cn, cc, m8, mf):
+    nt, nk, orows, ocols = tr_ref.shape
+    _, planes, rows, lanes = buf.shape
+
+    def place(dst, own, at):
+        dst[:orows, :ocols] = own
+        dst[orows:orows + WIDE, :ocols] = hn_ref[at]
+        dst[orows + WIDE:, :ocols] = hs_ref[at]
+        dst[:, ocols:] = hc_ref[at]
+
+    def fill(p, carry):
+        place(buf.at[0, p], tr_ref[p // nk, p % nk], p)
+        return carry
+
+    lax.fori_loop(0, planes, fill, 0)
+
+    def fill_uv(k, carry):
+        place(uu.at[k], u_ref[k].astype(jnp.float32), planes + k)
+        place(vv.at[k], v_ref[k].astype(jnp.float32), planes + nk + k)
+        return carry
+
+    lax.fori_loop(0, nk, fill_uv, 0)
+    place(mm, m_ref[...].astype(jnp.float32), planes + 2 * nk)
+    for t in range(nt):
+        ff[t, :orows, :ocols] = f_ref[t]
+        ff[t, orows:orows + WIDE, :ocols] = fn_ref[t]
+        ff[t, orows + WIDE:, :ocols] = fs_ref[t]
+        ff[t, :, ocols:] = fc_ref[t]
+
+    mask = mm[...]
     m8[...] = mask * 0.08
     for t in range(nt):
-        mf[t] = mask * f_ref[t]
+        mf[t] = mask * ff[t]
 
     def coef(k, carry):
-        u = u_ref[k]
-        v = v_ref[k]
+        u = uu[k]
+        v = vv[k]
         up = jnp.maximum(u, 0.0)
         um = jnp.minimum(u, 0.0)
         vp = jnp.maximum(v, 0.0)
@@ -85,60 +112,68 @@
         return carry
 
     lax.fori_loop(0, nk, coef, 0)
-    buf[0] = s_ref[...]
 
     def plane(src, dst, t, k, above, below, forced):
-        s = buf[src, t, k]
+        p = t * nk + k
+        s = buf[src, p]
         west = pltpu.roll(s, 1, 1)
         east = pltpu.roll(s, lanes - 1, 1)
         south = pltpu.roll(s, 1, 0)
         north = pltpu.roll(s, rows - 1, 0)
-        if above is None:
-            above = s
-        if below is None:
-            below = s
+        above = s if above is None else buf[src, t * nk + above]
+        below = s if below is None else buf[src, t * nk + below]
         tend = cw[k] * west + ce[k] * east + cs[k] * south + cn[k] * north + cc[k] * s
         tend = tend + m8[...] * (above + below)
         if forced:
             tend = tend + mf[t]
-        buf[dst, t, k] = s + tend
+        buf[dst, p] = s + tend
 
     def step(i, carry):
         src = i % 2
         dst = 1 - src
         for t in range(nt):
-            plane(src, dst, t, 0, None, buf[src, t, 1], True)
+            plane(src, dst, t, 0, None, 1, True)
 
             def mid(k, c):
-                plane(src, dst, t, k, buf[src, t, k - 1], buf[src, t, k + 1], False)
+                plane(src, dst, t, k, k - 1, k + 1, False)
                 return c
 
             lax.fori_loop(1, nk - 1, mid, 0)
-            plane(src, dst, t, nk - 1, buf[src, t, nk - 2], None, False)
+            plane(src, dst, t, nk - 1, nk - 2, None, False)
         return carry
 
     lax.fori_loop(0, STEPS, step, 0)
-    o_ref[...] = buf[STEPS % 2, :, :, : o_ref.shape[2], : o_ref.shape[3]]
-
-
-def evolve(state, u_x, v_x, m_x, f_x, out_rows, out_cols):
-    nt, nk, rows, lanes = state.shape
-    plane = (rows, lanes)
+
+    def out(p, carry):
+        o_ref[p // nk, p % nk] = buf[STEPS % 2, p, :orows, :ocols]
+        return carry
+
+    lax.fori_loop(0, planes, out, 0)
+
+
+def evolve(tracers, u_vel, v_vel, land_mask, forcing, halo, f_halo):
+    nt, nk, orows, ocols = tracers.shape
+    plane = (orows + 2 * WIDE, LANES)
+    vm = lambda *shape: pltpu.VMEM(shape, jnp.float32)
     return pl.pallas_call(
         stencil_kernel,
-        out_shape=jax.ShapeDtypeStruct((nt, nk, out_rows, out_cols), jnp.float32),
+        out_shape=jax.ShapeDtypeStruct(tracers.shape, jnp.float32),
         scratch_shapes=[
-            pltpu.VMEM((2, nt, nk) + plane, jnp.float32),
-            pltpu.VMEM((nk,) + plane, jnp.float32),
-            pltpu.VMEM((nk,) + plane, jnp.float32),
-            pltpu.VMEM((nk,) + plane, jnp.float32),
-            pltpu.VMEM((nk,) + plane, jnp.float32),
-            pltpu.VMEM((nk,) + plane, jnp.float32),
-            pltpu.VMEM(plane, jnp.float32),
-            pltpu.VMEM((nt,) + plane, jnp.float32),
+            vm(2, nt * nk, *plane),
+            vm(nk, *plane),
+            vm(nk, *plane),
+            vm(*plane),
+            vm(nt, *plane),
+            vm(nk, *plane),
+            vm(nk, *plane),
+            vm(nk, *plane),
+            vm(nk, *plane),
+            vm(nk, *plane),
+            vm(*plane),
+            vm(nt, *plane),
         ],
-        compiler_params=pltpu.CompilerParams(vmem_limit_bytes=60 * 1024 * 1024),
-    )(state, u_x, v_x, m_x, f_x)
+        compiler_params=pltpu.CompilerParams(vmem_limit_bytes=62 * 1024 * 1024),
+    )(tracers, u_vel, v_vel, land_mask, forcing, *halo, *f_halo)
 
 
 def remap(padded, remap_index, remap_weight):
@@ -182,24 +217,21 @@
 
 
 def on_device(atm_flux, remap_index, remap_weight, coupling, land_mask, tracers, u_vel, v_vel):
-    lev = tracers.shape[1]
     fields = [
         tracers.reshape((-1,) + tracers.shape[2:]),
         u_vel.astype(jnp.float32),
         v_vel.astype(jnp.float32),
         land_mask.astype(jnp.float32)[None],
     ]
-    state, u_x, v_x, m_x = extend(fields, [False, True, True, False])
-    state = state.reshape((-1, lev) + state.shape[1:])
+    halo = exchange(fields, [False, True, True, False])
 
     atm_tile = lax.all_to_all(atm_flux, "ox", split_axis=2, concat_axis=1, tiled=True)
     lon_wide = with_halo(atm_tile, (("ox", 2),), H, True)
     padded = with_halo(lon_wide, (("oy", 1),), H, False)
     ocean_flux = remap(padded, remap_index, remap_weight)
-    forcing = jnp.einsum("tf,frc->trc", coupling, ocean_flux, precision=HIGH)
-    (f_x,) = extend([forcing], [False])
-    rows, cols = tracers.shape[-2:]
-    final = evolve(state, u_x, v_x, m_x[0], f_x, rows, cols)
+    forcing = jnp.sum(coupling[:, :, None, None] * ocean_flux[None], axis=1)
+    f_halo = exchange([forcing], [False])
+    final = evolve(tracers, u_vel, v_vel, land_mask, forcing, halo, f_halo)
     return (ocean_flux, final)
 
 

time: 228 us -> 172 us (0.75)
  local copies, waits for them, and re-layouts: 63.6 us -> 27.3 us
  matrix products: 21.3 us -> 9.79 us
  other arithmetic: 37.1 us -> 28.1 us
  waiting for transfers between devices: 6.49 us -> 11 us
  Pallas kernels: 52.8 us -> 50.4 us
    slice x34 -> x17, local copies, waits for them, and re-layouts: 36.3 us -> 10.1 us  [the longest x5 4.51 us: exchange(): b[..., :WIDE]]
    dot_general x1 -> x0, matrix products: 10.7 us -> none  [on_device(): forcing = jnp.einsum('tf,frc->trc', coupling, ocean_flux, precision=HIGH)]
    unnamed x46 -> x49, local copies, waits for them, and re-layouts: 15.4 us -> 5.63 us
    reduce_sum x1 -> x0, local copies, waits for them, and re-layouts: 4.66 us -> none  [remap(): fast = jnp.sum(window * wsum.transpose(0, 2, 1, 3)[None], axis=(1, 3))]
    ppermute x10, waiting for transfers between devices: 6.47 us -> 11 us  [the longest x2 6.35 us: exchange(): lax.ppermute(easts, 'ox', [(i, (i + 1) % cols_n) for i in range(cols_n)])]
    concatenate x1 -> x3, local copies, waits for them, and re-layouts: 0.08 us -> 4.3 us  [the longest x1 2.9 us: exchange(): jnp.concatenate([b[..., :WIDE] for b in blocks], axis=0)]
    ppermute x0 -> x2, local copies, waits for them, and re-layouts: none -> 3.09 us  [the longest x1 2.32 us: exchange(): lax.ppermute(easts, 'ox', [(i, (i + 1) % cols_n) for i in range(cols_n)])]
    convert_element_type x2 -> x0, other arithmetic: 2.81 us -> none  [the longest x1 1.52 us: on_device(): v_vel.astype(jnp.float32)]
  transfers between devices with their start and end apart: 15 -> 15, of which waited for: 3 -> 3; matrix products, arithmetic and copies ran while one was open for 40% -> 31% of each run, Pallas kernels for 0% -> 0%
where the time goes in v2:
time: 172 us; the launch traced here: 170 us
  Pallas kernels  50.4 us (29%)
  starting transfers between devices  41.6 us (24%)
  other arithmetic  28.1 us (16%)
  local copies, waits for them, and re-layouts  27.3 us (16%)
  waiting for transfers between devices  11 us (6%)
  matrix products  9.79 us (6%)
  between operations  1.86 us (1%)
    pallas_call x1, Pallas kernels, evolve(): pl.pallas_call(stencil_kernel, out_shape=jax.ShapeDtypeStruct(tracers.sha...  50.4 us
    dot_general x1, matrix products, remap(): window = jnp.einsum('fpb,bq->fpq', lifted, pick_c, precision=HIGH)  9.23 us
    ppermute x2, starting transfers between devices, exchange(): lax.ppermute(wests, 'ox', [((i + 1) % cols_n, i) for i in range(cols_n)])  8.46 us
    ppermute x2, starting transfers between devices, exchange(): south = lax.ppermute(tops, 'oy', [(i, i + 1) for i in range(rows_n - 1)])  8.15 us
    all_to_all x1, starting transfers between devices, on_device(): lax.all_to_all(atm_flux, 'ox', split_axis=2, concat_axis=1, tiled=True)  7.82 us
    reduce_sum x1, other arithmetic, remap(): fast = jnp.sum(window * wsum.transpose(0, 2, 1, 3)[None], axis=(1, 3))  7.37 us
    ppermute x2, waiting for transfers between devices, exchange(): lax.ppermute(easts, 'ox', [(i, (i + 1) % cols_n) for i in range(cols_n)])  6.35 us
    ppermute x2, starting transfers between devices, with_halo(): lax.ppermute(tail, axis, [(i, (i + 1) % count) for i in range(ends)])  5.75 us
  transfers between devices with their start and end apart: 15, of which 3 were waited for; matrix products, arithmetic and copies ran while one was open for 31% of the time, Pallas kernels for 0%

profile of v2, /device:TPU:1, one launch (start us, length us, event | category | flops | bytes accessed | tf_op | source)
XLA Modules:
  0.0 170.2 jit_solution(13599763510371012919)
XLA Ops:
  0.6 1.8 %fusion.20 = (f32[32,8,256]{2,1,0:T(8,128)S(1)}, f32[32,8,256]{2,1,0:T(8,128)}) fusion(f32[32,64,256]{2,1,0:T(8,128)} %bitcast.95), kind=kLoop, calls=%fused_computation.78 | loop fusion | bytes 1048576 | tf_op jit(solution)/shard_map/slice | solution.py:40
  3.3 1.8 %fusion.25 = (f32[16,8,256]{2,1,0:T(8,128)S(1)}, f32[16,8,256]{2,1,0:T(8,128)}, f32[16,8,256]{2,1,0:T(8,128)}, f32[16,8,256]{2,1,0:T(8,128)S(1)}) fusion(bf16[16,64,256]{2,1,0:T(8,128)(2,1)} %u_ref.1, bf16[16,64,256]{2,1,0:T(8,128)(2,1)} %v_ref.1), kind=kLoop, calls=%fused_computation.83 | loop fusion | bytes 1048576 | tf_op jit(solution)/shard_map/slice | solution.py:40
  5.9 1.5 collective-permute-start.4
  7.5 4.5 %collective-permute-start.6 = (f32[65,8,256]{2,1,0:T(8,128)}, f32[65,8,256]{2,1,0:T(8,128)}, u32[]{:S(2)}, u32[]{:S(2)}) collective-permute-start(f32[65,8,256]{2,1,0:T(8,128)} %pad_maximum_fusion.3), channel_id=1, source_target_pairs={{0,16},{16,32},{32,48},{48,64},{64,80},{80,96},{96,112},{1,17},{17... | collective-permute-start | bytes 1597448 | tf_op jit(solution)/shard_map/ppermute | solution.py:42
  12.5 2.2 %reshape.179 = f32[16,1,1024]{2,1,0:T(1,128)} reshape(f32[1024,2,8]{2,1,0:T(2,128)S(1)} %bitcast.104) | data formatting | bytes 131072
  14.7 7.8 %all-to-all-start = ((f32[16,1,1024]{2,1,0:T(1,128)}), f32[16,1,1024]{2,1,0:T(1,128)}, u32[]{:S(2)}, u32[]{:S(2)}) async-start(f32[16,1,1024]{2,1,0:T(1,128)} %reshape.179), calls=%async_computation | async-start | bytes 131072 | tf_op jit(solution)/shard_map/all_to_all | solution.py:228
  22.6 2.0 %pad_maximum_fusion.4 = f32[65,8,256]{2,1,0:T(8,128)} fusion(f32[1,8,256]{2,1,0:T(8,128)S(1)} %get-tuple-element.89, f32[16,8,256]{2,1,0:T(8,128)} %get-tuple-element.94, f32[16,8,256]{2,1,0:T(8,128)} %get-tuple-element.75, f32[32,8,256]{2,1,0:T(8,128)} %get-tuple-element.65), kind=kLoop, calls=%fused_computation.40 | loop fusion | flops 399360 | bytes 1064960 | tf_op jit(solution)/shard_map/concatenate | solution.py:41
  24.5 1.9 %collective-permute-start.5 = (f32[65,8,256]{2,1,0:T(8,128)}, f32[65,8,256]{2,1,0:T(8,128)}, u32[]{:S(2)}, u32[]{:S(2)}) collective-permute-start(f32[65,8,256]{2,1,0:T(8,128)} %pad_maximum_fusion.4), channel_id=1, source_target_pairs={{16,0},{32,16},{48,32},{64,48},{80,64},{96,80},{112,96},{17,1},{33... | collective-permute-start | bytes 1597448 | tf_op jit(solution)/shard_map/ppermute | solution.py:43
  26.5 1.7 fusion.19
  30.9 1.9 %select_reduce_fusion = f32[25,64,256]{2,1,0:T(8,128)} fusion(f32[4,64,256]{2,1,0:T(8,128)S(1)} %copy-done.11, s32[4,64,256]{2,1,0:T(8,128)S(1)} %get-tuple-element.48), kind=kLoop, calls=%fused_computation.32 | loop fusion | flops 4505600 | bytes 2162688 | tf_op jit(solution)/shard_map/reduce_sum | solution.py:201
  34.0 1.6 reduce.4
  35.6 1.6 reshape.180
  37.8 1.4 collective-permute-start
  39.2 3.4 %collective-permute-start.1 = (f32[8,32,2]{2,1,0:T(8,128)S(1)}, f32[8,32,2]{2,1,0:T(8,128)S(1)}, u32[]{:S(2)}, u32[]{:S(2)}) collective-permute-start(f32[8,32,2]{2,1,0:T(8,128)S(1)} %get-tuple-element.85), channel_id=1, source_target_pairs={{1,0},{2,1},{3,2},{4,3},{5,4},{6,5},{7,6},{8,7},{9,8},{10,9},{11,1... | collective-permute-start | bytes 6152 | tf_op jit(solution)/shard_map/ppermute | solution.py:25
  42.6 3.8 %pad_maximum_fusion.1 = (f32[65,64,8]{2,1,0:T(8,128)}, f32[65,64,8]{2,1,0:T(8,128)S(1)}) fusion(f32[1,64,8]{2,1,0:T(8,128)S(1)} %copy-done.18, f32[16,64,8]{2,1,0:T(8,128)} %get-tuple-element.72, f32[16,64,8]{2,1,0:T(8,128)} %get-tuple-element.70, f32[32,64,8]{2,1,0:T(8,128)S(1)} %copy-done.5, f32[1,64,8]{2,1,0:T(8,128)S(1)} %copy-done.19, ...), kind=kLoop, calls=%fused_computation.35 | loop fusion | flops 199680 | bytes 532480 | tf_op jit(solution)/shard_map/concatenate | solution.py:56
  47.8 4.3 %collective-permute-start.2 = (f32[8,2,68]{2,1,0:T(2,128)S(1)}, f32[8,2,68]{2,1,0:T(2,128)S(1)}, u32[]{:S(2)}, u32[]{:S(2)}) collective-permute-start(f32[8,2,68]{2,1,0:T(2,128)S(1)} %get-tuple-element.78), channel_id=1, source_target_pairs={{0,16},{16,32},{32,48},{48,64},{64,80},{80,96},{96,112},{1,17},{17... | collective-permute-start | bytes 13064 | tf_op jit(solution)/shard_map/ppermute | solution.py:23
  52.1 1.9 %collective-permute-start.3 = (f32[8,2,68]{2,1,0:T(2,128)S(1)}, f32[8,2,68]{2,1,0:T(2,128)S(1)}, u32[]{:S(2)}, u32[]{:S(2)}) collective-permute-start(f32[8,2,68]{2,1,0:T(2,128)S(1)} %get-tuple-element.79), channel_id=1, source_target_pairs={{16,0},{32,16},{48,32},{64,48},{80,64},{96,80},{112,96},{17,1},{33... | collective-permute-start | bytes 13064 | tf_op jit(solution)/shard_map/ppermute | solution.py:25
  56.6 2.9 %copy.109 = f32[65,64,8]{1,2,0:T(8,128)} copy(f32[65,64,8]{2,1,0:T(8,128)} %get-tuple-element.96) | data formatting | bytes 266240 | tf_op jit(solution)/shard_map/concatenate | solution.py:56
  59.5 1.3 copy.112
  62.1 9.2 %fusion.7 = f32[8,5,64,5,256]{4,2,3,1,0:T(8,128)} fusion(f32[8,5,64,68,1]{3,2,4,1,0:T(8,128)S(1)} %bitcast.97, pred[5,256,68,1,1]{1,0,2,4,3:T(8,128)(4,1)} %bitcast.108), kind=kOutput, calls=%fused_computation.45 | convolution fusion | flops 2673868800 | bytes 13890560 | tf_op jit(solution)/shard_map/fpb,bq->fpq/dot_general | solution.py:194
  71.4 7.6 %conditional.1 = (f32[8,64,256]{2,1,0:T(8,128)}) conditional(s32[]{:T(128)} %convert_element_type.14, (f32[5,64,5,256]{3,1,2,0:T(8,128)S(1)}, f32[8,5,64,5,256]{4,2,3,1,0:T(8,128)}) %tuple.63, (f32[4,64,256]{2,1,0:T(8,128)}, f32[8,36,68]{2,1,0:T(8,128)S(1)}, s32[4,64,256]{2,1,0:T(8,128)S(1)}) %tuple.64), branch_computations={%region_2.4_spmd, %region_4.6_spmd} | conditional | flops 6422528 | bytes 15269896 | solution.py:216
  71.6 7.4 %multiply_reduce_fusion = f32[8,64,256]{2,1,0:T(8,128)} fusion(f32[8,5,64,5,256]{4,2,3,1,0:T(8,128)} %get-tuple-element.19, f32[5,64,5,256]{3,1,2,0:T(8,128)S(1)} %get-tuple-element.20), kind=kLoop, calls=%fused_computation.4 | loop fusion | flops 6422528 | bytes 15269888 | tf_op jit(solution)/shard_map/reduce_sum | solution.py:205
  80.8 1.9 %collective-permute-start.10 = (f32[2,8,256]{2,1,0:T(8,128)S(1)}, f32[2,8,256]{2,1,0:T(8,128)S(1)}, u32[]{:S(2)}, u32[]{:S(2)}) collective-permute-start(f32[2,8,256]{2,1,0:T(8,128)S(1)} %get-tuple-element.82), channel_id=1, source_target_pairs={{16,0},{32,16},{48,32},{64,48},{80,64},{96,80},{112,96},{17,1},{33... | collective-permute-start | bytes 49160 | tf_op jit(solution)/shard_map/ppermute | solution.py:43
  82.9 3.6 %collective-permute-start.11 = (f32[2,8,256]{2,1,0:T(8,128)S(1)}, f32[2,8,256]{2,1,0:T(8,128)S(1)}, u32[]{:S(2)}, u32[]{:S(2)}) collective-permute-start(f32[2,8,256]{2,1,0:T(8,128)S(1)} %get-tuple-element.83), channel_id=1, source_target_pairs={{0,16},{16,32},{32,48},{48,64},{64,80},{80,96},{96,112},{1,17},{17... | collective-permute-start | bytes 49160 | tf_op jit(solution)/shard_map/ppermute | solution.py:42
  87.4 3.6 %collective-permute-start.12 = (f32[2,80,8]{2,1,0:T(8,128)S(1)}, f32[2,80,8]{2,1,0:T(8,128)S(1)}, u32[]{:S(2)}, u32[]{:S(2)}) collective-permute-start(f32[2,80,8]{2,1,0:T(8,128)S(1)} %pad_maximum_fusion.8), channel_id=1, source_target_pairs={{1,0},{2,1},{3,2},{4,3},{5,4},{6,5},{7,6},{8,7},{9,8},{10,9},{11,1... | collective-permute-start | bytes 15368 | tf_op jit(solution)/shard_map/ppermute | solution.py:60
  91.2 1.2 rev.6
  95.5 4.8 %collective-permute-start.7 = (f32[65,80,8]{1,2,0:T(8,128)S(1)}, f32[65,80,8]{1,2,0:T(8,128)S(1)}, u32[]{:S(2)}, u32[]{:S(2)}) collective-permute-start(f32[65,80,8]{1,2,0:T(8,128)S(1)} %pad_maximum_fusion.5), channel_id=1, source_target_pairs={{1,0},{2,1},{3,2},{4,3},{5,4},{6,5},{7,6},{8,7},{9,8},{10,9},{11,1... | collective-permute-start | bytes 499208 | tf_op jit(solution)/shard_map/ppermute | solution.py:60
  102.3 4.0 %collective-permute-done.7 = f32[65,80,8]{1,2,0:T(8,128)S(1)} collective-permute-done((f32[65,80,8]{1,2,0:T(8,128)S(1)}, f32[65,80,8]{1,2,0:T(8,128)S(1)}, u32[]{:S(2)}, u32[]{:S(2)}) %collective-permute-start.7) | collective-permute-done | bytes 166432 | tf_op jit(solution)/shard_map/ppermute | solution.py:60
  107.1 6.3 %collective-permute-done.8 = f32[65,80,8]{1,2,0:T(8,128)S(1)} collective-permute-done((f32[65,80,8]{1,2,0:T(8,128)}, f32[65,80,8]{1,2,0:T(8,128)S(1)}, u32[]{:S(2)}, u32[]{:S(2)}) %collective-permute-start.8) | collective-permute-done | bytes 166432 | tf_op jit(solution)/shard_map/ppermute | solution.py:59
  113.5 2.3 %copy.116 = f32[65,80,8]{2,1,0:T(8,128)} copy(f32[65,80,8]{1,2,0:T(8,128)S(1)} %collective-permute-done.8) | data formatting | bytes 332800 | tf_op jit(solution)/shard_map/ppermute | solution.py:59
  115.8 4.0 %pad_maximum_fusion.hc_ref = f32[65,80,128]{2,1,0:T(8,128)} fusion(f32[65,80,8]{2,1,0:T(8,128)} %copy.116, f32[65,80,8]{2,1,0:T(8,128)S(1)} %copy.115, f32[128]{0:T(128)S(1)} %pad.10.clone), kind=kLoop, calls=%fused_computation.34 | loop fusion | flops 1331200 | bytes 2995712 | tf_op jit(solution)/shard_map/concatenate | solution.py:62
  119.8 50.4 %shard_map.95 = f32[2,16,64,256]{3,2,1,0:T(8,128)} custom-call(f32[2,16,64,256]{3,2,1,0:T(8,128)} %tr_ref.1, bf16[16,64,256]{2,1,0:T(8,128)(2,1)} %u_ref.1, bf16[16,64,256]{2,1,0:T(8,128)(2,1)} %v_ref.1, s32[64,256]{1,0:T(8,128)} %m_ref.1, f32[2,64,256]{2,1,0:T(8,128)} %copy-done.8, f32[65,8,256]{2,1,0:T(8,128)} %copy-done.4, ...), custom_call_target="tpu_custom_call" | custom-call | tf_op jit(solution)/shard_map/pallas_call | solution.py:158
  (115 shorter events, 19.7 us)
Async XLA Ops:
  0.6 11.3 %copy-start.21 = (f32[8,2,1024]{2,1,0:T(2,128)S(1)}, f32[8,2,1024]{2,1,0:T(2,128)}, u32[]{:S(2)}) copy-start(f32[8,2,1024]{2,1,0:T(2,128)} %param.12) | copy-start | bytes 196612
  3.3 23.2 %copy-start = (f32[2,16,64,256]{3,2,1,0:T(8,128)S(1)}, f32[2,16,64,256]{3,2,1,0:T(8,128)}, u32[]{:S(2)}) copy-start(f32[2,16,64,256]{3,2,1,0:T(8,128)} %tr_ref.1) | copy-start | bytes 6291460
  5.9 85.2 %collective-permute-start.4 = (f32[65,8,256]{2,1,0:T(8,128)}, f32[65,8,256]{2,1,0:T(8,128)}, u32[]{:S(2)}, u32[]{:S(2)}) collective-permute-start(f32[65,8,256]{2,1,0:T(8,128)} %pad_maximum_fusion.3), channel_id=1, source_target_pairs={{120,112},{119,113},{118,114},{117,115},{116,116},{115,117},{114,1... | collective-permute-start | bytes 1597448 | tf_op jit(solution)/shard_map/ppermute | solution.py:45
  7.5 86.5 %collective-permute-start.6 = (f32[65,8,256]{2,1,0:T(8,128)}, f32[65,8,256]{2,1,0:T(8,128)}, u32[]{:S(2)}, u32[]{:S(2)}) collective-permute-start(f32[65,8,256]{2,1,0:T(8,128)} %pad_maximum_fusion.3), channel_id=1, source_target_pairs={{0,16},{16,32},{32,48},{48,64},{64,80},{80,96},{96,112},{1,17},{17... | collective-permute-start | bytes 1597448 | tf_op jit(solution)/shard_map/ppermute | solution.py:42
  14.7 18.7 %all-to-all-start = ((f32[16,1,1024]{2,1,0:T(1,128)}), f32[16,1,1024]{2,1,0:T(1,128)}, u32[]{:S(2)}, u32[]{:S(2)}) async-start(f32[16,1,1024]{2,1,0:T(1,128)} %reshape.179), calls=%async_computation | async-start | bytes 131072 | tf_op jit(solution)/shard_map/all_to_all | solution.py:228
  22.6 5.6 %copy-start.2 = (bf16[16,64,256]{2,1,0:T(8,128)(2,1)S(1)}, bf16[16,64,256]{2,1,0:T(8,128)(2,1)}, u32[]{:S(2)}) copy-start(bf16[16,64,256]{2,1,0:T(8,128)(2,1)} %u_ref.1) | copy-start | bytes 1572868
  24.5 67.9 %collective-permute-start.5 = (f32[65,8,256]{2,1,0:T(8,128)}, f32[65,8,256]{2,1,0:T(8,128)}, u32[]{:S(2)}, u32[]{:S(2)}) collective-permute-start(f32[65,8,256]{2,1,0:T(8,128)} %pad_maximum_fusion.4), channel_id=1, source_target_pairs={{16,0},{32,16},{48,32},{64,48},{80,64},{96,80},{112,96},{17,1},{33... | collective-permute-start | bytes 1597448 | tf_op jit(solution)/shard_map/ppermute | solution.py:43
  30.8 11.8 %copy-start.5 = (f32[32,64,8]{2,1,0:T(8,128)S(1)}, f32[32,64,8]{2,1,0:T(8,128)}, u32[]{:S(2)}) copy-start(f32[32,64,8]{2,1,0:T(8,128)} %get-tuple-element.62) | copy-start | bytes 196612
  33.5 9.2 %copy-start.18 = (f32[1,64,8]{2,1,0:T(8,128)S(1)}, f32[1,64,8]{2,1,0:T(8,128)}, u32[]{:S(2)}) copy-start(f32[1,64,8]{2,1,0:T(8,128)} %get-tuple-element.86) | copy-start | bytes 6148
  33.5 9.2 %copy-start.19 = (f32[1,64,8]{2,1,0:T(8,128)S(1)}, f32[1,64,8]{2,1,0:T(8,128)}, u32[]{:S(2)}) copy-start(f32[1,64,8]{2,1,0:T(8,128)} %get-tuple-element.87) | copy-start | bytes 6148
  37.8 8.7 %collective-permute-start = (f32[8,32,2]{2,1,0:T(8,128)S(1)}, f32[8,32,2]{2,1,0:T(8,128)S(1)}, u32[]{:S(2)}, u32[]{:S(2)}) collective-permute-start(f32[8,32,2]{2,1,0:T(8,128)S(1)} %get-tuple-element.84), channel_id=1, source_target_pairs={{0,1},{1,2},{2,3},{3,4},{4,5},{5,6},{6,7},{7,8},{8,9},{9,10},{10,1... | collective-permute-start | bytes 6152 | tf_op jit(solution)/shard_map/ppermute | solution.py:23
  39.2 7.3 %collective-permute-start.1 = (f32[8,32,2]{2,1,0:T(8,128)S(1)}, f32[8,32,2]{2,1,0:T(8,128)S(1)}, u32[]{:S(2)}, u32[]{:S(2)}) collective-permute-start(f32[8,32,2]{2,1,0:T(8,128)S(1)} %get-tuple-element.85), channel_id=1, source_target_pairs={{1,0},{2,1},{3,2},{4,3},{5,4},{6,5},{7,6},{8,7},{9,8},{10,9},{11,1... | collective-permute-start | bytes 6152 | tf_op jit(solution)/shard_map/ppermute | solution.py:25
  47.8 13.2 %copy-start.14 = (f32[8,32,2]{2,1,0:T(8,128)S(1)}, f32[8,32,2]{2,1,0:T(8,128)}, u32[]{:S(2)}) copy-start(f32[8,32,2]{2,1,0:T(8,128)} %copy-done.13) | copy-start | bytes 6148
  47.8 13.2 %copy-start.16 = (f32[8,32,2]{2,1,0:T(8,128)S(1)}, f32[8,32,2]{2,1,0:T(8,128)}, u32[]{:S(2)}) copy-start(f32[8,32,2]{2,1,0:T(8,128)} %copy-done.15) | copy-start | bytes 6148
  47.8 13.2 %collective-permute-start.2 = (f32[8,2,68]{2,1,0:T(2,128)S(1)}, f32[8,2,68]{2,1,0:T(2,128)S(1)}, u32[]{:S(2)}, u32[]{:S(2)}) collective-permute-start(f32[8,2,68]{2,1,0:T(2,128)S(1)} %get-tuple-element.78), channel_id=1, source_target_pairs={{0,16},{16,32},{32,48},{48,64},{64,80},{80,96},{96,112},{1,17},{17... | collective-permute-start | bytes 13064 | tf_op jit(solution)/shard_map/ppermute | solution.py:23
  52.1 8.8 %collective-permute-start.3 = (f32[8,2,68]{2,1,0:T(2,128)S(1)}, f32[8,2,68]{2,1,0:T(2,128)S(1)}, u32[]{:S(2)}, u32[]{:S(2)}) collective-permute-start(f32[8,2,68]{2,1,0:T(2,128)S(1)} %get-tuple-element.79), channel_id=1, source_target_pairs={{16,0},{32,16},{48,32},{64,48},{80,64},{96,80},{112,96},{17,1},{33... | collective-permute-start | bytes 13064 | tf_op jit(solution)/shard_map/ppermute | solution.py:25
  62.1 9.3 %copy-start.1 = (f32[25,64,256]{2,1,0:T(8,128)S(1)}, f32[25,64,256]{2,1,0:T(8,128)}, u32[]{:S(2)}) copy-start(f32[25,64,256]{2,1,0:T(8,128)} %select_reduce_fusion) | copy-start | bytes 4915204
  62.1 9.2 %copy-start.7 = (s32[4,64,256]{2,1,0:T(8,128)S(1)}, s32[4,64,256]{2,1,0:T(8,128)}, u32[]{:S(2)}) copy-start(s32[4,64,256]{2,1,0:T(8,128)} %param.13) | copy-start | bytes 786436
  71.4 7.6 %copy-start.22 = (f32[2,8]{1,0:T(2,128)S(1)}, f32[2,8]{1,0:T(2,128)}, u32[]{:S(2)}) copy-start(f32[2,8]{1,0:T(2,128)} %param.15) | copy-start | bytes 196
  71.4 21.1 %copy-start.23 = (f32[65]{0:T(128)S(1)}, f32[65]{0:T(128)}, u32[]{:S(2)}) copy-start(f32[65]{0:T(128)} %constant.79.clone.1) | copy-start | bytes 784
  80.1 15.0 %copy-start.8 = (f32[2,64,256]{2,1,0:T(8,128)}, f32[2,64,256]{2,1,0:T(8,128)S(1)}, u32[]{:S(2)}) copy-start(f32[2,64,256]{2,1,0:T(8,128)S(1)} %multiply_reduce_fusion.1.f_ref) | copy-start | bytes 393220
  80.2 2.7 %collective-permute-start.9 = (f32[2,8,256]{2,1,0:T(8,128)S(1)}, f32[2,8,256]{2,1,0:T(8,128)S(1)}, u32[]{:S(2)}, u32[]{:S(2)}) collective-permute-start(f32[2,8,256]{2,1,0:T(8,128)S(1)} %get-tuple-element.83), channel_id=1, source_target_pairs={{120,112},{119,113},{118,114},{117,115},{116,116},{115,117},{114,1... | collective-permute-start | bytes 49160 | tf_op jit(solution)/shard_map/ppermute | solution.py:45
  80.8 5.8 %collective-permute-start.10 = (f32[2,8,256]{2,1,0:T(8,128)S(1)}, f32[2,8,256]{2,1,0:T(8,128)S(1)}, u32[]{:S(2)}, u32[]{:S(2)}) collective-permute-start(f32[2,8,256]{2,1,0:T(8,128)S(1)} %get-tuple-element.82), channel_id=1, source_target_pairs={{16,0},{32,16},{48,32},{64,48},{80,64},{96,80},{112,96},{17,1},{33... | collective-permute-start | bytes 49160 | tf_op jit(solution)/shard_map/ppermute | solution.py:43
  82.9 4.5 %collective-permute-start.11 = (f32[2,8,256]{2,1,0:T(8,128)S(1)}, f32[2,8,256]{2,1,0:T(8,128)S(1)}, u32[]{:S(2)}, u32[]{:S(2)}) collective-permute-start(f32[2,8,256]{2,1,0:T(8,128)S(1)} %get-tuple-element.83), channel_id=1, source_target_pairs={{0,16},{16,32},{32,48},{48,64},{64,80},{80,96},{96,112},{1,17},{17... | collective-permute-start | bytes 49160 | tf_op jit(solution)/shard_map/ppermute | solution.py:42
  86.7 8.5 %copy-start.17 = (f32[2,8,256]{2,1,0:T(8,128)}, f32[2,8,256]{2,1,0:T(8,128)S(1)}, u32[]{:S(2)}) copy-start(f32[2,8,256]{2,1,0:T(8,128)S(1)} %broadcast_select_fusion.fn_ref) | copy-start | bytes 49156
  87.4 7.8 %copy-start.20 = (f32[2,8,256]{2,1,0:T(8,128)}, f32[2,8,256]{2,1,0:T(8,128)S(1)}, u32[]{:S(2)}) copy-start(f32[2,8,256]{2,1,0:T(8,128)S(1)} %collective-permute-done.11.fs_ref) | copy-start | bytes 49156
  87.4 14.1 %collective-permute-start.12 = (f32[2,80,8]{2,1,0:T(8,128)S(1)}, f32[2,80,8]{2,1,0:T(8,128)S(1)}, u32[]{:S(2)}, u32[]{:S(2)}) collective-permute-start(f32[2,80,8]{2,1,0:T(8,128)S(1)} %pad_maximum_fusion.8), channel_id=1, source_target_pairs={{1,0},{2,1},{3,2},{4,3},{5,4},{6,5},{7,6},{8,7},{9,8},{10,9},{11,1... | collective-permute-start | bytes 15368 | tf_op jit(solution)/shard_map/ppermute | solution.py:60
  91.1 10.5 %collective-permute-start.13 = (f32[2,80,8]{2,1,0:T(8,128)S(1)}, f32[2,80,8]{2,1,0:T(8,128)S(1)}, u32[]{:S(2)}, u32[]{:S(2)}) collective-permute-start(f32[2,80,8]{2,1,0:T(8,128)S(1)} %pad_maximum_fusion.9), channel_id=1, source_target_pairs={{0,1},{1,2},{2,3},{3,4},{4,5},{5,6},{6,7},{7,8},{8,9},{9,10},{10,1... | collective-permute-start | bytes 15368 | tf_op jit(solution)/shard_map/ppermute | solution.py:59
  93.7 7.0 %copy-start.4 = (f32[65,8,256]{2,1,0:T(8,128)}, f32[65,8,256]{2,1,0:T(8,128)S(1)}, u32[]{:S(2)}) copy-start(f32[65,8,256]{2,1,0:T(8,128)S(1)} %multiply_select_fusion.hn_ref) | copy-start | bytes 1597444
  93.7 7.0 %copy-start.9 = (f32[65,64,8]{1,2,0:T(8,128)S(1)}, f32[65,64,8]{1,2,0:T(8,128)}, u32[]{:S(2)}) copy-start(f32[65,64,8]{1,2,0:T(8,128)} %copy.112) | copy-start | bytes 399364
  95.5 10.8 %collective-permute-start.7 = (f32[65,80,8]{1,2,0:T(8,128)S(1)}, f32[65,80,8]{1,2,0:T(8,128)S(1)}, u32[]{:S(2)}, u32[]{:S(2)}) collective-permute-start(f32[65,80,8]{1,2,0:T(8,128)S(1)} %pad_maximum_fusion.5), channel_id=1, source_target_pairs={{1,0},{2,1},{3,2},{4,3},{5,4},{6,5},{7,6},{8,7},{9,8},{10,9},{11,1... | collective-permute-start | bytes 499208 | tf_op jit(solution)/shard_map/ppermute | solution.py:60
  101.6 11.9 %collective-permute-start.8 = (f32[65,80,8]{1,2,0:T(8,128)}, f32[65,80,8]{1,2,0:T(8,128)S(1)}, u32[]{:S(2)}, u32[]{:S(2)}) collective-permute-start(f32[65,80,8]{1,2,0:T(8,128)} %pad_maximum_fusion.6), channel_id=1, source_target_pairs={{0,1},{1,2},{2,3},{3,4},{4,5},{5,6},{6,7},{7,8},{8,9},{9,10},{10,1... | collective-permute-start | bytes 499208 | tf_op jit(solution)/shard_map/ppermute | solution.py:59
  (6 other events, 11.8 us)

commit v3 on v2

--- a/solution.py
+++ b/solution.py
@@ -174,6 +174,18 @@
         ],
         compiler_params=pltpu.CompilerParams(vmem_limit_bytes=62 * 1024 * 1024),
     )(tracers, u_vel, v_vel, land_mask, forcing, *halo, *f_halo)
+
+
+def atmosphere_block(atm_flux):
+    cols_n = lax.axis_size("ox")
+    rows_n = lax.axis_size("oy")
+    band = lax.all_gather(atm_flux, "ox", axis=1, tiled=True)
+    width = band.shape[2] // cols_n
+    ring = jnp.concatenate([band[..., -H:], band, band[..., :H]], axis=2)
+    own = lax.dynamic_slice_in_dim(ring, lax.axis_index("ox") * width, width + 2 * H, axis=2)
+    below = lax.ppermute(own[:, -H:], "oy", [(i, i + 1) for i in range(rows_n - 1)])
+    above = lax.ppermute(own[:, :H], "oy", [(i + 1, i) for i in range(rows_n - 1)])
+    return jnp.concatenate([below, own, above], axis=1)
 
 
 def remap(padded, remap_index, remap_weight):
@@ -225,9 +237,7 @@
     ]
     halo = exchange(fields, [False, True, True, False])
 
-    atm_tile = lax.all_to_all(atm_flux, "ox", split_axis=2, concat_axis=1, tiled=True)
-    lon_wide = with_halo(atm_tile, (("ox", 2),), H, True)
-    padded = with_halo(lon_wide, (("oy", 1),), H, False)
+    padded = atmosphere_block(atm_flux)
     ocean_flux = remap(padded, remap_index, remap_weight)
     forcing = jnp.sum(coupling[:, :, None, None] * ocean_flux[None], axis=1)
     f_halo = exchange([forcing], [False])

time: 172 us -> 176 us (1.023)
  between operations: 1.86 us -> 15.1 us
  starting transfers between devices: 41.6 us -> 28.9 us
  waiting for transfers between devices: 11 us -> 17.8 us
    all_to_all x1 -> x0, starting transfers between devices: 7.82 us -> none  [on_device(): lax.all_to_all(atm_flux, 'ox', split_axis=2, concat_axis=1, tiled=True)]
    unnamed x49 -> x29, local copies, waits for them, and re-layouts: 5.63 us -> 0.74 us
    ppermute x4 -> x2, starting transfers between devices: 11.1 us -> 6.81 us  [the longest x1 4.89 us: atmosphere_block(): lax.ppermute(own[:, -H:], 'oy', [(i, i + 1) for i in range(rows_n - 1)])]
    all_gather x0 -> x1, waiting for transfers between devices: none -> 2.76 us  [atmosphere_block(): band = lax.all_gather(atm_flux, 'ox', axis=1, tiled=True)]
    ppermute x2, waiting for transfers between devices: 0.01 us -> 2.42 us  [exchange(): north = lax.ppermute(bots, 'oy', [(i + 1, i) for i in range(rows_n - 1)])]
    ppermute x4 -> x2, waiting for transfers between devices: 0.01 us -> 1.98 us  [the longest x1 1.97 us: atmosphere_block(): lax.ppermute(own[:, :H], 'oy', [(i + 1, i) for i in range(rows_n - 1)])]
    all_gather x0 -> x1, local copies, waits for them, and re-layouts: none -> 1.84 us  [atmosphere_block(): band = lax.all_gather(atm_flux, 'ox', axis=1, tiled=True)]
  transfers between devices with their start and end apart: 15 -> 13, of which waited for: 3 -> 6; matrix products, arithmetic and copies ran while one was open for 31% -> 19% of each run, Pallas kernels for 0% -> 0%
where the time goes in v3:
time: 176 us; the launch traced here: 175 us
  Pallas kernels  50.3 us (29%)
  starting transfers between devices  28.9 us (16%)
  other arithmetic  26.7 us (15%)
  local copies, waits for them, and re-layouts  25.8 us (15%)
  waiting for transfers between devices  17.8 us (10%)
  between operations  15.1 us (9%)
  matrix products  10.6 us (6%)
    pallas_call x1, Pallas kernels, evolve(): pl.pallas_call(stencil_kernel, out_shape=jax.ShapeDtypeStruct(tracers.sha...  50.3 us
    dot_general x1, matrix products, remap(): window = jnp.einsum('fpb,bq->fpq', lifted, pick_c, precision=HIGH)  9.13 us
    ppermute x2, starting transfers between devices, exchange(): lax.ppermute(wests, 'ox', [((i + 1) % cols_n, i) for i in range(cols_n)])  9.01 us
    reduce_sum x1, other arithmetic, remap(): fast = jnp.sum(window * wsum.transpose(0, 2, 1, 3)[None], axis=(1, 3))  7.37 us
    ppermute x2, starting transfers between devices, exchange(): south = lax.ppermute(tops, 'oy', [(i, i + 1) for i in range(rows_n - 1)])  6.44 us
    ppermute x2, waiting for transfers between devices, exchange(): lax.ppermute(easts, 'ox', [(i, (i + 1) % cols_n) for i in range(cols_n)])  6.13 us
    concatenate x2, other arithmetic, exchange(): return (north, south, jnp.concatenate([from_e, gap, from_w], axis=-1))  5.52 us
    ppermute x1, starting transfers between devices, atmosphere_block(): lax.ppermute(own[:, -H:], 'oy', [(i, i + 1) for i in range(rows_n - 1)])  4.89 us
  transfers between devices with their start and end apart: 13, of which 6 were waited for; matrix products, arithmetic and copies ran while one was open for 19% of the time, Pallas kernels for 0%

profile of v3, /device:TPU:1, one launch (start us, length us, event | category | flops | bytes accessed | tf_op | source)
XLA Modules:
  0.0 175.4 jit_solution(4572542187398389594)
XLA Ops:
  7.2 1.2 fusion.20
  11.1 1.5 collective-permute-start.2
  12.6 4.5 %collective-permute-start.4 = (f32[65,8,256]{2,1,0:T(8,128)}, f32[65,8,256]{2,1,0:T(8,128)}, u32[]{:S(2)}, u32[]{:S(2)}) collective-permute-start(f32[65,8,256]{2,1,0:T(8,128)} %pad_maximum_fusion.3), channel_id=1, source_target_pairs={{0,16},{16,32},{32,48},{48,64},{64,80},{80,96},{96,112},{1,17},{17... | collective-permute-start | bytes 1597448 | tf_op jit(solution)/shard_map/ppermute | solution.py:42
  18.7 1.9 %collective-permute-start.3 = (f32[65,8,256]{2,1,0:T(8,128)}, f32[65,8,256]{2,1,0:T(8,128)}, u32[]{:S(2)}, u32[]{:S(2)}) collective-permute-start(f32[65,8,256]{2,1,0:T(8,128)} %pad_maximum_fusion.4), channel_id=1, source_target_pairs={{16,0},{32,16},{48,32},{64,48},{80,64},{96,80},{112,96},{17,1},{33... | collective-permute-start | bytes 1597448 | tf_op jit(solution)/shard_map/ppermute | solution.py:43
  20.6 1.7 fusion.19
  25.7 4.0 %pad_maximum_fusion.1 = (f32[65,64,8]{2,1,0:T(8,128)}, f32[65,64,8]{2,1,0:T(8,128)S(1)}) fusion(f32[1,64,8]{2,1,0:T(8,128)S(1)} %get-tuple-element.82, f32[16,64,8]{2,1,0:T(8,128)} %get-tuple-element.72, f32[16,64,8]{2,1,0:T(8,128)S(1)} %copy-done.6, f32[32,64,8]{2,1,0:T(8,128)} %get-tuple-element.58, f32[1,64,8]{2,1,0:T(8,128)S(1)} %get-tuple-element.83, ...), kind=kLoop, calls=%fused_computation.35 | loop fusion | flops 199680 | bytes 532480 | tf_op jit(solution)/shard_map/concatenate | solution.py:56
  32.2 2.2 %copy.75 = f32[65,64,8]{1,2,0:T(8,128)S(1)} copy(f32[65,64,8]{2,1,0:T(8,128)} %get-tuple-element.92) | data formatting | bytes 266240 | tf_op jit(solution)/shard_map/concatenate | solution.py:56
  35.1 1.2 rev.6
  39.4 6.3 %collective-permute-start.5 = (f32[65,80,8]{1,2,0:T(8,128)S(1)}, f32[65,80,8]{1,2,0:T(8,128)S(1)}, u32[]{:S(2)}, u32[]{:S(2)}) collective-permute-start(f32[65,80,8]{1,2,0:T(8,128)S(1)} %pad_maximum_fusion.5), channel_id=1, source_target_pairs={{1,0},{2,1},{3,2},{4,3},{5,4},{6,5},{7,6},{8,7},{9,8},{10,9},{11,1... | collective-permute-start | bytes 499208 | tf_op jit(solution)/shard_map/ppermute | solution.py:60
  46.2 1.9 %select_reduce_fusion = f32[25,64,256]{2,1,0:T(8,128)S(1)} fusion(f32[4,64,256]{2,1,0:T(8,128)} %param.14, s32[4,64,256]{2,1,0:T(8,128)} %get-tuple-element.44), kind=kLoop, calls=%fused_computation.32 | loop fusion | flops 4505600 | bytes 2162688 | tf_op jit(solution)/shard_map/reduce_sum | solution.py:213
  48.2 4.5 %collective-permute-done.5 = f32[65,80,8]{1,2,0:T(8,128)S(1)} collective-permute-done((f32[65,80,8]{1,2,0:T(8,128)S(1)}, f32[65,80,8]{1,2,0:T(8,128)S(1)}, u32[]{:S(2)}, u32[]{:S(2)}) %collective-permute-start.5) | collective-permute-done | bytes 166432 | tf_op jit(solution)/shard_map/ppermute | solution.py:60
  52.7 2.3 %copy.81 = f32[65,80,8]{2,1,0:T(8,128)} copy(f32[65,80,8]{1,2,0:T(8,128)S(1)} %collective-permute-done.5) | data formatting | bytes 332800 | tf_op jit(solution)/shard_map/ppermute | solution.py:60
  55.0 4.2 %collective-permute-done.6 = f32[65,80,8]{1,2,0:T(8,128)S(1)} collective-permute-done((f32[65,80,8]{1,2,0:T(8,128)S(1)}, f32[65,80,8]{1,2,0:T(8,128)S(1)}, u32[]{:S(2)}, u32[]{:S(2)}) %collective-permute-start.6) | collective-permute-done | bytes 166432 | tf_op jit(solution)/shard_map/ppermute | solution.py:59
  59.2 2.3 %copy.82 = f32[65,80,8]{2,1,0:T(8,128)} copy(f32[65,80,8]{1,2,0:T(8,128)S(1)} %collective-permute-done.6) | data formatting | bytes 332800 | tf_op jit(solution)/shard_map/ppermute | solution.py:59
  61.5 2.8 %all-gather.2.cloned.1.call-done = f32[8,32,1024]{2,0,1:T(8,128)} async-done(((f32[8,2,1024]{2,0,1:T(8,128)}), f32[8,32,1024]{2,0,1:T(8,128)}) %all-gather.2.cloned.1.call-update) | async-done | bytes 1048592 | tf_op jit(solution)/shard_map/all_gather | solution.py:182
  64.2 1.8 %copy.69 = f32[8,32,1024]{2,1,0:T(8,128)S(1)} copy(f32[8,32,1024]{2,0,1:T(8,128)} %all-gather.2.cloned.1.call-done) | data formatting | bytes 2097152 | tf_op jit(solution)/shard_map/all_gather | solution.py:182
  66.2 1.4 concatenate.36
  68.5 4.9 %collective-permute-start = (f32[8,2,68]{2,1,0:T(2,128)S(1)}, f32[8,2,68]{2,1,0:T(2,128)S(1)}, u32[]{:S(2)}, u32[]{:S(2)}) collective-permute-start(f32[8,2,68]{2,1,0:T(2,128)S(1)} %get-tuple-element.62), channel_id=1, source_target_pairs={{0,16},{16,32},{32,48},{48,64},{64,80},{80,96},{96,112},{1,17},{17... | collective-permute-start | bytes 13064 | tf_op jit(solution)/shard_map/ppermute | solution.py:186
  73.4 1.9 %collective-permute-start.1 = (f32[8,2,68]{2,1,0:T(2,128)S(1)}, f32[8,2,68]{2,1,0:T(2,128)S(1)}, u32[]{:S(2)}, u32[]{:S(2)}) collective-permute-start(f32[8,2,68]{2,1,0:T(2,128)S(1)} %get-tuple-element.63), channel_id=1, source_target_pairs={{16,0},{32,16},{48,32},{64,48},{80,64},{96,80},{112,96},{17,1},{33... | collective-permute-start | bytes 13064 | tf_op jit(solution)/shard_map/ppermute | solution.py:187
  76.4 2.0 %collective-permute-done.1 = f32[8,2,68]{2,1,0:T(2,128)S(1)} collective-permute-done((f32[8,2,68]{2,1,0:T(2,128)S(1)}, f32[8,2,68]{2,1,0:T(2,128)S(1)}, u32[]{:S(2)}, u32[]{:S(2)}) %collective-permute-start.1) | collective-permute-done | bytes 4384 | tf_op jit(solution)/shard_map/ppermute | solution.py:187
  78.4 1.5 convolution_bitcast_fusion
  79.9 1.6 copy.72
  82.2 9.1 %fusion.7 = f32[8,5,64,5,256]{4,2,3,1,0:T(8,128)} fusion(f32[8,5,64,68,1]{3,2,4,1,0:T(8,128)S(1)} %bitcast.90, pred[5,256,68,1,1]{1,0,2,4,3:T(8,128)(4,1)} %bitcast.96), kind=kOutput, calls=%fused_computation.45 | convolution fusion | flops 2673868800 | bytes 13890560 | tf_op jit(solution)/shard_map/fpb,bq->fpq/dot_general | solution.py:206
  91.3 7.6 %conditional.1 = (f32[8,64,256]{2,1,0:T(8,128)}) conditional(s32[]{:T(128)} %convert_element_type.14, (f32[5,64,5,256]{3,1,2,0:T(8,128)S(1)}, f32[8,5,64,5,256]{4,2,3,1,0:T(8,128)}) %tuple.63, (f32[4,64,256]{2,1,0:T(8,128)S(1)}, f32[8,36,68]{2,1,0:T(8,128)}, s32[4,64,256]{2,1,0:T(8,128)S(1)}) %tuple.65), branch_computations={%region_2.4_spmd, %region_4.6_spmd} | conditional | flops 6422528 | bytes 15269896 | solution.py:228
  91.5 7.4 %multiply_reduce_fusion = f32[8,64,256]{2,1,0:T(8,128)} fusion(f32[8,5,64,5,256]{4,2,3,1,0:T(8,128)} %get-tuple-element.19, f32[5,64,5,256]{3,1,2,0:T(8,128)S(1)} %get-tuple-element.20), kind=kLoop, calls=%fused_computation.4 | loop fusion | flops 6422528 | bytes 15269888 | tf_op jit(solution)/shard_map/reduce_sum | solution.py:217
  100.8 1.9 %collective-permute-start.9 = (f32[2,8,256]{2,1,0:T(8,128)S(1)}, f32[2,8,256]{2,1,0:T(8,128)S(1)}, u32[]{:S(2)}, u32[]{:S(2)}) collective-permute-start(f32[2,8,256]{2,1,0:T(8,128)S(1)} %get-tuple-element.81), channel_id=1, source_target_pairs={{0,16},{16,32},{32,48},{48,64},{64,80},{80,96},{96,112},{1,17},{17... | collective-permute-start | bytes 49160 | tf_op jit(solution)/shard_map/ppermute | solution.py:42
  102.7 2.4 %collective-permute-start.8 = (f32[2,8,256]{2,1,0:T(8,128)S(1)}, f32[2,8,256]{2,1,0:T(8,128)S(1)}, u32[]{:S(2)}, u32[]{:S(2)}) collective-permute-start(f32[2,8,256]{2,1,0:T(8,128)S(1)} %get-tuple-element.80), channel_id=1, source_target_pairs={{16,0},{32,16},{48,32},{64,48},{80,64},{96,80},{112,96},{17,1},{33... | collective-permute-start | bytes 49160 | tf_op jit(solution)/shard_map/ppermute | solution.py:43
  105.4 2.4 %collective-permute-done.8 = f32[2,8,256]{2,1,0:T(8,128)S(1)} collective-permute-done((f32[2,8,256]{2,1,0:T(8,128)S(1)}, f32[2,8,256]{2,1,0:T(8,128)S(1)}, u32[]{:S(2)}, u32[]{:S(2)}) %collective-permute-start.8) | collective-permute-done | bytes 16416 | tf_op jit(solution)/shard_map/ppermute | solution.py:43
  108.0 2.7 %collective-permute-start.10 = (f32[2,80,8]{2,1,0:T(8,128)S(1)}, f32[2,80,8]{2,1,0:T(8,128)S(1)}, u32[]{:S(2)}, u32[]{:S(2)}) collective-permute-start(f32[2,80,8]{2,1,0:T(8,128)S(1)} %pad_maximum_fusion.8), channel_id=1, source_target_pairs={{1,0},{2,1},{3,2},{4,3},{5,4},{6,5},{7,6},{8,7},{9,8},{10,9},{11,1... | collective-permute-start | bytes 15368 | tf_op jit(solution)/shard_map/ppermute | solution.py:60
  110.8 4.8 %pad_maximum_fusion.hc_ref = f32[65,80,128]{2,1,0:T(8,128)} fusion(f32[65,80,8]{2,1,0:T(8,128)} %copy.82, f32[65,80,8]{2,1,0:T(8,128)} %copy.81, f32[128]{0:T(128)S(1)} %pad.10.clone), kind=kLoop, calls=%fused_computation.34 | loop fusion | flops 1331200 | bytes 2995712 | tf_op jit(solution)/shard_map/concatenate | solution.py:62
  115.6 1.9 %collective-permute-done.11 = f32[2,80,8]{2,1,0:T(8,128)S(1)} collective-permute-done((f32[2,80,8]{2,1,0:T(8,128)S(1)}, f32[2,80,8]{2,1,0:T(8,128)S(1)}, u32[]{:S(2)}, u32[]{:S(2)}) %collective-permute-start.11) | collective-permute-done | bytes 5152 | tf_op jit(solution)/shard_map/ppermute | solution.py:59
  118.2 50.3 %shard_map.95 = f32[2,16,64,256]{3,2,1,0:T(8,128)} custom-call(f32[2,16,64,256]{3,2,1,0:T(8,128)} %tr_ref.1, bf16[16,64,256]{2,1,0:T(8,128)(2,1)} %u_ref.1, bf16[16,64,256]{2,1,0:T(8,128)(2,1)} %v_ref.1, s32[64,256]{1,0:T(8,128)} %m_ref.1, f32[2,64,256]{2,1,0:T(8,128)} %copy-done.7, f32[65,8,256]{2,1,0:T(8,128)} %copy-done.3, ...), custom_call_target="tpu_custom_call" | custom-call | tf_op jit(solution)/shard_map/pallas_call | solution.py:158
  (92 shorter events, 19.6 us)
Async XLA Ops:
  7.2 13.5 %copy-start = (f32[2,16,64,256]{3,2,1,0:T(8,128)S(1)}, f32[2,16,64,256]{3,2,1,0:T(8,128)}, u32[]{:S(2)}) copy-start(f32[2,16,64,256]{3,2,1,0:T(8,128)} %tr_ref.1) | copy-start | bytes 6291460
  7.2 9.9 %copy-start.11 = (f32[8,2,1024]{2,1,0:T(2,128)S(1)}, f32[8,2,1024]{2,1,0:T(2,128)}, u32[]{:S(2)}) copy-start(f32[8,2,1024]{2,1,0:T(2,128)} %param.12) | copy-start | bytes 196612
  7.2 57.1 %all-gather.2.cloned.1.call-start = ((), (), s32[]{:S(2)}) async-start(), calls=%async_computation | async-start | bytes 1114112 | tf_op jit(solution)/shard_map/all_gather | solution.py:182
  11.1 24.0 %collective-permute-start.2 = (f32[65,8,256]{2,1,0:T(8,128)}, f32[65,8,256]{2,1,0:T(8,128)}, u32[]{:S(2)}, u32[]{:S(2)}) collective-permute-start(f32[65,8,256]{2,1,0:T(8,128)} %pad_maximum_fusion.3), channel_id=1, source_target_pairs={{120,112},{119,113},{118,114},{117,115},{116,116},{115,117},{114,1... | collective-permute-start | bytes 1597448 | tf_op jit(solution)/shard_map/ppermute | solution.py:45
  12.6 25.3 %collective-permute-start.4 = (f32[65,8,256]{2,1,0:T(8,128)}, f32[65,8,256]{2,1,0:T(8,128)}, u32[]{:S(2)}, u32[]{:S(2)}) collective-permute-start(f32[65,8,256]{2,1,0:T(8,128)} %pad_maximum_fusion.3), channel_id=1, source_target_pairs={{0,16},{16,32},{32,48},{48,64},{64,80},{80,96},{96,112},{1,17},{17... | collective-permute-start | bytes 1597448 | tf_op jit(solution)/shard_map/ppermute | solution.py:42
  17.8 4.6 %copy-start.1 = (bf16[16,64,256]{2,1,0:T(8,128)(2,1)S(1)}, bf16[16,64,256]{2,1,0:T(8,128)(2,1)}, u32[]{:S(2)}) copy-start(bf16[16,64,256]{2,1,0:T(8,128)(2,1)} %u_ref.1) | copy-start | bytes 1572868
  18.7 17.7 %collective-permute-start.3 = (f32[65,8,256]{2,1,0:T(8,128)}, f32[65,8,256]{2,1,0:T(8,128)}, u32[]{:S(2)}, u32[]{:S(2)}) collective-permute-start(f32[65,8,256]{2,1,0:T(8,128)} %pad_maximum_fusion.4), channel_id=1, source_target_pairs={{16,0},{32,16},{48,32},{64,48},{80,64},{96,80},{112,96},{17,1},{33... | collective-permute-start | bytes 1597448 | tf_op jit(solution)/shard_map/ppermute | solution.py:43
  20.6 2.8 %copy-start.2 = (bf16[16,64,256]{2,1,0:T(8,128)(2,1)S(1)}, bf16[16,64,256]{2,1,0:T(8,128)(2,1)}, u32[]{:S(2)}) copy-start(bf16[16,64,256]{2,1,0:T(8,128)(2,1)} %v_ref.1) | copy-start | bytes 1572868
  22.3 2.3 %copy-start.4 = (s32[4,64,256]{2,1,0:T(8,128)S(1)}, s32[4,64,256]{2,1,0:T(8,128)}, u32[]{:S(2)}) copy-start(s32[4,64,256]{2,1,0:T(8,128)} %param.13) | copy-start | bytes 786436
  23.4 2.2 %copy-start.6 = (f32[16,64,8]{2,1,0:T(8,128)S(1)}, f32[16,64,8]{2,1,0:T(8,128)}, u32[]{:S(2)}) copy-start(f32[16,64,8]{2,1,0:T(8,128)} %get-tuple-element.70) | copy-start | bytes 98308
  32.2 4.2 %copy-start.13 = (f32[65]{0:T(128)S(1)}, f32[65]{0:T(128)}, u32[]{:S(2)}) copy-start(f32[65]{0:T(128)} %constant.87.clone.1) | copy-start | bytes 784
  37.6 8.4 %copy-start.3 = (f32[65,8,256]{2,1,0:T(8,128)}, f32[65,8,256]{2,1,0:T(8,128)S(1)}, u32[]{:S(2)}) copy-start(f32[65,8,256]{2,1,0:T(8,128)S(1)} %multiply_select_fusion.hn_ref) | copy-start | bytes 1597444
  39.4 13.3 %collective-permute-start.5 = (f32[65,80,8]{1,2,0:T(8,128)S(1)}, f32[65,80,8]{1,2,0:T(8,128)S(1)}, u32[]{:S(2)}, u32[]{:S(2)}) collective-permute-start(f32[65,80,8]{1,2,0:T(8,128)S(1)} %pad_maximum_fusion.5), channel_id=1, source_target_pairs={{1,0},{2,1},{3,2},{4,3},{5,4},{6,5},{7,6},{8,7},{9,8},{10,9},{11,1... | collective-permute-start | bytes 499208 | tf_op jit(solution)/shard_map/ppermute | solution.py:60
  46.2 13.1 %collective-permute-start.6 = (f32[65,80,8]{1,2,0:T(8,128)S(1)}, f32[65,80,8]{1,2,0:T(8,128)S(1)}, u32[]{:S(2)}, u32[]{:S(2)}) collective-permute-start(f32[65,80,8]{1,2,0:T(8,128)S(1)} %pad_maximum_fusion.6), channel_id=1, source_target_pairs={{0,1},{1,2},{2,3},{3,4},{4,5},{5,6},{6,7},{7,8},{8,9},{9,10},{10,1... | collective-permute-start | bytes 499208 | tf_op jit(solution)/shard_map/ppermute | solution.py:59
  68.5 7.9 %collective-permute-start = (f32[8,2,68]{2,1,0:T(2,128)S(1)}, f32[8,2,68]{2,1,0:T(2,128)S(1)}, u32[]{:S(2)}, u32[]{:S(2)}) collective-permute-start(f32[8,2,68]{2,1,0:T(2,128)S(1)} %get-tuple-element.62), channel_id=1, source_target_pairs={{0,16},{16,32},{32,48},{48,64},{64,80},{80,96},{96,112},{1,17},{17... | collective-permute-start | bytes 13064 | tf_op jit(solution)/shard_map/ppermute | solution.py:186
  73.4 5.0 %collective-permute-start.1 = (f32[8,2,68]{2,1,0:T(2,128)S(1)}, f32[8,2,68]{2,1,0:T(2,128)S(1)}, u32[]{:S(2)}, u32[]{:S(2)}) collective-permute-start(f32[8,2,68]{2,1,0:T(2,128)S(1)} %get-tuple-element.63), channel_id=1, source_target_pairs={{16,0},{32,16},{48,32},{64,48},{80,64},{96,80},{112,96},{17,1},{33... | collective-permute-start | bytes 13064 | tf_op jit(solution)/shard_map/ppermute | solution.py:187
  82.2 9.1 %copy-start.5 = (s32[4,64,256]{2,1,0:T(8,128)S(1)}, s32[4,64,256]{2,1,0:T(8,128)}, u32[]{:S(2)}) copy-start(s32[4,64,256]{2,1,0:T(8,128)} %param.13) | copy-start | bytes 786436
  82.2 9.1 %copy-start.8 = (f32[4,64,256]{2,1,0:T(8,128)S(1)}, f32[4,64,256]{2,1,0:T(8,128)}, u32[]{:S(2)}) copy-start(f32[4,64,256]{2,1,0:T(8,128)} %param.14) | copy-start | bytes 786436
  91.3 7.6 %copy-start.12 = (f32[2,8]{1,0:T(2,128)S(1)}, f32[2,8]{1,0:T(2,128)}, u32[]{:S(2)}) copy-start(f32[2,8]{1,0:T(2,128)} %param.15) | copy-start | bytes 196
  100.1 15.5 %copy-start.7 = (f32[2,64,256]{2,1,0:T(8,128)}, f32[2,64,256]{2,1,0:T(8,128)S(1)}, u32[]{:S(2)}) copy-start(f32[2,64,256]{2,1,0:T(8,128)S(1)} %multiply_reduce_fusion.1.f_ref) | copy-start | bytes 393220
  100.1 5.1 %collective-permute-start.7 = (f32[2,8,256]{2,1,0:T(8,128)S(1)}, f32[2,8,256]{2,1,0:T(8,128)S(1)}, u32[]{:S(2)}, u32[]{:S(2)}) collective-permute-start(f32[2,8,256]{2,1,0:T(8,128)S(1)} %get-tuple-element.81), channel_id=1, source_target_pairs={{120,112},{119,113},{118,114},{117,115},{116,116},{115,117},{114,1... | collective-permute-start | bytes 49160 | tf_op jit(solution)/shard_map/ppermute | solution.py:45
  100.8 7.1 %collective-permute-start.9 = (f32[2,8,256]{2,1,0:T(8,128)S(1)}, f32[2,8,256]{2,1,0:T(8,128)S(1)}, u32[]{:S(2)}, u32[]{:S(2)}) collective-permute-start(f32[2,8,256]{2,1,0:T(8,128)S(1)} %get-tuple-element.81), channel_id=1, source_target_pairs={{0,16},{16,32},{32,48},{48,64},{64,80},{80,96},{96,112},{1,17},{17... | collective-permute-start | bytes 49160 | tf_op jit(solution)/shard_map/ppermute | solution.py:42
  102.7 5.1 %collective-permute-start.8 = (f32[2,8,256]{2,1,0:T(8,128)S(1)}, f32[2,8,256]{2,1,0:T(8,128)S(1)}, u32[]{:S(2)}, u32[]{:S(2)}) collective-permute-start(f32[2,8,256]{2,1,0:T(8,128)S(1)} %get-tuple-element.80), channel_id=1, source_target_pairs={{16,0},{32,16},{48,32},{64,48},{80,64},{96,80},{112,96},{17,1},{33... | collective-permute-start | bytes 49160 | tf_op jit(solution)/shard_map/ppermute | solution.py:43
  107.8 7.8 %copy-start.9 = (f32[2,8,256]{2,1,0:T(8,128)}, f32[2,8,256]{2,1,0:T(8,128)S(1)}, u32[]{:S(2)}) copy-start(f32[2,8,256]{2,1,0:T(8,128)S(1)} %broadcast_select_fusion.fn_ref) | copy-start | bytes 49156
  107.9 7.7 %copy-start.10 = (f32[2,8,256]{2,1,0:T(8,128)}, f32[2,8,256]{2,1,0:T(8,128)S(1)}, u32[]{:S(2)}) copy-start(f32[2,8,256]{2,1,0:T(8,128)S(1)} %collective-permute-done.9.fs_ref) | copy-start | bytes 49156
  108.0 7.6 %collective-permute-start.10 = (f32[2,80,8]{2,1,0:T(8,128)S(1)}, f32[2,80,8]{2,1,0:T(8,128)S(1)}, u32[]{:S(2)}, u32[]{:S(2)}) collective-permute-start(f32[2,80,8]{2,1,0:T(8,128)S(1)} %pad_maximum_fusion.8), channel_id=1, source_target_pairs={{1,0},{2,1},{3,2},{4,3},{5,4},{6,5},{7,6},{8,7},{9,8},{10,9},{11,1... | collective-permute-start | bytes 15368 | tf_op jit(solution)/shard_map/ppermute | solution.py:60
  110.7 6.8 %collective-permute-start.11 = (f32[2,80,8]{2,1,0:T(8,128)S(1)}, f32[2,80,8]{2,1,0:T(8,128)S(1)}, u32[]{:S(2)}, u32[]{:S(2)}) collective-permute-start(f32[2,80,8]{2,1,0:T(8,128)S(1)} %pad_maximum_fusion.9), channel_id=1, source_target_pairs={{0,1},{1,2},{2,3},{3,4},{4,5},{5,6},{6,7},{7,8},{8,9},{9,10},{10,1... | collective-permute-start | bytes 15368 | tf_op jit(solution)/shard_map/ppermute | solution.py:59
Sparse Core Ops, SparseCore 0:
  17.9 46.2 all-gather.1

commit v4 on v3

--- a/solution.py
+++ b/solution.py
@@ -179,10 +179,11 @@
 def atmosphere_block(atm_flux):
     cols_n = lax.axis_size("ox")
     rows_n = lax.axis_size("oy")
-    band = lax.all_gather(atm_flux, "ox", axis=1, tiled=True)
-    width = band.shape[2] // cols_n
-    ring = jnp.concatenate([band[..., -H:], band, band[..., :H]], axis=2)
-    own = lax.dynamic_slice_in_dim(ring, lax.axis_index("ox") * width, width + 2 * H, axis=2)
+    width = atm_flux.shape[2] // cols_n
+    ring = jnp.concatenate([atm_flux[..., -H:], atm_flux, atm_flux[..., :H]], axis=2)
+    pieces = jnp.stack([ring[..., i * width:(i + 1) * width + 2 * H] for i in range(cols_n)])
+    got = lax.all_to_all(pieces, "ox", split_axis=0, concat_axis=0, tiled=True)
+    own = jnp.concatenate(list(got), axis=1)
     below = lax.ppermute(own[:, -H:], "oy", [(i, i + 1) for i in range(rows_n - 1)])
     above = lax.ppermute(own[:, :H], "oy", [(i + 1, i) for i in range(rows_n - 1)])
     return jnp.concatenate([below, own, above], axis=1)

time: 176 us -> 166 us (0.943); the launches traced: 175 us -> 163 us
  between operations: 15.1 us -> 1.81 us
  starting transfers between devices: 28.9 us -> 37.1 us
  waiting for transfers between devices: 17.8 us -> 11 us
  local copies, waits for them, and re-layouts: 25.8 us -> 28.4 us
  matrix products: 10.6 us -> 8.76 us
    unnamed x29 -> x54, local copies, waits for them, and re-layouts: 0.74 us -> 9.48 us
    all_to_all x0 -> x1, starting transfers between devices: none -> 7.82 us  [atmosphere_block(): got = lax.all_to_all(pieces, 'ox', split_axis=0, concat_axis=0, tiled=True)]
    all_gather x1 -> x0, waiting for transfers between devices: 2.76 us -> none  [atmosphere_block(): band = lax.all_gather(atm_flux, 'ox', axis=1, tiled=True)]
    ppermute x2, waiting for transfers between devices: 2.42 us -> 0.01 us  [exchange(): north = lax.ppermute(bots, 'oy', [(i + 1, i) for i in range(rows_n - 1)])]
    ppermute x1, waiting for transfers between devices: 1.97 us -> 0.01 us  [atmosphere_block(): lax.ppermute(own[:, :H], 'oy', [(i + 1, i) for i in range(rows_n - 1)])]
    all_gather x1 -> x0, local copies, waits for them, and re-layouts: 1.84 us -> none  [atmosphere_block(): band = lax.all_gather(atm_flux, 'ox', axis=1, tiled=True)]
  transfers between devices with their start and end apart: 13 -> 13, of which waited for: 6 -> 3; matrix products, arithmetic and copies ran while one was open for 19% -> 32% of each run, Pallas kernels for 0% -> 0%
where the time goes in v4:
time: 166 us; the launch traced here: 163 us
  Pallas kernels  50.4 us (30%)
  starting transfers between devices  37.1 us (22%)
  local copies, waits for them, and re-layouts  28.4 us (17%)
  other arithmetic  25.8 us (16%)
  waiting for transfers between devices  11 us (7%)
  matrix products  8.76 us (5%)
  between operations  1.81 us (1%)
    pallas_call x1, Pallas kernels, evolve(): pl.pallas_call(stencil_kernel, out_shape=jax.ShapeDtypeStruct(tracers.sha...  50.4 us
    ppermute x2, starting transfers between devices, exchange(): lax.ppermute(wests, 'ox', [((i + 1) % cols_n, i) for i in range(cols_n)])  9.54 us
    unnamed x54, local copies, waits for them, and re-layouts  9.48 us
    dot_general x1, matrix products, remap(): window = jnp.einsum('fpb,bq->fpq', lifted, pick_c, precision=HIGH)  8.19 us
    ppermute x2, starting transfers between devices, exchange(): south = lax.ppermute(tops, 'oy', [(i, i + 1) for i in range(rows_n - 1)])  8.14 us
    all_to_all x1, starting transfers between devices, atmosphere_block(): got = lax.all_to_all(pieces, 'ox', split_axis=0, concat_axis=0, tiled=True)  7.82 us
    reduce_sum x1, other arithmetic, remap(): fast = jnp.sum(window * wsum.transpose(0, 2, 1, 3)[None], axis=(1, 3))  7.37 us
    ppermute x2, waiting for transfers between devices, exchange(): lax.ppermute(easts, 'ox', [(i, (i + 1) % cols_n) for i in range(cols_n)])  6.35 us
  transfers between devices with their start and end apart: 13, of which 3 were waited for; matrix products, arithmetic and copies ran while one was open for 32% of the time, Pallas kernels for 0%

profile of v4, /device:TPU:1, one launch (start us, length us, event | category | flops | bytes accessed | tf_op | source)
XLA Modules:
  0.0 163.4 jit_solution(8000482623243550210)
XLA Ops:
  0.7 1.2 fusion.22
  2.7 1.0 fusion.27
  4.5 1.5 collective-permute-start.2
  6.0 4.5 %collective-permute-start.4 = (f32[65,8,256]{2,1,0:T(8,128)}, f32[65,8,256]{2,1,0:T(8,128)}, u32[]{:S(2)}, u32[]{:S(2)}) collective-permute-start(f32[65,8,256]{2,1,0:T(8,128)} %pad_maximum_fusion.3), channel_id=1, source_target_pairs={{0,16},{16,32},{32,48},{48,64},{64,80},{80,96},{96,112},{1,17},{17... | collective-permute-start | bytes 1597448 | tf_op jit(solution)/shard_map/ppermute | solution.py:42
  21.4 7.8 %all-to-all-start = ((f32[16,8,2,68]{3,2,1,0:T(2,128)}), f32[16,8,2,68]{3,2,1,0:T(2,128)}, u32[]{:S(2)}, u32[]{:S(2)}) async-start(f32[16,8,2,68]{3,2,1,0:T(2,128)} %constant_dynamic-update-slice_fusion), calls=%async_computation | async-start | bytes 262144 | tf_op jit(solution)/shard_map/all_to_all | solution.py:185
  30.0 1.9 %collective-permute-start.3 = (f32[65,8,256]{2,1,0:T(8,128)}, f32[65,8,256]{2,1,0:T(8,128)}, u32[]{:S(2)}, u32[]{:S(2)}) collective-permute-start(f32[65,8,256]{2,1,0:T(8,128)} %pad_maximum_fusion.4), channel_id=1, source_target_pairs={{16,0},{32,16},{48,32},{64,48},{80,64},{96,80},{112,96},{17,1},{33... | collective-permute-start | bytes 1597448 | tf_op jit(solution)/shard_map/ppermute | solution.py:43
  32.0 1.7 %fusion.21 = (f32[32,64,8]{2,1,0:T(8,128)}, f32[32,64,8]{2,1,0:T(8,128)}) fusion(f32[32,64,256]{2,1,0:T(8,128)S(1)} %bitcast.158), kind=kLoop, calls=%fused_computation.109 | loop fusion | bytes 262144 | tf_op jit(solution)/shard_map/slice | solution.py:56
  33.8 1.0 fusion.25
  34.8 1.0 fusion.26
  36.5 1.9 %select_reduce_fusion = f32[25,64,256]{2,1,0:T(8,128)} fusion(f32[4,64,256]{2,1,0:T(8,128)S(1)} %copy-done.14, s32[4,64,256]{2,1,0:T(8,128)S(1)} %get-tuple-element.44), kind=kLoop, calls=%fused_computation.32 | loop fusion | flops 4505600 | bytes 2162688 | tf_op jit(solution)/shard_map/reduce_sum | solution.py:214
  38.4 3.3 %pad_maximum_fusion.1 = (f32[65,64,8]{2,1,0:T(8,128)}, f32[65,64,8]{2,1,0:T(8,128)S(1)}) fusion(f32[1,64,8]{2,1,0:T(8,128)S(1)} %get-tuple-element.94, f32[16,64,8]{2,1,0:T(8,128)S(1)} %copy-done.10, f32[16,64,8]{2,1,0:T(8,128)S(1)} %copy-done.8, f32[32,64,8]{2,1,0:T(8,128)S(1)} %copy-done.5, f32[1,64,8]{2,1,0:T(8,128)S(1)} %get-tuple-element.95, ...), kind=kLoop, calls=%fused_computation.35 | loop fusion | flops 199680 | bytes 532480 | tf_op jit(solution)/shard_map/concatenate | solution.py:56
  42.6 3.6 %collective-permute-start = (f32[8,2,68]{2,1,0:T(2,128)S(1)}, f32[8,2,68]{2,1,0:T(2,128)S(1)}, u32[]{:S(2)}, u32[]{:S(2)}) collective-permute-start(f32[8,2,68]{2,1,0:T(2,128)S(1)} %get-tuple-element.93), channel_id=1, source_target_pairs={{0,16},{16,32},{32,48},{48,64},{64,80},{80,96},{96,112},{1,17},{17... | collective-permute-start | bytes 13064 | tf_op jit(solution)/shard_map/ppermute | solution.py:187
  46.2 1.9 %collective-permute-start.1 = (f32[8,2,68]{2,1,0:T(2,128)S(1)}, f32[8,2,68]{2,1,0:T(2,128)S(1)}, u32[]{:S(2)}, u32[]{:S(2)}) collective-permute-start(f32[8,2,68]{2,1,0:T(2,128)S(1)} %get-tuple-element.92), channel_id=1, source_target_pairs={{16,0},{32,16},{48,32},{64,48},{80,64},{96,80},{112,96},{17,1},{33... | collective-permute-start | bytes 13064 | tf_op jit(solution)/shard_map/ppermute | solution.py:188
  50.0 2.9 %copy.67 = f32[65,64,8]{1,2,0:T(8,128)} copy(f32[65,64,8]{2,1,0:T(8,128)} %get-tuple-element.106) | data formatting | bytes 266240 | tf_op jit(solution)/shard_map/concatenate | solution.py:56
  52.9 1.3 copy.70
  55.5 8.2 %fusion.7 = f32[8,5,64,5,256]{4,2,3,1,0:T(8,128)} fusion(f32[8,5,64,68,1]{3,2,4,1,0:T(8,128)S(1)} %bitcast.159, pred[5,256,68,1,1]{1,0,2,4,3:T(8,128)(4,1)S(1)} %bitcast.165), kind=kOutput, calls=%fused_computation.45 | convolution fusion | flops 2673868800 | bytes 13890560 | tf_op jit(solution)/shard_map/fpb,bq->fpq/dot_general | solution.py:207
  63.7 7.4 %conditional.1 = (f32[8,64,256]{2,1,0:T(8,128)}) conditional(s32[]{:T(128)} %convert_element_type.14, (f32[5,64,5,256]{3,1,2,0:T(8,128)S(1)}, f32[8,5,64,5,256]{4,2,3,1,0:T(8,128)}) %tuple.75, (f32[4,64,256]{2,1,0:T(8,128)}, f32[8,36,68]{2,1,0:T(8,128)S(1)}, s32[4,64,256]{2,1,0:T(8,128)S(1)}) %tuple.76), branch_computations={%region_2.4_spmd, %region_4.6_spmd} | conditional | flops 6422528 | bytes 15269896 | solution.py:229
  63.7 7.4 %multiply_reduce_fusion = f32[8,64,256]{2,1,0:T(8,128)} fusion(f32[8,5,64,5,256]{4,2,3,1,0:T(8,128)} %get-tuple-element.19, f32[5,64,5,256]{3,1,2,0:T(8,128)S(1)} %get-tuple-element.20), kind=kLoop, calls=%fused_computation.4 | loop fusion | flops 6422528 | bytes 15269888 | tf_op jit(solution)/shard_map/reduce_sum | solution.py:218
  71.1 1.2 multiply_reduce_fusion.1.f_ref
  73.0 1.9 %collective-permute-start.8 = (f32[2,8,256]{2,1,0:T(8,128)S(1)}, f32[2,8,256]{2,1,0:T(8,128)S(1)}, u32[]{:S(2)}, u32[]{:S(2)}) collective-permute-start(f32[2,8,256]{2,1,0:T(8,128)S(1)} %get-tuple-element.76), channel_id=1, source_target_pairs={{16,0},{32,16},{48,32},{64,48},{80,64},{96,80},{112,96},{17,1},{33... | collective-permute-start | bytes 49160 | tf_op jit(solution)/shard_map/ppermute | solution.py:43
  75.0 3.6 %collective-permute-start.9 = (f32[2,8,256]{2,1,0:T(8,128)S(1)}, f32[2,8,256]{2,1,0:T(8,128)S(1)}, u32[]{:S(2)}, u32[]{:S(2)}) collective-permute-start(f32[2,8,256]{2,1,0:T(8,128)S(1)} %get-tuple-element.77), channel_id=1, source_target_pairs={{0,16},{16,32},{32,48},{48,64},{64,80},{80,96},{96,112},{1,17},{17... | collective-permute-start | bytes 49160 | tf_op jit(solution)/shard_map/ppermute | solution.py:42
  79.6 4.7 %collective-permute-start.10 = (f32[2,80,8]{2,1,0:T(8,128)S(1)}, f32[2,80,8]{2,1,0:T(8,128)S(1)}, u32[]{:S(2)}, u32[]{:S(2)}) collective-permute-start(f32[2,80,8]{2,1,0:T(8,128)S(1)} %pad_maximum_fusion.7), channel_id=1, source_target_pairs={{1,0},{2,1},{3,2},{4,3},{5,4},{6,5},{7,6},{8,7},{9,8},{10,9},{11,1... | collective-permute-start | bytes 15368 | tf_op jit(solution)/shard_map/ppermute | solution.py:60
  84.4 1.2 rev.6
  85.7 1.2 multiply_select_fusion.hn_ref
  87.2 1.2 fusion.24
  88.8 4.8 %collective-permute-start.5 = (f32[65,80,8]{1,2,0:T(8,128)S(1)}, f32[65,80,8]{1,2,0:T(8,128)S(1)}, u32[]{:S(2)}, u32[]{:S(2)}) collective-permute-start(f32[65,80,8]{1,2,0:T(8,128)S(1)} %pad_maximum_fusion.5), channel_id=1, source_target_pairs={{1,0},{2,1},{3,2},{4,3},{5,4},{6,5},{7,6},{8,7},{9,8},{10,9},{11,1... | collective-permute-start | bytes 499208 | tf_op jit(solution)/shard_map/ppermute | solution.py:60
  93.9 0.9 pad_maximum_fusion.6
  95.5 4.0 %collective-permute-done.5 = f32[65,80,8]{1,2,0:T(8,128)S(1)} collective-permute-done((f32[65,80,8]{1,2,0:T(8,128)S(1)}, f32[65,80,8]{1,2,0:T(8,128)S(1)}, u32[]{:S(2)}, u32[]{:S(2)}) %collective-permute-start.5) | collective-permute-done | bytes 166432 | tf_op jit(solution)/shard_map/ppermute | solution.py:60
  100.3 6.3 %collective-permute-done.6 = f32[65,80,8]{1,2,0:T(8,128)S(1)} collective-permute-done((f32[65,80,8]{1,2,0:T(8,128)}, f32[65,80,8]{1,2,0:T(8,128)S(1)}, u32[]{:S(2)}, u32[]{:S(2)}) %collective-permute-start.6) | collective-permute-done | bytes 166432 | tf_op jit(solution)/shard_map/ppermute | solution.py:59
  106.7 2.3 %copy.74 = f32[65,80,8]{2,1,0:T(8,128)} copy(f32[65,80,8]{1,2,0:T(8,128)S(1)} %collective-permute-done.6) | data formatting | bytes 332800 | tf_op jit(solution)/shard_map/ppermute | solution.py:59
  109.0 4.0 %pad_maximum_fusion.hc_ref = f32[65,80,128]{2,1,0:T(8,128)} fusion(f32[65,80,8]{2,1,0:T(8,128)} %copy.74, f32[65,80,8]{2,1,0:T(8,128)S(1)} %copy.73, f32[128]{0:T(128)S(1)} %pad.10.clone), kind=kLoop, calls=%fused_computation.34 | loop fusion | flops 1331200 | bytes 2995712 | tf_op jit(solution)/shard_map/concatenate | solution.py:62
  113.0 50.4 %shard_map.95 = f32[2,16,64,256]{3,2,1,0:T(8,128)} custom-call(f32[2,16,64,256]{3,2,1,0:T(8,128)} %tr_ref.1, bf16[16,64,256]{2,1,0:T(8,128)(2,1)} %u_ref.1, bf16[16,64,256]{2,1,0:T(8,128)(2,1)} %v_ref.1, s32[64,256]{1,0:T(8,128)} %m_ref.1, f32[2,64,256]{2,1,0:T(8,128)} %copy-done.11, f32[65,8,256]{2,1,0:T(8,128)} %copy-done.4, ...), custom_call_target="tpu_custom_call" | custom-call | tf_op jit(solution)/shard_map/pallas_call | solution.py:158
  (115 shorter events, 21.4 us)
Async XLA Ops:
  0.6 31.4 %copy-start = (f32[2,16,64,256]{3,2,1,0:T(8,128)S(1)}, f32[2,16,64,256]{3,2,1,0:T(8,128)}, u32[]{:S(2)}) copy-start(f32[2,16,64,256]{3,2,1,0:T(8,128)} %tr_ref.1) | copy-start | bytes 6291460
  0.6 9.9 %copy-start.16 = (f32[8,2,1024]{2,1,0:T(2,128)S(1)}, f32[8,2,1024]{2,1,0:T(2,128)}, u32[]{:S(2)}) copy-start(f32[8,2,1024]{2,1,0:T(2,128)} %param.12) | copy-start | bytes 196612
  4.5 79.8 %collective-permute-start.2 = (f32[65,8,256]{2,1,0:T(8,128)}, f32[65,8,256]{2,1,0:T(8,128)}, u32[]{:S(2)}, u32[]{:S(2)}) collective-permute-start(f32[65,8,256]{2,1,0:T(8,128)} %pad_maximum_fusion.3), channel_id=1, source_target_pairs={{120,112},{119,113},{118,114},{117,115},{116,116},{115,117},{114,1... | collective-permute-start | bytes 1597448 | tf_op jit(solution)/shard_map/ppermute | solution.py:45
  6.0 81.2 %collective-permute-start.4 = (f32[65,8,256]{2,1,0:T(8,128)}, f32[65,8,256]{2,1,0:T(8,128)}, u32[]{:S(2)}, u32[]{:S(2)}) collective-permute-start(f32[65,8,256]{2,1,0:T(8,128)} %pad_maximum_fusion.3), channel_id=1, source_target_pairs={{0,16},{16,32},{32,48},{48,64},{64,80},{80,96},{96,112},{1,17},{17... | collective-permute-start | bytes 1597448 | tf_op jit(solution)/shard_map/ppermute | solution.py:42
  21.4 20.3 %all-to-all-start = ((f32[16,8,2,68]{3,2,1,0:T(2,128)}), f32[16,8,2,68]{3,2,1,0:T(2,128)}, u32[]{:S(2)}, u32[]{:S(2)}) async-start(f32[16,8,2,68]{3,2,1,0:T(2,128)} %constant_dynamic-update-slice_fusion), calls=%async_computation | async-start | bytes 262144 | tf_op jit(solution)/shard_map/all_to_all | solution.py:185
  29.2 4.6 %copy-start.2 = (bf16[16,64,256]{2,1,0:T(8,128)(2,1)S(1)}, bf16[16,64,256]{2,1,0:T(8,128)(2,1)}, u32[]{:S(2)}) copy-start(bf16[16,64,256]{2,1,0:T(8,128)(2,1)} %u_ref.1) | copy-start | bytes 1572868
  30.0 55.6 %collective-permute-start.3 = (f32[65,8,256]{2,1,0:T(8,128)}, f32[65,8,256]{2,1,0:T(8,128)}, u32[]{:S(2)}, u32[]{:S(2)}) collective-permute-start(f32[65,8,256]{2,1,0:T(8,128)} %pad_maximum_fusion.4), channel_id=1, source_target_pairs={{16,0},{32,16},{48,32},{64,48},{80,64},{96,80},{112,96},{17,1},{33... | collective-permute-start | bytes 1597448 | tf_op jit(solution)/shard_map/ppermute | solution.py:43
  32.0 2.8 %copy-start.3 = (bf16[16,64,256]{2,1,0:T(8,128)(2,1)S(1)}, bf16[16,64,256]{2,1,0:T(8,128)(2,1)}, u32[]{:S(2)}) copy-start(bf16[16,64,256]{2,1,0:T(8,128)(2,1)} %v_ref.1) | copy-start | bytes 1572868
  33.7 2.8 %copy-start.14 = (f32[4,64,256]{2,1,0:T(8,128)S(1)}, f32[4,64,256]{2,1,0:T(8,128)}, u32[]{:S(2)}) copy-start(f32[4,64,256]{2,1,0:T(8,128)} %param.14) | copy-start | bytes 786436
  35.9 2.5 %copy-start.5 = (f32[32,64,8]{2,1,0:T(8,128)S(1)}, f32[32,64,8]{2,1,0:T(8,128)}, u32[]{:S(2)}) copy-start(f32[32,64,8]{2,1,0:T(8,128)} %get-tuple-element.58) | copy-start | bytes 196612
  36.0 2.4 %copy-start.8 = (f32[16,64,8]{2,1,0:T(8,128)S(1)}, f32[16,64,8]{2,1,0:T(8,128)}, u32[]{:S(2)}) copy-start(f32[16,64,8]{2,1,0:T(8,128)} %get-tuple-element.66) | copy-start | bytes 98308
  36.0 2.4 %copy-start.9 = (f32[16,64,8]{2,1,0:T(8,128)S(1)}, f32[16,64,8]{2,1,0:T(8,128)}, u32[]{:S(2)}) copy-start(f32[16,64,8]{2,1,0:T(8,128)} %get-tuple-element.67) | copy-start | bytes 98308
  36.0 2.4 %copy-start.10 = (f32[16,64,8]{2,1,0:T(8,128)S(1)}, f32[16,64,8]{2,1,0:T(8,128)}, u32[]{:S(2)}) copy-start(f32[16,64,8]{2,1,0:T(8,128)} %get-tuple-element.68) | copy-start | bytes 98308
  42.6 11.7 %collective-permute-start = (f32[8,2,68]{2,1,0:T(2,128)S(1)}, f32[8,2,68]{2,1,0:T(2,128)S(1)}, u32[]{:S(2)}, u32[]{:S(2)}) collective-permute-start(f32[8,2,68]{2,1,0:T(2,128)S(1)} %get-tuple-element.93), channel_id=1, source_target_pairs={{0,16},{16,32},{32,48},{48,64},{64,80},{80,96},{96,112},{1,17},{17... | collective-permute-start | bytes 13064 | tf_op jit(solution)/shard_map/ppermute | solution.py:187
  46.2 8.1 %collective-permute-start.1 = (f32[8,2,68]{2,1,0:T(2,128)S(1)}, f32[8,2,68]{2,1,0:T(2,128)S(1)}, u32[]{:S(2)}, u32[]{:S(2)}) collective-permute-start(f32[8,2,68]{2,1,0:T(2,128)S(1)} %get-tuple-element.92), channel_id=1, source_target_pairs={{16,0},{32,16},{48,32},{64,48},{80,64},{96,80},{112,96},{17,1},{33... | collective-permute-start | bytes 13064 | tf_op jit(solution)/shard_map/ppermute | solution.py:188
  55.5 8.2 %copy-start.1 = (f32[25,64,256]{2,1,0:T(8,128)S(1)}, f32[25,64,256]{2,1,0:T(8,128)}, u32[]{:S(2)}) copy-start(f32[25,64,256]{2,1,0:T(8,128)} %select_reduce_fusion) | copy-start | bytes 4915204
  55.5 8.2 %copy-start.7 = (s32[4,64,256]{2,1,0:T(8,128)S(1)}, s32[4,64,256]{2,1,0:T(8,128)}, u32[]{:S(2)}) copy-start(s32[4,64,256]{2,1,0:T(8,128)} %param.13) | copy-start | bytes 786436
  63.7 7.4 %copy-start.19 = (f32[2,8]{1,0:T(2,128)S(1)}, f32[2,8]{1,0:T(2,128)}, u32[]{:S(2)}) copy-start(f32[2,8]{1,0:T(2,128)} %param.15) | copy-start | bytes 196
  63.7 22.0 %copy-start.20 = (f32[65]{0:T(128)S(1)}, f32[65]{0:T(128)}, u32[]{:S(2)}) copy-start(f32[65]{0:T(128)} %constant.79.clone.1) | copy-start | bytes 784
  72.3 16.1 %copy-start.11 = (f32[2,64,256]{2,1,0:T(8,128)}, f32[2,64,256]{2,1,0:T(8,128)S(1)}, u32[]{:S(2)}) copy-start(f32[2,64,256]{2,1,0:T(8,128)S(1)} %multiply_reduce_fusion.1.f_ref) | copy-start | bytes 393220
  72.3 2.7 %collective-permute-start.7 = (f32[2,8,256]{2,1,0:T(8,128)S(1)}, f32[2,8,256]{2,1,0:T(8,128)S(1)}, u32[]{:S(2)}, u32[]{:S(2)}) collective-permute-start(f32[2,8,256]{2,1,0:T(8,128)S(1)} %get-tuple-element.77), channel_id=1, source_target_pairs={{120,112},{119,113},{118,114},{117,115},{116,116},{115,117},{114,1... | collective-permute-start | bytes 49160 | tf_op jit(solution)/shard_map/ppermute | solution.py:45
  73.0 5.8 %collective-permute-start.8 = (f32[2,8,256]{2,1,0:T(8,128)S(1)}, f32[2,8,256]{2,1,0:T(8,128)S(1)}, u32[]{:S(2)}, u32[]{:S(2)}) collective-permute-start(f32[2,8,256]{2,1,0:T(8,128)S(1)} %get-tuple-element.76), channel_id=1, source_target_pairs={{16,0},{32,16},{48,32},{64,48},{80,64},{96,80},{112,96},{17,1},{33... | collective-permute-start | bytes 49160 | tf_op jit(solution)/shard_map/ppermute | solution.py:43
  75.0 4.5 %collective-permute-start.9 = (f32[2,8,256]{2,1,0:T(8,128)S(1)}, f32[2,8,256]{2,1,0:T(8,128)S(1)}, u32[]{:S(2)}, u32[]{:S(2)}) collective-permute-start(f32[2,8,256]{2,1,0:T(8,128)S(1)} %get-tuple-element.77), channel_id=1, source_target_pairs={{0,16},{16,32},{32,48},{48,64},{64,80},{80,96},{96,112},{1,17},{17... | collective-permute-start | bytes 49160 | tf_op jit(solution)/shard_map/ppermute | solution.py:42
  78.8 9.6 %copy-start.17 = (f32[2,8,256]{2,1,0:T(8,128)}, f32[2,8,256]{2,1,0:T(8,128)S(1)}, u32[]{:S(2)}) copy-start(f32[2,8,256]{2,1,0:T(8,128)S(1)} %broadcast_select_fusion.fn_ref) | copy-start | bytes 49156
  79.5 8.9 %copy-start.18 = (f32[2,8,256]{2,1,0:T(8,128)}, f32[2,8,256]{2,1,0:T(8,128)S(1)}, u32[]{:S(2)}) copy-start(f32[2,8,256]{2,1,0:T(8,128)S(1)} %collective-permute-done.9.fs_ref) | copy-start | bytes 49156
  79.6 15.2 %collective-permute-start.10 = (f32[2,80,8]{2,1,0:T(8,128)S(1)}, f32[2,80,8]{2,1,0:T(8,128)S(1)}, u32[]{:S(2)}, u32[]{:S(2)}) collective-permute-start(f32[2,80,8]{2,1,0:T(8,128)S(1)} %pad_maximum_fusion.7), channel_id=1, source_target_pairs={{1,0},{2,1},{3,2},{4,3},{5,4},{6,5},{7,6},{8,7},{9,8},{10,9},{11,1... | collective-permute-start | bytes 15368 | tf_op jit(solution)/shard_map/ppermute | solution.py:60
  84.3 10.5 %collective-permute-start.11 = (f32[2,80,8]{2,1,0:T(8,128)S(1)}, f32[2,80,8]{2,1,0:T(8,128)S(1)}, u32[]{:S(2)}, u32[]{:S(2)}) collective-permute-start(f32[2,80,8]{2,1,0:T(8,128)S(1)} %pad_maximum_fusion.8), channel_id=1, source_target_pairs={{0,1},{1,2},{2,3},{3,4},{4,5},{5,6},{6,7},{7,8},{8,9},{9,10},{10,1... | collective-permute-start | bytes 15368 | tf_op jit(solution)/shard_map/ppermute | solution.py:59
  85.6 2.9 %copy-start.13 = (f32[65,64,8]{1,2,0:T(8,128)S(1)}, f32[65,64,8]{1,2,0:T(8,128)}, u32[]{:S(2)}) copy-start(f32[65,64,8]{1,2,0:T(8,128)} %copy.67) | copy-start | bytes 399364
  86.9 7.0 %copy-start.4 = (f32[65,8,256]{2,1,0:T(8,128)}, f32[65,8,256]{2,1,0:T(8,128)S(1)}, u32[]{:S(2)}) copy-start(f32[65,8,256]{2,1,0:T(8,128)S(1)} %multiply_select_fusion.hn_ref) | copy-start | bytes 1597444
  86.9 7.0 %copy-start.12 = (f32[65,64,8]{1,2,0:T(8,128)S(1)}, f32[65,64,8]{1,2,0:T(8,128)}, u32[]{:S(2)}) copy-start(f32[65,64,8]{1,2,0:T(8,128)} %copy.70) | copy-start | bytes 399364
  88.8 10.8 %collective-permute-start.5 = (f32[65,80,8]{1,2,0:T(8,128)S(1)}, f32[65,80,8]{1,2,0:T(8,128)S(1)}, u32[]{:S(2)}, u32[]{:S(2)}) collective-permute-start(f32[65,80,8]{1,2,0:T(8,128)S(1)} %pad_maximum_fusion.5), channel_id=1, source_target_pairs={{1,0},{2,1},{3,2},{4,3},{5,4},{6,5},{7,6},{8,7},{9,8},{10,9},{11,1... | collective-permute-start | bytes 499208 | tf_op jit(solution)/shard_map/ppermute | solution.py:60
  94.8 11.9 %collective-permute-start.6 = (f32[65,80,8]{1,2,0:T(8,128)}, f32[65,80,8]{1,2,0:T(8,128)S(1)}, u32[]{:S(2)}, u32[]{:S(2)}) collective-permute-start(f32[65,80,8]{1,2,0:T(8,128)} %pad_maximum_fusion.6), channel_id=1, source_target_pairs={{0,1},{1,2},{2,3},{3,4},{4,5},{5,6},{6,7},{7,8},{8,9},{9,10},{10,1... | collective-permute-start | bytes 499208 | tf_op jit(solution)/shard_map/ppermute | solution.py:59
  (1 other events, 2.4 us)

commit v5 on v4

--- a/solution.py
+++ b/solution.py
@@ -113,36 +113,44 @@
 
     lax.fori_loop(0, nk, coef, 0)
 
-    def plane(src, dst, t, k, above, below, forced):
-        p = t * nk + k
-        s = buf[src, p]
-        west = pltpu.roll(s, 1, 1)
-        east = pltpu.roll(s, lanes - 1, 1)
-        south = pltpu.roll(s, 1, 0)
-        north = pltpu.roll(s, rows - 1, 0)
-        above = s if above is None else buf[src, t * nk + above]
-        below = s if below is None else buf[src, t * nk + below]
-        tend = cw[k] * west + ce[k] * east + cs[k] * south + cn[k] * north + cc[k] * s
-        tend = tend + m8[...] * (above + below)
-        if forced:
-            tend = tend + mf[t]
-        buf[dst, p] = s + tend
+    strips = rows // 8
+    first_row = lax.broadcasted_iota(jnp.int32, (8, lanes), 0) == 0
+    last_row = lax.broadcasted_iota(jnp.int32, (8, lanes), 0) == 7
+
+    def plane(src, dst, k, above, below, forced):
+        for i in range(strips):
+            at = pl.ds(i * 8, 8)
+            before = pl.ds((i - 1) % strips * 8, 8)
+            after = pl.ds((i + 1) % strips * 8, 8)
+            c_w = cw[k, at, :]
+            c_e = ce[k, at, :]
+            c_s = cs[k, at, :]
+            c_n = cn[k, at, :]
+            c_c = cc[k, at, :]
+            c_8 = m8[at, :]
+            for t in range(nt):
+                p = t * nk + k
+                cur = buf[src, p, at, :]
+                south = jnp.where(first_row, pltpu.roll(buf[src, p, before, :], 1, 0), pltpu.roll(cur, 1, 0))
+                north = jnp.where(last_row, pltpu.roll(buf[src, p, after, :], 7, 0), pltpu.roll(cur, 7, 0))
+                west = pltpu.roll(cur, 1, 1)
+                east = pltpu.roll(cur, lanes - 1, 1)
+                up = cur if above is None else buf[src, t * nk + above, at, :]
+                down = cur if below is None else buf[src, t * nk + below, at, :]
+                tend = c_w * west + c_e * east + c_s * south + c_n * north + c_c * cur
+                tend = tend + c_8 * (up + down)
+                if forced:
+                    tend = tend + mf[t, at, :]
+                buf[dst, p, at, :] = cur + tend
 
     def step(i, carry):
-        src = i % 2
-        dst = 1 - src
-        for t in range(nt):
-            plane(src, dst, t, 0, None, 1, True)
-
-            def mid(k, c):
-                plane(src, dst, t, k, k - 1, k + 1, False)
-                return c
-
-            lax.fori_loop(1, nk - 1, mid, 0)
-            plane(src, dst, t, nk - 1, nk - 2, None, False)
-        return carry
-
-    lax.fori_loop(0, STEPS, step, 0)
+        for src in (0, 1):
+            dst = 1 - src
+            for k in range(nk):
+                plane(src, dst, k, k - 1 if k > 0 else None, k + 1 if k < nk - 1 else None, k == 0)
+        return carry
+
+    lax.fori_loop(0, STEPS // 2, step, 0)
 
     def out(p, carry):
         o_ref[p // nk, p % nk] = buf[STEPS % 2, p, :orows, :ocols]

time: 166 us -> 145 us (0.87)
  Pallas kernels: 50.4 us -> 29.4 us
    pallas_call x1, Pallas kernels: 50.4 us -> 29.4 us  [evolve(): pl.pallas_call(stencil_kernel, out_shape=jax.ShapeDtypeStruct(tracers.sha...]
  transfers between devices with their start and end apart: 13 -> 13, of which waited for: 3 -> 3; matrix products, arithmetic and copies ran while one was open for 32% -> 37% of each run, Pallas kernels for 0% -> 0%
where the time goes in v5:
time: 145 us; the launch traced here: 142 us
  starting transfers between devices  37.1 us (26%)
  Pallas kernels  29.4 us (20%)
  local copies, waits for them, and re-layouts  28.4 us (20%)
  other arithmetic  25.8 us (18%)
  waiting for transfers between devices  11 us (8%)
  matrix products  8.76 us (6%)
  between operations  1.81 us (1%)
    pallas_call x1, Pallas kernels, evolve(): pl.pallas_call(stencil_kernel, out_shape=jax.ShapeDtypeStruct(tracers.sha...  29.4 us
    ppermute x2, starting transfers between devices, exchange(): lax.ppermute(wests, 'ox', [((i + 1) % cols_n, i) for i in range(cols_n)])  9.54 us
    unnamed x54, local copies, waits for them, and re-layouts  9.48 us
    dot_general x1, matrix products, remap(): window = jnp.einsum('fpb,bq->fpq', lifted, pick_c, precision=HIGH)  8.19 us
    ppermute x2, starting transfers between devices, exchange(): south = lax.ppermute(tops, 'oy', [(i, i + 1) for i in range(rows_n - 1)])  8.14 us
    all_to_all x1, starting transfers between devices, atmosphere_block(): got = lax.all_to_all(pieces, 'ox', split_axis=0, concat_axis=0, tiled=True)  7.82 us
    reduce_sum x1, other arithmetic, remap(): fast = jnp.sum(window * wsum.transpose(0, 2, 1, 3)[None], axis=(1, 3))  7.37 us
    ppermute x2, waiting for transfers between devices, exchange(): lax.ppermute(easts, 'ox', [(i, (i + 1) % cols_n) for i in range(cols_n)])  6.35 us
  transfers between devices with their start and end apart: 13, of which 3 were waited for; matrix products, arithmetic and copies ran while one was open for 37% of the time, Pallas kernels for 0%

profile of v5, /device:TPU:1, one launch (start us, length us, event | category | flops | bytes accessed | tf_op | source)
XLA Modules:
  0.0 142.3 jit_solution(13666812992250502754)
XLA Ops:
  0.7 1.2 fusion.22
  2.7 1.0 fusion.27
  4.5 1.5 %collective-permute-start.2 = (f32[65,8,256]{2,1,0:T(8,128)}, f32[65,8,256]{2,1,0:T(8,128)}, u32[]{:S(2)}, u32[]{:S(2)}) collective-permute-start(f32[65,8,256]{2,1,0:T(8,128)} %pad_maximum_fusion.3), channel_id=1, source_target_pairs={{120,112},{119,113},{118,114},{117,115},{116,116},{115,117},{114,1... | collective-permute-start | bytes 1597448 | tf_op jit(solution)/shard_map/ppermute | solution.py:45
  6.0 4.5 %collective-permute-start.4 = (f32[65,8,256]{2,1,0:T(8,128)}, f32[65,8,256]{2,1,0:T(8,128)}, u32[]{:S(2)}, u32[]{:S(2)}) collective-permute-start(f32[65,8,256]{2,1,0:T(8,128)} %pad_maximum_fusion.3), channel_id=1, source_target_pairs={{0,16},{16,32},{32,48},{48,64},{64,80},{80,96},{96,112},{1,17},{17... | collective-permute-start | bytes 1597448 | tf_op jit(solution)/shard_map/ppermute | solution.py:42
  21.4 7.8 %all-to-all-start = ((f32[16,8,2,68]{3,2,1,0:T(2,128)}), f32[16,8,2,68]{3,2,1,0:T(2,128)}, u32[]{:S(2)}, u32[]{:S(2)}) async-start(f32[16,8,2,68]{3,2,1,0:T(2,128)} %constant_dynamic-update-slice_fusion), calls=%async_computation | async-start | bytes 262144 | tf_op jit(solution)/shard_map/all_to_all | solution.py:193
  30.0 1.9 %collective-permute-start.3 = (f32[65,8,256]{2,1,0:T(8,128)}, f32[65,8,256]{2,1,0:T(8,128)}, u32[]{:S(2)}, u32[]{:S(2)}) collective-permute-start(f32[65,8,256]{2,1,0:T(8,128)} %pad_maximum_fusion.4), channel_id=1, source_target_pairs={{16,0},{32,16},{48,32},{64,48},{80,64},{96,80},{112,96},{17,1},{33... | collective-permute-start | bytes 1597448 | tf_op jit(solution)/shard_map/ppermute | solution.py:43
  32.0 1.7 %fusion.21 = (f32[32,64,8]{2,1,0:T(8,128)}, f32[32,64,8]{2,1,0:T(8,128)}) fusion(f32[32,64,256]{2,1,0:T(8,128)S(1)} %bitcast.158), kind=kLoop, calls=%fused_computation.109 | loop fusion | bytes 262144 | tf_op jit(solution)/shard_map/slice | solution.py:56
  33.8 1.0 fusion.25
  34.8 1.0 fusion.26
  36.5 1.9 %select_reduce_fusion = f32[25,64,256]{2,1,0:T(8,128)} fusion(f32[4,64,256]{2,1,0:T(8,128)S(1)} %copy-done.14, s32[4,64,256]{2,1,0:T(8,128)S(1)} %get-tuple-element.44), kind=kLoop, calls=%fused_computation.32 | loop fusion | flops 4505600 | bytes 2162688 | tf_op jit(solution)/shard_map/reduce_sum | solution.py:222
  38.4 3.3 %pad_maximum_fusion.1 = (f32[65,64,8]{2,1,0:T(8,128)}, f32[65,64,8]{2,1,0:T(8,128)S(1)}) fusion(f32[1,64,8]{2,1,0:T(8,128)S(1)} %get-tuple-element.94, f32[16,64,8]{2,1,0:T(8,128)S(1)} %copy-done.10, f32[16,64,8]{2,1,0:T(8,128)S(1)} %copy-done.8, f32[32,64,8]{2,1,0:T(8,128)S(1)} %copy-done.5, f32[1,64,8]{2,1,0:T(8,128)S(1)} %get-tuple-element.95, ...), kind=kLoop, calls=%fused_computation.35 | loop fusion | flops 199680 | bytes 532480 | tf_op jit(solution)/shard_map/concatenate | solution.py:56
  42.6 3.6 %collective-permute-start = (f32[8,2,68]{2,1,0:T(2,128)S(1)}, f32[8,2,68]{2,1,0:T(2,128)S(1)}, u32[]{:S(2)}, u32[]{:S(2)}) collective-permute-start(f32[8,2,68]{2,1,0:T(2,128)S(1)} %get-tuple-element.93), channel_id=1, source_target_pairs={{0,16},{16,32},{32,48},{48,64},{64,80},{80,96},{96,112},{1,17},{17... | collective-permute-start | bytes 13064 | tf_op jit(solution)/shard_map/ppermute | solution.py:195
  46.2 1.9 %collective-permute-start.1 = (f32[8,2,68]{2,1,0:T(2,128)S(1)}, f32[8,2,68]{2,1,0:T(2,128)S(1)}, u32[]{:S(2)}, u32[]{:S(2)}) collective-permute-start(f32[8,2,68]{2,1,0:T(2,128)S(1)} %get-tuple-element.92), channel_id=1, source_target_pairs={{16,0},{32,16},{48,32},{64,48},{80,64},{96,80},{112,96},{17,1},{33... | collective-permute-start | bytes 13064 | tf_op jit(solution)/shard_map/ppermute | solution.py:196
  50.0 2.9 %copy.67 = f32[65,64,8]{1,2,0:T(8,128)} copy(f32[65,64,8]{2,1,0:T(8,128)} %get-tuple-element.106) | data formatting | bytes 266240 | tf_op jit(solution)/shard_map/concatenate | solution.py:56
  52.9 1.3 copy.70
  55.5 8.2 %fusion.7 = f32[8,5,64,5,256]{4,2,3,1,0:T(8,128)} fusion(f32[8,5,64,68,1]{3,2,4,1,0:T(8,128)S(1)} %bitcast.159, pred[5,256,68,1,1]{1,0,2,4,3:T(8,128)(4,1)S(1)} %bitcast.165), kind=kOutput, calls=%fused_computation.45 | convolution fusion | flops 2673868800 | bytes 13890560 | tf_op jit(solution)/shard_map/fpb,bq->fpq/dot_general | solution.py:215
  63.7 7.4 %conditional.1 = (f32[8,64,256]{2,1,0:T(8,128)}) conditional(s32[]{:T(128)} %convert_element_type.14, (f32[5,64,5,256]{3,1,2,0:T(8,128)S(1)}, f32[8,5,64,5,256]{4,2,3,1,0:T(8,128)}) %tuple.75, (f32[4,64,256]{2,1,0:T(8,128)}, f32[8,36,68]{2,1,0:T(8,128)S(1)}, s32[4,64,256]{2,1,0:T(8,128)S(1)}) %tuple.76), branch_computations={%region_2.4_spmd, %region_4.6_spmd} | conditional | flops 6422528 | bytes 15269896 | solution.py:237
  63.7 7.4 %multiply_reduce_fusion = f32[8,64,256]{2,1,0:T(8,128)} fusion(f32[8,5,64,5,256]{4,2,3,1,0:T(8,128)} %get-tuple-element.19, f32[5,64,5,256]{3,1,2,0:T(8,128)S(1)} %get-tuple-element.20), kind=kLoop, calls=%fused_computation.4 | loop fusion | flops 6422528 | bytes 15269888 | tf_op jit(solution)/shard_map/reduce_sum | solution.py:226
  71.1 1.2 multiply_reduce_fusion.1.f_ref
  73.0 1.9 %collective-permute-start.8 = (f32[2,8,256]{2,1,0:T(8,128)S(1)}, f32[2,8,256]{2,1,0:T(8,128)S(1)}, u32[]{:S(2)}, u32[]{:S(2)}) collective-permute-start(f32[2,8,256]{2,1,0:T(8,128)S(1)} %get-tuple-element.76), channel_id=1, source_target_pairs={{16,0},{32,16},{48,32},{64,48},{80,64},{96,80},{112,96},{17,1},{33... | collective-permute-start | bytes 49160 | tf_op jit(solution)/shard_map/ppermute | solution.py:43
  75.0 3.6 %collective-permute-start.9 = (f32[2,8,256]{2,1,0:T(8,128)S(1)}, f32[2,8,256]{2,1,0:T(8,128)S(1)}, u32[]{:S(2)}, u32[]{:S(2)}) collective-permute-start(f32[2,8,256]{2,1,0:T(8,128)S(1)} %get-tuple-element.77), channel_id=1, source_target_pairs={{0,16},{16,32},{32,48},{48,64},{64,80},{80,96},{96,112},{1,17},{17... | collective-permute-start | bytes 49160 | tf_op jit(solution)/shard_map/ppermute | solution.py:42
  79.6 4.7 %collective-permute-start.10 = (f32[2,80,8]{2,1,0:T(8,128)S(1)}, f32[2,80,8]{2,1,0:T(8,128)S(1)}, u32[]{:S(2)}, u32[]{:S(2)}) collective-permute-start(f32[2,80,8]{2,1,0:T(8,128)S(1)} %pad_maximum_fusion.7), channel_id=1, source_target_pairs={{1,0},{2,1},{3,2},{4,3},{5,4},{6,5},{7,6},{8,7},{9,8},{10,9},{11,1... | collective-permute-start | bytes 15368 | tf_op jit(solution)/shard_map/ppermute | solution.py:60
  84.4 1.2 rev.6
  85.7 1.2 multiply_select_fusion.hn_ref
  87.2 1.2 fusion.24
  88.8 4.8 %collective-permute-start.5 = (f32[65,80,8]{1,2,0:T(8,128)S(1)}, f32[65,80,8]{1,2,0:T(8,128)S(1)}, u32[]{:S(2)}, u32[]{:S(2)}) collective-permute-start(f32[65,80,8]{1,2,0:T(8,128)S(1)} %pad_maximum_fusion.5), channel_id=1, source_target_pairs={{1,0},{2,1},{3,2},{4,3},{5,4},{6,5},{7,6},{8,7},{9,8},{10,9},{11,1... | collective-permute-start | bytes 499208 | tf_op jit(solution)/shard_map/ppermute | solution.py:60
  93.9 0.9 pad_maximum_fusion.6
  95.5 4.0 %collective-permute-done.5 = f32[65,80,8]{1,2,0:T(8,128)S(1)} collective-permute-done((f32[65,80,8]{1,2,0:T(8,128)S(1)}, f32[65,80,8]{1,2,0:T(8,128)S(1)}, u32[]{:S(2)}, u32[]{:S(2)}) %collective-permute-start.5) | collective-permute-done | bytes 166432 | tf_op jit(solution)/shard_map/ppermute | solution.py:60
  100.3 6.3 %collective-permute-done.6 = f32[65,80,8]{1,2,0:T(8,128)S(1)} collective-permute-done((f32[65,80,8]{1,2,0:T(8,128)}, f32[65,80,8]{1,2,0:T(8,128)S(1)}, u32[]{:S(2)}, u32[]{:S(2)}) %collective-permute-start.6) | collective-permute-done | bytes 166432 | tf_op jit(solution)/shard_map/ppermute | solution.py:59
  106.7 2.3 %copy.74 = f32[65,80,8]{2,1,0:T(8,128)} copy(f32[65,80,8]{1,2,0:T(8,128)S(1)} %collective-permute-done.6) | data formatting | bytes 332800 | tf_op jit(solution)/shard_map/ppermute | solution.py:59
  109.0 4.0 %pad_maximum_fusion.hc_ref = f32[65,80,128]{2,1,0:T(8,128)} fusion(f32[65,80,8]{2,1,0:T(8,128)} %copy.74, f32[65,80,8]{2,1,0:T(8,128)S(1)} %copy.73, f32[128]{0:T(128)S(1)} %pad.10.clone), kind=kLoop, calls=%fused_computation.34 | loop fusion | flops 1331200 | bytes 2995712 | tf_op jit(solution)/shard_map/concatenate | solution.py:62
  113.0 29.4 %shard_map.95 = f32[2,16,64,256]{3,2,1,0:T(8,128)} custom-call(f32[2,16,64,256]{3,2,1,0:T(8,128)} %tr_ref.1, bf16[16,64,256]{2,1,0:T(8,128)(2,1)} %u_ref.1, bf16[16,64,256]{2,1,0:T(8,128)(2,1)} %v_ref.1, s32[64,256]{1,0:T(8,128)} %m_ref.1, f32[2,64,256]{2,1,0:T(8,128)} %copy-done.11, f32[65,8,256]{2,1,0:T(8,128)} %copy-done.4, ...), custom_call_target="tpu_custom_call" | custom-call | tf_op jit(solution)/shard_map/pallas_call | solution.py:166
  (115 shorter events, 21.4 us)
Async XLA Ops:
  0.6 31.4 %copy-start = (f32[2,16,64,256]{3,2,1,0:T(8,128)S(1)}, f32[2,16,64,256]{3,2,1,0:T(8,128)}, u32[]{:S(2)}) copy-start(f32[2,16,64,256]{3,2,1,0:T(8,128)} %tr_ref.1) | copy-start | bytes 6291460
  0.6 9.9 %copy-start.16 = (f32[8,2,1024]{2,1,0:T(2,128)S(1)}, f32[8,2,1024]{2,1,0:T(2,128)}, u32[]{:S(2)}) copy-start(f32[8,2,1024]{2,1,0:T(2,128)} %param.12) | copy-start | bytes 196612
  4.5 79.8 %collective-permute-start.2 = (f32[65,8,256]{2,1,0:T(8,128)}, f32[65,8,256]{2,1,0:T(8,128)}, u32[]{:S(2)}, u32[]{:S(2)}) collective-permute-start(f32[65,8,256]{2,1,0:T(8,128)} %pad_maximum_fusion.3), channel_id=1, source_target_pairs={{120,112},{119,113},{118,114},{117,115},{116,116},{115,117},{114,1... | collective-permute-start | bytes 1597448 | tf_op jit(solution)/shard_map/ppermute | solution.py:45
  6.0 81.2 %collective-permute-start.4 = (f32[65,8,256]{2,1,0:T(8,128)}, f32[65,8,256]{2,1,0:T(8,128)}, u32[]{:S(2)}, u32[]{:S(2)}) collective-permute-start(f32[65,8,256]{2,1,0:T(8,128)} %pad_maximum_fusion.3), channel_id=1, source_target_pairs={{0,16},{16,32},{32,48},{48,64},{64,80},{80,96},{96,112},{1,17},{17... | collective-permute-start | bytes 1597448 | tf_op jit(solution)/shard_map/ppermute | solution.py:42
  21.4 20.3 %all-to-all-start = ((f32[16,8,2,68]{3,2,1,0:T(2,128)}), f32[16,8,2,68]{3,2,1,0:T(2,128)}, u32[]{:S(2)}, u32[]{:S(2)}) async-start(f32[16,8,2,68]{3,2,1,0:T(2,128)} %constant_dynamic-update-slice_fusion), calls=%async_computation | async-start | bytes 262144 | tf_op jit(solution)/shard_map/all_to_all | solution.py:193
  29.2 4.6 %copy-start.2 = (bf16[16,64,256]{2,1,0:T(8,128)(2,1)S(1)}, bf16[16,64,256]{2,1,0:T(8,128)(2,1)}, u32[]{:S(2)}) copy-start(bf16[16,64,256]{2,1,0:T(8,128)(2,1)} %u_ref.1) | copy-start | bytes 1572868
  30.0 55.6 %collective-permute-start.3 = (f32[65,8,256]{2,1,0:T(8,128)}, f32[65,8,256]{2,1,0:T(8,128)}, u32[]{:S(2)}, u32[]{:S(2)}) collective-permute-start(f32[65,8,256]{2,1,0:T(8,128)} %pad_maximum_fusion.4), channel_id=1, source_target_pairs={{16,0},{32,16},{48,32},{64,48},{80,64},{96,80},{112,96},{17,1},{33... | collective-permute-start | bytes 1597448 | tf_op jit(solution)/shard_map/ppermute | solution.py:43
  32.0 2.8 %copy-start.3 = (bf16[16,64,256]{2,1,0:T(8,128)(2,1)S(1)}, bf16[16,64,256]{2,1,0:T(8,128)(2,1)}, u32[]{:S(2)}) copy-start(bf16[16,64,256]{2,1,0:T(8,128)(2,1)} %v_ref.1) | copy-start | bytes 1572868
  33.7 2.8 %copy-start.14 = (f32[4,64,256]{2,1,0:T(8,128)S(1)}, f32[4,64,256]{2,1,0:T(8,128)}, u32[]{:S(2)}) copy-start(f32[4,64,256]{2,1,0:T(8,128)} %param.14) | copy-start | bytes 786436
  35.9 2.5 %copy-start.5 = (f32[32,64,8]{2,1,0:T(8,128)S(1)}, f32[32,64,8]{2,1,0:T(8,128)}, u32[]{:S(2)}) copy-start(f32[32,64,8]{2,1,0:T(8,128)} %get-tuple-element.58) | copy-start | bytes 196612
  36.0 2.4 %copy-start.8 = (f32[16,64,8]{2,1,0:T(8,128)S(1)}, f32[16,64,8]{2,1,0:T(8,128)}, u32[]{:S(2)}) copy-start(f32[16,64,8]{2,1,0:T(8,128)} %get-tuple-element.66) | copy-start | bytes 98308
  36.0 2.4 %copy-start.9 = (f32[16,64,8]{2,1,0:T(8,128)S(1)}, f32[16,64,8]{2,1,0:T(8,128)}, u32[]{:S(2)}) copy-start(f32[16,64,8]{2,1,0:T(8,128)} %get-tuple-element.67) | copy-start | bytes 98308
  36.0 2.4 %copy-start.10 = (f32[16,64,8]{2,1,0:T(8,128)S(1)}, f32[16,64,8]{2,1,0:T(8,128)}, u32[]{:S(2)}) copy-start(f32[16,64,8]{2,1,0:T(8,128)} %get-tuple-element.68) | copy-start | bytes 98308
  42.6 11.7 %collective-permute-start = (f32[8,2,68]{2,1,0:T(2,128)S(1)}, f32[8,2,68]{2,1,0:T(2,128)S(1)}, u32[]{:S(2)}, u32[]{:S(2)}) collective-permute-start(f32[8,2,68]{2,1,0:T(2,128)S(1)} %get-tuple-element.93), channel_id=1, source_target_pairs={{0,16},{16,32},{32,48},{48,64},{64,80},{80,96},{96,112},{1,17},{17... | collective-permute-start | bytes 13064 | tf_op jit(solution)/shard_map/ppermute | solution.py:195
  46.2 8.1 %collective-permute-start.1 = (f32[8,2,68]{2,1,0:T(2,128)S(1)}, f32[8,2,68]{2,1,0:T(2,128)S(1)}, u32[]{:S(2)}, u32[]{:S(2)}) collective-permute-start(f32[8,2,68]{2,1,0:T(2,128)S(1)} %get-tuple-element.92), channel_id=1, source_target_pairs={{16,0},{32,16},{48,32},{64,48},{80,64},{96,80},{112,96},{17,1},{33... | collective-permute-start | bytes 13064 | tf_op jit(solution)/shard_map/ppermute | solution.py:196
  55.5 8.2 %copy-start.1 = (f32[25,64,256]{2,1,0:T(8,128)S(1)}, f32[25,64,256]{2,1,0:T(8,128)}, u32[]{:S(2)}) copy-start(f32[25,64,256]{2,1,0:T(8,128)} %select_reduce_fusion) | copy-start | bytes 4915204
  55.5 8.2 %copy-start.7 = (s32[4,64,256]{2,1,0:T(8,128)S(1)}, s32[4,64,256]{2,1,0:T(8,128)}, u32[]{:S(2)}) copy-start(s32[4,64,256]{2,1,0:T(8,128)} %param.13) | copy-start | bytes 786436
  63.7 7.4 %copy-start.19 = (f32[2,8]{1,0:T(2,128)S(1)}, f32[2,8]{1,0:T(2,128)}, u32[]{:S(2)}) copy-start(f32[2,8]{1,0:T(2,128)} %param.15) | copy-start | bytes 196
  63.7 22.0 %copy-start.20 = (f32[65]{0:T(128)S(1)}, f32[65]{0:T(128)}, u32[]{:S(2)}) copy-start(f32[65]{0:T(128)} %constant.79.clone.1) | copy-start | bytes 784
  72.3 16.1 %copy-start.11 = (f32[2,64,256]{2,1,0:T(8,128)}, f32[2,64,256]{2,1,0:T(8,128)S(1)}, u32[]{:S(2)}) copy-start(f32[2,64,256]{2,1,0:T(8,128)S(1)} %multiply_reduce_fusion.1.f_ref) | copy-start | bytes 393220
  72.3 2.7 %collective-permute-start.7 = (f32[2,8,256]{2,1,0:T(8,128)S(1)}, f32[2,8,256]{2,1,0:T(8,128)S(1)}, u32[]{:S(2)}, u32[]{:S(2)}) collective-permute-start(f32[2,8,256]{2,1,0:T(8,128)S(1)} %get-tuple-element.77), channel_id=1, source_target_pairs={{120,112},{119,113},{118,114},{117,115},{116,116},{115,117},{114,1... | collective-permute-start | bytes 49160 | tf_op jit(solution)/shard_map/ppermute | solution.py:45
  73.0 5.8 %collective-permute-start.8 = (f32[2,8,256]{2,1,0:T(8,128)S(1)}, f32[2,8,256]{2,1,0:T(8,128)S(1)}, u32[]{:S(2)}, u32[]{:S(2)}) collective-permute-start(f32[2,8,256]{2,1,0:T(8,128)S(1)} %get-tuple-element.76), channel_id=1, source_target_pairs={{16,0},{32,16},{48,32},{64,48},{80,64},{96,80},{112,96},{17,1},{33... | collective-permute-start | bytes 49160 | tf_op jit(solution)/shard_map/ppermute | solution.py:43
  75.0 4.5 %collective-permute-start.9 = (f32[2,8,256]{2,1,0:T(8,128)S(1)}, f32[2,8,256]{2,1,0:T(8,128)S(1)}, u32[]{:S(2)}, u32[]{:S(2)}) collective-permute-start(f32[2,8,256]{2,1,0:T(8,128)S(1)} %get-tuple-element.77), channel_id=1, source_target_pairs={{0,16},{16,32},{32,48},{48,64},{64,80},{80,96},{96,112},{1,17},{17... | collective-permute-start | bytes 49160 | tf_op jit(solution)/shard_map/ppermute | solution.py:42
  78.8 9.6 %copy-start.17 = (f32[2,8,256]{2,1,0:T(8,128)}, f32[2,8,256]{2,1,0:T(8,128)S(1)}, u32[]{:S(2)}) copy-start(f32[2,8,256]{2,1,0:T(8,128)S(1)} %broadcast_select_fusion.fn_ref) | copy-start | bytes 49156
  79.5 8.9 %copy-start.18 = (f32[2,8,256]{2,1,0:T(8,128)}, f32[2,8,256]{2,1,0:T(8,128)S(1)}, u32[]{:S(2)}) copy-start(f32[2,8,256]{2,1,0:T(8,128)S(1)} %collective-permute-done.9.fs_ref) | copy-start | bytes 49156
  79.6 15.2 %collective-permute-start.10 = (f32[2,80,8]{2,1,0:T(8,128)S(1)}, f32[2,80,8]{2,1,0:T(8,128)S(1)}, u32[]{:S(2)}, u32[]{:S(2)}) collective-permute-start(f32[2,80,8]{2,1,0:T(8,128)S(1)} %pad_maximum_fusion.7), channel_id=1, source_target_pairs={{1,0},{2,1},{3,2},{4,3},{5,4},{6,5},{7,6},{8,7},{9,8},{10,9},{11,1... | collective-permute-start | bytes 15368 | tf_op jit(solution)/shard_map/ppermute | solution.py:60
  84.3 10.5 %collective-permute-start.11 = (f32[2,80,8]{2,1,0:T(8,128)S(1)}, f32[2,80,8]{2,1,0:T(8,128)S(1)}, u32[]{:S(2)}, u32[]{:S(2)}) collective-permute-start(f32[2,80,8]{2,1,0:T(8,128)S(1)} %pad_maximum_fusion.8), channel_id=1, source_target_pairs={{0,1},{1,2},{2,3},{3,4},{4,5},{5,6},{6,7},{7,8},{8,9},{9,10},{10,1... | collective-permute-start | bytes 15368 | tf_op jit(solution)/shard_map/ppermute | solution.py:59
  85.6 2.9 %copy-start.13 = (f32[65,64,8]{1,2,0:T(8,128)S(1)}, f32[65,64,8]{1,2,0:T(8,128)}, u32[]{:S(2)}) copy-start(f32[65,64,8]{1,2,0:T(8,128)} %copy.67) | copy-start | bytes 399364
  86.9 7.0 %copy-start.4 = (f32[65,8,256]{2,1,0:T(8,128)}, f32[65,8,256]{2,1,0:T(8,128)S(1)}, u32[]{:S(2)}) copy-start(f32[65,8,256]{2,1,0:T(8,128)S(1)} %multiply_select_fusion.hn_ref) | copy-start | bytes 1597444
  86.9 7.0 %copy-start.12 = (f32[65,64,8]{1,2,0:T(8,128)S(1)}, f32[65,64,8]{1,2,0:T(8,128)}, u32[]{:S(2)}) copy-start(f32[65,64,8]{1,2,0:T(8,128)} %copy.70) | copy-start | bytes 399364
  88.8 10.8 %collective-permute-start.5 = (f32[65,80,8]{1,2,0:T(8,128)S(1)}, f32[65,80,8]{1,2,0:T(8,128)S(1)}, u32[]{:S(2)}, u32[]{:S(2)}) collective-permute-start(f32[65,80,8]{1,2,0:T(8,128)S(1)} %pad_maximum_fusion.5), channel_id=1, source_target_pairs={{1,0},{2,1},{3,2},{4,3},{5,4},{6,5},{7,6},{8,7},{9,8},{10,9},{11,1... | collective-permute-start | bytes 499208 | tf_op jit(solution)/shard_map/ppermute | solution.py:60
  94.8 11.9 %collective-permute-start.6 = (f32[65,80,8]{1,2,0:T(8,128)}, f32[65,80,8]{1,2,0:T(8,128)S(1)}, u32[]{:S(2)}, u32[]{:S(2)}) collective-permute-start(f32[65,80,8]{1,2,0:T(8,128)} %pad_maximum_fusion.6), channel_id=1, source_target_pairs={{0,1},{1,2},{2,3},{3,4},{4,5},{5,6},{6,7},{7,8},{8,9},{9,10},{10,1... | collective-permute-start | bytes 499208 | tf_op jit(solution)/shard_map/ppermute | solution.py:59
  (1 other events, 2.4 us)

commit v6 on v5

--- a/solution.py
+++ b/solution.py
@@ -188,10 +188,12 @@
     cols_n = lax.axis_size("ox")
     rows_n = lax.axis_size("oy")
     width = atm_flux.shape[2] // cols_n
-    ring = jnp.concatenate([atm_flux[..., -H:], atm_flux, atm_flux[..., :H]], axis=2)
-    pieces = jnp.stack([ring[..., i * width:(i + 1) * width + 2 * H] for i in range(cols_n)])
-    got = lax.all_to_all(pieces, "ox", split_axis=0, concat_axis=0, tiled=True)
-    own = jnp.concatenate(list(got), axis=1)
+    nf, lat = atm_flux.shape[:2]
+    body = jnp.roll(atm_flux, H, axis=2).reshape(nf, lat, cols_n, width)
+    tail = jnp.roll(atm_flux, H - width, axis=2).reshape(nf, lat, cols_n, width)[..., : 2 * H]
+    pieces = jnp.concatenate([body, tail], axis=3)
+    got = lax.all_to_all(pieces, "ox", split_axis=2, concat_axis=1, tiled=True)
+    own = got.reshape(nf, -1, width + 2 * H)
     below = lax.ppermute(own[:, -H:], "oy", [(i, i + 1) for i in range(rows_n - 1)])
     above = lax.ppermute(own[:, :H], "oy", [(i + 1, i) for i in range(rows_n - 1)])
     return jnp.concatenate([below, own, above], axis=1)

time: 145 us -> 138 us (0.952)
  local copies, waits for them, and re-layouts: 28.4 us -> 21.2 us
    unnamed x54 -> x46, local copies, waits for them, and re-layouts: 9.48 us -> 0.11 us
  transfers between devices with their start and end apart: 13 -> 13, of which waited for: 3 -> 3; matrix products, arithmetic and copies ran while one was open for 37% -> 34% of each run, Pallas kernels for 0% -> 0%
where the time goes in v6:
time: 138 us; the launch traced here: 136 us
  starting transfers between devices  37.2 us (27%)
  Pallas kernels  29.4 us (21%)
  other arithmetic  25.6 us (19%)
  local copies, waits for them, and re-layouts  21.2 us (15%)
  waiting for transfers between devices  11 us (8%)
  matrix products  9.76 us (7%)
  between operations  1.77 us (1%)
    pallas_call x1, Pallas kernels, evolve(): pl.pallas_call(stencil_kernel, out_shape=jax.ShapeDtypeStruct(tracers.sha...  29.4 us
    ppermute x2, starting transfers between devices, exchange(): lax.ppermute(wests, 'ox', [((i + 1) % cols_n, i) for i in range(cols_n)])  9.54 us
    dot_general x1, matrix products, remap(): window = jnp.einsum('fpb,bq->fpq', lifted, pick_c, precision=HIGH)  9.19 us
    ppermute x2, starting transfers between devices, exchange(): south = lax.ppermute(tops, 'oy', [(i, i + 1) for i in range(rows_n - 1)])  8.14 us
    all_to_all x1, starting transfers between devices, atmosphere_block(): got = lax.all_to_all(pieces, 'ox', split_axis=2, concat_axis=1, tiled=True)  7.82 us
    reduce_sum x1, other arithmetic, remap(): fast = jnp.sum(window * wsum.transpose(0, 2, 1, 3)[None], axis=(1, 3))  7.37 us
    ppermute x2, waiting for transfers between devices, exchange(): lax.ppermute(easts, 'ox', [(i, (i + 1) % cols_n) for i in range(cols_n)])  6.36 us
    concatenate x2, other arithmetic, exchange(): return (north, south, jnp.concatenate([from_e, gap, from_w], axis=-1))  4.72 us
  transfers between devices with their start and end apart: 13, of which 3 were waited for; matrix products, arithmetic and copies ran while one was open for 34% of the time, Pallas kernels for 0%

profile of v6, /device:TPU:1, one launch (start us, length us, event | category | flops | bytes accessed | tf_op | source)
XLA Modules:
  0.0 135.9 jit_solution(13580398155298349601)
XLA Ops:
  0.6 1.1 fusion.20
  1.8 1.0 convert_bitcast_fusion
  2.8 1.0 fusion.25
  4.6 1.5 %collective-permute-start.2 = (f32[65,8,256]{2,1,0:T(8,128)}, f32[65,8,256]{2,1,0:T(8,128)}, u32[]{:S(2)}, u32[]{:S(2)}) collective-permute-start(f32[65,8,256]{2,1,0:T(8,128)} %pad_maximum_fusion.3), channel_id=1, source_target_pairs={{120,112},{119,113},{118,114},{117,115},{116,116},{115,117},{114,1... | collective-permute-start | bytes 1597448 | tf_op jit(solution)/shard_map/ppermute | solution.py:45
  6.1 4.5 %collective-permute-start.4 = (f32[65,8,256]{2,1,0:T(8,128)}, f32[65,8,256]{2,1,0:T(8,128)}, u32[]{:S(2)}, u32[]{:S(2)}) collective-permute-start(f32[65,8,256]{2,1,0:T(8,128)} %pad_maximum_fusion.3), channel_id=1, source_target_pairs={{0,16},{16,32},{32,48},{48,64},{64,80},{80,96},{96,112},{1,17},{17... | collective-permute-start | bytes 1597448 | tf_op jit(solution)/shard_map/ppermute | solution.py:42
  12.1 7.8 %all-to-all-start = ((f32[8,2,16,68]{3,1,0,2:T(2,128)}), f32[8,2,16,68]{3,1,0,2:T(2,128)}, u32[]{:S(2)}, u32[]{:S(2)}) async-start(f32[8,2,16,68]{3,1,0,2:T(2,128)} %copy.109), calls=%async_computation | async-start | bytes 262144 | tf_op jit(solution)/shard_map/all_to_all | solution.py:195
  20.8 1.9 %collective-permute-start.3 = (f32[65,8,256]{2,1,0:T(8,128)}, f32[65,8,256]{2,1,0:T(8,128)}, u32[]{:S(2)}, u32[]{:S(2)}) collective-permute-start(f32[65,8,256]{2,1,0:T(8,128)} %pad_maximum_fusion.4), channel_id=1, source_target_pairs={{16,0},{32,16},{48,32},{64,48},{80,64},{96,80},{112,96},{17,1},{33... | collective-permute-start | bytes 1597448 | tf_op jit(solution)/shard_map/ppermute | solution.py:43
  22.8 1.7 %fusion.19 = (f32[32,64,8]{2,1,0:T(8,128)}, f32[32,64,8]{2,1,0:T(8,128)}) fusion(f32[32,64,256]{2,1,0:T(8,128)S(1)} %bitcast.99), kind=kLoop, calls=%fused_computation.77 | loop fusion | bytes 262144 | tf_op jit(solution)/shard_map/slice | solution.py:56
  25.1 1.0 fusion.23
  26.2 1.0 fusion.24
  27.8 1.9 %select_reduce_fusion = f32[25,64,256]{2,1,0:T(8,128)} fusion(f32[4,64,256]{2,1,0:T(8,128)S(1)} %copy-done.14, s32[4,64,256]{2,1,0:T(8,128)S(1)} %get-tuple-element.48), kind=kLoop, calls=%fused_computation.32 | loop fusion | flops 4505600 | bytes 2162688 | tf_op jit(solution)/shard_map/reduce_sum | solution.py:224
  29.8 3.3 %pad_maximum_fusion.1 = (f32[65,64,8]{2,1,0:T(8,128)}, f32[65,64,8]{2,1,0:T(8,128)S(1)}) fusion(f32[1,64,8]{2,1,0:T(8,128)S(1)} %copy-done.18, f32[16,64,8]{2,1,0:T(8,128)S(1)} %copy-done.10, f32[16,64,8]{2,1,0:T(8,128)S(1)} %copy-done.8, f32[32,64,8]{2,1,0:T(8,128)S(1)} %copy-done.5, f32[1,64,8]{2,1,0:T(8,128)S(1)} %copy-done.19, ...), kind=kLoop, calls=%fused_computation.35 | loop fusion | flops 199680 | bytes 532480 | tf_op jit(solution)/shard_map/concatenate | solution.py:56
  34.0 3.6 %collective-permute-start = (f32[8,2,68]{2,1,0:T(2,128)S(1)}, f32[8,2,68]{2,1,0:T(2,128)S(1)}, u32[]{:S(2)}, u32[]{:S(2)}) collective-permute-start(f32[8,2,68]{2,1,0:T(2,128)S(1)} %get-tuple-element.82), channel_id=1, source_target_pairs={{0,16},{16,32},{32,48},{48,64},{64,80},{80,96},{96,112},{1,17},{17... | collective-permute-start | bytes 13064 | tf_op jit(solution)/shard_map/ppermute | solution.py:197
  37.7 1.9 %collective-permute-start.1 = (f32[8,2,68]{2,1,0:T(2,128)S(1)}, f32[8,2,68]{2,1,0:T(2,128)S(1)}, u32[]{:S(2)}, u32[]{:S(2)}) collective-permute-start(f32[8,2,68]{2,1,0:T(2,128)S(1)} %get-tuple-element.83), channel_id=1, source_target_pairs={{16,0},{32,16},{48,32},{64,48},{80,64},{96,80},{112,96},{17,1},{33... | collective-permute-start | bytes 13064 | tf_op jit(solution)/shard_map/ppermute | solution.py:198
  41.9 2.9 %copy.114 = f32[65,64,8]{1,2,0:T(8,128)} copy(f32[65,64,8]{2,1,0:T(8,128)} %get-tuple-element.94) | data formatting | bytes 266240 | tf_op jit(solution)/shard_map/concatenate | solution.py:56
  44.8 1.3 copy.117
  47.9 9.2 %fusion.7 = f32[8,5,64,5,256]{4,2,3,1,0:T(8,128)} fusion(f32[8,5,64,68,1]{3,2,4,1,0:T(8,128)S(1)} %bitcast.100, pred[5,256,68,1,1]{1,0,2,4,3:T(8,128)(4,1)} %bitcast.110), kind=kOutput, calls=%fused_computation.45 | convolution fusion | flops 2673868800 | bytes 13890560 | tf_op jit(solution)/shard_map/fpb,bq->fpq/dot_general | solution.py:217
  57.2 7.4 %conditional.1 = (f32[8,64,256]{2,1,0:T(8,128)}) conditional(s32[]{:T(128)} %convert_element_type.14, (f32[5,64,5,256]{3,1,2,0:T(8,128)S(1)}, f32[8,5,64,5,256]{4,2,3,1,0:T(8,128)}) %tuple.62, (f32[4,64,256]{2,1,0:T(8,128)S(1)}, f32[8,36,68]{2,1,0:T(8,128)}, s32[4,64,256]{2,1,0:T(8,128)S(1)}) %tuple.64), branch_computations={%region_2.4_spmd, %region_4.6_spmd} | conditional | flops 6422528 | bytes 15269896 | solution.py:239
  57.2 7.4 %multiply_reduce_fusion = f32[8,64,256]{2,1,0:T(8,128)} fusion(f32[8,5,64,5,256]{4,2,3,1,0:T(8,128)} %get-tuple-element.19, f32[5,64,5,256]{3,1,2,0:T(8,128)S(1)} %get-tuple-element.20), kind=kLoop, calls=%fused_computation.4 | loop fusion | flops 6422528 | bytes 15269888 | tf_op jit(solution)/shard_map/reduce_sum | solution.py:228
  64.6 1.2 multiply_reduce_fusion.1.f_ref
  66.5 1.9 %collective-permute-start.8 = (f32[2,8,256]{2,1,0:T(8,128)S(1)}, f32[2,8,256]{2,1,0:T(8,128)S(1)}, u32[]{:S(2)}, u32[]{:S(2)}) collective-permute-start(f32[2,8,256]{2,1,0:T(8,128)S(1)} %get-tuple-element.80), channel_id=1, source_target_pairs={{16,0},{32,16},{48,32},{64,48},{80,64},{96,80},{112,96},{17,1},{33... | collective-permute-start | bytes 49160 | tf_op jit(solution)/shard_map/ppermute | solution.py:43
  68.5 3.6 %collective-permute-start.9 = (f32[2,8,256]{2,1,0:T(8,128)S(1)}, f32[2,8,256]{2,1,0:T(8,128)S(1)}, u32[]{:S(2)}, u32[]{:S(2)}) collective-permute-start(f32[2,8,256]{2,1,0:T(8,128)S(1)} %get-tuple-element.81), channel_id=1, source_target_pairs={{0,16},{16,32},{32,48},{48,64},{64,80},{80,96},{96,112},{1,17},{17... | collective-permute-start | bytes 49160 | tf_op jit(solution)/shard_map/ppermute | solution.py:42
  73.1 4.7 %collective-permute-start.10 = (f32[2,80,8]{2,1,0:T(8,128)S(1)}, f32[2,80,8]{2,1,0:T(8,128)S(1)}, u32[]{:S(2)}, u32[]{:S(2)}) collective-permute-start(f32[2,80,8]{2,1,0:T(8,128)S(1)} %pad_maximum_fusion.9), channel_id=1, source_target_pairs={{1,0},{2,1},{3,2},{4,3},{5,4},{6,5},{7,6},{8,7},{9,8},{10,9},{11,1... | collective-permute-start | bytes 15368 | tf_op jit(solution)/shard_map/ppermute | solution.py:60
  77.9 1.2 rev.6
  79.2 1.2 multiply_select_fusion.hn_ref
  80.7 1.2 fusion.22
  82.2 4.8 %collective-permute-start.5 = (f32[65,80,8]{1,2,0:T(8,128)S(1)}, f32[65,80,8]{1,2,0:T(8,128)S(1)}, u32[]{:S(2)}, u32[]{:S(2)}) collective-permute-start(f32[65,80,8]{1,2,0:T(8,128)S(1)} %pad_maximum_fusion.5), channel_id=1, source_target_pairs={{1,0},{2,1},{3,2},{4,3},{5,4},{6,5},{7,6},{8,7},{9,8},{10,9},{11,1... | collective-permute-start | bytes 499208 | tf_op jit(solution)/shard_map/ppermute | solution.py:60
  89.0 4.0 %collective-permute-done.5 = f32[65,80,8]{1,2,0:T(8,128)S(1)} collective-permute-done((f32[65,80,8]{1,2,0:T(8,128)S(1)}, f32[65,80,8]{1,2,0:T(8,128)S(1)}, u32[]{:S(2)}, u32[]{:S(2)}) %collective-permute-start.5) | collective-permute-done | bytes 166432 | tf_op jit(solution)/shard_map/ppermute | solution.py:60
  93.8 6.4 %collective-permute-done.6 = f32[65,80,8]{1,2,0:T(8,128)S(1)} collective-permute-done((f32[65,80,8]{1,2,0:T(8,128)}, f32[65,80,8]{1,2,0:T(8,128)S(1)}, u32[]{:S(2)}, u32[]{:S(2)}) %collective-permute-start.6) | collective-permute-done | bytes 166432 | tf_op jit(solution)/shard_map/ppermute | solution.py:59
  100.2 2.3 %copy.121 = f32[65,80,8]{2,1,0:T(8,128)} copy(f32[65,80,8]{1,2,0:T(8,128)S(1)} %collective-permute-done.6) | data formatting | bytes 332800 | tf_op jit(solution)/shard_map/ppermute | solution.py:59
  102.5 4.0 %pad_maximum_fusion.hc_ref = f32[65,80,128]{2,1,0:T(8,128)} fusion(f32[65,80,8]{2,1,0:T(8,128)} %copy.121, f32[65,80,8]{2,1,0:T(8,128)S(1)} %copy.120, f32[128]{0:T(128)S(1)} %pad.10.clone), kind=kLoop, calls=%fused_computation.34 | loop fusion | flops 1331200 | bytes 2995712 | tf_op jit(solution)/shard_map/concatenate | solution.py:62
  106.5 29.4 %shard_map.95 = f32[2,16,64,256]{3,2,1,0:T(8,128)} custom-call(f32[2,16,64,256]{3,2,1,0:T(8,128)} %tr_ref.1, bf16[16,64,256]{2,1,0:T(8,128)(2,1)} %u_ref.1, bf16[16,64,256]{2,1,0:T(8,128)(2,1)} %v_ref.1, s32[64,256]{1,0:T(8,128)} %m_ref.1, f32[2,64,256]{2,1,0:T(8,128)} %copy-done.11, f32[65,8,256]{2,1,0:T(8,128)} %copy-done.4, ...), custom_call_target="tpu_custom_call" | custom-call | tf_op jit(solution)/shard_map/pallas_call | solution.py:166
  (117 shorter events, 14.0 us)
Async XLA Ops:
  0.6 10.0 %copy-start.16 = (f32[8,2,1024]{2,1,0:T(2,128)S(1)}, f32[8,2,1024]{2,1,0:T(2,128)}, u32[]{:S(2)}) copy-start(f32[8,2,1024]{2,1,0:T(2,128)} %param.12) | copy-start | bytes 196612
  0.6 10.2 %slice-start = ((f32[8,2,1024]{2,1,0:T(2,128)}), f32[8,2,62]{2,1,0:T(2,128)S(1)}, s32[]{:S(2)}) async-start(f32[8,2,1024]{2,1,0:T(2,128)} %param.12), calls=%async_computation.1 | async-start | bytes 16384 | tf_op jit(solution)/shard_map/jit(_roll_static)/slice | solution.py:193
  1.8 21.0 %copy-start = (f32[2,16,64,256]{3,2,1,0:T(8,128)S(1)}, f32[2,16,64,256]{3,2,1,0:T(8,128)}, u32[]{:S(2)}) copy-start(f32[2,16,64,256]{3,2,1,0:T(8,128)} %tr_ref.1) | copy-start | bytes 6291460
  4.6 73.3 %collective-permute-start.2 = (f32[65,8,256]{2,1,0:T(8,128)}, f32[65,8,256]{2,1,0:T(8,128)}, u32[]{:S(2)}, u32[]{:S(2)}) collective-permute-start(f32[65,8,256]{2,1,0:T(8,128)} %pad_maximum_fusion.3), channel_id=1, source_target_pairs={{120,112},{119,113},{118,114},{117,115},{116,116},{115,117},{114,1... | collective-permute-start | bytes 1597448 | tf_op jit(solution)/shard_map/ppermute | solution.py:45
  6.1 74.6 %collective-permute-start.4 = (f32[65,8,256]{2,1,0:T(8,128)}, f32[65,8,256]{2,1,0:T(8,128)}, u32[]{:S(2)}, u32[]{:S(2)}) collective-permute-start(f32[65,8,256]{2,1,0:T(8,128)} %pad_maximum_fusion.3), channel_id=1, source_target_pairs={{0,16},{16,32},{32,48},{48,64},{64,80},{80,96},{96,112},{1,17},{17... | collective-permute-start | bytes 1597448 | tf_op jit(solution)/shard_map/ppermute | solution.py:42
  12.1 20.9 %all-to-all-start = ((f32[8,2,16,68]{3,1,0,2:T(2,128)}), f32[8,2,16,68]{3,1,0,2:T(2,128)}, u32[]{:S(2)}, u32[]{:S(2)}) async-start(f32[8,2,16,68]{3,1,0,2:T(2,128)} %copy.109), calls=%async_computation | async-start | bytes 262144 | tf_op jit(solution)/shard_map/all_to_all | solution.py:195
  20.0 5.2 %copy-start.2 = (bf16[16,64,256]{2,1,0:T(8,128)(2,1)S(1)}, bf16[16,64,256]{2,1,0:T(8,128)(2,1)}, u32[]{:S(2)}) copy-start(bf16[16,64,256]{2,1,0:T(8,128)(2,1)} %u_ref.1) | copy-start | bytes 1572868
  20.8 58.3 %collective-permute-start.3 = (f32[65,8,256]{2,1,0:T(8,128)}, f32[65,8,256]{2,1,0:T(8,128)}, u32[]{:S(2)}, u32[]{:S(2)}) collective-permute-start(f32[65,8,256]{2,1,0:T(8,128)} %pad_maximum_fusion.4), channel_id=1, source_target_pairs={{16,0},{32,16},{48,32},{64,48},{80,64},{96,80},{112,96},{17,1},{33... | collective-permute-start | bytes 1597448 | tf_op jit(solution)/shard_map/ppermute | solution.py:43
  22.8 3.4 %copy-start.3 = (bf16[16,64,256]{2,1,0:T(8,128)(2,1)S(1)}, bf16[16,64,256]{2,1,0:T(8,128)(2,1)}, u32[]{:S(2)}) copy-start(bf16[16,64,256]{2,1,0:T(8,128)(2,1)} %v_ref.1) | copy-start | bytes 1572868
  24.4 3.0 %copy-start.6 = (s32[4,64,256]{2,1,0:T(8,128)S(1)}, s32[4,64,256]{2,1,0:T(8,128)}, u32[]{:S(2)}) copy-start(s32[4,64,256]{2,1,0:T(8,128)} %param.13) | copy-start | bytes 786436
  24.4 3.4 %copy-start.14 = (f32[4,64,256]{2,1,0:T(8,128)S(1)}, f32[4,64,256]{2,1,0:T(8,128)}, u32[]{:S(2)}) copy-start(f32[4,64,256]{2,1,0:T(8,128)} %param.14) | copy-start | bytes 786436
  26.2 3.6 %copy-start.18 = (f32[1,64,8]{2,1,0:T(8,128)S(1)}, f32[1,64,8]{2,1,0:T(8,128)}, u32[]{:S(2)}) copy-start(f32[1,64,8]{2,1,0:T(8,128)} %get-tuple-element.84) | copy-start | bytes 6148
  26.2 3.6 %copy-start.19 = (f32[1,64,8]{2,1,0:T(8,128)S(1)}, f32[1,64,8]{2,1,0:T(8,128)}, u32[]{:S(2)}) copy-start(f32[1,64,8]{2,1,0:T(8,128)} %get-tuple-element.85) | copy-start | bytes 6148
  34.0 12.2 %collective-permute-start = (f32[8,2,68]{2,1,0:T(2,128)S(1)}, f32[8,2,68]{2,1,0:T(2,128)S(1)}, u32[]{:S(2)}, u32[]{:S(2)}) collective-permute-start(f32[8,2,68]{2,1,0:T(2,128)S(1)} %get-tuple-element.82), channel_id=1, source_target_pairs={{0,16},{16,32},{32,48},{48,64},{64,80},{80,96},{96,112},{1,17},{17... | collective-permute-start | bytes 13064 | tf_op jit(solution)/shard_map/ppermute | solution.py:197
  37.7 8.6 %collective-permute-start.1 = (f32[8,2,68]{2,1,0:T(2,128)S(1)}, f32[8,2,68]{2,1,0:T(2,128)S(1)}, u32[]{:S(2)}, u32[]{:S(2)}) collective-permute-start(f32[8,2,68]{2,1,0:T(2,128)S(1)} %get-tuple-element.83), channel_id=1, source_target_pairs={{16,0},{32,16},{48,32},{64,48},{80,64},{96,80},{112,96},{17,1},{33... | collective-permute-start | bytes 13064 | tf_op jit(solution)/shard_map/ppermute | solution.py:198
  47.9 9.2 %copy-start.1 = (f32[25,64,256]{2,1,0:T(8,128)S(1)}, f32[25,64,256]{2,1,0:T(8,128)}, u32[]{:S(2)}) copy-start(f32[25,64,256]{2,1,0:T(8,128)} %select_reduce_fusion) | copy-start | bytes 4915204
  47.9 9.2 %copy-start.7 = (s32[4,64,256]{2,1,0:T(8,128)S(1)}, s32[4,64,256]{2,1,0:T(8,128)}, u32[]{:S(2)}) copy-start(s32[4,64,256]{2,1,0:T(8,128)} %param.13) | copy-start | bytes 786436
  47.9 9.2 %copy-start.15 = (f32[4,64,256]{2,1,0:T(8,128)S(1)}, f32[4,64,256]{2,1,0:T(8,128)}, u32[]{:S(2)}) copy-start(f32[4,64,256]{2,1,0:T(8,128)} %param.14) | copy-start | bytes 786436
  57.1 7.4 %copy-start.21 = (f32[2,8]{1,0:T(2,128)S(1)}, f32[2,8]{1,0:T(2,128)}, u32[]{:S(2)}) copy-start(f32[2,8]{1,0:T(2,128)} %param.15) | copy-start | bytes 196
  57.2 22.0 %copy-start.22 = (f32[65]{0:T(128)S(1)}, f32[65]{0:T(128)}, u32[]{:S(2)}) copy-start(f32[65]{0:T(128)} %constant.79.clone.1) | copy-start | bytes 784
  65.8 16.1 %copy-start.11 = (f32[2,64,256]{2,1,0:T(8,128)}, f32[2,64,256]{2,1,0:T(8,128)S(1)}, u32[]{:S(2)}) copy-start(f32[2,64,256]{2,1,0:T(8,128)S(1)} %multiply_reduce_fusion.1.f_ref) | copy-start | bytes 393220
  65.8 2.7 %collective-permute-start.7 = (f32[2,8,256]{2,1,0:T(8,128)S(1)}, f32[2,8,256]{2,1,0:T(8,128)S(1)}, u32[]{:S(2)}, u32[]{:S(2)}) collective-permute-start(f32[2,8,256]{2,1,0:T(8,128)S(1)} %get-tuple-element.81), channel_id=1, source_target_pairs={{120,112},{119,113},{118,114},{117,115},{116,116},{115,117},{114,1... | collective-permute-start | bytes 49160 | tf_op jit(solution)/shard_map/ppermute | solution.py:45
  66.5 5.8 %collective-permute-start.8 = (f32[2,8,256]{2,1,0:T(8,128)S(1)}, f32[2,8,256]{2,1,0:T(8,128)S(1)}, u32[]{:S(2)}, u32[]{:S(2)}) collective-permute-start(f32[2,8,256]{2,1,0:T(8,128)S(1)} %get-tuple-element.80), channel_id=1, source_target_pairs={{16,0},{32,16},{48,32},{64,48},{80,64},{96,80},{112,96},{17,1},{33... | collective-permute-start | bytes 49160 | tf_op jit(solution)/shard_map/ppermute | solution.py:43
  68.5 4.5 %collective-permute-start.9 = (f32[2,8,256]{2,1,0:T(8,128)S(1)}, f32[2,8,256]{2,1,0:T(8,128)S(1)}, u32[]{:S(2)}, u32[]{:S(2)}) collective-permute-start(f32[2,8,256]{2,1,0:T(8,128)S(1)} %get-tuple-element.81), channel_id=1, source_target_pairs={{0,16},{16,32},{32,48},{48,64},{64,80},{80,96},{96,112},{1,17},{17... | collective-permute-start | bytes 49160 | tf_op jit(solution)/shard_map/ppermute | solution.py:42
  72.3 9.6 %copy-start.17 = (f32[2,8,256]{2,1,0:T(8,128)}, f32[2,8,256]{2,1,0:T(8,128)S(1)}, u32[]{:S(2)}) copy-start(f32[2,8,256]{2,1,0:T(8,128)S(1)} %broadcast_select_fusion.fn_ref) | copy-start | bytes 49156
  73.0 8.9 %copy-start.20 = (f32[2,8,256]{2,1,0:T(8,128)}, f32[2,8,256]{2,1,0:T(8,128)S(1)}, u32[]{:S(2)}) copy-start(f32[2,8,256]{2,1,0:T(8,128)S(1)} %collective-permute-done.9.fs_ref) | copy-start | bytes 49156
  73.1 15.2 %collective-permute-start.10 = (f32[2,80,8]{2,1,0:T(8,128)S(1)}, f32[2,80,8]{2,1,0:T(8,128)S(1)}, u32[]{:S(2)}, u32[]{:S(2)}) collective-permute-start(f32[2,80,8]{2,1,0:T(8,128)S(1)} %pad_maximum_fusion.9), channel_id=1, source_target_pairs={{1,0},{2,1},{3,2},{4,3},{5,4},{6,5},{7,6},{8,7},{9,8},{10,9},{11,1... | collective-permute-start | bytes 15368 | tf_op jit(solution)/shard_map/ppermute | solution.py:60
  77.8 10.5 %collective-permute-start.11 = (f32[2,80,8]{2,1,0:T(8,128)S(1)}, f32[2,80,8]{2,1,0:T(8,128)S(1)}, u32[]{:S(2)}, u32[]{:S(2)}) collective-permute-start(f32[2,80,8]{2,1,0:T(8,128)S(1)} %pad_maximum_fusion.10), channel_id=1, source_target_pairs={{0,1},{1,2},{2,3},{3,4},{4,5},{5,6},{6,7},{7,8},{8,9},{9,10},{10,1... | collective-permute-start | bytes 15368 | tf_op jit(solution)/shard_map/ppermute | solution.py:59
  80.4 7.0 %copy-start.4 = (f32[65,8,256]{2,1,0:T(8,128)}, f32[65,8,256]{2,1,0:T(8,128)S(1)}, u32[]{:S(2)}) copy-start(f32[65,8,256]{2,1,0:T(8,128)S(1)} %multiply_select_fusion.hn_ref) | copy-start | bytes 1597444
  80.4 7.0 %copy-start.12 = (f32[65,64,8]{1,2,0:T(8,128)S(1)}, f32[65,64,8]{1,2,0:T(8,128)}, u32[]{:S(2)}) copy-start(f32[65,64,8]{1,2,0:T(8,128)} %copy.117) | copy-start | bytes 399364
  82.2 10.8 %collective-permute-start.5 = (f32[65,80,8]{1,2,0:T(8,128)S(1)}, f32[65,80,8]{1,2,0:T(8,128)S(1)}, u32[]{:S(2)}, u32[]{:S(2)}) collective-permute-start(f32[65,80,8]{1,2,0:T(8,128)S(1)} %pad_maximum_fusion.5), channel_id=1, source_target_pairs={{1,0},{2,1},{3,2},{4,3},{5,4},{6,5},{7,6},{8,7},{9,8},{10,9},{11,1... | collective-permute-start | bytes 499208 | tf_op jit(solution)/shard_map/ppermute | solution.py:60
  88.3 11.9 %collective-permute-start.6 = (f32[65,80,8]{1,2,0:T(8,128)}, f32[65,80,8]{1,2,0:T(8,128)S(1)}, u32[]{:S(2)}, u32[]{:S(2)}) collective-permute-start(f32[65,80,8]{1,2,0:T(8,128)} %pad_maximum_fusion.6), channel_id=1, source_target_pairs={{0,1},{1,2},{2,3},{3,4},{4,5},{5,6},{6,7},{7,8},{8,9},{9,10},{10,1... | collective-permute-start | bytes 499208 | tf_op jit(solution)/shard_map/ppermute | solution.py:59
  (5 other events, 12.7 us)

commit v7 on v6

--- a/solution.py
+++ b/solution.py
@@ -249,6 +249,7 @@
     halo = exchange(fields, [False, True, True, False])
 
     padded = atmosphere_block(atm_flux)
+    halo, padded = lax.optimization_barrier((halo, padded))
     ocean_flux = remap(padded, remap_index, remap_weight)
     forcing = jnp.sum(coupling[:, :, None, None] * ocean_flux[None], axis=1)
     f_halo = exchange([forcing], [False])

time: 138 us -> 133 us (0.964); the launches traced: 136 us -> 132 us
  waiting for transfers between devices: 11 us -> 6.83 us
  starting transfers between devices: 37.2 us -> 39.5 us
    ppermute x2, waiting for transfers between devices: 6.36 us -> 1.51 us  [exchange(): lax.ppermute(easts, 'ox', [(i, (i + 1) % cols_n) for i in range(cols_n)])]
    ppermute x2, waiting for transfers between devices: 0.01 us -> 2.88 us  [exchange(): north = lax.ppermute(bots, 'oy', [(i + 1, i) for i in range(rows_n - 1)])]
    ppermute x2, waiting for transfers between devices: 4.04 us -> 2.42 us  [exchange(): lax.ppermute(wests, 'ox', [((i + 1) % cols_n, i) for i in range(cols_n)])]
  transfers between devices with their start and end apart: 13 -> 13, of which waited for: 3 -> 3; matrix products, arithmetic and copies ran while one was open for 34% -> 19% of each run, Pallas kernels for 0% -> 0%
where the time goes in v7:
time: 133 us; the launch traced here: 132 us
  starting transfers between devices  39.5 us (30%)
  Pallas kernels  29.3 us (22%)
  other arithmetic  25.5 us (19%)
  local copies, waits for them, and re-layouts  20.7 us (16%)
  matrix products  8.71 us (7%)
  waiting for transfers between devices  6.83 us (5%)
  between operations  1.84 us (1%)
    pallas_call x1, Pallas kernels, evolve(): pl.pallas_call(stencil_kernel, out_shape=jax.ShapeDtypeStruct(tracers.sha...  29.3 us
    ppermute x2, starting transfers between devices, exchange(): lax.ppermute(wests, 'ox', [((i + 1) % cols_n, i) for i in range(cols_n)])  9.64 us
    ppermute x2, starting transfers between devices, exchange(): south = lax.ppermute(tops, 'oy', [(i, i + 1) for i in range(rows_n - 1)])  9.15 us
    dot_general x1, matrix products, remap(): window = jnp.einsum('fpb,bq->fpq', lifted, pick_c, precision=HIGH)  8.15 us
    all_to_all x1, starting transfers between devices, atmosphere_block(): got = lax.all_to_all(pieces, 'ox', split_axis=2, concat_axis=1, tiled=True)  7.82 us
    reduce_sum x1, other arithmetic, remap(): fast = jnp.sum(window * wsum.transpose(0, 2, 1, 3)[None], axis=(1, 3))  7.37 us
    concatenate x2, other arithmetic, exchange(): return (north, south, jnp.concatenate([from_e, gap, from_w], axis=-1))  4.7 us
    ppermute x2, starting transfers between devices, exchange(): north = lax.ppermute(bots, 'oy', [(i + 1, i) for i in range(rows_n - 1)])  3.83 us
  transfers between devices with their start and end apart: 13, of which 3 were waited for; matrix products, arithmetic and copies ran while one was open for 19% of the time, Pallas kernels for 0%

profile of v7, /device:TPU:1, one launch (start us, length us, event | category | flops | bytes accessed | tf_op | source)
XLA Modules:
  0.0 132.5 jit_solution(9644476003120381835)
XLA Ops:
  1.5 1.1 fusion.21
  4.5 4.6 %collective-permute-start.2 = (f32[65,8,256]{2,1,0:T(8,128)}, f32[65,8,256]{2,1,0:T(8,128)}, u32[]{:S(2)}, u32[]{:S(2)}) collective-permute-start(f32[65,8,256]{2,1,0:T(8,128)} %pad_maximum_fusion.3), channel_id=1, source_target_pairs={{0,16},{16,32},{32,48},{48,64},{64,80},{80,96},{96,112},{1,17},{17... | collective-permute-start | bytes 1597448 | tf_op jit(solution)/shard_map/ppermute | solution.py:42
  9.1 1.5 %collective-permute-start = (f32[65,8,256]{2,1,0:T(8,128)}, f32[65,8,256]{2,1,0:T(8,128)}, u32[]{:S(2)}, u32[]{:S(2)}) collective-permute-start(f32[65,8,256]{2,1,0:T(8,128)} %pad_maximum_fusion.3), channel_id=1, source_target_pairs={{120,112},{119,113},{118,114},{117,115},{116,116},{115,117},{114,1... | collective-permute-start | bytes 1597448 | tf_op jit(solution)/shard_map/ppermute | solution.py:45
  12.1 7.8 %all-to-all-start = ((f32[8,2,16,68]{3,1,0,2:T(2,128)}), f32[8,2,16,68]{3,1,0,2:T(2,128)}, u32[]{:S(2)}, u32[]{:S(2)}) async-start(f32[8,2,16,68]{3,1,0,2:T(2,128)} %copy.118), calls=%async_computation | async-start | bytes 262144 | tf_op jit(solution)/shard_map/all_to_all | solution.py:195
  20.8 1.9 %collective-permute-start.1 = (f32[65,8,256]{2,1,0:T(8,128)}, f32[65,8,256]{2,1,0:T(8,128)}, u32[]{:S(2)}, u32[]{:S(2)}) collective-permute-start(f32[65,8,256]{2,1,0:T(8,128)} %pad_maximum_fusion.4), channel_id=1, source_target_pairs={{16,0},{32,16},{48,32},{64,48},{80,64},{96,80},{112,96},{17,1},{33... | collective-permute-start | bytes 1597448 | tf_op jit(solution)/shard_map/ppermute | solution.py:43
  22.8 1.1 fusion.24
  23.9 1.0 fusion.25
  24.9 1.4 %fusion.20 = (f32[32,64,8]{2,1,0:T(8,128)S(1)}, f32[32,64,8]{2,1,0:T(8,128)}) fusion(f32[32,64,256]{2,1,0:T(8,128)S(1)} %bitcast.100), kind=kLoop, calls=%fused_computation.78 | loop fusion | bytes 262144 | tf_op jit(solution)/shard_map/slice | solution.py:56
  27.5 1.9 %select_reduce_fusion = f32[25,64,256]{2,1,0:T(8,128)} fusion(f32[4,64,256]{2,1,0:T(8,128)S(1)} %copy-done.13, s32[4,64,256]{2,1,0:T(8,128)S(1)} %get-tuple-element.59), kind=kLoop, calls=%fused_computation.32 | loop fusion | flops 4505600 | bytes 2162688 | tf_op jit(solution)/shard_map/reduce_sum | solution.py:224
  29.5 3.2 %pad_maximum_fusion.1 = (f32[65,64,8]{2,1,0:T(8,128)}, f32[65,64,8]{2,1,0:T(8,128)S(1)}) fusion(f32[1,64,8]{2,1,0:T(8,128)S(1)} %get-tuple-element.95, f32[16,64,8]{2,1,0:T(8,128)S(1)} %copy-done.8, f32[16,64,8]{2,1,0:T(8,128)} %get-tuple-element.81, f32[32,64,8]{2,1,0:T(8,128)S(1)} %get-tuple-element.73, f32[1,64,8]{2,1,0:T(8,128)S(1)} %get-tuple-element.96, ...), kind=kLoop, calls=%fused_computation.35 | loop fusion | flops 199680 | bytes 532480 | tf_op jit(solution)/shard_map/concatenate | solution.py:56
  32.7 2.2 %copy.108 = f32[65,64,8]{1,2,0:T(8,128)S(1)} copy(f32[65,64,8]{2,1,0:T(8,128)} %get-tuple-element.105) | data formatting | bytes 266240 | tf_op jit(solution)/shard_map/concatenate | solution.py:56
  36.4 3.6 %collective-permute-start.5 = (f32[8,2,68]{2,0,1:T(8,128)S(1)}, f32[8,2,68]{2,0,1:T(8,128)S(1)}, u32[]{:S(2)}, u32[]{:S(2)}) collective-permute-start(f32[8,2,68]{2,0,1:T(8,128)S(1)} %get-tuple-element.93), channel_id=1, source_target_pairs={{0,16},{16,32},{32,48},{48,64},{64,80},{80,96},{96,112},{1,17},{17... | collective-permute-start | bytes 13064 | tf_op jit(solution)/shard_map/ppermute | solution.py:197
  40.1 1.9 %collective-permute-start.6 = (f32[8,2,68]{2,0,1:T(8,128)S(1)}, f32[8,2,68]{2,0,1:T(8,128)S(1)}, u32[]{:S(2)}, u32[]{:S(2)}) collective-permute-start(f32[8,2,68]{2,0,1:T(8,128)S(1)} %get-tuple-element.94), channel_id=1, source_target_pairs={{16,0},{32,16},{48,32},{64,48},{80,64},{96,80},{112,96},{17,1},{33... | collective-permute-start | bytes 13064 | tf_op jit(solution)/shard_map/ppermute | solution.py:198
  42.0 1.2 fusion.23
  43.5 1.2 rev.6
  44.8 1.2 multiply_select_fusion.hn_ref
  47.3 1.3 collective-permute-start.4
  48.8 3.7 %collective-permute-start.3 = (f32[65,80,8]{1,2,0:T(8,128)S(1)}, f32[65,80,8]{1,2,0:T(8,128)}, u32[]{:S(2)}, u32[]{:S(2)}) collective-permute-start(f32[65,80,8]{1,2,0:T(8,128)S(1)} %pad_maximum_fusion.5), channel_id=1, source_target_pairs={{1,0},{2,1},{3,2},{4,3},{5,4},{6,5},{7,6},{8,7},{9,8},{10,9},{11,1... | collective-permute-start | bytes 499208 | tf_op jit(solution)/shard_map/ppermute | solution.py:60
  55.3 2.4 %collective-permute-done.3 = f32[65,80,8]{1,2,0:T(8,128)} collective-permute-done((f32[65,80,8]{1,2,0:T(8,128)S(1)}, f32[65,80,8]{1,2,0:T(8,128)}, u32[]{:S(2)}, u32[]{:S(2)}) %collective-permute-start.3) | collective-permute-done | bytes 166432 | tf_op jit(solution)/shard_map/ppermute | solution.py:60
  57.7 1.7 %copy.114 = f32[65,80,8]{2,1,0:T(8,128)S(1)} copy(f32[65,80,8]{1,2,0:T(8,128)} %collective-permute-done.3) | data formatting | bytes 332800 | tf_op jit(solution)/shard_map/ppermute | solution.py:60
  59.4 3.2 %copy.115 = f32[65,80,8]{2,1,0:T(8,128)} copy(f32[65,80,8]{1,2,0:T(8,128)} %collective-permute-done.4) | data formatting | bytes 332800 | tf_op jit(solution)/shard_map/ppermute | solution.py:59
  62.6 4.0 %pad_maximum_fusion.hc_ref = f32[65,80,128]{2,1,0:T(8,128)} fusion(f32[65,80,8]{2,1,0:T(8,128)} %copy.115, f32[65,80,8]{2,1,0:T(8,128)S(1)} %copy.114, f32[128]{0:T(128)S(1)} %pad.19.clone), kind=kLoop, calls=%fused_computation.34 | loop fusion | flops 1331200 | bytes 2995712 | tf_op jit(solution)/shard_map/concatenate | solution.py:62
  67.7 8.1 %fusion.7 = f32[8,5,64,5,256]{4,2,3,1,0:T(8,128)} fusion(f32[8,5,64,68,1]{3,2,4,1,0:T(8,128)S(1)} %bitcast.101, pred[5,256,68,1,1]{1,0,2,4,3:T(8,128)(4,1)S(1)} %bitcast.110), kind=kOutput, calls=%fused_computation.45 | convolution fusion | flops 2673868800 | bytes 13890560 | tf_op jit(solution)/shard_map/fpb,bq->fpq/dot_general | solution.py:217
  75.8 7.4 %conditional.1 = (f32[8,64,256]{2,1,0:T(8,128)}) conditional(s32[]{:T(128)} %convert_element_type.14, (f32[5,64,5,256]{3,1,2,0:T(8,128)S(1)}, f32[8,5,64,5,256]{4,2,3,1,0:T(8,128)}) %tuple.65, (f32[4,64,256]{2,1,0:T(8,128)}, f32[8,36,68]{2,0,1:T(8,128)S(1)}, s32[4,64,256]{2,1,0:T(8,128)S(1)}) %tuple.67), branch_computations={%region_2.4_spmd, %region_4.6_spmd} | conditional | flops 6422528 | bytes 15269896 | solution.py:239
  75.9 7.4 %multiply_reduce_fusion = f32[8,64,256]{2,1,0:T(8,128)} fusion(f32[8,5,64,5,256]{4,2,3,1,0:T(8,128)} %get-tuple-element.19, f32[5,64,5,256]{3,1,2,0:T(8,128)S(1)} %get-tuple-element.20), kind=kLoop, calls=%fused_computation.4 | loop fusion | flops 6422528 | bytes 15269888 | tf_op jit(solution)/shard_map/reduce_sum | solution.py:228
  83.2 1.2 multiply_reduce_fusion.1.f_ref
  84.5 4.5 %collective-permute-start.9 = (f32[2,8,256]{2,1,0:T(8,128)S(1)}, f32[2,8,256]{2,1,0:T(8,128)S(1)}, u32[]{:S(2)}, u32[]{:S(2)}) collective-permute-start(f32[2,8,256]{2,1,0:T(8,128)S(1)} %get-tuple-element.92), channel_id=1, source_target_pairs={{0,16},{16,32},{32,48},{48,64},{64,80},{80,96},{96,112},{1,17},{17... | collective-permute-start | bytes 49160 | tf_op jit(solution)/shard_map/ppermute | solution.py:42
  89.7 1.9 %collective-permute-start.8 = (f32[2,8,256]{2,1,0:T(8,128)S(1)}, f32[2,8,256]{2,1,0:T(8,128)S(1)}, u32[]{:S(2)}, u32[]{:S(2)}) collective-permute-start(f32[2,8,256]{2,1,0:T(8,128)S(1)} %get-tuple-element.91), channel_id=1, source_target_pairs={{16,0},{32,16},{48,32},{64,48},{80,64},{96,80},{112,96},{17,1},{33... | collective-permute-start | bytes 49160 | tf_op jit(solution)/shard_map/ppermute | solution.py:43
  91.8 2.9 %collective-permute-done.8 = f32[2,8,256]{2,1,0:T(8,128)S(1)} collective-permute-done((f32[2,8,256]{2,1,0:T(8,128)S(1)}, f32[2,8,256]{2,1,0:T(8,128)S(1)}, u32[]{:S(2)}, u32[]{:S(2)}) %collective-permute-start.8) | collective-permute-done | bytes 16416 | tf_op jit(solution)/shard_map/ppermute | solution.py:43
  95.0 5.9 %collective-permute-start.10 = (f32[2,80,8]{2,1,0:T(8,128)S(1)}, f32[2,80,8]{2,1,0:T(8,128)S(1)}, u32[]{:S(2)}, u32[]{:S(2)}) collective-permute-start(f32[2,80,8]{2,1,0:T(8,128)S(1)} %pad_maximum_fusion.9), channel_id=1, source_target_pairs={{1,0},{2,1},{3,2},{4,3},{5,4},{6,5},{7,6},{8,7},{9,8},{10,9},{11,1... | collective-permute-start | bytes 15368 | tf_op jit(solution)/shard_map/ppermute | solution.py:60
  100.9 1.5 %collective-permute-done.11 = f32[2,80,8]{2,1,0:T(8,128)S(1)} collective-permute-done((f32[2,80,8]{2,1,0:T(8,128)S(1)}, f32[2,80,8]{2,1,0:T(8,128)S(1)}, u32[]{:S(2)}, u32[]{:S(2)}) %collective-permute-start.11) | collective-permute-done | bytes 5152 | tf_op jit(solution)/shard_map/ppermute | solution.py:59
  103.2 29.3 %shard_map.95 = f32[2,16,64,256]{3,2,1,0:T(8,128)} custom-call(f32[2,16,64,256]{3,2,1,0:T(8,128)} %tr_ref.1, bf16[16,64,256]{2,1,0:T(8,128)(2,1)} %u_ref.1, bf16[16,64,256]{2,1,0:T(8,128)(2,1)} %v_ref.1, s32[64,256]{1,0:T(8,128)} %m_ref.1, f32[2,64,256]{2,1,0:T(8,128)} %copy-done.12, f32[65,8,256]{2,1,0:T(8,128)} %copy-done.4, ...), custom_call_target="tpu_custom_call" | custom-call | tf_op jit(solution)/shard_map/pallas_call | solution.py:166
  (112 shorter events, 14.7 us)
Async XLA Ops:
  0.6 10.0 %copy-start.16 = (f32[8,2,1024]{2,1,0:T(2,128)S(1)}, f32[8,2,1024]{2,1,0:T(2,128)}, u32[]{:S(2)}) copy-start(f32[8,2,1024]{2,1,0:T(2,128)} %param.12) | copy-start | bytes 196612
  2.6 20.2 %copy-start.2 = (bf16[16,64,256]{2,1,0:T(8,128)(2,1)S(1)}, bf16[16,64,256]{2,1,0:T(8,128)(2,1)}, u32[]{:S(2)}) copy-start(bf16[16,64,256]{2,1,0:T(8,128)(2,1)} %u_ref.1) | copy-start | bytes 1572868
  4.5 19.4 %copy-start.3 = (bf16[16,64,256]{2,1,0:T(8,128)(2,1)S(1)}, bf16[16,64,256]{2,1,0:T(8,128)(2,1)}, u32[]{:S(2)}) copy-start(bf16[16,64,256]{2,1,0:T(8,128)(2,1)} %v_ref.1) | copy-start | bytes 1572868
  4.5 37.5 %collective-permute-start.2 = (f32[65,8,256]{2,1,0:T(8,128)}, f32[65,8,256]{2,1,0:T(8,128)}, u32[]{:S(2)}, u32[]{:S(2)}) collective-permute-start(f32[65,8,256]{2,1,0:T(8,128)} %pad_maximum_fusion.3), channel_id=1, source_target_pairs={{0,16},{16,32},{32,48},{48,64},{64,80},{80,96},{96,112},{1,17},{17... | collective-permute-start | bytes 1597448 | tf_op jit(solution)/shard_map/ppermute | solution.py:42
  9.1 34.3 %collective-permute-start = (f32[65,8,256]{2,1,0:T(8,128)}, f32[65,8,256]{2,1,0:T(8,128)}, u32[]{:S(2)}, u32[]{:S(2)}) collective-permute-start(f32[65,8,256]{2,1,0:T(8,128)} %pad_maximum_fusion.3), channel_id=1, source_target_pairs={{120,112},{119,113},{118,114},{117,115},{116,116},{115,117},{114,1... | collective-permute-start | bytes 1597448 | tf_op jit(solution)/shard_map/ppermute | solution.py:45
  12.1 23.4 %all-to-all-start = ((f32[8,2,16,68]{3,1,0,2:T(2,128)}), f32[8,2,16,68]{3,1,0,2:T(2,128)}, u32[]{:S(2)}, u32[]{:S(2)}) async-start(f32[8,2,16,68]{3,1,0,2:T(2,128)} %copy.118), calls=%async_computation | async-start | bytes 262144 | tf_op jit(solution)/shard_map/all_to_all | solution.py:195
  20.0 4.9 %copy-start = (f32[2,16,64,256]{3,2,1,0:T(8,128)S(1)}, f32[2,16,64,256]{3,2,1,0:T(8,128)}, u32[]{:S(2)}) copy-start(f32[2,16,64,256]{3,2,1,0:T(8,128)} %tr_ref.1) | copy-start | bytes 6291460
  20.8 23.9 %collective-permute-start.1 = (f32[65,8,256]{2,1,0:T(8,128)}, f32[65,8,256]{2,1,0:T(8,128)}, u32[]{:S(2)}, u32[]{:S(2)}) collective-permute-start(f32[65,8,256]{2,1,0:T(8,128)} %pad_maximum_fusion.4), channel_id=1, source_target_pairs={{16,0},{32,16},{48,32},{64,48},{80,64},{96,80},{112,96},{17,1},{33... | collective-permute-start | bytes 1597448 | tf_op jit(solution)/shard_map/ppermute | solution.py:43
  24.9 2.6 %copy-start.13 = (f32[4,64,256]{2,1,0:T(8,128)S(1)}, f32[4,64,256]{2,1,0:T(8,128)}, u32[]{:S(2)}) copy-start(f32[4,64,256]{2,1,0:T(8,128)} %param.14) | copy-start | bytes 786436
  26.4 3.1 %copy-start.5 = (f32[32,64,8]{2,1,0:T(8,128)S(1)}, f32[32,64,8]{2,1,0:T(8,128)}, u32[]{:S(2)}) copy-start(f32[32,64,8]{2,1,0:T(8,128)} %get-tuple-element.74) | copy-start | bytes 196612
  26.4 3.1 %copy-start.8 = (f32[16,64,8]{2,1,0:T(8,128)S(1)}, f32[16,64,8]{2,1,0:T(8,128)}, u32[]{:S(2)}) copy-start(f32[16,64,8]{2,1,0:T(8,128)} %get-tuple-element.83) | copy-start | bytes 98308
  26.4 3.1 %copy-start.9 = (f32[16,64,8]{2,1,0:T(8,128)S(1)}, f32[16,64,8]{2,1,0:T(8,128)}, u32[]{:S(2)}) copy-start(f32[16,64,8]{2,1,0:T(8,128)} %get-tuple-element.84) | copy-start | bytes 98308
  34.9 9.9 %copy-start.20 = (f32[65]{0:T(128)S(1)}, f32[65]{0:T(128)}, u32[]{:S(2)}) copy-start(f32[65]{0:T(128)} %constant.76.clone.1) | copy-start | bytes 784
  36.4 18.8 %collective-permute-start.5 = (f32[8,2,68]{2,0,1:T(8,128)S(1)}, f32[8,2,68]{2,0,1:T(8,128)S(1)}, u32[]{:S(2)}, u32[]{:S(2)}) collective-permute-start(f32[8,2,68]{2,0,1:T(8,128)S(1)} %get-tuple-element.93), channel_id=1, source_target_pairs={{0,16},{16,32},{32,48},{48,64},{64,80},{80,96},{96,112},{1,17},{17... | collective-permute-start | bytes 13064 | tf_op jit(solution)/shard_map/ppermute | solution.py:197
  40.1 15.1 %collective-permute-start.6 = (f32[8,2,68]{2,0,1:T(8,128)S(1)}, f32[8,2,68]{2,0,1:T(8,128)S(1)}, u32[]{:S(2)}, u32[]{:S(2)}) collective-permute-start(f32[8,2,68]{2,0,1:T(8,128)S(1)} %get-tuple-element.94), channel_id=1, source_target_pairs={{16,0},{32,16},{48,32},{64,48},{80,64},{96,80},{112,96},{17,1},{33... | collective-permute-start | bytes 13064 | tf_op jit(solution)/shard_map/ppermute | solution.py:198
  44.7 8.1 %copy-start.15 = (pred[1280,68]{0,1:T(8,128)(4,1)S(1)}, pred[1280,68]{0,1:T(8,128)(4,1)}, u32[]{:S(2)}) copy-start(pred[1280,68]{0,1:T(8,128)(4,1)} %iota_compare_fusion.1) | copy-start | bytes 261124
  46.0 13.4 %copy-start.4 = (f32[65,8,256]{2,1,0:T(8,128)}, f32[65,8,256]{2,1,0:T(8,128)S(1)}, u32[]{:S(2)}) copy-start(f32[65,8,256]{2,1,0:T(8,128)S(1)} %multiply_select_fusion.hn_ref) | copy-start | bytes 1597444
  47.3 12.1 %collective-permute-start.4 = (f32[65,80,8]{1,2,0:T(8,128)}, f32[65,80,8]{1,2,0:T(8,128)}, u32[]{:S(2)}, u32[]{:S(2)}) collective-permute-start(f32[65,80,8]{1,2,0:T(8,128)} %pad_maximum_fusion.6), channel_id=1, source_target_pairs={{0,1},{1,2},{2,3},{3,4},{4,5},{5,6},{6,7},{7,8},{8,9},{9,10},{10,1... | collective-permute-start | bytes 499208 | tf_op jit(solution)/shard_map/ppermute | solution.py:59
  48.8 8.8 %collective-permute-start.3 = (f32[65,80,8]{1,2,0:T(8,128)S(1)}, f32[65,80,8]{1,2,0:T(8,128)}, u32[]{:S(2)}, u32[]{:S(2)}) collective-permute-start(f32[65,80,8]{1,2,0:T(8,128)S(1)} %pad_maximum_fusion.5), channel_id=1, source_target_pairs={{1,0},{2,1},{3,2},{4,3},{5,4},{6,5},{7,6},{8,7},{9,8},{10,9},{11,1... | collective-permute-start | bytes 499208 | tf_op jit(solution)/shard_map/ppermute | solution.py:60
  55.2 11.4 %copy-start.10 = (f32[8,36,68]{2,0,1:T(8,128)}, f32[8,36,68]{2,0,1:T(8,128)S(1)}, u32[]{:S(2)}) copy-start(f32[8,36,68]{2,0,1:T(8,128)S(1)} %pad_maximum_fusion.7) | copy-start | bytes 235012
  67.6 8.2 %copy-start.1 = (f32[25,64,256]{2,1,0:T(8,128)S(1)}, f32[25,64,256]{2,1,0:T(8,128)}, u32[]{:S(2)}) copy-start(f32[25,64,256]{2,1,0:T(8,128)} %select_reduce_fusion) | copy-start | bytes 4915204
  67.7 8.2 %copy-start.7 = (s32[4,64,256]{2,1,0:T(8,128)S(1)}, s32[4,64,256]{2,1,0:T(8,128)}, u32[]{:S(2)}) copy-start(s32[4,64,256]{2,1,0:T(8,128)} %param.13) | copy-start | bytes 786436
  67.7 8.2 %copy-start.11 = (f32[8,36,68]{2,0,1:T(8,128)S(1)}, f32[8,36,68]{2,0,1:T(8,128)}, u32[]{:S(2)}) copy-start(f32[8,36,68]{2,0,1:T(8,128)} %copy-done.10) | copy-start | bytes 235012
  75.8 7.4 %copy-start.19 = (f32[2,8]{1,0:T(2,128)S(1)}, f32[2,8]{1,0:T(2,128)}, u32[]{:S(2)}) copy-start(f32[2,8]{1,0:T(2,128)} %param.15) | copy-start | bytes 196
  84.4 18.7 %copy-start.12 = (f32[2,64,256]{2,1,0:T(8,128)}, f32[2,64,256]{2,1,0:T(8,128)S(1)}, u32[]{:S(2)}) copy-start(f32[2,64,256]{2,1,0:T(8,128)S(1)} %multiply_reduce_fusion.1.f_ref) | copy-start | bytes 393220
  84.5 10.3 %collective-permute-start.9 = (f32[2,8,256]{2,1,0:T(8,128)S(1)}, f32[2,8,256]{2,1,0:T(8,128)S(1)}, u32[]{:S(2)}, u32[]{:S(2)}) collective-permute-start(f32[2,8,256]{2,1,0:T(8,128)S(1)} %get-tuple-element.92), channel_id=1, source_target_pairs={{0,16},{16,32},{32,48},{48,64},{64,80},{80,96},{96,112},{1,17},{17... | collective-permute-start | bytes 49160 | tf_op jit(solution)/shard_map/ppermute | solution.py:42
  89.0 2.7 %collective-permute-start.7 = (f32[2,8,256]{2,1,0:T(8,128)S(1)}, f32[2,8,256]{2,1,0:T(8,128)S(1)}, u32[]{:S(2)}, u32[]{:S(2)}) collective-permute-start(f32[2,8,256]{2,1,0:T(8,128)S(1)} %get-tuple-element.92), channel_id=1, source_target_pairs={{120,112},{119,113},{118,114},{117,115},{116,116},{115,117},{114,1... | collective-permute-start | bytes 49160 | tf_op jit(solution)/shard_map/ppermute | solution.py:45
  89.7 5.1 %collective-permute-start.8 = (f32[2,8,256]{2,1,0:T(8,128)S(1)}, f32[2,8,256]{2,1,0:T(8,128)S(1)}, u32[]{:S(2)}, u32[]{:S(2)}) collective-permute-start(f32[2,8,256]{2,1,0:T(8,128)S(1)} %get-tuple-element.91), channel_id=1, source_target_pairs={{16,0},{32,16},{48,32},{64,48},{80,64},{96,80},{112,96},{17,1},{33... | collective-permute-start | bytes 49160 | tf_op jit(solution)/shard_map/ppermute | solution.py:43
  94.7 8.4 %copy-start.17 = (f32[2,8,256]{2,1,0:T(8,128)}, f32[2,8,256]{2,1,0:T(8,128)S(1)}, u32[]{:S(2)}) copy-start(f32[2,8,256]{2,1,0:T(8,128)S(1)} %broadcast_select_fusion.fn_ref) | copy-start | bytes 49156
  94.8 8.4 %copy-start.18 = (f32[2,8,256]{2,1,0:T(8,128)}, f32[2,8,256]{2,1,0:T(8,128)S(1)}, u32[]{:S(2)}) copy-start(f32[2,8,256]{2,1,0:T(8,128)S(1)} %collective-permute-done.9.fs_ref) | copy-start | bytes 49156
  94.9 7.5 %collective-permute-start.11 = (f32[2,80,8]{2,1,0:T(8,128)S(1)}, f32[2,80,8]{2,1,0:T(8,128)S(1)}, u32[]{:S(2)}, u32[]{:S(2)}) collective-permute-start(f32[2,80,8]{2,1,0:T(8,128)S(1)} %pad_maximum_fusion.10), channel_id=1, source_target_pairs={{0,1},{1,2},{2,3},{3,4},{4,5},{5,6},{6,7},{7,8},{8,9},{9,10},{10,1... | collective-permute-start | bytes 15368 | tf_op jit(solution)/shard_map/ppermute | solution.py:59
  95.0 7.4 %collective-permute-start.10 = (f32[2,80,8]{2,1,0:T(8,128)S(1)}, f32[2,80,8]{2,1,0:T(8,128)S(1)}, u32[]{:S(2)}, u32[]{:S(2)}) collective-permute-start(f32[2,80,8]{2,1,0:T(8,128)S(1)} %pad_maximum_fusion.9), channel_id=1, source_target_pairs={{1,0},{2,1},{3,2},{4,3},{5,4},{6,5},{7,6},{8,7},{9,8},{10,9},{11,1... | collective-permute-start | bytes 15368 | tf_op jit(solution)/shard_map/ppermute | solution.py:60
  (2 other events, 3.2 us)

commit v8 on v7

--- a/solution.py
+++ b/solution.py
@@ -1,3 +1,5 @@
+import functools
+
 import jax
 import jax.numpy as jnp
 from jax import lax
@@ -62,7 +64,7 @@
     return north, south, jnp.concatenate([from_e, gap, from_w], axis=-1)
 
 
-def stencil_kernel(tr_ref, u_ref, v_ref, m_ref, f_ref, hn_ref, hs_ref, hc_ref, fn_ref, fs_ref, fc_ref,
+def stencil_kernel(alone, tr_ref, u_ref, v_ref, m_ref, f_ref, hn_ref, hs_ref, hc_ref, fn_ref, fs_ref, fc_ref,
                    o_ref, buf, uu, vv, mm, ff, cw, ce, cs, cn, cc, m8, mf):
     nt, nk, orows, ocols = tr_ref.shape
     _, planes, rows, lanes = buf.shape
@@ -74,7 +76,11 @@
         dst[:, ocols:] = hc_ref[at]
 
     def fill(p, carry):
-        place(buf.at[0, p], tr_ref[p // nk, p % nk], p)
+        if alone:
+            buf[0, p] = jnp.zeros((rows, lanes), jnp.float32)
+            buf[1, p] = jnp.zeros((rows, lanes), jnp.float32)
+        else:
+            place(buf.at[0, p], tr_ref[p // nk, p % nk], p)
         return carry
 
     lax.fori_loop(0, planes, fill, 0)
@@ -150,6 +156,20 @@
                 plane(src, dst, k, k - 1 if k > 0 else None, k + 1 if k < nk - 1 else None, k == 0)
         return carry
 
+    if alone:
+        for i in range(STEPS):
+            for k in range(min(i + 1, nk)):
+                plane(i % 2, 1 - i % 2, k, k - 1 if k > 0 else None, k + 1 if k < nk - 1 else None, k == 0)
+
+        def out(p, carry):
+            t = p // nk
+            k = p % nk
+            o_ref[t, k] = tr_ref[t, k] + buf[STEPS % 2, p, :orows, :ocols]
+            return carry
+
+        lax.fori_loop(0, planes, out, 0)
+        return
+
     lax.fori_loop(0, STEPS // 2, step, 0)
 
     def out(p, carry):
@@ -159,12 +179,12 @@
     lax.fori_loop(0, planes, out, 0)
 
 
-def evolve(tracers, u_vel, v_vel, land_mask, forcing, halo, f_halo):
+def evolve(alone, tracers, u_vel, v_vel, land_mask, forcing, halo, f_halo):
     nt, nk, orows, ocols = tracers.shape
     plane = (orows + 2 * WIDE, LANES)
     vm = lambda *shape: pltpu.VMEM(shape, jnp.float32)
     return pl.pallas_call(
-        stencil_kernel,
+        functools.partial(stencil_kernel, alone),
         out_shape=jax.ShapeDtypeStruct(tracers.shape, jnp.float32),
         scratch_shapes=[
             vm(2, nt * nk, *plane),
@@ -252,8 +272,15 @@
     halo, padded = lax.optimization_barrier((halo, padded))
     ocean_flux = remap(padded, remap_index, remap_weight)
     forcing = jnp.sum(coupling[:, :, None, None] * ocean_flux[None], axis=1)
+    nt, orows, ocols = forcing.shape
+    no_halo = (
+        jnp.zeros((nt, WIDE, ocols), jnp.float32),
+        jnp.zeros((nt, WIDE, ocols), jnp.float32),
+        jnp.zeros((nt, orows + 2 * WIDE, LANES - ocols), jnp.float32),
+    )
+    own = evolve(False, tracers, u_vel, v_vel, land_mask, forcing, halo, no_halo)
     f_halo = exchange([forcing], [False])
-    final = evolve(tracers, u_vel, v_vel, land_mask, forcing, halo, f_halo)
+    final = evolve(True, own, u_vel, v_vel, land_mask, jnp.zeros_like(forcing), halo, f_halo)
     return (ocean_flux, final)
 
 

time: 133 us -> 146 us (1.098)
  Pallas kernels: 29.3 us -> 43 us
  starting transfers between devices: 39.5 us -> 36.3 us
  local copies, waits for them, and re-layouts: 20.7 us -> 22.6 us
    pallas_call x1 -> x2, Pallas kernels: 29.3 us -> 43 us  [evolve(): pl.pallas_call(functools.partial(stencil_kernel, alone), out_shape=jax.Sh...]
    ppermute x2, starting transfers between devices: 9.64 us -> 5.49 us  [exchange(): lax.ppermute(wests, 'ox', [((i + 1) % cols_n, i) for i in range(cols_n)])]
    ppermute x2, waiting for transfers between devices: 1.51 us -> 5.19 us  [exchange(): lax.ppermute(easts, 'ox', [(i, (i + 1) % cols_n) for i in range(cols_n)])]
    ppermute x2, waiting for transfers between devices: 2.88 us -> 0.01 us  [exchange(): north = lax.ppermute(bots, 'oy', [(i + 1, i) for i in range(rows_n - 1)])]
    ppermute x2, waiting for transfers between devices: 2.42 us -> 0.59 us  [exchange(): lax.ppermute(wests, 'ox', [((i + 1) % cols_n, i) for i in range(cols_n)])]
  transfers between devices with their start and end apart: 13 -> 13, of which waited for: 3 -> 3; matrix products, arithmetic and copies ran while one was open for 19% -> 18% of each run, Pallas kernels for 0% -> 20%
where the time goes in v8:
time: 146 us; the launch traced here: 145 us
  Pallas kernels  43 us (29%)
  starting transfers between devices  36.3 us (25%)
  other arithmetic  25.4 us (17%)
  local copies, waits for them, and re-layouts  22.6 us (15%)
  matrix products  9.73 us (7%)
  waiting for transfers between devices  6.38 us (4%)
  between operations  1.76 us (1%)
    pallas_call x2, Pallas kernels, evolve(): pl.pallas_call(functools.partial(stencil_kernel, alone), out_shape=jax.Sh...  43 us
    ppermute x2, starting transfers between devices, exchange(): south = lax.ppermute(tops, 'oy', [(i, i + 1) for i in range(rows_n - 1)])  9.87 us
    dot_general x1, matrix products, remap(): window = jnp.einsum('fpb,bq->fpq', lifted, pick_c, precision=HIGH)  9.16 us
    all_to_all x1, starting transfers between devices, atmosphere_block(): got = lax.all_to_all(pieces, 'ox', split_axis=2, concat_axis=1, tiled=True)  7.82 us
    reduce_sum x1, other arithmetic, remap(): fast = jnp.sum(window * wsum.transpose(0, 2, 1, 3)[None], axis=(1, 3))  7.37 us
    ppermute x2, starting transfers between devices, exchange(): lax.ppermute(wests, 'ox', [((i + 1) % cols_n, i) for i in range(cols_n)])  5.49 us
    ppermute x2, waiting for transfers between devices, exchange(): lax.ppermute(easts, 'ox', [(i, (i + 1) % cols_n) for i in range(cols_n)])  5.19 us
    concatenate x2, other arithmetic, exchange(): return (north, south, jnp.concatenate([from_e, gap, from_w], axis=-1))  4.69 us
  transfers between devices with their start and end apart: 13, of which 3 were waited for; matrix products, arithmetic and copies ran while one was open for 18% of the time, Pallas kernels for 20%

profile of v8, /device:TPU:1, one launch (start us, length us, event | category | flops | bytes accessed | tf_op | source)
XLA Modules:
  0.0 145.2 jit_solution(3460648276013192142)
XLA Ops:
  0.6 1.1 fusion.21
  1.8 1.0 convert_bitcast_fusion
  5.2 1.5 %collective-permute-start = (f32[65,8,256]{2,1,0:T(8,128)}, f32[65,8,256]{2,1,0:T(8,128)}, u32[]{:S(2)}, u32[]{:S(2)}) collective-permute-start(f32[65,8,256]{2,1,0:T(8,128)} %pad_maximum_fusion.3), channel_id=1, source_target_pairs={{120,112},{119,113},{118,114},{117,115},{116,116},{115,117},{114,1... | collective-permute-start | bytes 1597448 | tf_op jit(solution)/shard_map/ppermute | solution.py:47
  6.7 4.5 %collective-permute-start.2 = (f32[65,8,256]{2,1,0:T(8,128)}, f32[65,8,256]{2,1,0:T(8,128)}, u32[]{:S(2)}, u32[]{:S(2)}) collective-permute-start(f32[65,8,256]{2,1,0:T(8,128)} %pad_maximum_fusion.3), channel_id=1, source_target_pairs={{0,16},{16,32},{32,48},{48,64},{64,80},{80,96},{96,112},{1,17},{17... | collective-permute-start | bytes 1597448 | tf_op jit(solution)/shard_map/ppermute | solution.py:44
  12.0 1.9 %collective-permute-start.1 = (f32[65,8,256]{2,1,0:T(8,128)}, f32[65,8,256]{2,1,0:T(8,128)}, u32[]{:S(2)}, u32[]{:S(2)}) collective-permute-start(f32[65,8,256]{2,1,0:T(8,128)} %pad_maximum_fusion.4), channel_id=1, source_target_pairs={{16,0},{32,16},{48,32},{64,48},{80,64},{96,80},{112,96},{17,1},{33... | collective-permute-start | bytes 1597448 | tf_op jit(solution)/shard_map/ppermute | solution.py:45
  15.5 7.8 %all-to-all-start = ((f32[8,2,16,68]{3,1,0,2:T(2,128)}), f32[8,2,16,68]{3,1,0,2:T(2,128)}, u32[]{:S(2)}, u32[]{:S(2)}) async-start(f32[8,2,16,68]{3,1,0,2:T(2,128)} %copy.118), calls=%async_computation | async-start | bytes 262144 | tf_op jit(solution)/shard_map/all_to_all | solution.py:215
  23.3 1.7 %fusion.20 = (f32[32,64,8]{2,1,0:T(8,128)}, f32[32,64,8]{2,1,0:T(8,128)}) fusion(f32[32,64,256]{2,1,0:T(8,128)S(1)} %bitcast.100), kind=kLoop, calls=%fused_computation.78 | loop fusion | bytes 262144 | tf_op jit(solution)/shard_map/slice | solution.py:58
  25.0 1.0 fusion.24
  26.0 1.0 fusion.25
  27.4 1.0 add_select_fusion.2
  28.4 1.9 %select_reduce_fusion = f32[25,64,256]{2,1,0:T(8,128)} fusion(f32[4,64,256]{2,1,0:T(8,128)S(1)} %copy-done.12, s32[4,64,256]{2,1,0:T(8,128)S(1)} %get-tuple-element.59), kind=kLoop, calls=%fused_computation.32 | loop fusion | flops 4505600 | bytes 2162688 | tf_op jit(solution)/shard_map/reduce_sum | solution.py:244
  30.4 3.1 %pad_maximum_fusion.1 = (f32[65,64,8]{2,1,0:T(8,128)}, f32[65,64,8]{2,1,0:T(8,128)S(1)}) fusion(f32[1,64,8]{2,1,0:T(8,128)S(1)} %get-tuple-element.95, f32[16,64,8]{2,1,0:T(8,128)S(1)} %copy-done.9, f32[16,64,8]{2,1,0:T(8,128)S(1)} %copy-done.7, f32[32,64,8]{2,1,0:T(8,128)S(1)} %copy-done.5, f32[1,64,8]{2,1,0:T(8,128)S(1)} %get-tuple-element.96, ...), kind=kLoop, calls=%fused_computation.35 | loop fusion | flops 199680 | bytes 532480 | tf_op jit(solution)/shard_map/concatenate | solution.py:58
  33.6 2.2 %copy.108 = f32[65,64,8]{1,2,0:T(8,128)S(1)} copy(f32[65,64,8]{2,1,0:T(8,128)} %get-tuple-element.105) | data formatting | bytes 266240 | tf_op jit(solution)/shard_map/concatenate | solution.py:58
  37.3 3.9 %collective-permute-start.5 = (f32[8,2,68]{2,0,1:T(8,128)S(1)}, f32[8,2,68]{2,0,1:T(8,128)S(1)}, u32[]{:S(2)}, u32[]{:S(2)}) collective-permute-start(f32[8,2,68]{2,0,1:T(8,128)S(1)} %get-tuple-element.93), channel_id=1, source_target_pairs={{0,16},{16,32},{32,48},{48,64},{64,80},{80,96},{96,112},{1,17},{17... | collective-permute-start | bytes 13064 | tf_op jit(solution)/shard_map/ppermute | solution.py:217
  41.2 1.9 %collective-permute-start.6 = (f32[8,2,68]{2,0,1:T(8,128)S(1)}, f32[8,2,68]{2,0,1:T(8,128)S(1)}, u32[]{:S(2)}, u32[]{:S(2)}) collective-permute-start(f32[8,2,68]{2,0,1:T(8,128)S(1)} %get-tuple-element.94), channel_id=1, source_target_pairs={{16,0},{32,16},{48,32},{64,48},{80,64},{96,80},{112,96},{17,1},{33... | collective-permute-start | bytes 13064 | tf_op jit(solution)/shard_map/ppermute | solution.py:218
  43.2 1.2 rev.6
  44.4 1.2 multiply_select_fusion.hn_ref
  45.9 1.2 fusion.23
  47.5 5.0 %collective-permute-start.3 = (f32[65,80,8]{1,2,0:T(8,128)S(1)}, f32[65,80,8]{1,2,0:T(8,128)}, u32[]{:S(2)}, u32[]{:S(2)}) collective-permute-start(f32[65,80,8]{1,2,0:T(8,128)S(1)} %pad_maximum_fusion.5), channel_id=1, source_target_pairs={{1,0},{2,1},{3,2},{4,3},{5,4},{6,5},{7,6},{8,7},{9,8},{10,9},{11,1... | collective-permute-start | bytes 499208 | tf_op jit(solution)/shard_map/ppermute | solution.py:62
  56.7 1.7 %copy.114 = f32[65,80,8]{2,1,0:T(8,128)S(1)} copy(f32[65,80,8]{1,2,0:T(8,128)} %collective-permute-done.3) | data formatting | bytes 332800 | tf_op jit(solution)/shard_map/ppermute | solution.py:62
  58.4 5.2 %collective-permute-done.4 = f32[65,80,8]{1,2,0:T(8,128)S(1)} collective-permute-done((f32[65,80,8]{1,2,0:T(8,128)}, f32[65,80,8]{1,2,0:T(8,128)S(1)}, u32[]{:S(2)}, u32[]{:S(2)}) %collective-permute-start.4) | collective-permute-done | bytes 166432 | tf_op jit(solution)/shard_map/ppermute | solution.py:61
  63.6 2.3 %copy.115 = f32[65,80,8]{2,1,0:T(8,128)} copy(f32[65,80,8]{1,2,0:T(8,128)S(1)} %collective-permute-done.4) | data formatting | bytes 332800 | tf_op jit(solution)/shard_map/ppermute | solution.py:61
  65.9 4.0 %pad_maximum_fusion.hc_ref = f32[65,80,128]{2,1,0:T(8,128)} fusion(f32[65,80,8]{2,1,0:T(8,128)} %copy.115, f32[65,80,8]{2,1,0:T(8,128)S(1)} %copy.114, f32[128]{0:T(128)S(1)} %pad.19.clone), kind=kLoop, calls=%fused_computation.34 | loop fusion | flops 1331200 | bytes 2995712 | tf_op jit(solution)/shard_map/concatenate | solution.py:64
  70.9 9.2 %fusion.7 = f32[8,5,64,5,256]{4,2,3,1,0:T(8,128)} fusion(f32[8,5,64,68,1]{3,2,4,1,0:T(8,128)S(1)} %bitcast.101, pred[5,256,68,1,1]{1,0,2,4,3:T(8,128)(4,1)} %bitcast.110), kind=kOutput, calls=%fused_computation.45 | convolution fusion | flops 2673868800 | bytes 13890560 | tf_op jit(solution)/shard_map/fpb,bq->fpq/dot_general | solution.py:237
  80.1 7.4 %conditional.1 = (f32[8,64,256]{2,1,0:T(8,128)}) conditional(s32[]{:T(128)} %convert_element_type.14, (f32[5,64,5,256]{3,1,2,0:T(8,128)S(1)}, f32[8,5,64,5,256]{4,2,3,1,0:T(8,128)}) %tuple.65, (f32[4,64,256]{2,1,0:T(8,128)}, f32[8,36,68]{2,0,1:T(8,128)S(1)}, s32[4,64,256]{2,1,0:T(8,128)S(1)}) %tuple.66), branch_computations={%region_2.4_spmd, %region_4.6_spmd} | conditional | flops 6422528 | bytes 15269896 | solution.py:259
  80.1 7.4 %multiply_reduce_fusion = f32[8,64,256]{2,1,0:T(8,128)} fusion(f32[8,5,64,5,256]{4,2,3,1,0:T(8,128)} %get-tuple-element.19, f32[5,64,5,256]{3,1,2,0:T(8,128)S(1)} %get-tuple-element.20), kind=kLoop, calls=%fused_computation.4 | loop fusion | flops 6422528 | bytes 15269888 | tf_op jit(solution)/shard_map/reduce_sum | solution.py:248
  87.4 1.2 multiply_reduce_fusion.1.f_ref
  89.3 1.9 %collective-permute-start.8 = (f32[2,8,256]{2,1,0:T(8,128)S(1)}, f32[2,8,256]{2,1,0:T(8,128)S(1)}, u32[]{:S(2)}, u32[]{:S(2)}) collective-permute-start(f32[2,8,256]{2,1,0:T(8,128)S(1)} %get-tuple-element.91), channel_id=1, source_target_pairs={{16,0},{32,16},{48,32},{64,48},{80,64},{96,80},{112,96},{17,1},{33... | collective-permute-start | bytes 49160 | tf_op jit(solution)/shard_map/ppermute | solution.py:45
  91.3 5.4 %collective-permute-start.9 = (f32[2,8,256]{2,1,0:T(8,128)S(1)}, f32[2,8,256]{2,1,0:T(8,128)S(1)}, u32[]{:S(2)}, u32[]{:S(2)}) collective-permute-start(f32[2,8,256]{2,1,0:T(8,128)S(1)} %get-tuple-element.92), channel_id=1, source_target_pairs={{0,16},{16,32},{32,48},{48,64},{64,80},{80,96},{96,112},{1,17},{17... | collective-permute-start | bytes 49160 | tf_op jit(solution)/shard_map/ppermute | solution.py:44
  98.2 1.3 collective-permute-start.11
  100.7 29.3 %shard_map.95.tr_ref = f32[2,16,64,256]{3,2,1,0:T(8,128)} custom-call(f32[2,16,64,256]{3,2,1,0:T(8,128)} %tr_ref.1, bf16[16,64,256]{2,1,0:T(8,128)(2,1)} %u_ref.3, bf16[16,64,256]{2,1,0:T(8,128)(2,1)} %v_ref.3, s32[64,256]{1,0:T(8,128)} %m_ref.3, f32[2,64,256]{2,1,0:T(8,128)} %copy-done.11, f32[65,8,256]{2,1,0:T(8,128)} %copy-done.3, ...), custom_call_target="tpu_custom_call" | custom-call | tf_op jit(solution)/shard_map/pallas_call | solution.py:186
  131.5 13.7 %shard_map.96 = f32[2,16,64,256]{3,2,1,0:T(8,128)} custom-call(f32[2,16,64,256]{3,2,1,0:T(8,128)} %shard_map.95.tr_ref, bf16[16,64,256]{2,1,0:T(8,128)(2,1)} %u_ref.3, bf16[16,64,256]{2,1,0:T(8,128)(2,1)} %v_ref.3, s32[64,256]{1,0:T(8,128)} %m_ref.3, f32[2,64,256]{2,1,0:T(8,128)} %broadcast_in_dim.57.f_ref, f32[65,8,256]{2,1,0:T(8,128)} %copy-done.3, ...), custom_call_target="tpu_custom_call" | custom-call | tf_op jit(solution)/shard_map/pallas_call | solution.py:186
  (119 shorter events, 16.7 us)
Async XLA Ops:
  0.6 13.3 %copy-start.14 = (f32[8,2,1024]{2,1,0:T(2,128)S(1)}, f32[8,2,1024]{2,1,0:T(2,128)}, u32[]{:S(2)}) copy-start(f32[8,2,1024]{2,1,0:T(2,128)} %param.12) | copy-start | bytes 196612
  0.6 13.5 %slice-start = ((f32[8,2,1024]{2,1,0:T(2,128)}), f32[8,2,62]{2,1,0:T(2,128)S(1)}, s32[]{:S(2)}) async-start(f32[8,2,1024]{2,1,0:T(2,128)} %param.12), calls=%async_computation.1 | async-start | bytes 16384 | tf_op jit(solution)/shard_map/jit(_roll_static)/slice | solution.py:213
  1.8 21.6 %copy-start = (f32[2,16,64,256]{3,2,1,0:T(8,128)S(1)}, f32[2,16,64,256]{3,2,1,0:T(8,128)}, u32[]{:S(2)}) copy-start(f32[2,16,64,256]{3,2,1,0:T(8,128)} %tr_ref.1) | copy-start | bytes 6291460
  5.2 38.0 %collective-permute-start = (f32[65,8,256]{2,1,0:T(8,128)}, f32[65,8,256]{2,1,0:T(8,128)}, u32[]{:S(2)}, u32[]{:S(2)}) collective-permute-start(f32[65,8,256]{2,1,0:T(8,128)} %pad_maximum_fusion.3), channel_id=1, source_target_pairs={{120,112},{119,113},{118,114},{117,115},{116,116},{115,117},{114,1... | collective-permute-start | bytes 1597448 | tf_op jit(solution)/shard_map/ppermute | solution.py:47
  6.7 39.3 %collective-permute-start.2 = (f32[65,8,256]{2,1,0:T(8,128)}, f32[65,8,256]{2,1,0:T(8,128)}, u32[]{:S(2)}, u32[]{:S(2)}) collective-permute-start(f32[65,8,256]{2,1,0:T(8,128)} %pad_maximum_fusion.3), channel_id=1, source_target_pairs={{0,16},{16,32},{32,48},{48,64},{64,80},{80,96},{96,112},{1,17},{17... | collective-permute-start | bytes 1597448 | tf_op jit(solution)/shard_map/ppermute | solution.py:44
  12.0 32.4 %collective-permute-start.1 = (f32[65,8,256]{2,1,0:T(8,128)}, f32[65,8,256]{2,1,0:T(8,128)}, u32[]{:S(2)}, u32[]{:S(2)}) collective-permute-start(f32[65,8,256]{2,1,0:T(8,128)} %pad_maximum_fusion.4), channel_id=1, source_target_pairs={{16,0},{32,16},{48,32},{64,48},{80,64},{96,80},{112,96},{17,1},{33... | collective-permute-start | bytes 1597448 | tf_op jit(solution)/shard_map/ppermute | solution.py:45
  14.5 10.5 %copy-start.1 = (bf16[16,64,256]{2,1,0:T(8,128)(2,1)S(1)}, bf16[16,64,256]{2,1,0:T(8,128)(2,1)}, u32[]{:S(2)}) copy-start(bf16[16,64,256]{2,1,0:T(8,128)(2,1)} %u_ref.3) | copy-start | bytes 1572868
  15.5 20.9 %all-to-all-start = ((f32[8,2,16,68]{3,1,0,2:T(2,128)}), f32[8,2,16,68]{3,1,0,2:T(2,128)}, u32[]{:S(2)}, u32[]{:S(2)}) async-start(f32[8,2,16,68]{3,1,0,2:T(2,128)} %copy.118), calls=%async_computation | async-start | bytes 262144 | tf_op jit(solution)/shard_map/all_to_all | solution.py:215
  25.0 3.4 %copy-start.12 = (f32[4,64,256]{2,1,0:T(8,128)S(1)}, f32[4,64,256]{2,1,0:T(8,128)}, u32[]{:S(2)}) copy-start(f32[4,64,256]{2,1,0:T(8,128)} %param.14) | copy-start | bytes 786436
  26.0 4.3 %copy-start.16 = (f32[1,64,256]{2,1,0:T(8,128)S(1)}, f32[1,64,256]{2,1,0:T(8,128)}, u32[]{:S(2)}) copy-start(f32[1,64,256]{2,1,0:T(8,128)} %copy-done.15) | copy-start | bytes 196612
  26.0 4.3 %copy-start.5 = (f32[32,64,8]{2,1,0:T(8,128)S(1)}, f32[32,64,8]{2,1,0:T(8,128)}, u32[]{:S(2)}) copy-start(f32[32,64,8]{2,1,0:T(8,128)} %get-tuple-element.73) | copy-start | bytes 196612
  27.1 3.3 %copy-start.20 = (s32[64]{0:T(128)}, s32[64]{0:T(128)S(1)}, u32[]{:S(2)}) copy-start(s32[64]{0:T(128)S(1)} %fusion.19) | copy-start | bytes 772
  27.3 3.1 %copy-start.7 = (f32[16,64,8]{2,1,0:T(8,128)S(1)}, f32[16,64,8]{2,1,0:T(8,128)}, u32[]{:S(2)}) copy-start(f32[16,64,8]{2,1,0:T(8,128)} %get-tuple-element.81) | copy-start | bytes 98308
  27.3 3.1 %copy-start.8 = (f32[16,64,8]{2,1,0:T(8,128)S(1)}, f32[16,64,8]{2,1,0:T(8,128)}, u32[]{:S(2)}) copy-start(f32[16,64,8]{2,1,0:T(8,128)} %get-tuple-element.82) | copy-start | bytes 98308
  27.3 3.1 %copy-start.9 = (f32[16,64,8]{2,1,0:T(8,128)S(1)}, f32[16,64,8]{2,1,0:T(8,128)}, u32[]{:S(2)}) copy-start(f32[16,64,8]{2,1,0:T(8,128)} %get-tuple-element.83) | copy-start | bytes 98308
  37.3 18.8 %collective-permute-start.5 = (f32[8,2,68]{2,0,1:T(8,128)S(1)}, f32[8,2,68]{2,0,1:T(8,128)S(1)}, u32[]{:S(2)}, u32[]{:S(2)}) collective-permute-start(f32[8,2,68]{2,0,1:T(8,128)S(1)} %get-tuple-element.93), channel_id=1, source_target_pairs={{0,16},{16,32},{32,48},{48,64},{64,80},{80,96},{96,112},{1,17},{17... | collective-permute-start | bytes 13064 | tf_op jit(solution)/shard_map/ppermute | solution.py:217
  41.2 14.9 %collective-permute-start.6 = (f32[8,2,68]{2,0,1:T(8,128)S(1)}, f32[8,2,68]{2,0,1:T(8,128)S(1)}, u32[]{:S(2)}, u32[]{:S(2)}) collective-permute-start(f32[8,2,68]{2,0,1:T(8,128)S(1)} %get-tuple-element.94), channel_id=1, source_target_pairs={{16,0},{32,16},{48,32},{64,48},{80,64},{96,80},{112,96},{17,1},{33... | collective-permute-start | bytes 13064 | tf_op jit(solution)/shard_map/ppermute | solution.py:218
  45.6 7.1 %copy-start.3 = (f32[65,8,256]{2,1,0:T(8,128)}, f32[65,8,256]{2,1,0:T(8,128)S(1)}, u32[]{:S(2)}) copy-start(f32[65,8,256]{2,1,0:T(8,128)S(1)} %multiply_select_fusion.hn_ref) | copy-start | bytes 1597444
  45.8 7.9 %copy-start.21 = (s32[64]{0:T(128)S(1)}, s32[64]{0:T(128)}, u32[]{:S(2)}) copy-start(s32[64]{0:T(128)} %copy-done.20) | copy-start | bytes 772
  45.8 9.0 %copy-start.17 = (pred[4,64,256]{2,1,0:T(8,128)(4,1)S(1)}, pred[4,64,256]{2,1,0:T(8,128)(4,1)}, u32[]{:S(2)}) copy-start(pred[4,64,256]{2,1,0:T(8,128)(4,1)} %get-tuple-element.60) | copy-start | bytes 196612
  47.5 9.2 %collective-permute-start.3 = (f32[65,80,8]{1,2,0:T(8,128)S(1)}, f32[65,80,8]{1,2,0:T(8,128)}, u32[]{:S(2)}, u32[]{:S(2)}) collective-permute-start(f32[65,80,8]{1,2,0:T(8,128)S(1)} %pad_maximum_fusion.5), channel_id=1, source_target_pairs={{1,0},{2,1},{3,2},{4,3},{5,4},{6,5},{7,6},{8,7},{9,8},{10,9},{11,1... | collective-permute-start | bytes 499208 | tf_op jit(solution)/shard_map/ppermute | solution.py:62
  53.6 10.0 %collective-permute-start.4 = (f32[65,80,8]{1,2,0:T(8,128)}, f32[65,80,8]{1,2,0:T(8,128)S(1)}, u32[]{:S(2)}, u32[]{:S(2)}) collective-permute-start(f32[65,80,8]{1,2,0:T(8,128)} %pad_maximum_fusion.6), channel_id=1, source_target_pairs={{0,1},{1,2},{2,3},{3,4},{4,5},{5,6},{6,7},{7,8},{8,9},{9,10},{10,1... | collective-permute-start | bytes 499208 | tf_op jit(solution)/shard_map/ppermute | solution.py:61
  70.9 9.2 %copy-start.4 = (f32[25,64,256]{2,1,0:T(8,128)S(1)}, f32[25,64,256]{2,1,0:T(8,128)}, u32[]{:S(2)}) copy-start(f32[25,64,256]{2,1,0:T(8,128)} %select_reduce_fusion) | copy-start | bytes 4915204
  80.1 7.4 %copy-start.22 = (f32[2,8]{1,0:T(2,128)S(1)}, f32[2,8]{1,0:T(2,128)}, u32[]{:S(2)}) copy-start(f32[2,8]{1,0:T(2,128)} %param.15) | copy-start | bytes 196
  88.6 12.1 %copy-start.11 = (f32[2,64,256]{2,1,0:T(8,128)}, f32[2,64,256]{2,1,0:T(8,128)S(1)}, u32[]{:S(2)}) copy-start(f32[2,64,256]{2,1,0:T(8,128)S(1)} %multiply_reduce_fusion.1.f_ref) | copy-start | bytes 393220
  88.7 8.1 %collective-permute-start.7 = (f32[2,8,256]{2,1,0:T(8,128)S(1)}, f32[2,8,256]{2,1,0:T(8,128)S(1)}, u32[]{:S(2)}, u32[]{:S(2)}) collective-permute-start(f32[2,8,256]{2,1,0:T(8,128)S(1)} %get-tuple-element.92), channel_id=1, source_target_pairs={{120,112},{119,113},{118,114},{117,115},{116,116},{115,117},{114,1... | collective-permute-start | bytes 49160 | tf_op jit(solution)/shard_map/ppermute | solution.py:47
  89.3 7.6 %collective-permute-start.8 = (f32[2,8,256]{2,1,0:T(8,128)S(1)}, f32[2,8,256]{2,1,0:T(8,128)S(1)}, u32[]{:S(2)}, u32[]{:S(2)}) collective-permute-start(f32[2,8,256]{2,1,0:T(8,128)S(1)} %get-tuple-element.91), channel_id=1, source_target_pairs={{16,0},{32,16},{48,32},{64,48},{80,64},{96,80},{112,96},{17,1},{33... | collective-permute-start | bytes 49160 | tf_op jit(solution)/shard_map/ppermute | solution.py:45
  91.3 6.2 %collective-permute-start.9 = (f32[2,8,256]{2,1,0:T(8,128)S(1)}, f32[2,8,256]{2,1,0:T(8,128)S(1)}, u32[]{:S(2)}, u32[]{:S(2)}) collective-permute-start(f32[2,8,256]{2,1,0:T(8,128)S(1)} %get-tuple-element.92), channel_id=1, source_target_pairs={{0,16},{16,32},{32,48},{48,64},{64,80},{80,96},{96,112},{1,17},{17... | collective-permute-start | bytes 49160 | tf_op jit(solution)/shard_map/ppermute | solution.py:44
  96.9 33.2 %copy-start.18 = (f32[2,8,256]{2,1,0:T(8,128)}, f32[2,8,256]{2,1,0:T(8,128)S(1)}, u32[]{:S(2)}) copy-start(f32[2,8,256]{2,1,0:T(8,128)S(1)} %broadcast_select_fusion.fn_ref) | copy-start | bytes 49156
  97.6 32.5 %copy-start.19 = (f32[2,8,256]{2,1,0:T(8,128)}, f32[2,8,256]{2,1,0:T(8,128)S(1)}, u32[]{:S(2)}) copy-start(f32[2,8,256]{2,1,0:T(8,128)S(1)} %collective-permute-done.9.fs_ref) | copy-start | bytes 49156
  97.7 32.4 %collective-permute-start.10 = (f32[2,80,8]{2,1,0:T(8,128)S(1)}, f32[2,80,8]{2,1,0:T(8,128)S(1)}, u32[]{:S(2)}, u32[]{:S(2)}) collective-permute-start(f32[2,80,8]{2,1,0:T(8,128)S(1)} %pad_maximum_fusion.9), channel_id=1, source_target_pairs={{1,0},{2,1},{3,2},{4,3},{5,4},{6,5},{7,6},{8,7},{9,8},{10,9},{11,1... | collective-permute-start | bytes 15368 | tf_op jit(solution)/shard_map/ppermute | solution.py:62
  98.2 31.9 %collective-permute-start.11 = (f32[2,80,8]{2,1,0:T(8,128)S(1)}, f32[2,80,8]{2,1,0:T(8,128)S(1)}, u32[]{:S(2)}, u32[]{:S(2)}) collective-permute-start(f32[2,80,8]{2,1,0:T(8,128)S(1)} %pad_maximum_fusion.10), channel_id=1, source_target_pairs={{0,1},{1,2},{2,3},{3,4},{4,5},{5,6},{6,7},{7,8},{8,9},{9,10},{10,1... | collective-permute-start | bytes 15368 | tf_op jit(solution)/shard_map/ppermute | solution.py:61
  (4 other events, 8.9 us)

commit v9 on v7

--- a/solution.py
+++ b/solution.py
@@ -58,8 +58,13 @@
     )
     from_w = lax.ppermute(easts, "ox", [(i, (i + 1) % cols_n) for i in range(cols_n)])
     from_e = lax.ppermute(wests, "ox", [((i + 1) % cols_n, i) for i in range(cols_n)])
-    gap = jnp.zeros(from_e.shape[:-1] + (LANES - blocks[0].shape[-1] - 2 * WIDE,), jnp.float32)
-    return north, south, jnp.concatenate([from_e, gap, from_w], axis=-1)
+    return north, south, (from_e, from_w)
+
+
+def lane_tile(sides, cols):
+    from_e, from_w = sides
+    gap = jnp.zeros(from_e.shape[:-1] + (LANES - cols - 2 * WIDE,), jnp.float32)
+    return jnp.concatenate([from_e, gap, from_w], axis=-1)
 
 
 def stencil_kernel(tr_ref, u_ref, v_ref, m_ref, f_ref, hn_ref, hs_ref, hc_ref, fn_ref, fs_ref, fc_ref,
@@ -252,7 +257,10 @@
     halo, padded = lax.optimization_barrier((halo, padded))
     ocean_flux = remap(padded, remap_index, remap_weight)
     forcing = jnp.sum(coupling[:, :, None, None] * ocean_flux[None], axis=1)
+    sides, forcing = lax.optimization_barrier((halo[2], forcing))
+    halo = (halo[0], halo[1], lane_tile(sides, tracers.shape[-1]))
     f_halo = exchange([forcing], [False])
+    f_halo = (f_halo[0], f_halo[1], lane_tile(f_halo[2], tracers.shape[-1]))
     final = evolve(tracers, u_vel, v_vel, land_mask, forcing, halo, f_halo)
     return (ocean_flux, final)
 

time: 133 us -> 132 us (level)
  waiting for transfers between devices: 6.83 us -> 5.33 us
    ppermute x2 -> x0, local copies, waits for them, and re-layouts: 4.94 us -> none  [the longest x1 3.22 us: exchange(): lax.ppermute(easts, 'ox', [(i, (i + 1) % cols_n) for i in range(cols_n)])]
    optimization_barrier x0 -> x2, local copies, waits for them, and re-layouts: none -> 4.04 us  [on_device(): sides, forcing = lax.optimization_barrier((halo[2], forcing))]
    slice x0 -> x4, local copies, waits for them, and re-layouts: none -> 3.93 us  [exchange(): b[..., -WIDE:]]
    slice x5 -> x1, local copies, waits for them, and re-layouts: 3.62 us -> 0.08 us  [exchange(): b[..., :WIDE]]
    ppermute x2, waiting for transfers between devices: 1.51 us -> 4.91 us  [exchange(): lax.ppermute(easts, 'ox', [(i, (i + 1) % cols_n) for i in range(cols_n)])]
    ppermute x2, waiting for transfers between devices: 2.88 us -> 0.01 us  [exchange(): north = lax.ppermute(bots, 'oy', [(i + 1, i) for i in range(rows_n - 1)])]
    ppermute x2, waiting for transfers between devices: 2.42 us -> 0.4 us  [exchange(): lax.ppermute(wests, 'ox', [((i + 1) % cols_n, i) for i in range(cols_n)])]
    concatenate x1, local copies, waits for them, and re-layouts: 0.61 us -> 2.2 us  [exchange(): jnp.concatenate([b[..., -WIDE:] for b in blocks], axis=0)]
  transfers between devices with their start and end apart: 13 -> 13, of which waited for: 3 -> 3; matrix products, arithmetic and copies ran while one was open for 19% -> 24% of each run, Pallas kernels for 0% -> 0%
where the time goes in v9:
time: 132 us; the launch traced here: 131 us
  starting transfers between devices  40 us (30%)
  Pallas kernels  29.3 us (22%)
  other arithmetic  25.6 us (19%)
  local copies, waits for them, and re-layouts  20.3 us (15%)
  matrix products  8.77 us (7%)
  waiting for transfers between devices  5.33 us (4%)
  between operations  1.84 us (1%)
    pallas_call x1, Pallas kernels, evolve(): pl.pallas_call(stencil_kernel, out_shape=jax.ShapeDtypeStruct(tracers.sha...  29.3 us
    ppermute x2, starting transfers between devices, exchange(): south = lax.ppermute(tops, 'oy', [(i, i + 1) for i in range(rows_n - 1)])  9.75 us
    ppermute x2, starting transfers between devices, exchange(): lax.ppermute(wests, 'ox', [((i + 1) % cols_n, i) for i in range(cols_n)])  8.68 us
    dot_general x1, matrix products, remap(): window = jnp.einsum('fpb,bq->fpq', lifted, pick_c, precision=HIGH)  8.21 us
    all_to_all x1, starting transfers between devices, atmosphere_block(): got = lax.all_to_all(pieces, 'ox', split_axis=2, concat_axis=1, tiled=True)  7.82 us
    reduce_sum x1, other arithmetic, remap(): fast = jnp.sum(window * wsum.transpose(0, 2, 1, 3)[None], axis=(1, 3))  7.37 us
    ppermute x2, waiting for transfers between devices, exchange(): lax.ppermute(easts, 'ox', [(i, (i + 1) % cols_n) for i in range(cols_n)])  4.91 us
    concatenate x2, other arithmetic, lane_tile(): return jnp.concatenate([from_e, gap, from_w], axis=-1)  4.72 us
  transfers between devices with their start and end apart: 13, of which 3 were waited for; matrix products, arithmetic and copies ran while one was open for 24% of the time, Pallas kernels for 0%

profile of v9, /device:TPU:1, one launch (start us, length us, event | category | flops | bytes accessed | tf_op | source)
XLA Modules:
  0.0 131.3 jit_solution(9147591315053830839)
XLA Ops:
  0.6 1.1 fusion.21
  4.6 1.5 %collective-permute-start = (f32[65,8,256]{2,1,0:T(8,128)}, f32[65,8,256]{2,1,0:T(8,128)}, u32[]{:S(2)}, u32[]{:S(2)}) collective-permute-start(f32[65,8,256]{2,1,0:T(8,128)} %pad_maximum_fusion.3), channel_id=1, source_target_pairs={{120,112},{119,113},{118,114},{117,115},{116,116},{115,117},{114,1... | collective-permute-start | bytes 1597448 | tf_op jit(solution)/shard_map/ppermute | solution.py:45
  6.0 4.5 %collective-permute-start.2 = (f32[65,8,256]{2,1,0:T(8,128)}, f32[65,8,256]{2,1,0:T(8,128)}, u32[]{:S(2)}, u32[]{:S(2)}) collective-permute-start(f32[65,8,256]{2,1,0:T(8,128)} %pad_maximum_fusion.3), channel_id=1, source_target_pairs={{0,16},{16,32},{32,48},{48,64},{64,80},{80,96},{96,112},{1,17},{17... | collective-permute-start | bytes 1597448 | tf_op jit(solution)/shard_map/ppermute | solution.py:42
  11.4 1.9 %collective-permute-start.1 = (f32[65,8,256]{2,1,0:T(8,128)}, f32[65,8,256]{2,1,0:T(8,128)}, u32[]{:S(2)}, u32[]{:S(2)}) collective-permute-start(f32[65,8,256]{2,1,0:T(8,128)} %pad_maximum_fusion.4), channel_id=1, source_target_pairs={{16,0},{32,16},{48,32},{64,48},{80,64},{96,80},{112,96},{17,1},{33... | collective-permute-start | bytes 1597448 | tf_op jit(solution)/shard_map/ppermute | solution.py:43
  14.9 7.8 %all-to-all-start = ((f32[8,2,16,68]{3,1,0,2:T(2,128)}), f32[8,2,16,68]{3,1,0,2:T(2,128)}, u32[]{:S(2)}, u32[]{:S(2)}) async-start(f32[8,2,16,68]{3,1,0,2:T(2,128)} %copy.116), calls=%async_computation | async-start | bytes 262144 | tf_op jit(solution)/shard_map/all_to_all | solution.py:200
  22.7 1.7 %fusion.20 = (f32[32,64,8]{2,1,0:T(8,128)}, f32[32,64,8]{2,1,0:T(8,128)}) fusion(f32[32,64,256]{2,1,0:T(8,128)S(1)} %bitcast.100), kind=kLoop, calls=%fused_computation.78 | loop fusion | bytes 262144 | tf_op jit(solution)/shard_map/slice | solution.py:52
  24.4 1.1 fusion.24
  25.5 1.1 fusion.25
  27.5 1.0 add_select_fusion.2
  28.5 1.9 %select_reduce_fusion = f32[25,64,256]{2,1,0:T(8,128)} fusion(f32[4,64,256]{2,1,0:T(8,128)S(1)} %copy-done.12, s32[4,64,256]{2,1,0:T(8,128)S(1)} %get-tuple-element.67), kind=kLoop, calls=%fused_computation.32 | loop fusion | flops 4505600 | bytes 2162688 | tf_op jit(solution)/shard_map/reduce_sum | solution.py:229
  30.5 3.3 %pad_maximum_fusion.1 = (f32[65,64,8]{2,1,0:T(8,128)S(1)}, f32[65,64,8]{2,1,0:T(8,128)}) fusion(f32[1,64,8]{2,1,0:T(8,128)S(1)} %get-tuple-element.104, f32[16,64,8]{2,1,0:T(8,128)} %get-tuple-element.92, f32[16,64,8]{2,1,0:T(8,128)S(1)} %copy-done.9, f32[32,64,8]{2,1,0:T(8,128)} %get-tuple-element.82, f32[1,64,8]{2,1,0:T(8,128)S(1)} %get-tuple-element.103, ...), kind=kLoop, calls=%fused_computation.35 | loop fusion | flops 199680 | bytes 532480 | tf_op jit(solution)/shard_map/concatenate | solution.py:56
  33.8 2.2 %copy.111 = f32[65,64,8]{1,2,0:T(8,128)S(1)} copy(f32[65,64,8]{2,1,0:T(8,128)} %get-tuple-element.114) | data formatting | bytes 266240 | tf_op jit(solution)/shard_map/concatenate | solution.py:52
  37.5 3.9 %collective-permute-start.5 = (f32[8,2,68]{2,0,1:T(8,128)S(1)}, f32[8,2,68]{2,0,1:T(8,128)S(1)}, u32[]{:S(2)}, u32[]{:S(2)}) collective-permute-start(f32[8,2,68]{2,0,1:T(8,128)S(1)} %get-tuple-element.101), channel_id=1, source_target_pairs={{0,16},{16,32},{32,48},{48,64},{64,80},{80,96},{96,112},{1,17},{17... | collective-permute-start | bytes 13064 | tf_op jit(solution)/shard_map/ppermute | solution.py:202
  41.5 1.9 %collective-permute-start.6 = (f32[8,2,68]{2,0,1:T(8,128)S(1)}, f32[8,2,68]{2,0,1:T(8,128)S(1)}, u32[]{:S(2)}, u32[]{:S(2)}) collective-permute-start(f32[8,2,68]{2,0,1:T(8,128)S(1)} %get-tuple-element.102), channel_id=1, source_target_pairs={{16,0},{32,16},{48,32},{64,48},{80,64},{96,80},{112,96},{17,1},{33... | collective-permute-start | bytes 13064 | tf_op jit(solution)/shard_map/ppermute | solution.py:203
  43.4 1.2 rev.6
  44.7 1.2 multiply_select_fusion.hn_ref
  46.2 1.2 fusion.23
  47.7 1.7 %collective-permute-start.4 = (f32[65,80,8]{1,2,0:T(8,128)S(1)}, f32[65,80,8]{1,2,0:T(8,128)S(1)}, u32[]{:S(2)}, u32[]{:S(2)}) collective-permute-start(f32[65,80,8]{1,2,0:T(8,128)S(1)} %pad_maximum_fusion.6), channel_id=1, source_target_pairs={{0,1},{1,2},{2,3},{3,4},{4,5},{5,6},{6,7},{7,8},{8,9},{9,10},{10,1... | collective-permute-start | bytes 499208 | tf_op jit(solution)/shard_map/ppermute | solution.py:59
  49.8 3.4 %collective-permute-start.3 = (f32[65,80,8]{1,2,0:T(8,128)S(1)}, f32[65,80,8]{1,2,0:T(8,128)S(1)}, u32[]{:S(2)}, u32[]{:S(2)}) collective-permute-start(f32[65,80,8]{1,2,0:T(8,128)S(1)} %pad_maximum_fusion.5), channel_id=1, source_target_pairs={{1,0},{2,1},{3,2},{4,3},{5,4},{6,5},{7,6},{8,7},{9,8},{10,9},{11,1... | collective-permute-start | bytes 499208 | tf_op jit(solution)/shard_map/ppermute | solution.py:60
  55.2 2.3 %collective-permute-done.4 = f32[65,80,8]{1,2,0:T(8,128)S(1)} collective-permute-done((f32[65,80,8]{1,2,0:T(8,128)S(1)}, f32[65,80,8]{1,2,0:T(8,128)S(1)}, u32[]{:S(2)}, u32[]{:S(2)}) %collective-permute-start.4) | collective-permute-done | bytes 166432 | tf_op jit(solution)/shard_map/ppermute | solution.py:59
  59.7 8.2 %fusion.7 = f32[8,5,64,5,256]{4,2,3,1,0:T(8,128)} fusion(f32[8,5,64,68,1]{3,2,4,1,0:T(8,128)S(1)} %bitcast.101, pred[5,256,68,1,1]{1,0,2,4,3:T(8,128)(4,1)S(1)} %bitcast.110), kind=kOutput, calls=%fused_computation.45 | convolution fusion | flops 2673868800 | bytes 13890560 | tf_op jit(solution)/shard_map/fpb,bq->fpq/dot_general | solution.py:222
  67.9 7.6 %conditional.1 = (f32[8,64,256]{2,1,0:T(8,128)}) conditional(s32[]{:T(128)} %convert_element_type.14, (f32[5,64,5,256]{3,1,2,0:T(8,128)S(1)}, f32[8,5,64,5,256]{4,2,3,1,0:T(8,128)}) %tuple.67, (f32[4,64,256]{2,1,0:T(8,128)}, f32[8,36,68]{2,0,1:T(8,128)S(1)}, s32[4,64,256]{2,1,0:T(8,128)S(1)}) %tuple.68), branch_computations={%region_2.4_spmd, %region_4.6_spmd} | conditional | flops 6422528 | bytes 15269896 | solution.py:244
  68.1 7.4 %multiply_reduce_fusion = f32[8,64,256]{2,1,0:T(8,128)} fusion(f32[8,5,64,5,256]{4,2,3,1,0:T(8,128)} %get-tuple-element.19, f32[5,64,5,256]{3,1,2,0:T(8,128)S(1)} %get-tuple-element.20), kind=kLoop, calls=%fused_computation.4 | loop fusion | flops 6422528 | bytes 15269888 | tf_op jit(solution)/shard_map/reduce_sum | solution.py:233
  75.4 1.2 multiply_reduce_fusion.1.f_ref
  77.4 1.9 %collective-permute-start.8 = (f32[2,8,256]{2,1,0:T(8,128)S(1)}, f32[2,8,256]{2,1,0:T(8,128)S(1)}, u32[]{:S(2)}, u32[]{:S(2)}) collective-permute-start(f32[2,8,256]{2,1,0:T(8,128)S(1)} %get-tuple-element.99), channel_id=1, source_target_pairs={{16,0},{32,16},{48,32},{64,48},{80,64},{96,80},{112,96},{17,1},{33... | collective-permute-start | bytes 49160 | tf_op jit(solution)/shard_map/ppermute | solution.py:43
  79.4 5.3 %collective-permute-start.9 = (f32[2,8,256]{2,1,0:T(8,128)S(1)}, f32[2,8,256]{2,1,0:T(8,128)S(1)}, u32[]{:S(2)}, u32[]{:S(2)}) collective-permute-start(f32[2,8,256]{2,1,0:T(8,128)S(1)} %get-tuple-element.100), channel_id=1, source_target_pairs={{0,16},{16,32},{32,48},{48,64},{64,80},{80,96},{96,112},{1,17},{17... | collective-permute-start | bytes 49160 | tf_op jit(solution)/shard_map/ppermute | solution.py:42
  84.7 1.7 %copy.123 = f32[65,80,8]{2,1,0:T(8,128)S(1)} copy(f32[65,80,8]{1,2,0:T(8,128)} %copy-done.18) | data formatting | bytes 332800 | tf_op jit(solution)/shard_map/optimization_barrier | solution.py:260
  86.4 2.3 %copy.124 = f32[65,80,8]{2,1,0:T(8,128)} copy(f32[65,80,8]{1,2,0:T(8,128)S(1)} %copy-done.17) | data formatting | bytes 332800 | tf_op jit(solution)/shard_map/optimization_barrier | solution.py:260
  89.1 5.3 %collective-permute-start.10 = (f32[2,80,8]{2,1,0:T(8,128)S(1)}, f32[2,80,8]{2,1,0:T(8,128)S(1)}, u32[]{:S(2)}, u32[]{:S(2)}) collective-permute-start(f32[2,80,8]{2,1,0:T(8,128)S(1)} %pad_maximum_fusion.9), channel_id=1, source_target_pairs={{1,0},{2,1},{3,2},{4,3},{5,4},{6,5},{7,6},{8,7},{9,8},{10,9},{11,1... | collective-permute-start | bytes 15368 | tf_op jit(solution)/shard_map/ppermute | solution.py:60
  94.7 4.0 %pad_maximum_fusion.hc_ref = f32[65,80,128]{2,1,0:T(8,128)} fusion(f32[65,80,8]{2,1,0:T(8,128)} %copy.124, f32[65,80,8]{2,1,0:T(8,128)S(1)} %copy.123, f32[128]{0:T(128)S(1)} %pad.10.clone), kind=kLoop, calls=%fused_computation.34 | loop fusion | flops 1331200 | bytes 2995712 | tf_op jit(solution)/shard_map/concatenate | solution.py:67
  98.7 2.6 %collective-permute-done.11 = f32[2,80,8]{2,1,0:T(8,128)S(1)} collective-permute-done((f32[2,80,8]{2,1,0:T(8,128)S(1)}, f32[2,80,8]{2,1,0:T(8,128)S(1)}, u32[]{:S(2)}, u32[]{:S(2)}) %collective-permute-start.11) | collective-permute-done | bytes 5152 | tf_op jit(solution)/shard_map/ppermute | solution.py:59
  102.0 29.3 %shard_map.95 = f32[2,16,64,256]{3,2,1,0:T(8,128)} custom-call(f32[2,16,64,256]{3,2,1,0:T(8,128)} %tr_ref.1, bf16[16,64,256]{2,1,0:T(8,128)(2,1)} %u_ref.1, bf16[16,64,256]{2,1,0:T(8,128)(2,1)} %v_ref.1, s32[64,256]{1,0:T(8,128)} %m_ref.1, f32[2,64,256]{2,1,0:T(8,128)} %copy-done.11, f32[65,8,256]{2,1,0:T(8,128)} %copy-done.4, ...), custom_call_target="tpu_custom_call" | custom-call | tf_op jit(solution)/shard_map/pallas_call | solution.py:171
  (117 shorter events, 14.2 us)
Async XLA Ops:
  0.6 12.7 %copy-start.15 = (f32[8,2,1024]{2,1,0:T(2,128)S(1)}, f32[8,2,1024]{2,1,0:T(2,128)}, u32[]{:S(2)}) copy-start(f32[8,2,1024]{2,1,0:T(2,128)} %param.12) | copy-start | bytes 196612
  0.6 12.9 %slice-start = ((f32[8,2,1024]{2,1,0:T(2,128)}), f32[8,2,62]{2,1,0:T(2,128)S(1)}, s32[]{:S(2)}) async-start(f32[8,2,1024]{2,1,0:T(2,128)} %param.12), calls=%async_computation.1 | async-start | bytes 16384 | tf_op jit(solution)/shard_map/jit(_roll_static)/slice | solution.py:198
  1.8 20.9 %copy-start = (f32[2,16,64,256]{3,2,1,0:T(8,128)S(1)}, f32[2,16,64,256]{3,2,1,0:T(8,128)}, u32[]{:S(2)}) copy-start(f32[2,16,64,256]{3,2,1,0:T(8,128)} %tr_ref.1) | copy-start | bytes 6291460
  4.6 38.8 %collective-permute-start = (f32[65,8,256]{2,1,0:T(8,128)}, f32[65,8,256]{2,1,0:T(8,128)}, u32[]{:S(2)}, u32[]{:S(2)}) collective-permute-start(f32[65,8,256]{2,1,0:T(8,128)} %pad_maximum_fusion.3), channel_id=1, source_target_pairs={{120,112},{119,113},{118,114},{117,115},{116,116},{115,117},{114,1... | collective-permute-start | bytes 1597448 | tf_op jit(solution)/shard_map/ppermute | solution.py:45
  6.0 40.1 %collective-permute-start.2 = (f32[65,8,256]{2,1,0:T(8,128)}, f32[65,8,256]{2,1,0:T(8,128)}, u32[]{:S(2)}, u32[]{:S(2)}) collective-permute-start(f32[65,8,256]{2,1,0:T(8,128)} %pad_maximum_fusion.3), channel_id=1, source_target_pairs={{0,16},{16,32},{32,48},{48,64},{64,80},{80,96},{96,112},{1,17},{17... | collective-permute-start | bytes 1597448 | tf_op jit(solution)/shard_map/ppermute | solution.py:42
  11.4 33.3 %collective-permute-start.1 = (f32[65,8,256]{2,1,0:T(8,128)}, f32[65,8,256]{2,1,0:T(8,128)}, u32[]{:S(2)}, u32[]{:S(2)}) collective-permute-start(f32[65,8,256]{2,1,0:T(8,128)} %pad_maximum_fusion.4), channel_id=1, source_target_pairs={{16,0},{32,16},{48,32},{64,48},{80,64},{96,80},{112,96},{17,1},{33... | collective-permute-start | bytes 1597448 | tf_op jit(solution)/shard_map/ppermute | solution.py:43
  13.9 10.5 %copy-start.2 = (bf16[16,64,256]{2,1,0:T(8,128)(2,1)S(1)}, bf16[16,64,256]{2,1,0:T(8,128)(2,1)}, u32[]{:S(2)}) copy-start(bf16[16,64,256]{2,1,0:T(8,128)(2,1)} %u_ref.1) | copy-start | bytes 1572868
  14.9 21.7 %all-to-all-start = ((f32[8,2,16,68]{3,1,0,2:T(2,128)}), f32[8,2,16,68]{3,1,0,2:T(2,128)}, u32[]{:S(2)}, u32[]{:S(2)}) async-start(f32[8,2,16,68]{3,1,0,2:T(2,128)} %copy.116), calls=%async_computation | async-start | bytes 262144 | tf_op jit(solution)/shard_map/all_to_all | solution.py:200
  24.4 4.1 %copy-start.12 = (f32[4,64,256]{2,1,0:T(8,128)S(1)}, f32[4,64,256]{2,1,0:T(8,128)}, u32[]{:S(2)}) copy-start(f32[4,64,256]{2,1,0:T(8,128)} %param.14) | copy-start | bytes 786436
  26.6 3.9 %copy-start.5 = (f32[32,64,8]{2,1,0:T(8,128)S(1)}, f32[32,64,8]{2,1,0:T(8,128)}, u32[]{:S(2)}) copy-start(f32[32,64,8]{2,1,0:T(8,128)} %get-tuple-element.81) | copy-start | bytes 196612
  26.8 3.7 %copy-start.8 = (f32[16,64,8]{2,1,0:T(8,128)S(1)}, f32[16,64,8]{2,1,0:T(8,128)}, u32[]{:S(2)}) copy-start(f32[16,64,8]{2,1,0:T(8,128)} %get-tuple-element.89) | copy-start | bytes 98308
  26.8 3.7 %copy-start.9 = (f32[16,64,8]{2,1,0:T(8,128)S(1)}, f32[16,64,8]{2,1,0:T(8,128)}, u32[]{:S(2)}) copy-start(f32[16,64,8]{2,1,0:T(8,128)} %get-tuple-element.90) | copy-start | bytes 98308
  33.8 10.9 %copy-start.23 = (f32[65]{0:T(128)S(1)}, f32[65]{0:T(128)}, u32[]{:S(2)}) copy-start(f32[65]{0:T(128)} %constant.76.clone.1) | copy-start | bytes 784
  37.5 17.7 %collective-permute-start.5 = (f32[8,2,68]{2,0,1:T(8,128)S(1)}, f32[8,2,68]{2,0,1:T(8,128)S(1)}, u32[]{:S(2)}, u32[]{:S(2)}) collective-permute-start(f32[8,2,68]{2,0,1:T(8,128)S(1)} %get-tuple-element.101), channel_id=1, source_target_pairs={{0,16},{16,32},{32,48},{48,64},{64,80},{80,96},{96,112},{1,17},{17... | collective-permute-start | bytes 13064 | tf_op jit(solution)/shard_map/ppermute | solution.py:202
  41.5 13.7 %collective-permute-start.6 = (f32[8,2,68]{2,0,1:T(8,128)S(1)}, f32[8,2,68]{2,0,1:T(8,128)S(1)}, u32[]{:S(2)}, u32[]{:S(2)}) collective-permute-start(f32[8,2,68]{2,0,1:T(8,128)S(1)} %get-tuple-element.102), channel_id=1, source_target_pairs={{16,0},{32,16},{48,32},{64,48},{80,64},{96,80},{112,96},{17,1},{33... | collective-permute-start | bytes 13064 | tf_op jit(solution)/shard_map/ppermute | solution.py:203
  45.9 3.8 %copy-start.4 = (f32[65,8,256]{2,1,0:T(8,128)}, f32[65,8,256]{2,1,0:T(8,128)S(1)}, u32[]{:S(2)}) copy-start(f32[65,8,256]{2,1,0:T(8,128)S(1)} %multiply_select_fusion.hn_ref) | copy-start | bytes 1597444
  46.0 7.5 %copy-start.14 = (pred[1280,68]{0,1:T(8,128)(4,1)S(1)}, pred[1280,68]{0,1:T(8,128)(4,1)}, u32[]{:S(2)}) copy-start(pred[1280,68]{0,1:T(8,128)(4,1)} %iota_compare_fusion.1) | copy-start | bytes 261124
  46.0 7.7 %copy-start.19 = (pred[4,64,256]{2,1,0:T(8,128)(4,1)S(1)}, pred[4,64,256]{2,1,0:T(8,128)(4,1)}, u32[]{:S(2)}) copy-start(pred[4,64,256]{2,1,0:T(8,128)(4,1)} %get-tuple-element.68) | copy-start | bytes 196612
  47.7 9.8 %collective-permute-start.4 = (f32[65,80,8]{1,2,0:T(8,128)S(1)}, f32[65,80,8]{1,2,0:T(8,128)S(1)}, u32[]{:S(2)}, u32[]{:S(2)}) collective-permute-start(f32[65,80,8]{1,2,0:T(8,128)S(1)} %pad_maximum_fusion.6), channel_id=1, source_target_pairs={{0,1},{1,2},{2,3},{3,4},{4,5},{5,6},{6,7},{7,8},{8,9},{9,10},{10,1... | collective-permute-start | bytes 499208 | tf_op jit(solution)/shard_map/ppermute | solution.py:59
  49.8 8.1 %collective-permute-start.3 = (f32[65,80,8]{1,2,0:T(8,128)S(1)}, f32[65,80,8]{1,2,0:T(8,128)S(1)}, u32[]{:S(2)}, u32[]{:S(2)}) collective-permute-start(f32[65,80,8]{1,2,0:T(8,128)S(1)} %pad_maximum_fusion.5), channel_id=1, source_target_pairs={{1,0},{2,1},{3,2},{4,3},{5,4},{6,5},{7,6},{8,7},{9,8},{10,9},{11,1... | collective-permute-start | bytes 499208 | tf_op jit(solution)/shard_map/ppermute | solution.py:60
  59.6 8.2 %copy-start.1 = (f32[25,64,256]{2,1,0:T(8,128)S(1)}, f32[25,64,256]{2,1,0:T(8,128)}, u32[]{:S(2)}) copy-start(f32[25,64,256]{2,1,0:T(8,128)} %select_reduce_fusion) | copy-start | bytes 4915204
  59.7 8.2 %copy-start.7 = (s32[4,64,256]{2,1,0:T(8,128)S(1)}, s32[4,64,256]{2,1,0:T(8,128)}, u32[]{:S(2)}) copy-start(s32[4,64,256]{2,1,0:T(8,128)} %param.13) | copy-start | bytes 786436
  67.9 7.6 %copy-start.22 = (f32[2,8]{1,0:T(2,128)S(1)}, f32[2,8]{1,0:T(2,128)}, u32[]{:S(2)}) copy-start(f32[2,8]{1,0:T(2,128)} %param.15) | copy-start | bytes 196
  75.4 10.9 %copy-start.17 = (f32[65,80,8]{1,2,0:T(8,128)S(1)}, f32[65,80,8]{1,2,0:T(8,128)}, u32[]{:S(2)}) copy-start(f32[65,80,8]{1,2,0:T(8,128)} %copy-done.16) | copy-start | bytes 499204
  76.7 12.0 %copy-start.11 = (f32[2,64,256]{2,1,0:T(8,128)}, f32[2,64,256]{2,1,0:T(8,128)S(1)}, u32[]{:S(2)}) copy-start(f32[2,64,256]{2,1,0:T(8,128)S(1)} %multiply_reduce_fusion.1.f_ref) | copy-start | bytes 393220
  76.7 12.0 %collective-permute-start.7 = (f32[2,8,256]{2,1,0:T(8,128)S(1)}, f32[2,8,256]{2,1,0:T(8,128)S(1)}, u32[]{:S(2)}, u32[]{:S(2)}) collective-permute-start(f32[2,8,256]{2,1,0:T(8,128)S(1)} %get-tuple-element.100), channel_id=1, source_target_pairs={{120,112},{119,113},{118,114},{117,115},{116,116},{115,117},{114,1... | collective-permute-start | bytes 49160 | tf_op jit(solution)/shard_map/ppermute | solution.py:45
  77.4 11.5 %collective-permute-start.8 = (f32[2,8,256]{2,1,0:T(8,128)S(1)}, f32[2,8,256]{2,1,0:T(8,128)S(1)}, u32[]{:S(2)}, u32[]{:S(2)}) collective-permute-start(f32[2,8,256]{2,1,0:T(8,128)S(1)} %get-tuple-element.99), channel_id=1, source_target_pairs={{16,0},{32,16},{48,32},{64,48},{80,64},{96,80},{112,96},{17,1},{33... | collective-permute-start | bytes 49160 | tf_op jit(solution)/shard_map/ppermute | solution.py:43
  79.4 9.6 %collective-permute-start.9 = (f32[2,8,256]{2,1,0:T(8,128)S(1)}, f32[2,8,256]{2,1,0:T(8,128)S(1)}, u32[]{:S(2)}, u32[]{:S(2)}) collective-permute-start(f32[2,8,256]{2,1,0:T(8,128)S(1)} %get-tuple-element.100), channel_id=1, source_target_pairs={{0,16},{16,32},{32,48},{48,64},{64,80},{80,96},{96,112},{1,17},{17... | collective-permute-start | bytes 49160 | tf_op jit(solution)/shard_map/ppermute | solution.py:42
  88.9 9.8 %copy-start.20 = (f32[2,8,256]{2,1,0:T(8,128)}, f32[2,8,256]{2,1,0:T(8,128)S(1)}, u32[]{:S(2)}) copy-start(f32[2,8,256]{2,1,0:T(8,128)S(1)} %broadcast_select_fusion.fn_ref) | copy-start | bytes 49156
  89.0 9.7 %copy-start.21 = (f32[2,8,256]{2,1,0:T(8,128)}, f32[2,8,256]{2,1,0:T(8,128)S(1)}, u32[]{:S(2)}) copy-start(f32[2,8,256]{2,1,0:T(8,128)S(1)} %collective-permute-done.9.fs_ref) | copy-start | bytes 49156
  89.1 9.6 %collective-permute-start.10 = (f32[2,80,8]{2,1,0:T(8,128)S(1)}, f32[2,80,8]{2,1,0:T(8,128)S(1)}, u32[]{:S(2)}, u32[]{:S(2)}) collective-permute-start(f32[2,80,8]{2,1,0:T(8,128)S(1)} %pad_maximum_fusion.9), channel_id=1, source_target_pairs={{1,0},{2,1},{3,2},{4,3},{5,4},{6,5},{7,6},{8,7},{9,8},{10,9},{11,1... | collective-permute-start | bytes 15368 | tf_op jit(solution)/shard_map/ppermute | solution.py:60
  94.3 6.9 %collective-permute-start.11 = (f32[2,80,8]{2,1,0:T(8,128)S(1)}, f32[2,80,8]{2,1,0:T(8,128)S(1)}, u32[]{:S(2)}, u32[]{:S(2)}) collective-permute-start(f32[2,80,8]{2,1,0:T(8,128)S(1)} %pad_maximum_fusion.10), channel_id=1, source_target_pairs={{0,1},{1,2},{2,3},{3,4},{4,5},{5,6},{6,7},{7,8},{8,9},{9,10},{10,1... | collective-permute-start | bytes 15368 | tf_op jit(solution)/shard_map/ppermute | solution.py:59
  (5 other events, 11.1 us)

commit v10 on v9

--- a/solution.py
+++ b/solution.py
@@ -210,17 +210,13 @@
     base_r = jnp.arange(orows, dtype=jnp.int32) * (arows - 2 * H - 1) // (orows - 1) + H
     base_c = jnp.arange(ocols, dtype=jnp.int32) * (acols - 2 * H - 1) // (ocols - 1) + H
     offs = jnp.arange(2 * H + 1, dtype=jnp.int32) - H
-    pick_r = (
-        (base_r[None, :, None] + offs[:, None, None])
-        == jnp.arange(arows, dtype=jnp.int32)[None, None, :]
-    ).astype(jnp.float32).reshape(-1, arows)
     pick_c = (
         jnp.arange(acols, dtype=jnp.int32)[:, None, None]
         == (base_c[None, None, :] + offs[None, :, None])
     ).astype(jnp.float32).reshape(acols, -1)
-    lifted = jnp.einsum("pa,fab->fpb", pick_r, padded, precision=HIGH)
-    window = jnp.einsum("fpb,bq->fpq", lifted, pick_c, precision=HIGH)
-    window = window.reshape(nf, 2 * H + 1, orows, 2 * H + 1, ocols)
+    lifted = jnp.einsum("fab,bq->faq", padded, pick_c, precision=HIGH)
+    lifted = lifted.reshape(nf, arows, 2 * H + 1, ocols)
+    window = lifted[:, base_r[None, :] + offs[:, None]]
     row_of = remap_index // acols - base_r[None, :, None] + H
     col_of = remap_index % acols - base_c[None, None, :] + H
     inside = (row_of >= 0) & (row_of <= 2 * H) & (col_of >= 0) & (col_of <= 2 * H)

time: 132 us -> 129 us (0.977)
  matrix products: 8.77 us -> 0.79 us
  local copies, waits for them, and re-layouts: 20.3 us -> 27.6 us
  other arithmetic: 25.6 us -> 23.2 us
    dot_general x2 -> x1, matrix products: 8.77 us -> 0.79 us  [remap(): lifted = jnp.einsum('fab,bq->faq', padded, pick_c, precision=HIGH)]
    gather x0 -> x1, local copies, waits for them, and re-layouts: none -> 6.04 us  [remap(): window = lifted[:, base_r[None, :] + offs[:, None]]]
    another operation x0 -> x2, local copies, waits for them, and re-layouts: none -> 2.9 us
  transfers between devices with their start and end apart: 13 -> 13, of which waited for: 3 -> 3; matrix products, arithmetic and copies ran while one was open for 24% -> 23% of each run, Pallas kernels for 0% -> 0%
where the time goes in v10:
time: 129 us; the launch traced here: 128 us
  starting transfers between devices  39.9 us (31%)
  Pallas kernels  29.3 us (23%)
  local copies, waits for them, and re-layouts  27.6 us (21%)
  other arithmetic  23.2 us (18%)
  waiting for transfers between devices  5.75 us (4%)
  between operations  1.77 us (1%)
    pallas_call x1, Pallas kernels, evolve(): pl.pallas_call(stencil_kernel, out_shape=jax.ShapeDtypeStruct(tracers.sha...  29.3 us
    ppermute x2, starting transfers between devices, exchange(): south = lax.ppermute(tops, 'oy', [(i, i + 1) for i in range(rows_n - 1)])  9.61 us
    ppermute x2, starting transfers between devices, exchange(): lax.ppermute(wests, 'ox', [((i + 1) % cols_n, i) for i in range(cols_n)])  8.83 us
    all_to_all x1, starting transfers between devices, atmosphere_block(): got = lax.all_to_all(pieces, 'ox', split_axis=2, concat_axis=1, tiled=True)  7.82 us
    reduce_sum x1, other arithmetic, remap(): fast = jnp.sum(window * wsum.transpose(0, 2, 1, 3)[None], axis=(1, 3))  6.49 us
    gather x1, local copies, waits for them, and re-layouts, remap(): window = lifted[:, base_r[None, :] + offs[:, None]]  6.04 us
    ppermute x2, waiting for transfers between devices, exchange(): lax.ppermute(easts, 'ox', [(i, (i + 1) % cols_n) for i in range(cols_n)])  5.33 us
    concatenate x2, other arithmetic, lane_tile(): return jnp.concatenate([from_e, gap, from_w], axis=-1)  4.71 us
  transfers between devices with their start and end apart: 13, of which 3 were waited for; matrix products, arithmetic and copies ran while one was open for 23% of the time, Pallas kernels for 0%

profile of v10, /device:TPU:1, one launch (start us, length us, event | category | flops | bytes accessed | tf_op | source)
XLA Modules:
  0.0 128.5 jit_solution(5234708925188332731)
XLA Ops:
  0.6 1.1 fusion.20
  1.8 1.0 convert_bitcast_fusion
  2.8 1.0 fusion.25
  4.6 1.5 %collective-permute-start = (f32[65,8,256]{2,1,0:T(8,128)}, f32[65,8,256]{2,1,0:T(8,128)}, u32[]{:S(2)}, u32[]{:S(2)}) collective-permute-start(f32[65,8,256]{2,1,0:T(8,128)} %pad_maximum_fusion.3), channel_id=1, source_target_pairs={{120,112},{119,113},{118,114},{117,115},{116,116},{115,117},{114,1... | collective-permute-start | bytes 1597448 | tf_op jit(solution)/shard_map/ppermute | solution.py:45
  6.0 4.5 %collective-permute-start.2 = (f32[65,8,256]{2,1,0:T(8,128)}, f32[65,8,256]{2,1,0:T(8,128)}, u32[]{:S(2)}, u32[]{:S(2)}) collective-permute-start(f32[65,8,256]{2,1,0:T(8,128)} %pad_maximum_fusion.3), channel_id=1, source_target_pairs={{0,16},{16,32},{32,48},{48,64},{64,80},{80,96},{96,112},{1,17},{17... | collective-permute-start | bytes 1597448 | tf_op jit(solution)/shard_map/ppermute | solution.py:42
  11.4 1.9 %collective-permute-start.1 = (f32[65,8,256]{2,1,0:T(8,128)}, f32[65,8,256]{2,1,0:T(8,128)}, u32[]{:S(2)}, u32[]{:S(2)}) collective-permute-start(f32[65,8,256]{2,1,0:T(8,128)} %pad_maximum_fusion.4), channel_id=1, source_target_pairs={{16,0},{32,16},{48,32},{64,48},{80,64},{96,80},{112,96},{17,1},{33... | collective-permute-start | bytes 1597448 | tf_op jit(solution)/shard_map/ppermute | solution.py:43
  14.8 7.8 %all-to-all-start = ((f32[8,2,16,68]{3,1,0,2:T(2,128)}), f32[8,2,16,68]{3,1,0,2:T(2,128)}, u32[]{:S(2)}, u32[]{:S(2)}) async-start(f32[8,2,16,68]{3,1,0,2:T(2,128)} %copy.132), calls=%async_computation | async-start | bytes 262144 | tf_op jit(solution)/shard_map/all_to_all | solution.py:200
  22.7 1.7 %fusion.19 = (f32[32,64,8]{2,1,0:T(8,128)}, f32[32,64,8]{2,1,0:T(8,128)}) fusion(f32[32,64,256]{2,1,0:T(8,128)S(1)} %bitcast.95), kind=kLoop, calls=%fused_computation.77 | loop fusion | bytes 262144 | tf_op jit(solution)/shard_map/slice | solution.py:52
  24.4 1.1 fusion.23
  26.5 4.0 %pad_maximum_fusion.1 = (f32[65,64,8]{2,1,0:T(8,128)S(1)}, f32[65,64,8]{2,1,0:T(8,128)}) fusion(f32[1,64,8]{2,1,0:T(8,128)S(1)} %get-tuple-element.170, f32[16,64,8]{2,1,0:T(8,128)} %get-tuple-element.158, f32[16,64,8]{2,1,0:T(8,128)} %get-tuple-element.156, f32[32,64,8]{2,1,0:T(8,128)} %get-tuple-element.148, f32[1,64,8]{2,1,0:T(8,128)S(1)} %get-tuple-element.169, ...), kind=kLoop, calls=%fused_computation.38 | loop fusion | flops 199680 | bytes 532480 | tf_op jit(solution)/shard_map/concatenate | solution.py:56
  30.5 2.2 %copy.127 = f32[65,64,8]{1,2,0:T(8,128)S(1)} copy(f32[65,64,8]{2,1,0:T(8,128)} %get-tuple-element.180) | data formatting | bytes 266240 | tf_op jit(solution)/shard_map/concatenate | solution.py:52
  33.8 1.9 %select_reduce_fusion = f32[25,64,256]{2,1,0:T(8,128)} fusion(f32[4,64,256]{2,1,0:T(8,128)S(1)} %copy-done.7, s32[4,64,256]{2,1,0:T(8,128)S(1)} %get-tuple-element.133), kind=kLoop, calls=%fused_computation.35 | loop fusion | flops 4505600 | bytes 2162688 | tf_op jit(solution)/shard_map/reduce_sum | solution.py:225
  36.6 3.9 %collective-permute-start.5 = (f32[8,2,68]{2,0,1:T(8,128)S(1)}, f32[8,2,68]{2,0,1:T(8,128)S(1)}, u32[]{:S(2)}, u32[]{:S(2)}) collective-permute-start(f32[8,2,68]{2,0,1:T(8,128)S(1)} %get-tuple-element.167), channel_id=1, source_target_pairs={{0,16},{16,32},{32,48},{48,64},{64,80},{80,96},{96,112},{1,17},{17... | collective-permute-start | bytes 13064 | tf_op jit(solution)/shard_map/ppermute | solution.py:202
  40.6 1.9 %collective-permute-start.6 = (f32[8,2,68]{2,0,1:T(8,128)S(1)}, f32[8,2,68]{2,0,1:T(8,128)S(1)}, u32[]{:S(2)}, u32[]{:S(2)}) collective-permute-start(f32[8,2,68]{2,0,1:T(8,128)S(1)} %get-tuple-element.168), channel_id=1, source_target_pairs={{16,0},{32,16},{48,32},{64,48},{80,64},{96,80},{112,96},{17,1},{33... | collective-permute-start | bytes 13064 | tf_op jit(solution)/shard_map/ppermute | solution.py:203
  42.5 1.2 rev.6
  43.8 1.2 multiply_select_fusion.hn_ref
  45.3 1.2 fusion.22
  46.8 1.7 %collective-permute-start.4 = (f32[65,80,8]{1,2,0:T(8,128)S(1)}, f32[65,80,8]{1,2,0:T(8,128)S(1)}, u32[]{:S(2)}, u32[]{:S(2)}) collective-permute-start(f32[65,80,8]{1,2,0:T(8,128)S(1)} %pad_maximum_fusion.6), channel_id=1, source_target_pairs={{0,1},{1,2},{2,3},{3,4},{4,5},{5,6},{6,7},{7,8},{8,9},{9,10},{10,1... | collective-permute-start | bytes 499208 | tf_op jit(solution)/shard_map/ppermute | solution.py:59
  48.9 3.4 %collective-permute-start.3 = (f32[65,80,8]{1,2,0:T(8,128)S(1)}, f32[65,80,8]{1,2,0:T(8,128)S(1)}, u32[]{:S(2)}, u32[]{:S(2)}) collective-permute-start(f32[65,80,8]{1,2,0:T(8,128)S(1)} %pad_maximum_fusion.5), channel_id=1, source_target_pairs={{1,0},{2,1},{3,2},{4,3},{5,4},{6,5},{7,6},{8,7},{9,8},{10,9},{11,1... | collective-permute-start | bytes 499208 | tf_op jit(solution)/shard_map/ppermute | solution.py:60
  53.9 2.7 %collective-permute-done.4 = f32[65,80,8]{1,2,0:T(8,128)S(1)} collective-permute-done((f32[65,80,8]{1,2,0:T(8,128)S(1)}, f32[65,80,8]{1,2,0:T(8,128)S(1)}, u32[]{:S(2)}, u32[]{:S(2)}) %collective-permute-start.4) | collective-permute-done | bytes 166432 | tf_op jit(solution)/shard_map/ppermute | solution.py:59
  57.8 16.0 %conditional.1 = (f32[8,64,256]{2,1,0:T(8,128)S(1)}) conditional(s32[]{:T(128)} %convert_element_type.13, (s32[64]{0:T(128)S(1)}, s32[5]{0:T(128)S(1)}, f32[8,36,5,256]{3,1,2,0:T(8,128)S(1)}, f32[5,64,5,256]{3,1,2,0:T(8,128)}) %tuple.77, (f32[4,64,256]{2,1,0:T(8,128)}, f32[8,36,68]{2,0,1:T(8,128)S(1)}, s32[4,64,256]{2,1,0:T(8,128)S(1)}) %tuple.78), branch_computations={%region_2.4_spmd, %region_4.6_spmd} | conditional | flops 6424832 | bytes 48769564 | solution.py:240
  58.5 6.0 %gather_fusion = f32[320,8,5,256]{3,1,2,0:T(8,128)} fusion(f32[8,36,5,256]{3,0,2,1:T(8,128)S(1)} %copy.135, s32[1024]{0:T(1024)S(1)} %pad_clamp_fusion), kind=kCustom, calls=%fused_computation | custom fusion | bytes 26215680 | tf_op jit(solution)/shard_map/gather | solution.py:219
  64.5 2.4 %copy.136 = f32[5,64,5,256]{3,2,1,0:T(8,128)S(1)} copy(f32[5,64,5,256]{3,1,2,0:T(8,128)} %get-tuple-element.126) | data formatting | bytes 3276800 | tf_op jit(solution)/shard_map
  67.0 6.5 %multiply_reduce_fusion = f32[64,8,256]{2,1,0:T(8,128)S(1)} fusion(f32[5,64,8,5,256]{4,2,3,1,0:T(8,128)} %bitcast.93, f32[5,64,5,256]{3,2,1,0:T(8,128)S(1)} %copy.136), kind=kLoop, calls=%fused_computation.5 | loop fusion | flops 6422528 | bytes 15269888 | tf_op jit(solution)/shard_map/reduce_sum | solution.py:229
  74.8 1.9 %collective-permute-start.8 = (f32[2,8,256]{2,1,0:T(8,128)S(1)}, f32[2,8,256]{2,1,0:T(8,128)S(1)}, u32[]{:S(2)}, u32[]{:S(2)}) collective-permute-start(f32[2,8,256]{2,1,0:T(8,128)S(1)} %get-tuple-element.165), channel_id=1, source_target_pairs={{16,0},{32,16},{48,32},{64,48},{80,64},{96,80},{112,96},{17,1},{33... | collective-permute-start | bytes 49160 | tf_op jit(solution)/shard_map/ppermute | solution.py:43
  76.9 5.1 %collective-permute-start.9 = (f32[2,8,256]{2,1,0:T(8,128)S(1)}, f32[2,8,256]{2,1,0:T(8,128)S(1)}, u32[]{:S(2)}, u32[]{:S(2)}) collective-permute-start(f32[2,8,256]{2,1,0:T(8,128)S(1)} %get-tuple-element.166), channel_id=1, source_target_pairs={{0,16},{16,32},{32,48},{48,64},{64,80},{80,96},{96,112},{1,17},{17... | collective-permute-start | bytes 49160 | tf_op jit(solution)/shard_map/ppermute | solution.py:42
  82.0 1.7 %copy.139 = f32[65,80,8]{2,1,0:T(8,128)S(1)} copy(f32[65,80,8]{1,2,0:T(8,128)} %copy-done.12) | data formatting | bytes 332800 | tf_op jit(solution)/shard_map/optimization_barrier | solution.py:256
  83.7 2.3 %copy.140 = f32[65,80,8]{2,1,0:T(8,128)} copy(f32[65,80,8]{1,2,0:T(8,128)S(1)} %copy-done.11) | data formatting | bytes 332800 | tf_op jit(solution)/shard_map/optimization_barrier | solution.py:256
  86.4 5.4 %collective-permute-start.10 = (f32[2,80,8]{2,1,0:T(8,128)S(1)}, f32[2,80,8]{2,1,0:T(8,128)S(1)}, u32[]{:S(2)}, u32[]{:S(2)}) collective-permute-start(f32[2,80,8]{2,1,0:T(8,128)S(1)} %pad_maximum_fusion.9), channel_id=1, source_target_pairs={{1,0},{2,1},{3,2},{4,3},{5,4},{6,5},{7,6},{8,7},{9,8},{10,9},{11,1... | collective-permute-start | bytes 15368 | tf_op jit(solution)/shard_map/ppermute | solution.py:60
  91.9 4.0 %pad_maximum_fusion.hc_ref = f32[65,80,128]{2,1,0:T(8,128)} fusion(f32[65,80,8]{2,1,0:T(8,128)} %copy.140, f32[65,80,8]{2,1,0:T(8,128)S(1)} %copy.139, f32[128]{0:T(128)S(1)} %pad.10.clone), kind=kLoop, calls=%fused_computation.37 | loop fusion | flops 1331200 | bytes 2995712 | tf_op jit(solution)/shard_map/concatenate | solution.py:67
  95.9 2.6 %collective-permute-done.11 = f32[2,80,8]{2,1,0:T(8,128)S(1)} collective-permute-done((f32[2,80,8]{2,1,0:T(8,128)S(1)}, f32[2,80,8]{2,1,0:T(8,128)S(1)}, u32[]{:S(2)}, u32[]{:S(2)}) %collective-permute-start.11) | collective-permute-done | bytes 5152 | tf_op jit(solution)/shard_map/ppermute | solution.py:59
  99.2 29.3 %shard_map.95 = f32[2,16,64,256]{3,2,1,0:T(8,128)} custom-call(f32[2,16,64,256]{3,2,1,0:T(8,128)} %tr_ref.1, bf16[16,64,256]{2,1,0:T(8,128)(2,1)} %u_ref.1, bf16[16,64,256]{2,1,0:T(8,128)(2,1)} %v_ref.1, s32[64,256]{1,0:T(8,128)} %m_ref.1, f32[2,64,256]{2,1,0:T(8,128)} %copy-done.6, f32[65,8,256]{2,1,0:T(8,128)} %copy-done.3, ...), custom_call_target="tpu_custom_call" | custom-call | tf_op jit(solution)/shard_map/pallas_call | solution.py:171
  (97 shorter events, 12.2 us)
Async XLA Ops:
  0.6 12.7 %copy-start.9 = (f32[8,2,1024]{2,1,0:T(2,128)S(1)}, f32[8,2,1024]{2,1,0:T(2,128)}, u32[]{:S(2)}) copy-start(f32[8,2,1024]{2,1,0:T(2,128)} %param.12) | copy-start | bytes 196612
  0.6 12.9 %slice-start = ((f32[8,2,1024]{2,1,0:T(2,128)}), f32[8,2,62]{2,1,0:T(2,128)S(1)}, s32[]{:S(2)}) async-start(f32[8,2,1024]{2,1,0:T(2,128)} %param.12), calls=%async_computation.1 | async-start | bytes 16384 | tf_op jit(solution)/shard_map/jit(_roll_static)/slice | solution.py:198
  1.8 20.9 %copy-start = (f32[2,16,64,256]{3,2,1,0:T(8,128)S(1)}, f32[2,16,64,256]{3,2,1,0:T(8,128)}, u32[]{:S(2)}) copy-start(f32[2,16,64,256]{3,2,1,0:T(8,128)} %tr_ref.1) | copy-start | bytes 6291460
  4.6 37.9 %collective-permute-start = (f32[65,8,256]{2,1,0:T(8,128)}, f32[65,8,256]{2,1,0:T(8,128)}, u32[]{:S(2)}, u32[]{:S(2)}) collective-permute-start(f32[65,8,256]{2,1,0:T(8,128)} %pad_maximum_fusion.3), channel_id=1, source_target_pairs={{120,112},{119,113},{118,114},{117,115},{116,116},{115,117},{114,1... | collective-permute-start | bytes 1597448 | tf_op jit(solution)/shard_map/ppermute | solution.py:45
  6.0 39.2 %collective-permute-start.2 = (f32[65,8,256]{2,1,0:T(8,128)}, f32[65,8,256]{2,1,0:T(8,128)}, u32[]{:S(2)}, u32[]{:S(2)}) collective-permute-start(f32[65,8,256]{2,1,0:T(8,128)} %pad_maximum_fusion.3), channel_id=1, source_target_pairs={{0,16},{16,32},{32,48},{48,64},{64,80},{80,96},{96,112},{1,17},{17... | collective-permute-start | bytes 1597448 | tf_op jit(solution)/shard_map/ppermute | solution.py:42
  11.4 32.4 %collective-permute-start.1 = (f32[65,8,256]{2,1,0:T(8,128)}, f32[65,8,256]{2,1,0:T(8,128)}, u32[]{:S(2)}, u32[]{:S(2)}) collective-permute-start(f32[65,8,256]{2,1,0:T(8,128)} %pad_maximum_fusion.4), channel_id=1, source_target_pairs={{16,0},{32,16},{48,32},{64,48},{80,64},{96,80},{112,96},{17,1},{33... | collective-permute-start | bytes 1597448 | tf_op jit(solution)/shard_map/ppermute | solution.py:43
  14.0 10.5 %copy-start.1 = (bf16[16,64,256]{2,1,0:T(8,128)(2,1)S(1)}, bf16[16,64,256]{2,1,0:T(8,128)(2,1)}, u32[]{:S(2)}) copy-start(bf16[16,64,256]{2,1,0:T(8,128)(2,1)} %u_ref.1) | copy-start | bytes 1572868
  14.8 20.9 %all-to-all-start = ((f32[8,2,16,68]{3,1,0,2:T(2,128)}), f32[8,2,16,68]{3,1,0,2:T(2,128)}, u32[]{:S(2)}, u32[]{:S(2)}) async-start(f32[8,2,16,68]{3,1,0,2:T(2,128)} %copy.132), calls=%async_computation | async-start | bytes 262144 | tf_op jit(solution)/shard_map/all_to_all | solution.py:200
  22.7 2.9 %copy-start.2 = (bf16[16,64,256]{2,1,0:T(8,128)(2,1)S(1)}, bf16[16,64,256]{2,1,0:T(8,128)(2,1)}, u32[]{:S(2)}) copy-start(bf16[16,64,256]{2,1,0:T(8,128)(2,1)} %v_ref.1) | copy-start | bytes 1572868
  30.5 2.9 %copy-start.4 = (s32[4,64,256]{2,1,0:T(8,128)S(1)}, s32[4,64,256]{2,1,0:T(8,128)}, u32[]{:S(2)}) copy-start(s32[4,64,256]{2,1,0:T(8,128)} %param.13) | copy-start | bytes 786436
  30.5 3.3 %copy-start.7 = (f32[4,64,256]{2,1,0:T(8,128)S(1)}, f32[4,64,256]{2,1,0:T(8,128)}, u32[]{:S(2)}) copy-start(f32[4,64,256]{2,1,0:T(8,128)} %param.14) | copy-start | bytes 786436
  32.8 11.0 %copy-start.16 = (f32[65]{0:T(128)S(1)}, f32[65]{0:T(128)}, u32[]{:S(2)}) copy-start(f32[65]{0:T(128)} %constant.83.clone.1) | copy-start | bytes 784
  36.6 17.2 %collective-permute-start.5 = (f32[8,2,68]{2,0,1:T(8,128)S(1)}, f32[8,2,68]{2,0,1:T(8,128)S(1)}, u32[]{:S(2)}, u32[]{:S(2)}) collective-permute-start(f32[8,2,68]{2,0,1:T(8,128)S(1)} %get-tuple-element.167), channel_id=1, source_target_pairs={{0,16},{16,32},{32,48},{48,64},{64,80},{80,96},{96,112},{1,17},{17... | collective-permute-start | bytes 13064 | tf_op jit(solution)/shard_map/ppermute | solution.py:202
  40.6 13.3 %collective-permute-start.6 = (f32[8,2,68]{2,0,1:T(8,128)S(1)}, f32[8,2,68]{2,0,1:T(8,128)S(1)}, u32[]{:S(2)}, u32[]{:S(2)}) collective-permute-start(f32[8,2,68]{2,0,1:T(8,128)S(1)} %get-tuple-element.168), channel_id=1, source_target_pairs={{16,0},{32,16},{48,32},{64,48},{80,64},{96,80},{112,96},{17,1},{33... | collective-permute-start | bytes 13064 | tf_op jit(solution)/shard_map/ppermute | solution.py:203
  45.0 3.7 %copy-start.3 = (f32[65,8,256]{2,1,0:T(8,128)}, f32[65,8,256]{2,1,0:T(8,128)S(1)}, u32[]{:S(2)}) copy-start(f32[65,8,256]{2,1,0:T(8,128)S(1)} %multiply_select_fusion.hn_ref) | copy-start | bytes 1597444
  46.8 9.8 %collective-permute-start.4 = (f32[65,80,8]{1,2,0:T(8,128)S(1)}, f32[65,80,8]{1,2,0:T(8,128)S(1)}, u32[]{:S(2)}, u32[]{:S(2)}) collective-permute-start(f32[65,80,8]{1,2,0:T(8,128)S(1)} %pad_maximum_fusion.6), channel_id=1, source_target_pairs={{0,1},{1,2},{2,3},{3,4},{4,5},{5,6},{6,7},{7,8},{8,9},{9,10},{10,1... | collective-permute-start | bytes 499208 | tf_op jit(solution)/shard_map/ppermute | solution.py:59
  48.9 8.1 %collective-permute-start.3 = (f32[65,80,8]{1,2,0:T(8,128)S(1)}, f32[65,80,8]{1,2,0:T(8,128)S(1)}, u32[]{:S(2)}, u32[]{:S(2)}) collective-permute-start(f32[65,80,8]{1,2,0:T(8,128)S(1)} %pad_maximum_fusion.5), channel_id=1, source_target_pairs={{1,0},{2,1},{3,2},{4,3},{5,4},{6,5},{7,6},{8,7},{9,8},{10,9},{11,1... | collective-permute-start | bytes 499208 | tf_op jit(solution)/shard_map/ppermute | solution.py:60
  56.6 1.2 copy-start.10
  57.0 0.8 copy-start.12
  57.8 16.1 %copy-start.15 = (f32[2,8]{1,0:T(2,128)S(1)}, f32[2,8]{1,0:T(2,128)}, u32[]{:S(2)}) copy-start(f32[2,8]{1,0:T(2,128)} %param.15) | copy-start | bytes 196
  73.8 3.0 %copy-start.5 = (f32[8,64,256]{2,1,0:T(8,128)}, f32[8,64,256]{2,1,0:T(8,128)S(1)}, u32[]{:S(2)}) copy-start(f32[8,64,256]{2,1,0:T(8,128)S(1)} %get-tuple-element.132) | copy-start | bytes 1572868
  73.8 9.9 %copy-start.11 = (f32[65,80,8]{1,2,0:T(8,128)S(1)}, f32[65,80,8]{1,2,0:T(8,128)}, u32[]{:S(2)}) copy-start(f32[65,80,8]{1,2,0:T(8,128)} %copy-done.10) | copy-start | bytes 499204
  74.0 12.0 %copy-start.6 = (f32[2,64,256]{2,1,0:T(8,128)}, f32[2,64,256]{2,1,0:T(8,128)S(1)}, u32[]{:S(2)}) copy-start(f32[2,64,256]{2,1,0:T(8,128)S(1)} %multiply_reduce_fusion.1.f_ref) | copy-start | bytes 393220
  74.0 12.0 %collective-permute-start.7 = (f32[2,8,256]{2,1,0:T(8,128)S(1)}, f32[2,8,256]{2,1,0:T(8,128)S(1)}, u32[]{:S(2)}, u32[]{:S(2)}) collective-permute-start(f32[2,8,256]{2,1,0:T(8,128)S(1)} %get-tuple-element.166), channel_id=1, source_target_pairs={{120,112},{119,113},{118,114},{117,115},{116,116},{115,117},{114,1... | collective-permute-start | bytes 49160 | tf_op jit(solution)/shard_map/ppermute | solution.py:45
  74.8 11.3 %collective-permute-start.8 = (f32[2,8,256]{2,1,0:T(8,128)S(1)}, f32[2,8,256]{2,1,0:T(8,128)S(1)}, u32[]{:S(2)}, u32[]{:S(2)}) collective-permute-start(f32[2,8,256]{2,1,0:T(8,128)S(1)} %get-tuple-element.165), channel_id=1, source_target_pairs={{16,0},{32,16},{48,32},{64,48},{80,64},{96,80},{112,96},{17,1},{33... | collective-permute-start | bytes 49160 | tf_op jit(solution)/shard_map/ppermute | solution.py:43
  76.9 9.4 %collective-permute-start.9 = (f32[2,8,256]{2,1,0:T(8,128)S(1)}, f32[2,8,256]{2,1,0:T(8,128)S(1)}, u32[]{:S(2)}, u32[]{:S(2)}) collective-permute-start(f32[2,8,256]{2,1,0:T(8,128)S(1)} %get-tuple-element.166), channel_id=1, source_target_pairs={{0,16},{16,32},{32,48},{48,64},{64,80},{80,96},{96,112},{1,17},{17... | collective-permute-start | bytes 49160 | tf_op jit(solution)/shard_map/ppermute | solution.py:42
  86.2 9.7 %copy-start.13 = (f32[2,8,256]{2,1,0:T(8,128)}, f32[2,8,256]{2,1,0:T(8,128)S(1)}, u32[]{:S(2)}) copy-start(f32[2,8,256]{2,1,0:T(8,128)S(1)} %broadcast_select_fusion.fn_ref) | copy-start | bytes 49156
  86.3 9.6 %copy-start.14 = (f32[2,8,256]{2,1,0:T(8,128)}, f32[2,8,256]{2,1,0:T(8,128)S(1)}, u32[]{:S(2)}) copy-start(f32[2,8,256]{2,1,0:T(8,128)S(1)} %collective-permute-done.9.fs_ref) | copy-start | bytes 49156
  86.4 9.5 %collective-permute-start.10 = (f32[2,80,8]{2,1,0:T(8,128)S(1)}, f32[2,80,8]{2,1,0:T(8,128)S(1)}, u32[]{:S(2)}, u32[]{:S(2)}) collective-permute-start(f32[2,80,8]{2,1,0:T(8,128)S(1)} %pad_maximum_fusion.9), channel_id=1, source_target_pairs={{1,0},{2,1},{3,2},{4,3},{5,4},{6,5},{7,6},{8,7},{9,8},{10,9},{11,1... | collective-permute-start | bytes 15368 | tf_op jit(solution)/shard_map/ppermute | solution.py:60
  91.8 6.7 %collective-permute-start.11 = (f32[2,80,8]{2,1,0:T(8,128)S(1)}, f32[2,80,8]{2,1,0:T(8,128)S(1)}, u32[]{:S(2)}, u32[]{:S(2)}) collective-permute-start(f32[2,80,8]{2,1,0:T(8,128)S(1)} %pad_maximum_fusion.10), channel_id=1, source_target_pairs={{0,1},{1,2},{2,3},{3,4},{4,5},{5,6},{6,7},{7,8},{8,9},{9,10},{10,1... | collective-permute-start | bytes 15368 | tf_op jit(solution)/shard_map/ppermute | solution.py:59

commit v11 on v10

--- a/solution.py
+++ b/solution.py
@@ -113,7 +113,7 @@
         ce[k] = mask * (0.08 - um)
         cs[k] = mask * (vp + 0.08)
         cn[k] = mask * (0.08 - vm)
-        cc[k] = mask * ((um - up) + (vm - vp) - 0.48)
+        cc[k] = 1.0 + mask * ((um - up) + (vm - vp) - 0.48)
         return carry
 
     lax.fori_loop(0, nk, coef, 0)
@@ -142,11 +142,11 @@
                 east = pltpu.roll(cur, lanes - 1, 1)
                 up = cur if above is None else buf[src, t * nk + above, at, :]
                 down = cur if below is None else buf[src, t * nk + below, at, :]
-                tend = c_w * west + c_e * east + c_s * south + c_n * north + c_c * cur
-                tend = tend + c_8 * (up + down)
+                new = c_w * west + c_e * east + c_s * south + c_n * north + c_c * cur
+                new = new + c_8 * (up + down)
                 if forced:
-                    tend = tend + mf[t, at, :]
-                buf[dst, p, at, :] = cur + tend
+                    new = new + mf[t, at, :]
+                buf[dst, p, at, :] = new
 
     def step(i, carry):
         for src in (0, 1):
@@ -220,13 +220,12 @@
     row_of = remap_index // acols - base_r[None, :, None] + H
     col_of = remap_index % acols - base_c[None, None, :] + H
     inside = (row_of >= 0) & (row_of <= 2 * H) & (col_of >= 0) & (col_of <= 2 * H)
-    slot = jnp.where(inside, row_of * (2 * H + 1) + col_of, -1)
-    slots = jnp.arange((2 * H + 1) ** 2, dtype=jnp.int32)
-    wsum = jnp.sum(
-        jnp.where(slot[:, None] == slots[None, :, None, None], remap_weight[:, None], 0.0),
-        axis=0,
-    ).reshape(2 * H + 1, 2 * H + 1, orows, ocols)
-    fast = jnp.sum(window * wsum.transpose(0, 2, 1, 3)[None], axis=(1, 3))
+    ar = jnp.arange(2 * H + 1, dtype=jnp.int32)
+    hit = (row_of[:, None, :, None, :] == ar[None, :, None, None, None]) & (
+        col_of[:, None, :, None, :] == ar[None, None, None, :, None]
+    )
+    wsum = jnp.sum(jnp.where(hit, remap_weight[:, None, :, None, :], 0.0), axis=0)
+    fast = jnp.sum(window * wsum[None], axis=(1, 3))
     missed = jnp.logical_not(jnp.all(inside))
 
     def general():

time: 129 us -> 132 us (1.023)
  other arithmetic: 23.2 us -> 25.4 us
    another operation x2 -> x1, local copies, waits for them, and re-layouts: 2.9 us -> 0.48 us
    and x0 -> x2, other arithmetic: none -> 1.72 us  [remap(): (row_of[:, None, :, None, :] == ar[None, :, None, None, None]) & (col_of[...]
  transfers between devices with their start and end apart: 13 -> 13, of which waited for: 3 -> 3; matrix products, arithmetic and copies ran while one was open for 23% -> 22% of each run, Pallas kernels for 0% -> 0%
where the time goes in v11:
time: 132 us
  starting transfers between devices  40.1 us (30%)
  Pallas kernels  29.5 us (22%)
  local copies, waits for them, and re-layouts  27.8 us (21%)
  other arithmetic  25.4 us (19%)
  waiting for transfers between devices  5.83 us (4%)
  between operations  1.85 us (1%)
    pallas_call x1, Pallas kernels, evolve(): pl.pallas_call(stencil_kernel, out_shape=jax.ShapeDtypeStruct(tracers.sha...  29.5 us
    ppermute x2, starting transfers between devices, exchange(): south = lax.ppermute(tops, 'oy', [(i, i + 1) for i in range(rows_n - 1)])  9.63 us
    ppermute x2, starting transfers between devices, exchange(): lax.ppermute(wests, 'ox', [((i + 1) % cols_n, i) for i in range(cols_n)])  8.86 us
    all_to_all x1, starting transfers between devices, atmosphere_block(): got = lax.all_to_all(pieces, 'ox', split_axis=2, concat_axis=1, tiled=True)  7.77 us
    reduce_sum x1, other arithmetic, remap(): fast = jnp.sum(window * wsum[None], axis=(1, 3))  6.49 us
    gather x1, local copies, waits for them, and re-layouts, remap(): window = lifted[:, base_r[None, :] + offs[:, None]]  6.06 us
    ppermute x2, waiting for transfers between devices, exchange(): lax.ppermute(easts, 'ox', [(i, (i + 1) % cols_n) for i in range(cols_n)])  5.37 us
    concatenate x2, other arithmetic, lane_tile(): return jnp.concatenate([from_e, gap, from_w], axis=-1)  4.73 us
  transfers between devices with their start and end apart: 13, of which 3 were waited for; matrix products, arithmetic and copies ran while one was open for 22% of the time, Pallas kernels for 0%

profile of v11, /device:TPU:1, one launch (start us, length us, event | category | flops | bytes accessed | tf_op | source)
XLA Modules:
  0.0 131.5 jit_solution(10053954659440343602)
XLA Ops:
  0.6 1.1 fusion.22
  4.6 1.5 %collective-permute-start = (f32[65,8,256]{2,1,0:T(8,128)}, f32[65,8,256]{2,1,0:T(8,128)}, u32[]{:S(2)}, u32[]{:S(2)}) collective-permute-start(f32[65,8,256]{2,1,0:T(8,128)} %pad_maximum_fusion.3), channel_id=1, source_target_pairs={{120,112},{119,113},{118,114},{117,115},{116,116},{115,117},{114,1... | collective-permute-start | bytes 1597448 | tf_op jit(solution)/shard_map/ppermute | solution.py:45
  6.0 4.5 %collective-permute-start.2 = (f32[65,8,256]{2,1,0:T(8,128)}, f32[65,8,256]{2,1,0:T(8,128)}, u32[]{:S(2)}, u32[]{:S(2)}) collective-permute-start(f32[65,8,256]{2,1,0:T(8,128)} %pad_maximum_fusion.3), channel_id=1, source_target_pairs={{0,16},{16,32},{32,48},{48,64},{64,80},{80,96},{96,112},{1,17},{17... | collective-permute-start | bytes 1597448 | tf_op jit(solution)/shard_map/ppermute | solution.py:42
  11.4 1.9 %collective-permute-start.1 = (f32[65,8,256]{2,1,0:T(8,128)}, f32[65,8,256]{2,1,0:T(8,128)}, u32[]{:S(2)}, u32[]{:S(2)}) collective-permute-start(f32[65,8,256]{2,1,0:T(8,128)} %pad_maximum_fusion.4), channel_id=1, source_target_pairs={{16,0},{32,16},{48,32},{64,48},{80,64},{96,80},{112,96},{17,1},{33... | collective-permute-start | bytes 1597448 | tf_op jit(solution)/shard_map/ppermute | solution.py:43
  14.9 7.8 %all-to-all-start = ((f32[8,2,16,68]{3,1,0,2:T(2,128)}), f32[8,2,16,68]{3,1,0,2:T(2,128)S(1)}, u32[]{:S(2)}, u32[]{:S(2)}) async-start(f32[8,2,16,68]{3,1,0,2:T(2,128)} %copy.130), calls=%async_computation | async-start | bytes 262144 | tf_op jit(solution)/shard_map/all_to_all | solution.py:200
  22.7 1.7 %fusion.21 = (f32[32,64,8]{2,1,0:T(8,128)}, f32[32,64,8]{2,1,0:T(8,128)}) fusion(f32[32,64,256]{2,1,0:T(8,128)S(1)} %bitcast.96), kind=kLoop, calls=%fused_computation.77 | loop fusion | bytes 262144 | tf_op jit(solution)/shard_map/slice | solution.py:52
  24.4 1.1 fusion.25
  26.5 4.0 %pad_maximum_fusion.1 = (f32[65,64,8]{2,1,0:T(8,128)S(1)}, f32[65,64,8]{2,1,0:T(8,128)}) fusion(f32[1,64,8]{2,1,0:T(8,128)S(1)} %get-tuple-element.243, f32[16,64,8]{2,1,0:T(8,128)} %get-tuple-element.231, f32[16,64,8]{2,1,0:T(8,128)} %get-tuple-element.229, f32[32,64,8]{2,1,0:T(8,128)} %get-tuple-element.221, f32[1,64,8]{2,1,0:T(8,128)S(1)} %get-tuple-element.242, ...), kind=kLoop, calls=%fused_computation.39 | loop fusion | flops 199680 | bytes 532480 | tf_op jit(solution)/shard_map/concatenate | solution.py:56
  30.5 3.0 %copy.125 = f32[65,64,8]{1,2,0:T(8,128)} copy(f32[65,64,8]{2,1,0:T(8,128)} %get-tuple-element.253) | data formatting | bytes 266240 | tf_op jit(solution)/shard_map/concatenate | solution.py:52
  34.0 1.7 %and_reduce_fusion = (pred[]{:T(512)}, s32[4,64,256]{2,1,0:T(8,128)}, s32[4,64,256]{2,1,0:T(8,128)}) fusion(s32[64]{0:T(128)S(1)} %fusion.18, s32[4,64,256]{2,1,0:T(8,128)S(1)} %copy-done.4, s32[256]{0:T(256)S(1)} %fusion.17), kind=kLoop, calls=%fused_computation.58 | loop fusion | flops 1572863 | bytes 787713 | tf_op jit(solution)/shard_map/reduce_and | solution.py:229
  35.8 3.9 %collective-permute-start.5 = (f32[8,2,68]{2,0,1:T(8,128)S(1)}, f32[8,2,68]{2,0,1:T(8,128)S(1)}, u32[]{:S(2)}, u32[]{:S(2)}) collective-permute-start(f32[8,2,68]{2,0,1:T(8,128)S(1)} %get-tuple-element.240), channel_id=1, source_target_pairs={{0,16},{16,32},{32,48},{48,64},{64,80},{80,96},{96,112},{1,17},{17... | collective-permute-start | bytes 13064 | tf_op jit(solution)/shard_map/ppermute | solution.py:202
  39.7 1.9 %collective-permute-start.6 = (f32[8,2,68]{2,0,1:T(8,128)S(1)}, f32[8,2,68]{2,0,1:T(8,128)S(1)}, u32[]{:S(2)}, u32[]{:S(2)}) collective-permute-start(f32[8,2,68]{2,0,1:T(8,128)S(1)} %get-tuple-element.241), channel_id=1, source_target_pairs={{16,0},{32,16},{48,32},{64,48},{80,64},{96,80},{112,96},{17,1},{33... | collective-permute-start | bytes 13064 | tf_op jit(solution)/shard_map/ppermute | solution.py:203
  41.6 1.2 rev.6
  42.9 1.2 multiply_select_fusion.hn_ref
  44.5 1.2 fusion.24
  46.0 1.7 %collective-permute-start.4 = (f32[65,80,8]{1,2,0:T(8,128)S(1)}, f32[65,80,8]{1,2,0:T(8,128)S(1)}, u32[]{:S(2)}, u32[]{:S(2)}) collective-permute-start(f32[65,80,8]{1,2,0:T(8,128)S(1)} %pad_maximum_fusion.6), channel_id=1, source_target_pairs={{0,1},{1,2},{2,3},{3,4},{4,5},{5,6},{6,7},{7,8},{8,9},{9,10},{10,1... | collective-permute-start | bytes 499208 | tf_op jit(solution)/shard_map/ppermute | solution.py:59
  48.2 3.4 %collective-permute-start.3 = (f32[65,80,8]{1,2,0:T(8,128)S(1)}, f32[65,80,8]{1,2,0:T(8,128)S(1)}, u32[]{:S(2)}, u32[]{:S(2)}) collective-permute-start(f32[65,80,8]{1,2,0:T(8,128)S(1)} %pad_maximum_fusion.5), channel_id=1, source_target_pairs={{1,0},{2,1},{3,2},{4,3},{5,4},{6,5},{7,6},{8,7},{9,8},{10,9},{11,1... | collective-permute-start | bytes 499208 | tf_op jit(solution)/shard_map/ppermute | solution.py:60
  53.0 2.8 %collective-permute-done.4 = f32[65,80,8]{1,2,0:T(8,128)S(1)} collective-permute-done((f32[65,80,8]{1,2,0:T(8,128)S(1)}, f32[65,80,8]{1,2,0:T(8,128)S(1)}, u32[]{:S(2)}, u32[]{:S(2)}) %collective-permute-start.4) | collective-permute-done | bytes 166432 | tf_op jit(solution)/shard_map/ppermute | solution.py:59
  57.2 1.2 eq.63
  58.4 17.3 %conditional.1 = (f32[8,64,256]{2,1,0:T(8,128)S(1)}) conditional(s32[]{:T(128)} %convert_element_type.13, (s32[64]{0:T(128)S(1)}, s32[5]{0:T(128)S(1)}, f32[8,36,5,256]{3,1,2,0:T(8,128)S(1)}, s32[4,64,256]{2,1,0:T(8,128)}, s32[4,5,64,1,256]{4,2,1,0,3:T(8,128)S(1)}, /*index=5*/s32[4,64,256]{2,1,0:T(8,128)}, s32[4,1,64,5,256]{4,2,3,0,1:T(8,128)}, ...), branch_computations={%region_1.4_spmd, %region_4.6_spmd} | conditional | flops 11585792 | bytes 56175160 | solution.py:239
  59.2 6.1 %gather_fusion = f32[320,8,5,256]{3,1,2,0:T(8,128)} fusion(f32[8,36,5,256]{3,0,2,1:T(8,128)S(1)} %copy.133, s32[1024]{0:T(1024)S(1)} %pad_clamp_fusion), kind=kCustom, calls=%fused_computation | custom fusion | bytes 26215680 | tf_op jit(solution)/shard_map/gather | solution.py:219
  65.3 1.5 %compare_bitcast_fusion = pred[4,64,5,256]{3,1,2,0:T(8,128)(4,1)S(1)} fusion(s32[4,1,64,5,256]{4,2,3,0,1:T(8,128)} %get-tuple-element.112, s32[4,64,256]{2,1,0:T(8,128)} %get-tuple-element.111), kind=kLoop, calls=%fused_computation.7 | loop fusion | flops 327680 | bytes 1900544 | tf_op jit(solution)/shard_map/and | solution.py:224
  68.0 1.0 copy.116
  69.0 6.5 %multiply_reduce_fusion = f32[64,8,256]{2,1,0:T(8,128)S(1)} fusion(f32[5,64,8,5,256]{4,2,3,1,0:T(8,128)} %bitcast.94, f32[5,64,5,256]{3,2,1,0:T(8,128)S(1)} %copy.116), kind=kLoop, calls=%fused_computation.5 | loop fusion | flops 6422528 | bytes 15269888 | tf_op jit(solution)/shard_map/reduce_sum | solution.py:228
  77.4 1.9 %collective-permute-start.8 = (f32[2,8,256]{2,1,0:T(8,128)S(1)}, f32[2,8,256]{2,1,0:T(8,128)S(1)}, u32[]{:S(2)}, u32[]{:S(2)}) collective-permute-start(f32[2,8,256]{2,1,0:T(8,128)S(1)} %get-tuple-element.238), channel_id=1, source_target_pairs={{16,0},{32,16},{48,32},{64,48},{80,64},{96,80},{112,96},{17,1},{33... | collective-permute-start | bytes 49160 | tf_op jit(solution)/shard_map/ppermute | solution.py:43
  79.4 5.1 %collective-permute-start.9 = (f32[2,8,256]{2,1,0:T(8,128)S(1)}, f32[2,8,256]{2,1,0:T(8,128)S(1)}, u32[]{:S(2)}, u32[]{:S(2)}) collective-permute-start(f32[2,8,256]{2,1,0:T(8,128)S(1)} %get-tuple-element.239), channel_id=1, source_target_pairs={{0,16},{16,32},{32,48},{48,64},{64,80},{80,96},{96,112},{1,17},{17... | collective-permute-start | bytes 49160 | tf_op jit(solution)/shard_map/ppermute | solution.py:42
  84.5 1.7 %copy.136 = f32[65,80,8]{2,1,0:T(8,128)S(1)} copy(f32[65,80,8]{1,2,0:T(8,128)} %copy-done.14) | data formatting | bytes 332800 | tf_op jit(solution)/shard_map/optimization_barrier | solution.py:255
  86.3 2.3 %copy.137 = f32[65,80,8]{2,1,0:T(8,128)} copy(f32[65,80,8]{1,2,0:T(8,128)S(1)} %copy-done.13) | data formatting | bytes 332800 | tf_op jit(solution)/shard_map/optimization_barrier | solution.py:255
  88.9 5.5 %collective-permute-start.10 = (f32[2,80,8]{2,1,0:T(8,128)S(1)}, f32[2,80,8]{2,1,0:T(8,128)S(1)}, u32[]{:S(2)}, u32[]{:S(2)}) collective-permute-start(f32[2,80,8]{2,1,0:T(8,128)S(1)} %pad_maximum_fusion.9), channel_id=1, source_target_pairs={{1,0},{2,1},{3,2},{4,3},{5,4},{6,5},{7,6},{8,7},{9,8},{10,9},{11,1... | collective-permute-start | bytes 15368 | tf_op jit(solution)/shard_map/ppermute | solution.py:60
  94.7 4.0 %pad_maximum_fusion.hc_ref = f32[65,80,128]{2,1,0:T(8,128)} fusion(f32[65,80,8]{2,1,0:T(8,128)} %copy.137, f32[65,80,8]{2,1,0:T(8,128)S(1)} %copy.136, f32[128]{0:T(128)S(1)} %copy-done.19), kind=kLoop, calls=%fused_computation.38 | loop fusion | flops 1331200 | bytes 2995712 | tf_op jit(solution)/shard_map/concatenate | solution.py:67
  98.7 2.6 %collective-permute-done.11 = f32[2,80,8]{2,1,0:T(8,128)S(1)} collective-permute-done((f32[2,80,8]{2,1,0:T(8,128)S(1)}, f32[2,80,8]{2,1,0:T(8,128)S(1)}, u32[]{:S(2)}, u32[]{:S(2)}) %collective-permute-start.11) | collective-permute-done | bytes 5152 | tf_op jit(solution)/shard_map/ppermute | solution.py:59
  102.0 29.5 %shard_map.95 = f32[2,16,64,256]{3,2,1,0:T(8,128)} custom-call(f32[2,16,64,256]{3,2,1,0:T(8,128)} %tr_ref.1, bf16[16,64,256]{2,1,0:T(8,128)(2,1)} %u_ref.1, bf16[16,64,256]{2,1,0:T(8,128)(2,1)} %v_ref.1, s32[64,256]{1,0:T(8,128)} %m_ref.1, f32[2,64,256]{2,1,0:T(8,128)} %copy-done.7, f32[65,8,256]{2,1,0:T(8,128)} %copy-done.3, ...), custom_call_target="tpu_custom_call" | custom-call | tf_op jit(solution)/shard_map/pallas_call | solution.py:171
  (118 shorter events, 15.0 us)
Async XLA Ops:
  0.6 12.7 %copy-start.11 = (f32[8,2,1024]{2,1,0:T(2,128)S(1)}, f32[8,2,1024]{2,1,0:T(2,128)}, u32[]{:S(2)}) copy-start(f32[8,2,1024]{2,1,0:T(2,128)} %param.12) | copy-start | bytes 196612
  0.6 12.9 %slice-start = ((f32[8,2,1024]{2,1,0:T(2,128)}), f32[8,2,62]{2,1,0:T(2,128)S(1)}, s32[]{:S(2)}) async-start(f32[8,2,1024]{2,1,0:T(2,128)} %param.12), calls=%async_computation.1 | async-start | bytes 16384 | tf_op jit(solution)/shard_map/jit(_roll_static)/slice | solution.py:198
  1.8 20.9 %copy-start = (f32[2,16,64,256]{3,2,1,0:T(8,128)S(1)}, f32[2,16,64,256]{3,2,1,0:T(8,128)}, u32[]{:S(2)}) copy-start(f32[2,16,64,256]{3,2,1,0:T(8,128)} %tr_ref.1) | copy-start | bytes 6291460
  4.6 37.1 %collective-permute-start = (f32[65,8,256]{2,1,0:T(8,128)}, f32[65,8,256]{2,1,0:T(8,128)}, u32[]{:S(2)}, u32[]{:S(2)}) collective-permute-start(f32[65,8,256]{2,1,0:T(8,128)} %pad_maximum_fusion.3), channel_id=1, source_target_pairs={{120,112},{119,113},{118,114},{117,115},{116,116},{115,117},{114,1... | collective-permute-start | bytes 1597448 | tf_op jit(solution)/shard_map/ppermute | solution.py:45
  6.0 38.4 %collective-permute-start.2 = (f32[65,8,256]{2,1,0:T(8,128)}, f32[65,8,256]{2,1,0:T(8,128)}, u32[]{:S(2)}, u32[]{:S(2)}) collective-permute-start(f32[65,8,256]{2,1,0:T(8,128)} %pad_maximum_fusion.3), channel_id=1, source_target_pairs={{0,16},{16,32},{32,48},{48,64},{64,80},{80,96},{96,112},{1,17},{17... | collective-permute-start | bytes 1597448 | tf_op jit(solution)/shard_map/ppermute | solution.py:42
  11.4 31.5 %collective-permute-start.1 = (f32[65,8,256]{2,1,0:T(8,128)}, f32[65,8,256]{2,1,0:T(8,128)}, u32[]{:S(2)}, u32[]{:S(2)}) collective-permute-start(f32[65,8,256]{2,1,0:T(8,128)} %pad_maximum_fusion.4), channel_id=1, source_target_pairs={{16,0},{32,16},{48,32},{64,48},{80,64},{96,80},{112,96},{17,1},{33... | collective-permute-start | bytes 1597448 | tf_op jit(solution)/shard_map/ppermute | solution.py:43
  14.0 10.4 %copy-start.1 = (bf16[16,64,256]{2,1,0:T(8,128)(2,1)S(1)}, bf16[16,64,256]{2,1,0:T(8,128)(2,1)}, u32[]{:S(2)}) copy-start(bf16[16,64,256]{2,1,0:T(8,128)(2,1)} %u_ref.1) | copy-start | bytes 1572868
  14.9 20.9 %all-to-all-start = ((f32[8,2,16,68]{3,1,0,2:T(2,128)}), f32[8,2,16,68]{3,1,0,2:T(2,128)S(1)}, u32[]{:S(2)}, u32[]{:S(2)}) async-start(f32[8,2,16,68]{3,1,0,2:T(2,128)} %copy.130), calls=%async_computation | async-start | bytes 262144 | tf_op jit(solution)/shard_map/all_to_all | solution.py:200
  26.4 7.6 %copy-start.17 = (s32[256]{0:T(256)}, s32[256]{0:T(256)S(1)}, u32[]{:S(2)}) copy-start(s32[256]{0:T(256)S(1)} %fusion.17) | copy-start | bytes 3076
  26.5 7.6 %copy-start.20 = (s32[64]{0:T(128)}, s32[64]{0:T(128)S(1)}, u32[]{:S(2)}) copy-start(s32[64]{0:T(128)S(1)} %fusion.18) | copy-start | bytes 772
  33.4 9.5 %copy-start.24 = (f32[65]{0:T(128)S(1)}, f32[65]{0:T(128)}, u32[]{:S(2)}) copy-start(f32[65]{0:T(128)} %constant.81.clone.1) | copy-start | bytes 784
  35.7 15.9 %copy-start.22 = (s32[5]{0:T(128)}, s32[5]{0:T(128)S(1)}, u32[]{:S(2)}) copy-start(s32[5]{0:T(128)S(1)} %iota_add_fusion) | copy-start | bytes 64
  35.8 17.2 %collective-permute-start.5 = (f32[8,2,68]{2,0,1:T(8,128)S(1)}, f32[8,2,68]{2,0,1:T(8,128)S(1)}, u32[]{:S(2)}, u32[]{:S(2)}) collective-permute-start(f32[8,2,68]{2,0,1:T(8,128)S(1)} %get-tuple-element.240), channel_id=1, source_target_pairs={{0,16},{16,32},{32,48},{48,64},{64,80},{80,96},{96,112},{1,17},{17... | collective-permute-start | bytes 13064 | tf_op jit(solution)/shard_map/ppermute | solution.py:202
  39.7 13.3 %collective-permute-start.6 = (f32[8,2,68]{2,0,1:T(8,128)S(1)}, f32[8,2,68]{2,0,1:T(8,128)S(1)}, u32[]{:S(2)}, u32[]{:S(2)}) collective-permute-start(f32[8,2,68]{2,0,1:T(8,128)S(1)} %get-tuple-element.241), channel_id=1, source_target_pairs={{16,0},{32,16},{48,32},{64,48},{80,64},{96,80},{112,96},{17,1},{33... | collective-permute-start | bytes 13064 | tf_op jit(solution)/shard_map/ppermute | solution.py:203
  44.3 7.3 %copy-start.18 = (s32[256]{0:T(256)S(1)}, s32[256]{0:T(256)}, u32[]{:S(2)}) copy-start(s32[256]{0:T(256)} %copy-done.17) | copy-start | bytes 3076
  46.0 9.8 %collective-permute-start.4 = (f32[65,80,8]{1,2,0:T(8,128)S(1)}, f32[65,80,8]{1,2,0:T(8,128)S(1)}, u32[]{:S(2)}, u32[]{:S(2)}) collective-permute-start(f32[65,80,8]{1,2,0:T(8,128)S(1)} %pad_maximum_fusion.6), channel_id=1, source_target_pairs={{0,1},{1,2},{2,3},{3,4},{4,5},{5,6},{6,7},{7,8},{8,9},{9,10},{10,1... | collective-permute-start | bytes 499208 | tf_op jit(solution)/shard_map/ppermute | solution.py:59
  48.2 10.2 %copy-start.5 = (s32[4,64,256]{2,1,0:T(8,128)S(1)}, s32[4,64,256]{2,1,0:T(8,128)}, u32[]{:S(2)}) copy-start(s32[4,64,256]{2,1,0:T(8,128)} %param.13) | copy-start | bytes 786436
  48.2 10.2 %copy-start.9 = (f32[4,64,256]{2,1,0:T(8,128)S(1)}, f32[4,64,256]{2,1,0:T(8,128)}, u32[]{:S(2)}) copy-start(f32[4,64,256]{2,1,0:T(8,128)} %param.14) | copy-start | bytes 786436
  48.2 10.2 %copy-start.21 = (s32[64]{0:T(128)S(1)}, s32[64]{0:T(128)}, u32[]{:S(2)}) copy-start(s32[64]{0:T(128)} %copy-done.20) | copy-start | bytes 772
  48.2 8.0 %collective-permute-start.3 = (f32[65,80,8]{1,2,0:T(8,128)S(1)}, f32[65,80,8]{1,2,0:T(8,128)S(1)}, u32[]{:S(2)}, u32[]{:S(2)}) collective-permute-start(f32[65,80,8]{1,2,0:T(8,128)S(1)} %pad_maximum_fusion.5), channel_id=1, source_target_pairs={{1,0},{2,1},{3,2},{4,3},{5,4},{6,5},{7,6},{8,7},{9,8},{10,9},{11,1... | collective-permute-start | bytes 499208 | tf_op jit(solution)/shard_map/ppermute | solution.py:60
  51.7 6.7 %copy-start.23 = (s32[5]{0:T(128)S(1)}, s32[5]{0:T(128)}, u32[]{:S(2)}) copy-start(s32[5]{0:T(128)} %copy-done.22) | copy-start | bytes 64
  59.2 7.6 %copy-start.10 = (s32[4,64,256]{2,1,0:T(8,128)S(1)}, s32[4,64,256]{2,1,0:T(8,128)}, u32[]{:S(2)}) copy-start(s32[4,64,256]{2,1,0:T(8,128)} %get-tuple-element.109) | copy-start | bytes 786436 | tf_op jit(solution)/shard_map/cond
  75.7 10.5 %copy-start.13 = (f32[65,80,8]{1,2,0:T(8,128)S(1)}, f32[65,80,8]{1,2,0:T(8,128)}, u32[]{:S(2)}) copy-start(f32[65,80,8]{1,2,0:T(8,128)} %copy-done.12) | copy-start | bytes 499204
  76.7 11.9 %copy-start.7 = (f32[2,64,256]{2,1,0:T(8,128)}, f32[2,64,256]{2,1,0:T(8,128)S(1)}, u32[]{:S(2)}) copy-start(f32[2,64,256]{2,1,0:T(8,128)S(1)} %multiply_reduce_fusion.1.f_ref) | copy-start | bytes 393220
  76.7 11.9 %collective-permute-start.7 = (f32[2,8,256]{2,1,0:T(8,128)S(1)}, f32[2,8,256]{2,1,0:T(8,128)S(1)}, u32[]{:S(2)}, u32[]{:S(2)}) collective-permute-start(f32[2,8,256]{2,1,0:T(8,128)S(1)} %get-tuple-element.239), channel_id=1, source_target_pairs={{120,112},{119,113},{118,114},{117,115},{116,116},{115,117},{114,1... | collective-permute-start | bytes 49160 | tf_op jit(solution)/shard_map/ppermute | solution.py:45
  77.4 11.4 %collective-permute-start.8 = (f32[2,8,256]{2,1,0:T(8,128)S(1)}, f32[2,8,256]{2,1,0:T(8,128)S(1)}, u32[]{:S(2)}, u32[]{:S(2)}) collective-permute-start(f32[2,8,256]{2,1,0:T(8,128)S(1)} %get-tuple-element.238), channel_id=1, source_target_pairs={{16,0},{32,16},{48,32},{64,48},{80,64},{96,80},{112,96},{17,1},{33... | collective-permute-start | bytes 49160 | tf_op jit(solution)/shard_map/ppermute | solution.py:43
  79.4 15.3 %copy-start.19 = (f32[128]{0:T(128)S(1)}, f32[128]{0:T(128)}, u32[]{:S(2)}) copy-start(f32[128]{0:T(128)} %pad.10.clone) | copy-start | bytes 1540
  79.4 9.4 %collective-permute-start.9 = (f32[2,8,256]{2,1,0:T(8,128)S(1)}, f32[2,8,256]{2,1,0:T(8,128)S(1)}, u32[]{:S(2)}, u32[]{:S(2)}) collective-permute-start(f32[2,8,256]{2,1,0:T(8,128)S(1)} %get-tuple-element.239), channel_id=1, source_target_pairs={{0,16},{16,32},{32,48},{48,64},{64,80},{80,96},{96,112},{1,17},{17... | collective-permute-start | bytes 49160 | tf_op jit(solution)/shard_map/ppermute | solution.py:42
  88.7 10.0 %copy-start.15 = (f32[2,8,256]{2,1,0:T(8,128)}, f32[2,8,256]{2,1,0:T(8,128)S(1)}, u32[]{:S(2)}) copy-start(f32[2,8,256]{2,1,0:T(8,128)S(1)} %broadcast_select_fusion.fn_ref) | copy-start | bytes 49156
  88.8 9.9 %copy-start.16 = (f32[2,8,256]{2,1,0:T(8,128)}, f32[2,8,256]{2,1,0:T(8,128)S(1)}, u32[]{:S(2)}) copy-start(f32[2,8,256]{2,1,0:T(8,128)S(1)} %collective-permute-done.9.fs_ref) | copy-start | bytes 49156
  88.9 9.8 %collective-permute-start.10 = (f32[2,80,8]{2,1,0:T(8,128)S(1)}, f32[2,80,8]{2,1,0:T(8,128)S(1)}, u32[]{:S(2)}, u32[]{:S(2)}) collective-permute-start(f32[2,80,8]{2,1,0:T(8,128)S(1)} %pad_maximum_fusion.9), channel_id=1, source_target_pairs={{1,0},{2,1},{3,2},{4,3},{5,4},{6,5},{7,6},{8,7},{9,8},{10,9},{11,1... | collective-permute-start | bytes 15368 | tf_op jit(solution)/shard_map/ppermute | solution.py:60
  94.4 6.9 %collective-permute-start.11 = (f32[2,80,8]{2,1,0:T(8,128)S(1)}, f32[2,80,8]{2,1,0:T(8,128)S(1)}, u32[]{:S(2)}, u32[]{:S(2)}) collective-permute-start(f32[2,80,8]{2,1,0:T(8,128)S(1)} %pad_maximum_fusion.10), channel_id=1, source_target_pairs={{0,1},{1,2},{2,3},{3,4},{4,5},{5,6},{6,7},{7,8},{8,9},{9,10},{10,1... | collective-permute-start | bytes 15368 | tf_op jit(solution)/shard_map/ppermute | solution.py:59
  (7 other events, 18.8 us)

commit v12 on v10

--- a/solution.py
+++ b/solution.py
@@ -56,9 +56,9 @@
         [jnp.concatenate([b[..., :WIDE] for b in blocks], axis=0), north[..., :WIDE], south[..., :WIDE]],
         axis=1,
     )
-    from_w = lax.ppermute(easts, "ox", [(i, (i + 1) % cols_n) for i in range(cols_n)])
-    from_e = lax.ppermute(wests, "ox", [((i + 1) % cols_n, i) for i in range(cols_n)])
-    return north, south, (from_e, from_w)
+    from_w = lax.ppermute(easts.swapaxes(1, 2), "ox", [(i, (i + 1) % cols_n) for i in range(cols_n)])
+    from_e = lax.ppermute(wests.swapaxes(1, 2), "ox", [((i + 1) % cols_n, i) for i in range(cols_n)])
+    return north, south, (from_e.swapaxes(1, 2), from_w.swapaxes(1, 2))
 
 
 def lane_tile(sides, cols):

time: 129 us -> 129 us (level)
  starting transfers between devices: 39.9 us -> 38.2 us
    ppermute x0 -> x2, local copies, waits for them, and re-layouts: none -> 4.62 us  [the longest x1 2.34 us: exchange(): lax.ppermute(wests.swapaxes(1, 2), 'ox', [((i + 1) % cols_n, i) for i in...]
    optimization_barrier x2 -> x0, local copies, waits for them, and re-layouts: 4.03 us -> none  [on_device(): sides, forcing = lax.optimization_barrier((halo[2], forcing))]
    ppermute x4, starting transfers between devices: 10.6 us -> 8.55 us  [the longest x2 6.55 us: exchange(): lax.ppermute(wests.swapaxes(1, 2), 'ox', [((i + 1) % cols_n, i) for i in...]
where the time goes in v12:
time: 129 us; the launch traced here: 127 us
  starting transfers between devices  38.2 us (30%)
  Pallas kernels  29.3 us (23%)
  local copies, waits for them, and re-layouts  28 us (22%)
  other arithmetic  24 us (19%)
  waiting for transfers between devices  5.05 us (4%)
  between operations  1.79 us (1%)
    pallas_call x1, Pallas kernels, evolve(): pl.pallas_call(stencil_kernel, out_shape=jax.ShapeDtypeStruct(tracers.sha...  29.3 us
    ppermute x2, starting transfers between devices, exchange(): south = lax.ppermute(tops, 'oy', [(i, i + 1) for i in range(rows_n - 1)])  10 us
    all_to_all x1, starting transfers between devices, atmosphere_block(): got = lax.all_to_all(pieces, 'ox', split_axis=2, concat_axis=1, tiled=True)  7.77 us
    ppermute x2, starting transfers between devices, exchange(): lax.ppermute(wests.swapaxes(1, 2), 'ox', [((i + 1) % cols_n, i) for i in...  6.55 us
    reduce_sum x1, other arithmetic, remap(): fast = jnp.sum(window * wsum.transpose(0, 2, 1, 3)[None], axis=(1, 3))  6.49 us
    gather x1, local copies, waits for them, and re-layouts, remap(): window = lifted[:, base_r[None, :] + offs[:, None]]  6.04 us
    concatenate x2, other arithmetic, lane_tile(): return jnp.concatenate([from_e, gap, from_w], axis=-1)  5.52 us
    ppermute x2, waiting for transfers between devices, exchange(): lax.ppermute(easts.swapaxes(1, 2), 'ox', [(i, (i + 1) % cols_n) for i in...  4.45 us
  transfers between devices with their start and end apart: 13, of which 3 were waited for; matrix products, arithmetic and copies ran while one was open for 23% of the time, Pallas kernels for 0%

profile of v12, /device:TPU:1, one launch (start us, length us, event | category | flops | bytes accessed | tf_op | source)
XLA Modules:
  0.0 127.3 jit_solution(5021969092622254155)
XLA Ops:
  0.6 1.1 fusion.20
  1.8 1.0 convert_bitcast_fusion
  2.8 1.0 fusion.25
  4.6 1.5 %collective-permute-start = (f32[65,8,256]{2,1,0:T(8,128)}, f32[65,8,256]{2,1,0:T(8,128)}, u32[]{:S(2)}, u32[]{:S(2)}) collective-permute-start(f32[65,8,256]{2,1,0:T(8,128)} %pad_maximum_fusion.3), channel_id=1, source_target_pairs={{120,112},{119,113},{118,114},{117,115},{116,116},{115,117},{114,1... | collective-permute-start | bytes 1597448 | tf_op jit(solution)/shard_map/ppermute | solution.py:45
  6.0 4.5 %collective-permute-start.2 = (f32[65,8,256]{2,1,0:T(8,128)}, f32[65,8,256]{2,1,0:T(8,128)}, u32[]{:S(2)}, u32[]{:S(2)}) collective-permute-start(f32[65,8,256]{2,1,0:T(8,128)} %pad_maximum_fusion.3), channel_id=1, source_target_pairs={{0,16},{16,32},{32,48},{48,64},{64,80},{80,96},{96,112},{1,17},{17... | collective-permute-start | bytes 1597448 | tf_op jit(solution)/shard_map/ppermute | solution.py:42
  11.4 1.9 %collective-permute-start.1 = (f32[65,8,256]{2,1,0:T(8,128)}, f32[65,8,256]{2,1,0:T(8,128)}, u32[]{:S(2)}, u32[]{:S(2)}) collective-permute-start(f32[65,8,256]{2,1,0:T(8,128)} %pad_maximum_fusion.4), channel_id=1, source_target_pairs={{16,0},{32,16},{48,32},{64,48},{80,64},{96,80},{112,96},{17,1},{33... | collective-permute-start | bytes 1597448 | tf_op jit(solution)/shard_map/ppermute | solution.py:43
  14.8 7.8 %all-to-all-start = ((f32[8,2,16,68]{3,1,0,2:T(2,128)}), f32[8,2,16,68]{3,1,0,2:T(2,128)S(1)}, u32[]{:S(2)}, u32[]{:S(2)}) async-start(f32[8,2,16,68]{3,1,0,2:T(2,128)} %copy.134), calls=%async_computation | async-start | bytes 262144 | tf_op jit(solution)/shard_map/all_to_all | solution.py:200
  22.6 1.7 %fusion.19 = (f32[32,64,8]{2,1,0:T(8,128)}, f32[32,64,8]{2,1,0:T(8,128)}) fusion(f32[32,64,256]{2,1,0:T(8,128)S(1)} %bitcast.109), kind=kLoop, calls=%fused_computation.77 | loop fusion | bytes 262144 | tf_op jit(solution)/shard_map/slice | solution.py:52
  24.4 1.1 fusion.23
  26.5 4.0 %pad_maximum_fusion.1 = (f32[65,64,8]{2,1,0:T(8,128)S(1)}, f32[65,64,8]{2,1,0:T(8,128)}) fusion(f32[1,64,8]{2,1,0:T(8,128)S(1)} %get-tuple-element.170, f32[16,64,8]{2,1,0:T(8,128)} %get-tuple-element.158, f32[16,64,8]{2,1,0:T(8,128)} %get-tuple-element.156, f32[32,64,8]{2,1,0:T(8,128)} %get-tuple-element.148, f32[1,64,8]{2,1,0:T(8,128)S(1)} %get-tuple-element.169, ...), kind=kLoop, calls=%fused_computation.38 | loop fusion | flops 199680 | bytes 532480 | tf_op jit(solution)/shard_map/concatenate | solution.py:56
  30.5 3.0 %copy.128 = f32[65,64,8]{1,2,0:T(8,128)} copy(f32[65,64,8]{2,1,0:T(8,128)} %get-tuple-element.180) | data formatting | bytes 266240 | tf_op jit(solution)/shard_map/concatenate | solution.py:52
  34.4 1.9 %select_reduce_fusion = f32[25,64,256]{2,1,0:T(8,128)} fusion(f32[4,64,256]{2,1,0:T(8,128)S(1)} %copy-done.8, s32[4,64,256]{2,1,0:T(8,128)S(1)} %get-tuple-element.133), kind=kLoop, calls=%fused_computation.35 | loop fusion | flops 4505600 | bytes 2162688 | tf_op jit(solution)/shard_map/reduce_sum | solution.py:225
  36.4 3.9 %collective-permute-start.5 = (f32[8,2,68]{2,0,1:T(8,128)S(1)}, f32[8,2,68]{2,0,1:T(8,128)S(1)}, u32[]{:S(2)}, u32[]{:S(2)}) collective-permute-start(f32[8,2,68]{2,0,1:T(8,128)S(1)} %get-tuple-element.167), channel_id=1, source_target_pairs={{0,16},{16,32},{32,48},{48,64},{64,80},{80,96},{96,112},{1,17},{17... | collective-permute-start | bytes 13064 | tf_op jit(solution)/shard_map/ppermute | solution.py:202
  40.3 1.9 %collective-permute-start.6 = (f32[8,2,68]{2,0,1:T(8,128)S(1)}, f32[8,2,68]{2,0,1:T(8,128)S(1)}, u32[]{:S(2)}, u32[]{:S(2)}) collective-permute-start(f32[8,2,68]{2,0,1:T(8,128)S(1)} %get-tuple-element.168), channel_id=1, source_target_pairs={{16,0},{32,16},{48,32},{64,48},{80,64},{96,80},{112,96},{17,1},{33... | collective-permute-start | bytes 13064 | tf_op jit(solution)/shard_map/ppermute | solution.py:203
  42.3 1.2 rev.6
  43.5 1.2 multiply_select_fusion.hn_ref
  45.1 1.2 fusion.22
  46.6 1.7 %collective-permute-start.4 = (f32[65,8,80]{2,1,0:T(8,128)S(1)}, f32[65,8,80]{2,1,0:T(8,128)S(1)}, u32[]{:S(2)}, u32[]{:S(2)}) collective-permute-start(f32[65,8,80]{2,1,0:T(8,128)S(1)} %maximum_bitcast_fusion.1), channel_id=1, source_target_pairs={{0,1},{1,2},{2,3},{3,4},{4,5},{5,6},{6,7},{7,8},{8,9},{9,10},{10,1... | collective-permute-start | bytes 499208 | tf_op jit(solution)/shard_map/ppermute | solution.py:59
  48.8 3.4 %collective-permute-start.3 = (f32[65,8,80]{2,1,0:T(8,128)S(1)}, f32[65,8,80]{2,1,0:T(8,128)S(1)}, u32[]{:S(2)}, u32[]{:S(2)}) collective-permute-start(f32[65,8,80]{2,1,0:T(8,128)S(1)} %maximum_bitcast_fusion), channel_id=1, source_target_pairs={{1,0},{2,1},{3,2},{4,3},{5,4},{6,5},{7,6},{8,7},{9,8},{10,9},{11,1... | collective-permute-start | bytes 499208 | tf_op jit(solution)/shard_map/ppermute | solution.py:60
  53.7 2.7 %collective-permute-done.4 = f32[65,8,80]{2,1,0:T(8,128)S(1)} collective-permute-done((f32[65,8,80]{2,1,0:T(8,128)S(1)}, f32[65,8,80]{2,1,0:T(8,128)S(1)}, u32[]{:S(2)}, u32[]{:S(2)}) %collective-permute-start.4) | collective-permute-done | bytes 166432 | tf_op jit(solution)/shard_map/ppermute | solution.py:59
  56.4 2.3 %copy.131 = f32[65,8,80]{1,2,0:T(8,128)} copy(f32[65,8,80]{2,1,0:T(8,128)S(1)} %collective-permute-done.4) | data formatting | bytes 332800 | tf_op jit(solution)/shard_map/ppermute | solution.py:59
  58.7 2.3 %copy.127 = f32[65,8,80]{1,2,0:T(8,128)} copy(f32[65,8,80]{2,1,0:T(8,128)S(1)} %collective-permute-done.3) | data formatting | bytes 332800 | tf_op jit(solution)/shard_map/ppermute | solution.py:60
  61.9 16.0 %conditional.1 = (f32[8,64,256]{2,1,0:T(8,128)S(1)}) conditional(s32[]{:T(128)} %convert_element_type.13, (s32[64]{0:T(128)S(1)}, s32[5]{0:T(128)S(1)}, f32[8,36,5,256]{3,1,2,0:T(8,128)S(1)}, f32[5,64,5,256]{3,1,2,0:T(8,128)}) %tuple.79, (f32[4,64,256]{2,1,0:T(8,128)}, f32[8,36,68]{2,0,1:T(8,128)S(1)}, s32[4,64,256]{2,1,0:T(8,128)S(1)}) %tuple.78), branch_computations={%region_2.4_spmd, %region_4.6_spmd} | conditional | flops 6424832 | bytes 48769564 | solution.py:240
  62.7 6.0 %gather_fusion = f32[320,8,5,256]{3,1,2,0:T(8,128)} fusion(f32[8,36,5,256]{3,0,2,1:T(8,128)S(1)} %copy.137, s32[1024]{0:T(1024)S(1)} %pad_clamp_fusion), kind=kCustom, calls=%fused_computation | custom fusion | bytes 26215680 | tf_op jit(solution)/shard_map/gather | solution.py:219
  68.8 2.4 %copy.138 = f32[5,64,5,256]{3,2,1,0:T(8,128)S(1)} copy(f32[5,64,5,256]{3,1,2,0:T(8,128)} %get-tuple-element.126) | data formatting | bytes 3276800 | tf_op jit(solution)/shard_map
  71.2 6.5 %multiply_reduce_fusion = f32[64,8,256]{2,1,0:T(8,128)S(1)} fusion(f32[5,64,8,5,256]{4,2,3,1,0:T(8,128)} %bitcast.105, f32[5,64,5,256]{3,2,1,0:T(8,128)S(1)} %copy.138), kind=kLoop, calls=%fused_computation.5 | loop fusion | flops 6422528 | bytes 15269888 | tf_op jit(solution)/shard_map/reduce_sum | solution.py:229
  78.7 1.9 %collective-permute-start.8 = (f32[2,8,256]{2,1,0:T(8,128)S(1)}, f32[2,8,256]{2,1,0:T(8,128)S(1)}, u32[]{:S(2)}, u32[]{:S(2)}) collective-permute-start(f32[2,8,256]{2,1,0:T(8,128)S(1)} %get-tuple-element.165), channel_id=1, source_target_pairs={{16,0},{32,16},{48,32},{64,48},{80,64},{96,80},{112,96},{17,1},{33... | collective-permute-start | bytes 49160 | tf_op jit(solution)/shard_map/ppermute | solution.py:43
  80.7 5.5 %collective-permute-start.9 = (f32[2,8,256]{2,1,0:T(8,128)S(1)}, f32[2,8,256]{2,1,0:T(8,128)S(1)}, u32[]{:S(2)}, u32[]{:S(2)}) collective-permute-start(f32[2,8,256]{2,1,0:T(8,128)S(1)} %get-tuple-element.166), channel_id=1, source_target_pairs={{0,16},{16,32},{32,48},{48,64},{64,80},{80,96},{96,112},{1,17},{17... | collective-permute-start | bytes 49160 | tf_op jit(solution)/shard_map/ppermute | solution.py:42
  87.2 3.1 %collective-permute-start.10 = (f32[2,8,80]{1,2,0:T(8,128)S(1)}, f32[2,8,80]{1,2,0:T(8,128)S(1)}, u32[]{:S(2)}, u32[]{:S(2)}) collective-permute-start(f32[2,8,80]{1,2,0:T(8,128)S(1)} %maximum_bitcast_fusion.2), channel_id=1, source_target_pairs={{1,0},{2,1},{3,2},{4,3},{5,4},{6,5},{7,6},{8,7},{9,8},{10,9},{11,1... | collective-permute-start | bytes 15368 | tf_op jit(solution)/shard_map/ppermute | solution.py:60
  90.7 4.8 %pad_maximum_fusion.hc_ref = f32[65,80,128]{2,1,0:T(8,128)} fusion(f32[65,80,8]{2,1,0:T(8,128)} %bitcast.106, f32[65,80,8]{2,1,0:T(8,128)} %bitcast.107, f32[128]{0:T(128)S(1)} %pad.10.clone), kind=kLoop, calls=%fused_computation.37 | loop fusion | flops 1331200 | bytes 2995712 | tf_op jit(solution)/shard_map/concatenate | solution.py:67
  95.5 1.8 %collective-permute-done.11 = f32[2,8,80]{1,2,0:T(8,128)S(1)} collective-permute-done((f32[2,8,80]{1,2,0:T(8,128)S(1)}, f32[2,8,80]{1,2,0:T(8,128)S(1)}, u32[]{:S(2)}, u32[]{:S(2)}) %collective-permute-start.11) | collective-permute-done | bytes 5152 | tf_op jit(solution)/shard_map/ppermute | solution.py:59
  98.0 29.3 %shard_map.95 = f32[2,16,64,256]{3,2,1,0:T(8,128)} custom-call(f32[2,16,64,256]{3,2,1,0:T(8,128)} %tr_ref.1, bf16[16,64,256]{2,1,0:T(8,128)(2,1)} %u_ref.1, bf16[16,64,256]{2,1,0:T(8,128)(2,1)} %v_ref.1, s32[64,256]{1,0:T(8,128)} %m_ref.1, f32[2,64,256]{2,1,0:T(8,128)} %copy-done.6, f32[65,8,256]{2,1,0:T(8,128)} %copy-done.3, ...), custom_call_target="tpu_custom_call" | custom-call | tf_op jit(solution)/shard_map/pallas_call | solution.py:171
  (97 shorter events, 11.6 us)
Async XLA Ops:
  0.6 12.7 %copy-start.10 = (f32[8,2,1024]{2,1,0:T(2,128)S(1)}, f32[8,2,1024]{2,1,0:T(2,128)}, u32[]{:S(2)}) copy-start(f32[8,2,1024]{2,1,0:T(2,128)} %param.12) | copy-start | bytes 196612
  0.6 12.9 %slice-start = ((f32[8,2,1024]{2,1,0:T(2,128)}), f32[8,2,62]{2,1,0:T(2,128)S(1)}, s32[]{:S(2)}) async-start(f32[8,2,1024]{2,1,0:T(2,128)} %param.12), calls=%async_computation.1 | async-start | bytes 16384 | tf_op jit(solution)/shard_map/jit(_roll_static)/slice | solution.py:198
  1.8 20.9 %copy-start = (f32[2,16,64,256]{3,2,1,0:T(8,128)S(1)}, f32[2,16,64,256]{3,2,1,0:T(8,128)}, u32[]{:S(2)}) copy-start(f32[2,16,64,256]{3,2,1,0:T(8,128)} %tr_ref.1) | copy-start | bytes 6291460
  4.6 37.7 %collective-permute-start = (f32[65,8,256]{2,1,0:T(8,128)}, f32[65,8,256]{2,1,0:T(8,128)}, u32[]{:S(2)}, u32[]{:S(2)}) collective-permute-start(f32[65,8,256]{2,1,0:T(8,128)} %pad_maximum_fusion.3), channel_id=1, source_target_pairs={{120,112},{119,113},{118,114},{117,115},{116,116},{115,117},{114,1... | collective-permute-start | bytes 1597448 | tf_op jit(solution)/shard_map/ppermute | solution.py:45
  6.0 39.0 %collective-permute-start.2 = (f32[65,8,256]{2,1,0:T(8,128)}, f32[65,8,256]{2,1,0:T(8,128)}, u32[]{:S(2)}, u32[]{:S(2)}) collective-permute-start(f32[65,8,256]{2,1,0:T(8,128)} %pad_maximum_fusion.3), channel_id=1, source_target_pairs={{0,16},{16,32},{32,48},{48,64},{64,80},{80,96},{96,112},{1,17},{17... | collective-permute-start | bytes 1597448 | tf_op jit(solution)/shard_map/ppermute | solution.py:42
  11.4 32.1 %collective-permute-start.1 = (f32[65,8,256]{2,1,0:T(8,128)}, f32[65,8,256]{2,1,0:T(8,128)}, u32[]{:S(2)}, u32[]{:S(2)}) collective-permute-start(f32[65,8,256]{2,1,0:T(8,128)} %pad_maximum_fusion.4), channel_id=1, source_target_pairs={{16,0},{32,16},{48,32},{64,48},{80,64},{96,80},{112,96},{17,1},{33... | collective-permute-start | bytes 1597448 | tf_op jit(solution)/shard_map/ppermute | solution.py:43
  14.0 10.4 %copy-start.1 = (bf16[16,64,256]{2,1,0:T(8,128)(2,1)S(1)}, bf16[16,64,256]{2,1,0:T(8,128)(2,1)}, u32[]{:S(2)}) copy-start(bf16[16,64,256]{2,1,0:T(8,128)(2,1)} %u_ref.1) | copy-start | bytes 1572868
  14.8 21.5 %all-to-all-start = ((f32[8,2,16,68]{3,1,0,2:T(2,128)}), f32[8,2,16,68]{3,1,0,2:T(2,128)S(1)}, u32[]{:S(2)}, u32[]{:S(2)}) async-start(f32[8,2,16,68]{3,1,0,2:T(2,128)} %copy.134), calls=%async_computation | async-start | bytes 262144 | tf_op jit(solution)/shard_map/all_to_all | solution.py:200
  22.6 2.9 %copy-start.2 = (bf16[16,64,256]{2,1,0:T(8,128)(2,1)S(1)}, bf16[16,64,256]{2,1,0:T(8,128)(2,1)}, u32[]{:S(2)}) copy-start(bf16[16,64,256]{2,1,0:T(8,128)(2,1)} %v_ref.1) | copy-start | bytes 1572868
  26.4 7.6 %copy-start.13 = (s32[64]{0:T(128)}, s32[64]{0:T(128)S(1)}, u32[]{:S(2)}) copy-start(s32[64]{0:T(128)S(1)} %fusion.18) | copy-start | bytes 772
  30.5 3.6 %copy-start.4 = (s32[4,64,256]{2,1,0:T(8,128)S(1)}, s32[4,64,256]{2,1,0:T(8,128)}, u32[]{:S(2)}) copy-start(s32[4,64,256]{2,1,0:T(8,128)} %param.13) | copy-start | bytes 786436
  30.5 4.0 %copy-start.8 = (f32[4,64,256]{2,1,0:T(8,128)S(1)}, f32[4,64,256]{2,1,0:T(8,128)}, u32[]{:S(2)}) copy-start(f32[4,64,256]{2,1,0:T(8,128)} %param.14) | copy-start | bytes 786436
  34.0 9.5 %copy-start.16 = (f32[65]{0:T(128)S(1)}, f32[65]{0:T(128)}, u32[]{:S(2)}) copy-start(f32[65]{0:T(128)} %constant.83.clone.1) | copy-start | bytes 784
  36.4 17.3 %collective-permute-start.5 = (f32[8,2,68]{2,0,1:T(8,128)S(1)}, f32[8,2,68]{2,0,1:T(8,128)S(1)}, u32[]{:S(2)}, u32[]{:S(2)}) collective-permute-start(f32[8,2,68]{2,0,1:T(8,128)S(1)} %get-tuple-element.167), channel_id=1, source_target_pairs={{0,16},{16,32},{32,48},{48,64},{64,80},{80,96},{96,112},{1,17},{17... | collective-permute-start | bytes 13064 | tf_op jit(solution)/shard_map/ppermute | solution.py:202
  40.3 13.4 %collective-permute-start.6 = (f32[8,2,68]{2,0,1:T(8,128)S(1)}, f32[8,2,68]{2,0,1:T(8,128)S(1)}, u32[]{:S(2)}, u32[]{:S(2)}) collective-permute-start(f32[8,2,68]{2,0,1:T(8,128)S(1)} %get-tuple-element.168), channel_id=1, source_target_pairs={{16,0},{32,16},{48,32},{64,48},{80,64},{96,80},{112,96},{17,1},{33... | collective-permute-start | bytes 13064 | tf_op jit(solution)/shard_map/ppermute | solution.py:203
  43.5 2.9 %copy-start.7 = (f32[65,64,8]{1,2,0:T(8,128)S(1)}, f32[65,64,8]{1,2,0:T(8,128)}, u32[]{:S(2)}) copy-start(f32[65,64,8]{1,2,0:T(8,128)} %copy.128) | copy-start | bytes 399364
  44.8 3.8 %copy-start.3 = (f32[65,8,256]{2,1,0:T(8,128)}, f32[65,8,256]{2,1,0:T(8,128)S(1)}, u32[]{:S(2)}) copy-start(f32[65,8,256]{2,1,0:T(8,128)S(1)} %multiply_select_fusion.hn_ref) | copy-start | bytes 1597444
  46.6 9.8 %collective-permute-start.4 = (f32[65,8,80]{2,1,0:T(8,128)S(1)}, f32[65,8,80]{2,1,0:T(8,128)S(1)}, u32[]{:S(2)}, u32[]{:S(2)}) collective-permute-start(f32[65,8,80]{2,1,0:T(8,128)S(1)} %maximum_bitcast_fusion.1), channel_id=1, source_target_pairs={{0,1},{1,2},{2,3},{3,4},{4,5},{5,6},{6,7},{7,8},{8,9},{9,10},{10,1... | collective-permute-start | bytes 499208 | tf_op jit(solution)/shard_map/ppermute | solution.py:59
  48.8 9.9 %collective-permute-start.3 = (f32[65,8,80]{2,1,0:T(8,128)S(1)}, f32[65,8,80]{2,1,0:T(8,128)S(1)}, u32[]{:S(2)}, u32[]{:S(2)}) collective-permute-start(f32[65,8,80]{2,1,0:T(8,128)S(1)} %maximum_bitcast_fusion), channel_id=1, source_target_pairs={{1,0},{2,1},{3,2},{4,3},{5,4},{6,5},{7,6},{8,7},{9,8},{10,9},{11,1... | collective-permute-start | bytes 499208 | tf_op jit(solution)/shard_map/ppermute | solution.py:60
  58.7 3.1 %copy-start.14 = (s32[64]{0:T(128)S(1)}, s32[64]{0:T(128)}, u32[]{:S(2)}) copy-start(s32[64]{0:T(128)} %copy-done.13) | copy-start | bytes 772
  61.9 16.0 %copy-start.15 = (f32[2,8]{1,0:T(2,128)S(1)}, f32[2,8]{1,0:T(2,128)}, u32[]{:S(2)}) copy-start(f32[2,8]{1,0:T(2,128)} %param.15) | copy-start | bytes 196
  77.9 17.6 %copy-start.5 = (f32[8,64,256]{2,1,0:T(8,128)}, f32[8,64,256]{2,1,0:T(8,128)S(1)}, u32[]{:S(2)}) copy-start(f32[8,64,256]{2,1,0:T(8,128)S(1)} %get-tuple-element.132) | copy-start | bytes 1572868
  78.0 17.5 %copy-start.6 = (f32[2,64,256]{2,1,0:T(8,128)}, f32[2,64,256]{2,1,0:T(8,128)S(1)}, u32[]{:S(2)}) copy-start(f32[2,64,256]{2,1,0:T(8,128)S(1)} %multiply_reduce_fusion.1.f_ref) | copy-start | bytes 393220
  78.1 8.2 %collective-permute-start.7 = (f32[2,8,256]{2,1,0:T(8,128)S(1)}, f32[2,8,256]{2,1,0:T(8,128)S(1)}, u32[]{:S(2)}, u32[]{:S(2)}) collective-permute-start(f32[2,8,256]{2,1,0:T(8,128)S(1)} %get-tuple-element.166), channel_id=1, source_target_pairs={{120,112},{119,113},{118,114},{117,115},{116,116},{115,117},{114,1... | collective-permute-start | bytes 49160 | tf_op jit(solution)/shard_map/ppermute | solution.py:45
  78.7 7.7 %collective-permute-start.8 = (f32[2,8,256]{2,1,0:T(8,128)S(1)}, f32[2,8,256]{2,1,0:T(8,128)S(1)}, u32[]{:S(2)}, u32[]{:S(2)}) collective-permute-start(f32[2,8,256]{2,1,0:T(8,128)S(1)} %get-tuple-element.165), channel_id=1, source_target_pairs={{16,0},{32,16},{48,32},{64,48},{80,64},{96,80},{112,96},{17,1},{33... | collective-permute-start | bytes 49160 | tf_op jit(solution)/shard_map/ppermute | solution.py:43
  80.7 6.4 %collective-permute-start.9 = (f32[2,8,256]{2,1,0:T(8,128)S(1)}, f32[2,8,256]{2,1,0:T(8,128)S(1)}, u32[]{:S(2)}, u32[]{:S(2)}) collective-permute-start(f32[2,8,256]{2,1,0:T(8,128)S(1)} %get-tuple-element.166), channel_id=1, source_target_pairs={{0,16},{16,32},{32,48},{48,64},{64,80},{80,96},{96,112},{1,17},{17... | collective-permute-start | bytes 49160 | tf_op jit(solution)/shard_map/ppermute | solution.py:42
  86.5 9.0 %copy-start.11 = (f32[2,8,256]{2,1,0:T(8,128)}, f32[2,8,256]{2,1,0:T(8,128)S(1)}, u32[]{:S(2)}) copy-start(f32[2,8,256]{2,1,0:T(8,128)S(1)} %broadcast_select_fusion.fn_ref) | copy-start | bytes 49156
  87.1 8.4 %copy-start.12 = (f32[2,8,256]{2,1,0:T(8,128)}, f32[2,8,256]{2,1,0:T(8,128)S(1)}, u32[]{:S(2)}) copy-start(f32[2,8,256]{2,1,0:T(8,128)S(1)} %collective-permute-done.9.fs_ref) | copy-start | bytes 49156
  87.2 8.3 %collective-permute-start.10 = (f32[2,8,80]{1,2,0:T(8,128)S(1)}, f32[2,8,80]{1,2,0:T(8,128)S(1)}, u32[]{:S(2)}, u32[]{:S(2)}) collective-permute-start(f32[2,8,80]{1,2,0:T(8,128)S(1)} %maximum_bitcast_fusion.2), channel_id=1, source_target_pairs={{1,0},{2,1},{3,2},{4,3},{5,4},{6,5},{7,6},{8,7},{9,8},{10,9},{11,1... | collective-permute-start | bytes 15368 | tf_op jit(solution)/shard_map/ppermute | solution.py:60
  90.4 6.9 %collective-permute-start.11 = (f32[2,8,80]{1,2,0:T(8,128)S(1)}, f32[2,8,80]{1,2,0:T(8,128)S(1)}, u32[]{:S(2)}, u32[]{:S(2)}) collective-permute-start(f32[2,8,80]{1,2,0:T(8,128)S(1)} %maximum_bitcast_fusion.3), channel_id=1, source_target_pairs={{0,1},{1,2},{2,3},{3,4},{4,5},{5,6},{6,7},{7,8},{8,9},{9,10},{10,1... | collective-permute-start | bytes 15368 | tf_op jit(solution)/shard_map/ppermute | solution.py:59

commit v13 on v10

--- a/solution.py
+++ b/solution.py
@@ -78,18 +78,12 @@
         dst[orows + WIDE:, :ocols] = hs_ref[at]
         dst[:, ocols:] = hc_ref[at]
 
-    def fill(p, carry):
+    for p in range(planes):
         place(buf.at[0, p], tr_ref[p // nk, p % nk], p)
-        return carry
-
-    lax.fori_loop(0, planes, fill, 0)
-
-    def fill_uv(k, carry):
+
+    for k in range(nk):
         place(uu.at[k], u_ref[k].astype(jnp.float32), planes + k)
         place(vv.at[k], v_ref[k].astype(jnp.float32), planes + nk + k)
-        return carry
-
-    lax.fori_loop(0, nk, fill_uv, 0)
     place(mm, m_ref[...].astype(jnp.float32), planes + 2 * nk)
     for t in range(nt):
         ff[t, :orows, :ocols] = f_ref[t]
@@ -116,7 +110,8 @@
         cc[k] = mask * ((um - up) + (vm - vp) - 0.48)
         return carry
 
-    lax.fori_loop(0, nk, coef, 0)
+    for k in range(nk):
+        coef(k, 0)
 
     strips = rows // 8
     first_row = lax.broadcasted_iota(jnp.int32, (8, lanes), 0) == 0
@@ -157,11 +152,8 @@
 
     lax.fori_loop(0, STEPS // 2, step, 0)
 
-    def out(p, carry):
+    for p in range(planes):
         o_ref[p // nk, p % nk] = buf[STEPS % 2, p, :orows, :ocols]
-        return carry
-
-    lax.fori_loop(0, planes, out, 0)
 
 
 def evolve(tracers, u_vel, v_vel, land_mask, forcing, halo, f_halo):

time: 129 us -> 129 us (level)
  transfers between devices with their start and end apart: 13 -> 13, of which waited for: 3 -> 3; matrix products, arithmetic and copies ran while one was open for 23% -> 24% of each run, Pallas kernels for 0% -> 0%
where the time goes in v13:
time: 129 us; the launch traced here: 128 us
  starting transfers between devices  39.9 us (31%)
  Pallas kernels  28.4 us (22%)
  local copies, waits for them, and re-layouts  27.6 us (21%)
  other arithmetic  23.2 us (18%)
  waiting for transfers between devices  5.75 us (4%)
  between operations  1.77 us (1%)
    pallas_call x1, Pallas kernels, evolve(): pl.pallas_call(stencil_kernel, out_shape=jax.ShapeDtypeStruct(tracers.sha...  28.4 us
    ppermute x2, starting transfers between devices, exchange(): south = lax.ppermute(tops, 'oy', [(i, i + 1) for i in range(rows_n - 1)])  9.61 us
    ppermute x2, starting transfers between devices, exchange(): lax.ppermute(wests, 'ox', [((i + 1) % cols_n, i) for i in range(cols_n)])  8.83 us
    all_to_all x1, starting transfers between devices, atmosphere_block(): got = lax.all_to_all(pieces, 'ox', split_axis=2, concat_axis=1, tiled=True)  7.82 us
    reduce_sum x1, other arithmetic, remap(): fast = jnp.sum(window * wsum.transpose(0, 2, 1, 3)[None], axis=(1, 3))  6.49 us
    gather x1, local copies, waits for them, and re-layouts, remap(): window = lifted[:, base_r[None, :] + offs[:, None]]  6.04 us
    ppermute x2, waiting for transfers between devices, exchange(): lax.ppermute(easts, 'ox', [(i, (i + 1) % cols_n) for i in range(cols_n)])  5.33 us
    concatenate x2, other arithmetic, lane_tile(): return jnp.concatenate([from_e, gap, from_w], axis=-1)  4.71 us
  transfers between devices with their start and end apart: 13, of which 3 were waited for; matrix products, arithmetic and copies ran while one was open for 24% of the time, Pallas kernels for 0%

profile of v13, /device:TPU:1, one launch (start us, length us, event | category | flops | bytes accessed | tf_op | source)
XLA Modules:
  0.0 127.6 jit_solution(16411703268295682822)
XLA Ops:
  0.6 1.1 fusion.20
  1.8 1.0 convert_bitcast_fusion
  2.8 1.0 fusion.25
  4.6 1.5 %collective-permute-start = (f32[65,8,256]{2,1,0:T(8,128)}, f32[65,8,256]{2,1,0:T(8,128)}, u32[]{:S(2)}, u32[]{:S(2)}) collective-permute-start(f32[65,8,256]{2,1,0:T(8,128)} %pad_maximum_fusion.3), channel_id=1, source_target_pairs={{120,112},{119,113},{118,114},{117,115},{116,116},{115,117},{114,1... | collective-permute-start | bytes 1597448 | tf_op jit(solution)/shard_map/ppermute | solution.py:45
  6.0 4.5 %collective-permute-start.2 = (f32[65,8,256]{2,1,0:T(8,128)}, f32[65,8,256]{2,1,0:T(8,128)}, u32[]{:S(2)}, u32[]{:S(2)}) collective-permute-start(f32[65,8,256]{2,1,0:T(8,128)} %pad_maximum_fusion.3), channel_id=1, source_target_pairs={{0,16},{16,32},{32,48},{48,64},{64,80},{80,96},{96,112},{1,17},{17... | collective-permute-start | bytes 1597448 | tf_op jit(solution)/shard_map/ppermute | solution.py:42
  11.4 1.9 %collective-permute-start.1 = (f32[65,8,256]{2,1,0:T(8,128)}, f32[65,8,256]{2,1,0:T(8,128)}, u32[]{:S(2)}, u32[]{:S(2)}) collective-permute-start(f32[65,8,256]{2,1,0:T(8,128)} %pad_maximum_fusion.4), channel_id=1, source_target_pairs={{16,0},{32,16},{48,32},{64,48},{80,64},{96,80},{112,96},{17,1},{33... | collective-permute-start | bytes 1597448 | tf_op jit(solution)/shard_map/ppermute | solution.py:43
  14.8 7.8 %all-to-all-start = ((f32[8,2,16,68]{3,1,0,2:T(2,128)}), f32[8,2,16,68]{3,1,0,2:T(2,128)}, u32[]{:S(2)}, u32[]{:S(2)}) async-start(f32[8,2,16,68]{3,1,0,2:T(2,128)} %copy.132), calls=%async_computation | async-start | bytes 262144 | tf_op jit(solution)/shard_map/all_to_all | solution.py:192
  22.7 1.7 %fusion.19 = (f32[32,64,8]{2,1,0:T(8,128)}, f32[32,64,8]{2,1,0:T(8,128)}) fusion(f32[32,64,256]{2,1,0:T(8,128)S(1)} %bitcast.95), kind=kLoop, calls=%fused_computation.77 | loop fusion | bytes 262144 | tf_op jit(solution)/shard_map/slice | solution.py:52
  24.4 1.1 fusion.23
  26.5 4.0 %pad_maximum_fusion.1 = (f32[65,64,8]{2,1,0:T(8,128)S(1)}, f32[65,64,8]{2,1,0:T(8,128)}) fusion(f32[1,64,8]{2,1,0:T(8,128)S(1)} %get-tuple-element.170, f32[16,64,8]{2,1,0:T(8,128)} %get-tuple-element.158, f32[16,64,8]{2,1,0:T(8,128)} %get-tuple-element.156, f32[32,64,8]{2,1,0:T(8,128)} %get-tuple-element.148, f32[1,64,8]{2,1,0:T(8,128)S(1)} %get-tuple-element.169, ...), kind=kLoop, calls=%fused_computation.38 | loop fusion | flops 199680 | bytes 532480 | tf_op jit(solution)/shard_map/concatenate | solution.py:56
  30.5 2.2 %copy.127 = f32[65,64,8]{1,2,0:T(8,128)S(1)} copy(f32[65,64,8]{2,1,0:T(8,128)} %get-tuple-element.180) | data formatting | bytes 266240 | tf_op jit(solution)/shard_map/concatenate | solution.py:52
  33.8 1.9 %select_reduce_fusion = f32[25,64,256]{2,1,0:T(8,128)} fusion(f32[4,64,256]{2,1,0:T(8,128)S(1)} %copy-done.7, s32[4,64,256]{2,1,0:T(8,128)S(1)} %get-tuple-element.133), kind=kLoop, calls=%fused_computation.35 | loop fusion | flops 4505600 | bytes 2162688 | tf_op jit(solution)/shard_map/reduce_sum | solution.py:217
  36.6 3.9 %collective-permute-start.5 = (f32[8,2,68]{2,0,1:T(8,128)S(1)}, f32[8,2,68]{2,0,1:T(8,128)S(1)}, u32[]{:S(2)}, u32[]{:S(2)}) collective-permute-start(f32[8,2,68]{2,0,1:T(8,128)S(1)} %get-tuple-element.167), channel_id=1, source_target_pairs={{0,16},{16,32},{32,48},{48,64},{64,80},{80,96},{96,112},{1,17},{17... | collective-permute-start | bytes 13064 | tf_op jit(solution)/shard_map/ppermute | solution.py:194
  40.6 1.9 %collective-permute-start.6 = (f32[8,2,68]{2,0,1:T(8,128)S(1)}, f32[8,2,68]{2,0,1:T(8,128)S(1)}, u32[]{:S(2)}, u32[]{:S(2)}) collective-permute-start(f32[8,2,68]{2,0,1:T(8,128)S(1)} %get-tuple-element.168), channel_id=1, source_target_pairs={{16,0},{32,16},{48,32},{64,48},{80,64},{96,80},{112,96},{17,1},{33... | collective-permute-start | bytes 13064 | tf_op jit(solution)/shard_map/ppermute | solution.py:195
  42.5 1.2 rev.6
  43.8 1.2 multiply_select_fusion.hn_ref
  45.3 1.2 fusion.22
  46.8 1.7 %collective-permute-start.4 = (f32[65,80,8]{1,2,0:T(8,128)S(1)}, f32[65,80,8]{1,2,0:T(8,128)S(1)}, u32[]{:S(2)}, u32[]{:S(2)}) collective-permute-start(f32[65,80,8]{1,2,0:T(8,128)S(1)} %pad_maximum_fusion.6), channel_id=1, source_target_pairs={{0,1},{1,2},{2,3},{3,4},{4,5},{5,6},{6,7},{7,8},{8,9},{9,10},{10,1... | collective-permute-start | bytes 499208 | tf_op jit(solution)/shard_map/ppermute | solution.py:59
  48.9 3.4 %collective-permute-start.3 = (f32[65,80,8]{1,2,0:T(8,128)S(1)}, f32[65,80,8]{1,2,0:T(8,128)S(1)}, u32[]{:S(2)}, u32[]{:S(2)}) collective-permute-start(f32[65,80,8]{1,2,0:T(8,128)S(1)} %pad_maximum_fusion.5), channel_id=1, source_target_pairs={{1,0},{2,1},{3,2},{4,3},{5,4},{6,5},{7,6},{8,7},{9,8},{10,9},{11,1... | collective-permute-start | bytes 499208 | tf_op jit(solution)/shard_map/ppermute | solution.py:60
  53.9 2.7 %collective-permute-done.4 = f32[65,80,8]{1,2,0:T(8,128)S(1)} collective-permute-done((f32[65,80,8]{1,2,0:T(8,128)S(1)}, f32[65,80,8]{1,2,0:T(8,128)S(1)}, u32[]{:S(2)}, u32[]{:S(2)}) %collective-permute-start.4) | collective-permute-done | bytes 166432 | tf_op jit(solution)/shard_map/ppermute | solution.py:59
  57.8 16.0 %conditional.1 = (f32[8,64,256]{2,1,0:T(8,128)S(1)}) conditional(s32[]{:T(128)} %convert_element_type.13, (s32[64]{0:T(128)S(1)}, s32[5]{0:T(128)S(1)}, f32[8,36,5,256]{3,1,2,0:T(8,128)S(1)}, f32[5,64,5,256]{3,1,2,0:T(8,128)}) %tuple.77, (f32[4,64,256]{2,1,0:T(8,128)}, f32[8,36,68]{2,0,1:T(8,128)S(1)}, s32[4,64,256]{2,1,0:T(8,128)S(1)}) %tuple.78), branch_computations={%region_2.4_spmd, %region_4.6_spmd} | conditional | flops 6424832 | bytes 48769564 | solution.py:232
  58.5 6.0 %gather_fusion = f32[320,8,5,256]{3,1,2,0:T(8,128)} fusion(f32[8,36,5,256]{3,0,2,1:T(8,128)S(1)} %copy.135, s32[1024]{0:T(1024)S(1)} %pad_clamp_fusion), kind=kCustom, calls=%fused_computation | custom fusion | bytes 26215680 | tf_op jit(solution)/shard_map/gather | solution.py:211
  64.5 2.4 %copy.136 = f32[5,64,5,256]{3,2,1,0:T(8,128)S(1)} copy(f32[5,64,5,256]{3,1,2,0:T(8,128)} %get-tuple-element.126) | data formatting | bytes 3276800 | tf_op jit(solution)/shard_map
  67.0 6.5 %multiply_reduce_fusion = f32[64,8,256]{2,1,0:T(8,128)S(1)} fusion(f32[5,64,8,5,256]{4,2,3,1,0:T(8,128)} %bitcast.93, f32[5,64,5,256]{3,2,1,0:T(8,128)S(1)} %copy.136), kind=kLoop, calls=%fused_computation.5 | loop fusion | flops 6422528 | bytes 15269888 | tf_op jit(solution)/shard_map/reduce_sum | solution.py:221
  74.8 1.9 %collective-permute-start.8 = (f32[2,8,256]{2,1,0:T(8,128)S(1)}, f32[2,8,256]{2,1,0:T(8,128)S(1)}, u32[]{:S(2)}, u32[]{:S(2)}) collective-permute-start(f32[2,8,256]{2,1,0:T(8,128)S(1)} %get-tuple-element.165), channel_id=1, source_target_pairs={{16,0},{32,16},{48,32},{64,48},{80,64},{96,80},{112,96},{17,1},{33... | collective-permute-start | bytes 49160 | tf_op jit(solution)/shard_map/ppermute | solution.py:43
  76.9 5.1 %collective-permute-start.9 = (f32[2,8,256]{2,1,0:T(8,128)S(1)}, f32[2,8,256]{2,1,0:T(8,128)S(1)}, u32[]{:S(2)}, u32[]{:S(2)}) collective-permute-start(f32[2,8,256]{2,1,0:T(8,128)S(1)} %get-tuple-element.166), channel_id=1, source_target_pairs={{0,16},{16,32},{32,48},{48,64},{64,80},{80,96},{96,112},{1,17},{17... | collective-permute-start | bytes 49160 | tf_op jit(solution)/shard_map/ppermute | solution.py:42
  82.0 1.7 %copy.139 = f32[65,80,8]{2,1,0:T(8,128)S(1)} copy(f32[65,80,8]{1,2,0:T(8,128)} %copy-done.12) | data formatting | bytes 332800 | tf_op jit(solution)/shard_map/optimization_barrier | solution.py:248
  83.7 2.3 %copy.140 = f32[65,80,8]{2,1,0:T(8,128)} copy(f32[65,80,8]{1,2,0:T(8,128)S(1)} %copy-done.11) | data formatting | bytes 332800 | tf_op jit(solution)/shard_map/optimization_barrier | solution.py:248
  86.4 5.4 %collective-permute-start.10 = (f32[2,80,8]{2,1,0:T(8,128)S(1)}, f32[2,80,8]{2,1,0:T(8,128)S(1)}, u32[]{:S(2)}, u32[]{:S(2)}) collective-permute-start(f32[2,80,8]{2,1,0:T(8,128)S(1)} %pad_maximum_fusion.9), channel_id=1, source_target_pairs={{1,0},{2,1},{3,2},{4,3},{5,4},{6,5},{7,6},{8,7},{9,8},{10,9},{11,1... | collective-permute-start | bytes 15368 | tf_op jit(solution)/shard_map/ppermute | solution.py:60
  91.9 4.0 %pad_maximum_fusion.hc_ref = f32[65,80,128]{2,1,0:T(8,128)} fusion(f32[65,80,8]{2,1,0:T(8,128)} %copy.140, f32[65,80,8]{2,1,0:T(8,128)S(1)} %copy.139, f32[128]{0:T(128)S(1)} %pad.10.clone), kind=kLoop, calls=%fused_computation.37 | loop fusion | flops 1331200 | bytes 2995712 | tf_op jit(solution)/shard_map/concatenate | solution.py:67
  95.9 2.6 %collective-permute-done.11 = f32[2,80,8]{2,1,0:T(8,128)S(1)} collective-permute-done((f32[2,80,8]{2,1,0:T(8,128)S(1)}, f32[2,80,8]{2,1,0:T(8,128)S(1)}, u32[]{:S(2)}, u32[]{:S(2)}) %collective-permute-start.11) | collective-permute-done | bytes 5152 | tf_op jit(solution)/shard_map/ppermute | solution.py:59
  99.2 28.4 %shard_map.95 = f32[2,16,64,256]{3,2,1,0:T(8,128)} custom-call(f32[2,16,64,256]{3,2,1,0:T(8,128)} %tr_ref.1, bf16[16,64,256]{2,1,0:T(8,128)(2,1)} %u_ref.1, bf16[16,64,256]{2,1,0:T(8,128)(2,1)} %v_ref.1, s32[64,256]{1,0:T(8,128)} %m_ref.1, f32[2,64,256]{2,1,0:T(8,128)} %copy-done.6, f32[65,8,256]{2,1,0:T(8,128)} %copy-done.3, ...), custom_call_target="tpu_custom_call" | custom-call | tf_op jit(solution)/shard_map/pallas_call | solution.py:163
  (97 shorter events, 12.2 us)
Async XLA Ops:
  0.6 12.7 %copy-start.9 = (f32[8,2,1024]{2,1,0:T(2,128)S(1)}, f32[8,2,1024]{2,1,0:T(2,128)}, u32[]{:S(2)}) copy-start(f32[8,2,1024]{2,1,0:T(2,128)} %param.12) | copy-start | bytes 196612
  0.6 12.9 %slice-start = ((f32[8,2,1024]{2,1,0:T(2,128)}), f32[8,2,62]{2,1,0:T(2,128)S(1)}, s32[]{:S(2)}) async-start(f32[8,2,1024]{2,1,0:T(2,128)} %param.12), calls=%async_computation.1 | async-start | bytes 16384 | tf_op jit(solution)/shard_map/jit(_roll_static)/slice | solution.py:190
  1.8 20.9 %copy-start = (f32[2,16,64,256]{3,2,1,0:T(8,128)S(1)}, f32[2,16,64,256]{3,2,1,0:T(8,128)}, u32[]{:S(2)}) copy-start(f32[2,16,64,256]{3,2,1,0:T(8,128)} %tr_ref.1) | copy-start | bytes 6291460
  4.6 37.9 %collective-permute-start = (f32[65,8,256]{2,1,0:T(8,128)}, f32[65,8,256]{2,1,0:T(8,128)}, u32[]{:S(2)}, u32[]{:S(2)}) collective-permute-start(f32[65,8,256]{2,1,0:T(8,128)} %pad_maximum_fusion.3), channel_id=1, source_target_pairs={{120,112},{119,113},{118,114},{117,115},{116,116},{115,117},{114,1... | collective-permute-start | bytes 1597448 | tf_op jit(solution)/shard_map/ppermute | solution.py:45
  6.0 39.2 %collective-permute-start.2 = (f32[65,8,256]{2,1,0:T(8,128)}, f32[65,8,256]{2,1,0:T(8,128)}, u32[]{:S(2)}, u32[]{:S(2)}) collective-permute-start(f32[65,8,256]{2,1,0:T(8,128)} %pad_maximum_fusion.3), channel_id=1, source_target_pairs={{0,16},{16,32},{32,48},{48,64},{64,80},{80,96},{96,112},{1,17},{17... | collective-permute-start | bytes 1597448 | tf_op jit(solution)/shard_map/ppermute | solution.py:42
  11.4 32.4 %collective-permute-start.1 = (f32[65,8,256]{2,1,0:T(8,128)}, f32[65,8,256]{2,1,0:T(8,128)}, u32[]{:S(2)}, u32[]{:S(2)}) collective-permute-start(f32[65,8,256]{2,1,0:T(8,128)} %pad_maximum_fusion.4), channel_id=1, source_target_pairs={{16,0},{32,16},{48,32},{64,48},{80,64},{96,80},{112,96},{17,1},{33... | collective-permute-start | bytes 1597448 | tf_op jit(solution)/shard_map/ppermute | solution.py:43
  14.0 10.5 %copy-start.1 = (bf16[16,64,256]{2,1,0:T(8,128)(2,1)S(1)}, bf16[16,64,256]{2,1,0:T(8,128)(2,1)}, u32[]{:S(2)}) copy-start(bf16[16,64,256]{2,1,0:T(8,128)(2,1)} %u_ref.1) | copy-start | bytes 1572868
  14.8 20.9 %all-to-all-start = ((f32[8,2,16,68]{3,1,0,2:T(2,128)}), f32[8,2,16,68]{3,1,0,2:T(2,128)}, u32[]{:S(2)}, u32[]{:S(2)}) async-start(f32[8,2,16,68]{3,1,0,2:T(2,128)} %copy.132), calls=%async_computation | async-start | bytes 262144 | tf_op jit(solution)/shard_map/all_to_all | solution.py:192
  22.7 2.9 %copy-start.2 = (bf16[16,64,256]{2,1,0:T(8,128)(2,1)S(1)}, bf16[16,64,256]{2,1,0:T(8,128)(2,1)}, u32[]{:S(2)}) copy-start(bf16[16,64,256]{2,1,0:T(8,128)(2,1)} %v_ref.1) | copy-start | bytes 1572868
  30.5 2.9 %copy-start.4 = (s32[4,64,256]{2,1,0:T(8,128)S(1)}, s32[4,64,256]{2,1,0:T(8,128)}, u32[]{:S(2)}) copy-start(s32[4,64,256]{2,1,0:T(8,128)} %param.13) | copy-start | bytes 786436
  30.5 3.3 %copy-start.7 = (f32[4,64,256]{2,1,0:T(8,128)S(1)}, f32[4,64,256]{2,1,0:T(8,128)}, u32[]{:S(2)}) copy-start(f32[4,64,256]{2,1,0:T(8,128)} %param.14) | copy-start | bytes 786436
  32.8 11.0 %copy-start.16 = (f32[65]{0:T(128)S(1)}, f32[65]{0:T(128)}, u32[]{:S(2)}) copy-start(f32[65]{0:T(128)} %constant.83.clone.1) | copy-start | bytes 784
  36.6 17.2 %collective-permute-start.5 = (f32[8,2,68]{2,0,1:T(8,128)S(1)}, f32[8,2,68]{2,0,1:T(8,128)S(1)}, u32[]{:S(2)}, u32[]{:S(2)}) collective-permute-start(f32[8,2,68]{2,0,1:T(8,128)S(1)} %get-tuple-element.167), channel_id=1, source_target_pairs={{0,16},{16,32},{32,48},{48,64},{64,80},{80,96},{96,112},{1,17},{17... | collective-permute-start | bytes 13064 | tf_op jit(solution)/shard_map/ppermute | solution.py:194
  40.6 13.3 %collective-permute-start.6 = (f32[8,2,68]{2,0,1:T(8,128)S(1)}, f32[8,2,68]{2,0,1:T(8,128)S(1)}, u32[]{:S(2)}, u32[]{:S(2)}) collective-permute-start(f32[8,2,68]{2,0,1:T(8,128)S(1)} %get-tuple-element.168), channel_id=1, source_target_pairs={{16,0},{32,16},{48,32},{64,48},{80,64},{96,80},{112,96},{17,1},{33... | collective-permute-start | bytes 13064 | tf_op jit(solution)/shard_map/ppermute | solution.py:195
  45.0 3.7 %copy-start.3 = (f32[65,8,256]{2,1,0:T(8,128)}, f32[65,8,256]{2,1,0:T(8,128)S(1)}, u32[]{:S(2)}) copy-start(f32[65,8,256]{2,1,0:T(8,128)S(1)} %multiply_select_fusion.hn_ref) | copy-start | bytes 1597444
  46.8 9.8 %collective-permute-start.4 = (f32[65,80,8]{1,2,0:T(8,128)S(1)}, f32[65,80,8]{1,2,0:T(8,128)S(1)}, u32[]{:S(2)}, u32[]{:S(2)}) collective-permute-start(f32[65,80,8]{1,2,0:T(8,128)S(1)} %pad_maximum_fusion.6), channel_id=1, source_target_pairs={{0,1},{1,2},{2,3},{3,4},{4,5},{5,6},{6,7},{7,8},{8,9},{9,10},{10,1... | collective-permute-start | bytes 499208 | tf_op jit(solution)/shard_map/ppermute | solution.py:59
  48.9 8.1 %collective-permute-start.3 = (f32[65,80,8]{1,2,0:T(8,128)S(1)}, f32[65,80,8]{1,2,0:T(8,128)S(1)}, u32[]{:S(2)}, u32[]{:S(2)}) collective-permute-start(f32[65,80,8]{1,2,0:T(8,128)S(1)} %pad_maximum_fusion.5), channel_id=1, source_target_pairs={{1,0},{2,1},{3,2},{4,3},{5,4},{6,5},{7,6},{8,7},{9,8},{10,9},{11,1... | collective-permute-start | bytes 499208 | tf_op jit(solution)/shard_map/ppermute | solution.py:60
  56.6 1.2 copy-start.10
  57.0 0.8 copy-start.12
  57.8 16.1 %copy-start.15 = (f32[2,8]{1,0:T(2,128)S(1)}, f32[2,8]{1,0:T(2,128)}, u32[]{:S(2)}) copy-start(f32[2,8]{1,0:T(2,128)} %param.15) | copy-start | bytes 196
  73.8 3.0 %copy-start.5 = (f32[8,64,256]{2,1,0:T(8,128)}, f32[8,64,256]{2,1,0:T(8,128)S(1)}, u32[]{:S(2)}) copy-start(f32[8,64,256]{2,1,0:T(8,128)S(1)} %get-tuple-element.132) | copy-start | bytes 1572868
  73.8 9.9 %copy-start.11 = (f32[65,80,8]{1,2,0:T(8,128)S(1)}, f32[65,80,8]{1,2,0:T(8,128)}, u32[]{:S(2)}) copy-start(f32[65,80,8]{1,2,0:T(8,128)} %copy-done.10) | copy-start | bytes 499204
  74.0 12.0 %copy-start.6 = (f32[2,64,256]{2,1,0:T(8,128)}, f32[2,64,256]{2,1,0:T(8,128)S(1)}, u32[]{:S(2)}) copy-start(f32[2,64,256]{2,1,0:T(8,128)S(1)} %multiply_reduce_fusion.1.f_ref) | copy-start | bytes 393220
  74.0 12.0 %collective-permute-start.7 = (f32[2,8,256]{2,1,0:T(8,128)S(1)}, f32[2,8,256]{2,1,0:T(8,128)S(1)}, u32[]{:S(2)}, u32[]{:S(2)}) collective-permute-start(f32[2,8,256]{2,1,0:T(8,128)S(1)} %get-tuple-element.166), channel_id=1, source_target_pairs={{120,112},{119,113},{118,114},{117,115},{116,116},{115,117},{114,1... | collective-permute-start | bytes 49160 | tf_op jit(solution)/shard_map/ppermute | solution.py:45
  74.8 11.3 %collective-permute-start.8 = (f32[2,8,256]{2,1,0:T(8,128)S(1)}, f32[2,8,256]{2,1,0:T(8,128)S(1)}, u32[]{:S(2)}, u32[]{:S(2)}) collective-permute-start(f32[2,8,256]{2,1,0:T(8,128)S(1)} %get-tuple-element.165), channel_id=1, source_target_pairs={{16,0},{32,16},{48,32},{64,48},{80,64},{96,80},{112,96},{17,1},{33... | collective-permute-start | bytes 49160 | tf_op jit(solution)/shard_map/ppermute | solution.py:43
  76.9 9.4 %collective-permute-start.9 = (f32[2,8,256]{2,1,0:T(8,128)S(1)}, f32[2,8,256]{2,1,0:T(8,128)S(1)}, u32[]{:S(2)}, u32[]{:S(2)}) collective-permute-start(f32[2,8,256]{2,1,0:T(8,128)S(1)} %get-tuple-element.166), channel_id=1, source_target_pairs={{0,16},{16,32},{32,48},{48,64},{64,80},{80,96},{96,112},{1,17},{17... | collective-permute-start | bytes 49160 | tf_op jit(solution)/shard_map/ppermute | solution.py:42
  86.2 9.7 %copy-start.13 = (f32[2,8,256]{2,1,0:T(8,128)}, f32[2,8,256]{2,1,0:T(8,128)S(1)}, u32[]{:S(2)}) copy-start(f32[2,8,256]{2,1,0:T(8,128)S(1)} %broadcast_select_fusion.fn_ref) | copy-start | bytes 49156
  86.3 9.6 %copy-start.14 = (f32[2,8,256]{2,1,0:T(8,128)}, f32[2,8,256]{2,1,0:T(8,128)S(1)}, u32[]{:S(2)}) copy-start(f32[2,8,256]{2,1,0:T(8,128)S(1)} %collective-permute-done.9.fs_ref) | copy-start | bytes 49156
  86.4 9.5 %collective-permute-start.10 = (f32[2,80,8]{2,1,0:T(8,128)S(1)}, f32[2,80,8]{2,1,0:T(8,128)S(1)}, u32[]{:S(2)}, u32[]{:S(2)}) collective-permute-start(f32[2,80,8]{2,1,0:T(8,128)S(1)} %pad_maximum_fusion.9), channel_id=1, source_target_pairs={{1,0},{2,1},{3,2},{4,3},{5,4},{6,5},{7,6},{8,7},{9,8},{10,9},{11,1... | collective-permute-start | bytes 15368 | tf_op jit(solution)/shard_map/ppermute | solution.py:60
  91.8 6.7 %collective-permute-start.11 = (f32[2,80,8]{2,1,0:T(8,128)S(1)}, f32[2,80,8]{2,1,0:T(8,128)S(1)}, u32[]{:S(2)}, u32[]{:S(2)}) collective-permute-start(f32[2,80,8]{2,1,0:T(8,128)S(1)} %pad_maximum_fusion.10), channel_id=1, source_target_pairs={{0,1},{1,2},{2,3},{3,4},{4,5},{5,6},{6,7},{7,8},{8,9},{9,10},{10,1... | collective-permute-start | bytes 15368 | tf_op jit(solution)/shard_map/ppermute | solution.py:59

commit v14 on v13

--- a/solution.py
+++ b/solution.py
@@ -117,8 +117,8 @@
     first_row = lax.broadcasted_iota(jnp.int32, (8, lanes), 0) == 0
     last_row = lax.broadcasted_iota(jnp.int32, (8, lanes), 0) == 7
 
-    def plane(src, dst, k, above, below, forced):
-        for i in range(strips):
+    def plane(src, dst, k, above, below, forced, final=False):
+        for i in range(orows // 8 if final else strips):
             at = pl.ds(i * 8, 8)
             before = pl.ds((i - 1) % strips * 8, 8)
             after = pl.ds((i + 1) % strips * 8, 8)
@@ -141,7 +141,10 @@
                 tend = tend + c_8 * (up + down)
                 if forced:
                     tend = tend + mf[t, at, :]
-                buf[dst, p, at, :] = cur + tend
+                if final:
+                    o_ref[t, k, at, :] = (cur + tend)[:, :ocols]
+                else:
+                    buf[dst, p, at, :] = cur + tend
 
     def step(i, carry):
         for src in (0, 1):
@@ -150,10 +153,11 @@
                 plane(src, dst, k, k - 1 if k > 0 else None, k + 1 if k < nk - 1 else None, k == 0)
         return carry
 
-    lax.fori_loop(0, STEPS // 2, step, 0)
-
-    for p in range(planes):
-        o_ref[p // nk, p % nk] = buf[STEPS % 2, p, :orows, :ocols]
+    lax.fori_loop(0, STEPS // 2 - 1, step, 0)
+    for k in range(nk):
+        plane(0, 1, k, k - 1 if k > 0 else None, k + 1 if k < nk - 1 else None, k == 0)
+    for k in range(nk):
+        plane(1, None, k, k - 1 if k > 0 else None, k + 1 if k < nk - 1 else None, k == 0, True)
 
 
 def evolve(tracers, u_vel, v_vel, land_mask, forcing, halo, f_halo):

time: 129 us -> 127 us (0.984)
  no operation moved by 1% of the time
where the time goes in v14:
time: 127 us
  starting transfers between devices  39.9 us (31%)
  local copies, waits for them, and re-layouts  27.6 us (22%)
  Pallas kernels  27.3 us (21%)
  other arithmetic  23.2 us (18%)
  waiting for transfers between devices  5.75 us (5%)
  between operations  1.77 us (1%)
    pallas_call x1, Pallas kernels, evolve(): pl.pallas_call(stencil_kernel, out_shape=jax.ShapeDtypeStruct(tracers.sha...  27.3 us
    ppermute x2, starting transfers between devices, exchange(): south = lax.ppermute(tops, 'oy', [(i, i + 1) for i in range(rows_n - 1)])  9.61 us
    ppermute x2, starting transfers between devices, exchange(): lax.ppermute(wests, 'ox', [((i + 1) % cols_n, i) for i in range(cols_n)])  8.83 us
    all_to_all x1, starting transfers between devices, atmosphere_block(): got = lax.all_to_all(pieces, 'ox', split_axis=2, concat_axis=1, tiled=True)  7.82 us
    reduce_sum x1, other arithmetic, remap(): fast = jnp.sum(window * wsum.transpose(0, 2, 1, 3)[None], axis=(1, 3))  6.49 us
    gather x1, local copies, waits for them, and re-layouts, remap(): window = lifted[:, base_r[None, :] + offs[:, None]]  6.04 us
    ppermute x2, waiting for transfers between devices, exchange(): lax.ppermute(easts, 'ox', [(i, (i + 1) % cols_n) for i in range(cols_n)])  5.33 us
    concatenate x2, other arithmetic, lane_tile(): return jnp.concatenate([from_e, gap, from_w], axis=-1)  4.71 us
  transfers between devices with their start and end apart: 13, of which 3 were waited for; matrix products, arithmetic and copies ran while one was open for 24% of the time, Pallas kernels for 0%

profile of v14, /device:TPU:1, one launch (start us, length us, event | category | flops | bytes accessed | tf_op | source)
XLA Modules:
  0.0 126.5 jit_solution(7791192415462973359)
XLA Ops:
  0.6 1.1 fusion.20
  1.8 1.0 convert_bitcast_fusion
  2.8 1.0 fusion.25
  4.6 1.5 %collective-permute-start = (f32[65,8,256]{2,1,0:T(8,128)}, f32[65,8,256]{2,1,0:T(8,128)}, u32[]{:S(2)}, u32[]{:S(2)}) collective-permute-start(f32[65,8,256]{2,1,0:T(8,128)} %pad_maximum_fusion.3), channel_id=1, source_target_pairs={{120,112},{119,113},{118,114},{117,115},{116,116},{115,117},{114,1... | collective-permute-start | bytes 1597448 | tf_op jit(solution)/shard_map/ppermute | solution.py:45
  6.0 4.5 %collective-permute-start.2 = (f32[65,8,256]{2,1,0:T(8,128)}, f32[65,8,256]{2,1,0:T(8,128)}, u32[]{:S(2)}, u32[]{:S(2)}) collective-permute-start(f32[65,8,256]{2,1,0:T(8,128)} %pad_maximum_fusion.3), channel_id=1, source_target_pairs={{0,16},{16,32},{32,48},{48,64},{64,80},{80,96},{96,112},{1,17},{17... | collective-permute-start | bytes 1597448 | tf_op jit(solution)/shard_map/ppermute | solution.py:42
  11.4 1.9 %collective-permute-start.1 = (f32[65,8,256]{2,1,0:T(8,128)}, f32[65,8,256]{2,1,0:T(8,128)}, u32[]{:S(2)}, u32[]{:S(2)}) collective-permute-start(f32[65,8,256]{2,1,0:T(8,128)} %pad_maximum_fusion.4), channel_id=1, source_target_pairs={{16,0},{32,16},{48,32},{64,48},{80,64},{96,80},{112,96},{17,1},{33... | collective-permute-start | bytes 1597448 | tf_op jit(solution)/shard_map/ppermute | solution.py:43
  14.8 7.8 %all-to-all-start = ((f32[8,2,16,68]{3,1,0,2:T(2,128)}), f32[8,2,16,68]{3,1,0,2:T(2,128)}, u32[]{:S(2)}, u32[]{:S(2)}) async-start(f32[8,2,16,68]{3,1,0,2:T(2,128)} %copy.132), calls=%async_computation | async-start | bytes 262144 | tf_op jit(solution)/shard_map/all_to_all | solution.py:196
  22.7 1.7 %fusion.19 = (f32[32,64,8]{2,1,0:T(8,128)}, f32[32,64,8]{2,1,0:T(8,128)}) fusion(f32[32,64,256]{2,1,0:T(8,128)S(1)} %bitcast.95), kind=kLoop, calls=%fused_computation.77 | loop fusion | bytes 262144 | tf_op jit(solution)/shard_map/slice | solution.py:52
  24.4 1.1 fusion.23
  26.5 4.0 %pad_maximum_fusion.1 = (f32[65,64,8]{2,1,0:T(8,128)S(1)}, f32[65,64,8]{2,1,0:T(8,128)}) fusion(f32[1,64,8]{2,1,0:T(8,128)S(1)} %get-tuple-element.170, f32[16,64,8]{2,1,0:T(8,128)} %get-tuple-element.158, f32[16,64,8]{2,1,0:T(8,128)} %get-tuple-element.156, f32[32,64,8]{2,1,0:T(8,128)} %get-tuple-element.148, f32[1,64,8]{2,1,0:T(8,128)S(1)} %get-tuple-element.169, ...), kind=kLoop, calls=%fused_computation.38 | loop fusion | flops 199680 | bytes 532480 | tf_op jit(solution)/shard_map/concatenate | solution.py:56
  30.5 2.2 %copy.127 = f32[65,64,8]{1,2,0:T(8,128)S(1)} copy(f32[65,64,8]{2,1,0:T(8,128)} %get-tuple-element.180) | data formatting | bytes 266240 | tf_op jit(solution)/shard_map/concatenate | solution.py:52
  33.8 1.9 %select_reduce_fusion = f32[25,64,256]{2,1,0:T(8,128)} fusion(f32[4,64,256]{2,1,0:T(8,128)S(1)} %copy-done.7, s32[4,64,256]{2,1,0:T(8,128)S(1)} %get-tuple-element.133), kind=kLoop, calls=%fused_computation.35 | loop fusion | flops 4505600 | bytes 2162688 | tf_op jit(solution)/shard_map/reduce_sum | solution.py:221
  36.6 3.9 %collective-permute-start.5 = (f32[8,2,68]{2,0,1:T(8,128)S(1)}, f32[8,2,68]{2,0,1:T(8,128)S(1)}, u32[]{:S(2)}, u32[]{:S(2)}) collective-permute-start(f32[8,2,68]{2,0,1:T(8,128)S(1)} %get-tuple-element.167), channel_id=1, source_target_pairs={{0,16},{16,32},{32,48},{48,64},{64,80},{80,96},{96,112},{1,17},{17... | collective-permute-start | bytes 13064 | tf_op jit(solution)/shard_map/ppermute | solution.py:198
  40.6 1.9 %collective-permute-start.6 = (f32[8,2,68]{2,0,1:T(8,128)S(1)}, f32[8,2,68]{2,0,1:T(8,128)S(1)}, u32[]{:S(2)}, u32[]{:S(2)}) collective-permute-start(f32[8,2,68]{2,0,1:T(8,128)S(1)} %get-tuple-element.168), channel_id=1, source_target_pairs={{16,0},{32,16},{48,32},{64,48},{80,64},{96,80},{112,96},{17,1},{33... | collective-permute-start | bytes 13064 | tf_op jit(solution)/shard_map/ppermute | solution.py:199
  42.5 1.2 rev.6
  43.8 1.2 multiply_select_fusion.hn_ref
  45.3 1.2 fusion.22
  46.8 1.7 %collective-permute-start.4 = (f32[65,80,8]{1,2,0:T(8,128)S(1)}, f32[65,80,8]{1,2,0:T(8,128)S(1)}, u32[]{:S(2)}, u32[]{:S(2)}) collective-permute-start(f32[65,80,8]{1,2,0:T(8,128)S(1)} %pad_maximum_fusion.6), channel_id=1, source_target_pairs={{0,1},{1,2},{2,3},{3,4},{4,5},{5,6},{6,7},{7,8},{8,9},{9,10},{10,1... | collective-permute-start | bytes 499208 | tf_op jit(solution)/shard_map/ppermute | solution.py:59
  48.9 3.4 %collective-permute-start.3 = (f32[65,80,8]{1,2,0:T(8,128)S(1)}, f32[65,80,8]{1,2,0:T(8,128)S(1)}, u32[]{:S(2)}, u32[]{:S(2)}) collective-permute-start(f32[65,80,8]{1,2,0:T(8,128)S(1)} %pad_maximum_fusion.5), channel_id=1, source_target_pairs={{1,0},{2,1},{3,2},{4,3},{5,4},{6,5},{7,6},{8,7},{9,8},{10,9},{11,1... | collective-permute-start | bytes 499208 | tf_op jit(solution)/shard_map/ppermute | solution.py:60
  53.9 2.7 %collective-permute-done.4 = f32[65,80,8]{1,2,0:T(8,128)S(1)} collective-permute-done((f32[65,80,8]{1,2,0:T(8,128)S(1)}, f32[65,80,8]{1,2,0:T(8,128)S(1)}, u32[]{:S(2)}, u32[]{:S(2)}) %collective-permute-start.4) | collective-permute-done | bytes 166432 | tf_op jit(solution)/shard_map/ppermute | solution.py:59
  57.8 16.0 %conditional.1 = (f32[8,64,256]{2,1,0:T(8,128)S(1)}) conditional(s32[]{:T(128)} %convert_element_type.13, (s32[64]{0:T(128)S(1)}, s32[5]{0:T(128)S(1)}, f32[8,36,5,256]{3,1,2,0:T(8,128)S(1)}, f32[5,64,5,256]{3,1,2,0:T(8,128)}) %tuple.77, (f32[4,64,256]{2,1,0:T(8,128)}, f32[8,36,68]{2,0,1:T(8,128)S(1)}, s32[4,64,256]{2,1,0:T(8,128)S(1)}) %tuple.78), branch_computations={%region_2.4_spmd, %region_4.6_spmd} | conditional | flops 6424832 | bytes 48769564 | solution.py:236
  58.5 6.0 %gather_fusion = f32[320,8,5,256]{3,1,2,0:T(8,128)} fusion(f32[8,36,5,256]{3,0,2,1:T(8,128)S(1)} %copy.135, s32[1024]{0:T(1024)S(1)} %pad_clamp_fusion), kind=kCustom, calls=%fused_computation | custom fusion | bytes 26215680 | tf_op jit(solution)/shard_map/gather | solution.py:215
  64.5 2.4 %copy.136 = f32[5,64,5,256]{3,2,1,0:T(8,128)S(1)} copy(f32[5,64,5,256]{3,1,2,0:T(8,128)} %get-tuple-element.126) | data formatting | bytes 3276800 | tf_op jit(solution)/shard_map
  67.0 6.5 %multiply_reduce_fusion = f32[64,8,256]{2,1,0:T(8,128)S(1)} fusion(f32[5,64,8,5,256]{4,2,3,1,0:T(8,128)} %bitcast.93, f32[5,64,5,256]{3,2,1,0:T(8,128)S(1)} %copy.136), kind=kLoop, calls=%fused_computation.5 | loop fusion | flops 6422528 | bytes 15269888 | tf_op jit(solution)/shard_map/reduce_sum | solution.py:225
  74.8 1.9 %collective-permute-start.8 = (f32[2,8,256]{2,1,0:T(8,128)S(1)}, f32[2,8,256]{2,1,0:T(8,128)S(1)}, u32[]{:S(2)}, u32[]{:S(2)}) collective-permute-start(f32[2,8,256]{2,1,0:T(8,128)S(1)} %get-tuple-element.165), channel_id=1, source_target_pairs={{16,0},{32,16},{48,32},{64,48},{80,64},{96,80},{112,96},{17,1},{33... | collective-permute-start | bytes 49160 | tf_op jit(solution)/shard_map/ppermute | solution.py:43
  76.9 5.1 %collective-permute-start.9 = (f32[2,8,256]{2,1,0:T(8,128)S(1)}, f32[2,8,256]{2,1,0:T(8,128)S(1)}, u32[]{:S(2)}, u32[]{:S(2)}) collective-permute-start(f32[2,8,256]{2,1,0:T(8,128)S(1)} %get-tuple-element.166), channel_id=1, source_target_pairs={{0,16},{16,32},{32,48},{48,64},{64,80},{80,96},{96,112},{1,17},{17... | collective-permute-start | bytes 49160 | tf_op jit(solution)/shard_map/ppermute | solution.py:42
  82.0 1.7 %copy.139 = f32[65,80,8]{2,1,0:T(8,128)S(1)} copy(f32[65,80,8]{1,2,0:T(8,128)} %copy-done.12) | data formatting | bytes 332800 | tf_op jit(solution)/shard_map/optimization_barrier | solution.py:252
  83.7 2.3 %copy.140 = f32[65,80,8]{2,1,0:T(8,128)} copy(f32[65,80,8]{1,2,0:T(8,128)S(1)} %copy-done.11) | data formatting | bytes 332800 | tf_op jit(solution)/shard_map/optimization_barrier | solution.py:252
  86.4 5.4 %collective-permute-start.10 = (f32[2,80,8]{2,1,0:T(8,128)S(1)}, f32[2,80,8]{2,1,0:T(8,128)S(1)}, u32[]{:S(2)}, u32[]{:S(2)}) collective-permute-start(f32[2,80,8]{2,1,0:T(8,128)S(1)} %pad_maximum_fusion.9), channel_id=1, source_target_pairs={{1,0},{2,1},{3,2},{4,3},{5,4},{6,5},{7,6},{8,7},{9,8},{10,9},{11,1... | collective-permute-start | bytes 15368 | tf_op jit(solution)/shard_map/ppermute | solution.py:60
  91.9 4.0 %pad_maximum_fusion.hc_ref = f32[65,80,128]{2,1,0:T(8,128)} fusion(f32[65,80,8]{2,1,0:T(8,128)} %copy.140, f32[65,80,8]{2,1,0:T(8,128)S(1)} %copy.139, f32[128]{0:T(128)S(1)} %pad.10.clone), kind=kLoop, calls=%fused_computation.37 | loop fusion | flops 1331200 | bytes 2995712 | tf_op jit(solution)/shard_map/concatenate | solution.py:67
  95.9 2.6 %collective-permute-done.11 = f32[2,80,8]{2,1,0:T(8,128)S(1)} collective-permute-done((f32[2,80,8]{2,1,0:T(8,128)S(1)}, f32[2,80,8]{2,1,0:T(8,128)S(1)}, u32[]{:S(2)}, u32[]{:S(2)}) %collective-permute-start.11) | collective-permute-done | bytes 5152 | tf_op jit(solution)/shard_map/ppermute | solution.py:59
  99.2 27.3 %shard_map.95 = f32[2,16,64,256]{3,2,1,0:T(8,128)} custom-call(f32[2,16,64,256]{3,2,1,0:T(8,128)} %tr_ref.1, bf16[16,64,256]{2,1,0:T(8,128)(2,1)} %u_ref.1, bf16[16,64,256]{2,1,0:T(8,128)(2,1)} %v_ref.1, s32[64,256]{1,0:T(8,128)} %m_ref.1, f32[2,64,256]{2,1,0:T(8,128)} %copy-done.6, f32[65,8,256]{2,1,0:T(8,128)} %copy-done.3, ...), custom_call_target="tpu_custom_call" | custom-call | tf_op jit(solution)/shard_map/pallas_call | solution.py:167
  (97 shorter events, 12.2 us)
Async XLA Ops:
  0.6 12.7 %copy-start.9 = (f32[8,2,1024]{2,1,0:T(2,128)S(1)}, f32[8,2,1024]{2,1,0:T(2,128)}, u32[]{:S(2)}) copy-start(f32[8,2,1024]{2,1,0:T(2,128)} %param.12) | copy-start | bytes 196612
  0.6 12.9 %slice-start = ((f32[8,2,1024]{2,1,0:T(2,128)}), f32[8,2,62]{2,1,0:T(2,128)S(1)}, s32[]{:S(2)}) async-start(f32[8,2,1024]{2,1,0:T(2,128)} %param.12), calls=%async_computation.1 | async-start | bytes 16384 | tf_op jit(solution)/shard_map/jit(_roll_static)/slice | solution.py:194
  1.8 20.9 %copy-start = (f32[2,16,64,256]{3,2,1,0:T(8,128)S(1)}, f32[2,16,64,256]{3,2,1,0:T(8,128)}, u32[]{:S(2)}) copy-start(f32[2,16,64,256]{3,2,1,0:T(8,128)} %tr_ref.1) | copy-start | bytes 6291460
  4.6 37.9 %collective-permute-start = (f32[65,8,256]{2,1,0:T(8,128)}, f32[65,8,256]{2,1,0:T(8,128)}, u32[]{:S(2)}, u32[]{:S(2)}) collective-permute-start(f32[65,8,256]{2,1,0:T(8,128)} %pad_maximum_fusion.3), channel_id=1, source_target_pairs={{120,112},{119,113},{118,114},{117,115},{116,116},{115,117},{114,1... | collective-permute-start | bytes 1597448 | tf_op jit(solution)/shard_map/ppermute | solution.py:45
  6.0 39.2 %collective-permute-start.2 = (f32[65,8,256]{2,1,0:T(8,128)}, f32[65,8,256]{2,1,0:T(8,128)}, u32[]{:S(2)}, u32[]{:S(2)}) collective-permute-start(f32[65,8,256]{2,1,0:T(8,128)} %pad_maximum_fusion.3), channel_id=1, source_target_pairs={{0,16},{16,32},{32,48},{48,64},{64,80},{80,96},{96,112},{1,17},{17... | collective-permute-start | bytes 1597448 | tf_op jit(solution)/shard_map/ppermute | solution.py:42
  11.4 32.4 %collective-permute-start.1 = (f32[65,8,256]{2,1,0:T(8,128)}, f32[65,8,256]{2,1,0:T(8,128)}, u32[]{:S(2)}, u32[]{:S(2)}) collective-permute-start(f32[65,8,256]{2,1,0:T(8,128)} %pad_maximum_fusion.4), channel_id=1, source_target_pairs={{16,0},{32,16},{48,32},{64,48},{80,64},{96,80},{112,96},{17,1},{33... | collective-permute-start | bytes 1597448 | tf_op jit(solution)/shard_map/ppermute | solution.py:43
  14.0 10.5 %copy-start.1 = (bf16[16,64,256]{2,1,0:T(8,128)(2,1)S(1)}, bf16[16,64,256]{2,1,0:T(8,128)(2,1)}, u32[]{:S(2)}) copy-start(bf16[16,64,256]{2,1,0:T(8,128)(2,1)} %u_ref.1) | copy-start | bytes 1572868
  14.8 20.9 %all-to-all-start = ((f32[8,2,16,68]{3,1,0,2:T(2,128)}), f32[8,2,16,68]{3,1,0,2:T(2,128)}, u32[]{:S(2)}, u32[]{:S(2)}) async-start(f32[8,2,16,68]{3,1,0,2:T(2,128)} %copy.132), calls=%async_computation | async-start | bytes 262144 | tf_op jit(solution)/shard_map/all_to_all | solution.py:196
  22.7 2.9 %copy-start.2 = (bf16[16,64,256]{2,1,0:T(8,128)(2,1)S(1)}, bf16[16,64,256]{2,1,0:T(8,128)(2,1)}, u32[]{:S(2)}) copy-start(bf16[16,64,256]{2,1,0:T(8,128)(2,1)} %v_ref.1) | copy-start | bytes 1572868
  30.5 2.9 %copy-start.4 = (s32[4,64,256]{2,1,0:T(8,128)S(1)}, s32[4,64,256]{2,1,0:T(8,128)}, u32[]{:S(2)}) copy-start(s32[4,64,256]{2,1,0:T(8,128)} %param.13) | copy-start | bytes 786436
  30.5 3.3 %copy-start.7 = (f32[4,64,256]{2,1,0:T(8,128)S(1)}, f32[4,64,256]{2,1,0:T(8,128)}, u32[]{:S(2)}) copy-start(f32[4,64,256]{2,1,0:T(8,128)} %param.14) | copy-start | bytes 786436
  32.8 11.0 %copy-start.16 = (f32[65]{0:T(128)S(1)}, f32[65]{0:T(128)}, u32[]{:S(2)}) copy-start(f32[65]{0:T(128)} %constant.83.clone.1) | copy-start | bytes 784
  36.6 17.2 %collective-permute-start.5 = (f32[8,2,68]{2,0,1:T(8,128)S(1)}, f32[8,2,68]{2,0,1:T(8,128)S(1)}, u32[]{:S(2)}, u32[]{:S(2)}) collective-permute-start(f32[8,2,68]{2,0,1:T(8,128)S(1)} %get-tuple-element.167), channel_id=1, source_target_pairs={{0,16},{16,32},{32,48},{48,64},{64,80},{80,96},{96,112},{1,17},{17... | collective-permute-start | bytes 13064 | tf_op jit(solution)/shard_map/ppermute | solution.py:198
  40.6 13.3 %collective-permute-start.6 = (f32[8,2,68]{2,0,1:T(8,128)S(1)}, f32[8,2,68]{2,0,1:T(8,128)S(1)}, u32[]{:S(2)}, u32[]{:S(2)}) collective-permute-start(f32[8,2,68]{2,0,1:T(8,128)S(1)} %get-tuple-element.168), channel_id=1, source_target_pairs={{16,0},{32,16},{48,32},{64,48},{80,64},{96,80},{112,96},{17,1},{33... | collective-permute-start | bytes 13064 | tf_op jit(solution)/shard_map/ppermute | solution.py:199
  45.0 3.7 %copy-start.3 = (f32[65,8,256]{2,1,0:T(8,128)}, f32[65,8,256]{2,1,0:T(8,128)S(1)}, u32[]{:S(2)}) copy-start(f32[65,8,256]{2,1,0:T(8,128)S(1)} %multiply_select_fusion.hn_ref) | copy-start | bytes 1597444
  46.8 9.8 %collective-permute-start.4 = (f32[65,80,8]{1,2,0:T(8,128)S(1)}, f32[65,80,8]{1,2,0:T(8,128)S(1)}, u32[]{:S(2)}, u32[]{:S(2)}) collective-permute-start(f32[65,80,8]{1,2,0:T(8,128)S(1)} %pad_maximum_fusion.6), channel_id=1, source_target_pairs={{0,1},{1,2},{2,3},{3,4},{4,5},{5,6},{6,7},{7,8},{8,9},{9,10},{10,1... | collective-permute-start | bytes 499208 | tf_op jit(solution)/shard_map/ppermute | solution.py:59
  48.9 8.1 %collective-permute-start.3 = (f32[65,80,8]{1,2,0:T(8,128)S(1)}, f32[65,80,8]{1,2,0:T(8,128)S(1)}, u32[]{:S(2)}, u32[]{:S(2)}) collective-permute-start(f32[65,80,8]{1,2,0:T(8,128)S(1)} %pad_maximum_fusion.5), channel_id=1, source_target_pairs={{1,0},{2,1},{3,2},{4,3},{5,4},{6,5},{7,6},{8,7},{9,8},{10,9},{11,1... | collective-permute-start | bytes 499208 | tf_op jit(solution)/shard_map/ppermute | solution.py:60
  56.6 1.2 copy-start.10
  57.0 0.8 copy-start.12
  57.8 16.1 %copy-start.15 = (f32[2,8]{1,0:T(2,128)S(1)}, f32[2,8]{1,0:T(2,128)}, u32[]{:S(2)}) copy-start(f32[2,8]{1,0:T(2,128)} %param.15) | copy-start | bytes 196
  73.8 3.0 %copy-start.5 = (f32[8,64,256]{2,1,0:T(8,128)}, f32[8,64,256]{2,1,0:T(8,128)S(1)}, u32[]{:S(2)}) copy-start(f32[8,64,256]{2,1,0:T(8,128)S(1)} %get-tuple-element.132) | copy-start | bytes 1572868
  73.8 9.9 %copy-start.11 = (f32[65,80,8]{1,2,0:T(8,128)S(1)}, f32[65,80,8]{1,2,0:T(8,128)}, u32[]{:S(2)}) copy-start(f32[65,80,8]{1,2,0:T(8,128)} %copy-done.10) | copy-start | bytes 499204
  74.0 12.0 %copy-start.6 = (f32[2,64,256]{2,1,0:T(8,128)}, f32[2,64,256]{2,1,0:T(8,128)S(1)}, u32[]{:S(2)}) copy-start(f32[2,64,256]{2,1,0:T(8,128)S(1)} %multiply_reduce_fusion.1.f_ref) | copy-start | bytes 393220
  74.0 12.0 %collective-permute-start.7 = (f32[2,8,256]{2,1,0:T(8,128)S(1)}, f32[2,8,256]{2,1,0:T(8,128)S(1)}, u32[]{:S(2)}, u32[]{:S(2)}) collective-permute-start(f32[2,8,256]{2,1,0:T(8,128)S(1)} %get-tuple-element.166), channel_id=1, source_target_pairs={{120,112},{119,113},{118,114},{117,115},{116,116},{115,117},{114,1... | collective-permute-start | bytes 49160 | tf_op jit(solution)/shard_map/ppermute | solution.py:45
  74.8 11.3 %collective-permute-start.8 = (f32[2,8,256]{2,1,0:T(8,128)S(1)}, f32[2,8,256]{2,1,0:T(8,128)S(1)}, u32[]{:S(2)}, u32[]{:S(2)}) collective-permute-start(f32[2,8,256]{2,1,0:T(8,128)S(1)} %get-tuple-element.165), channel_id=1, source_target_pairs={{16,0},{32,16},{48,32},{64,48},{80,64},{96,80},{112,96},{17,1},{33... | collective-permute-start | bytes 49160 | tf_op jit(solution)/shard_map/ppermute | solution.py:43
  76.9 9.4 %collective-permute-start.9 = (f32[2,8,256]{2,1,0:T(8,128)S(1)}, f32[2,8,256]{2,1,0:T(8,128)S(1)}, u32[]{:S(2)}, u32[]{:S(2)}) collective-permute-start(f32[2,8,256]{2,1,0:T(8,128)S(1)} %get-tuple-element.166), channel_id=1, source_target_pairs={{0,16},{16,32},{32,48},{48,64},{64,80},{80,96},{96,112},{1,17},{17... | collective-permute-start | bytes 49160 | tf_op jit(solution)/shard_map/ppermute | solution.py:42
  86.2 9.7 %copy-start.13 = (f32[2,8,256]{2,1,0:T(8,128)}, f32[2,8,256]{2,1,0:T(8,128)S(1)}, u32[]{:S(2)}) copy-start(f32[2,8,256]{2,1,0:T(8,128)S(1)} %broadcast_select_fusion.fn_ref) | copy-start | bytes 49156
  86.3 9.6 %copy-start.14 = (f32[2,8,256]{2,1,0:T(8,128)}, f32[2,8,256]{2,1,0:T(8,128)S(1)}, u32[]{:S(2)}) copy-start(f32[2,8,256]{2,1,0:T(8,128)S(1)} %collective-permute-done.9.fs_ref) | copy-start | bytes 49156
  86.4 9.5 %collective-permute-start.10 = (f32[2,80,8]{2,1,0:T(8,128)S(1)}, f32[2,80,8]{2,1,0:T(8,128)S(1)}, u32[]{:S(2)}, u32[]{:S(2)}) collective-permute-start(f32[2,80,8]{2,1,0:T(8,128)S(1)} %pad_maximum_fusion.9), channel_id=1, source_target_pairs={{1,0},{2,1},{3,2},{4,3},{5,4},{6,5},{7,6},{8,7},{9,8},{10,9},{11,1... | collective-permute-start | bytes 15368 | tf_op jit(solution)/shard_map/ppermute | solution.py:60
  91.8 6.7 %collective-permute-start.11 = (f32[2,80,8]{2,1,0:T(8,128)S(1)}, f32[2,80,8]{2,1,0:T(8,128)S(1)}, u32[]{:S(2)}, u32[]{:S(2)}) collective-permute-start(f32[2,80,8]{2,1,0:T(8,128)S(1)} %pad_maximum_fusion.10), channel_id=1, source_target_pairs={{0,1},{1,2},{2,3},{3,4},{4,5},{5,6},{6,7},{7,8},{8,9},{9,10},{10,1... | collective-permute-start | bytes 15368 | tf_op jit(solution)/shard_map/ppermute | solution.py:59
